TPU v7x, 32 devices: a whole 2x2x4 slice. The times are simulated.
32 devices in a mesh: tok: 8 (over z, x), hv: 4 (over y, core).
Axes of the slice: x: 2, y: 2, z: 4, core: 2. Of those that a mesh axis runs over, the one named last changes fastest.
Arguments:
- tokens: bfloat16 [2048, 2048], P(('tok', 'hv')), may hold values from -6 to 6
- prompt_lengths: int32 [5], replicated, may hold values from 1 to 1365, 2048 in all
- query_weight: bfloat16 [2048, 1024], P(None, 'hv'), may hold values from -0.125 to 0.125
- key_weight: bfloat16 [2048, 1024], P(None, 'hv'), may hold values from -0.125 to 0.125
- value_weight: bfloat16 [2048, 2048], P(None, 'hv'), may hold values from -0.125 to 0.125
- query_conv: bfloat16 [4, 1024], P(None, 'hv'), may hold values from -3 to 3
- key_conv: bfloat16 [4, 1024], P(None, 'hv'), may hold values from -3 to 3
- value_conv: bfloat16 [4, 2048], P(None, 'hv'), may hold values from -3 to 3
- decay_down: bfloat16 [2048, 16], replicated, may hold values from -0.125 to 0.125
- decay_up: bfloat16 [16, 1024], P(None, 'hv'), may hold values from -3 to 3
- decay_bias: float32 [1024], P('hv')
- gate_weight: bfloat16 [2048, 2048], P(None, 'hv'), may hold values from -0.125 to 0.125
- norm_gain: float32 [512], replicated, may hold values from 0.1 to 1.9
- out_weight: bfloat16 [2048, 2048], P('hv'), may hold values from -0.125 to 0.125
Outputs:
- mixed: bfloat16 [2048, 2048], P(('tok', 'hv'))
- segment_states: float32 [8, 4, 256, 512], P('tok', 'hv')
- conv_edges: bfloat16 [8, 3, 4, 1024], P('tok', None, 'hv')
Inputs may be any that keep to these rules, and one draw needn't show every extreme that they name: `prompt_lengths`: the rows of 5 prompts that fill all 2048 packed rows; exactly one prompt has 1365 rows.
All inputs are finite; a program needn't handle non-finite values.
Results may differ from a plain program's by a relative error of at most 0.022.
Values may be sent and summed in bfloat16 or wider, within the bound.
No kernel may reach another device: no remote copies, remote signals or barrier semaphores. Data moves between devices by JAX's collectives and lax.ppermute only.
A program may use at most 128 MiB of HBM per device.

v0:
```python
import jax
import jax.numpy as jnp
from jax import lax
from jax.sharding import PartitionSpec as P

SPAN = 64


HIGHEST_PRECISION = lax.Precision.HIGHEST


def shifted(value, axis, steps):
    count = lax.axis_size(axis)
    initial, last = (max(0, -steps), min(count, count - steps))
    return lax.ppermute(value, axis, [(source, source + steps) for source in range(initial, last)])


def carried_in(part, axis, combine, identity):
    place = lax.axis_index(axis)
    gathered = jax.tree.map(lambda a: lax.all_gather(a, axis), part)
    state = jax.tree.map(lambda a, e: jnp.zeros_like(a) + jnp.asarray(e, a.dtype), part, identity)

    def one(lap, state):
        return combine(
            state, jax.tree.map(lambda a: lax.dynamic_index_in_dim(a, lap, 0, False), gathered)
        )

    return lax.fori_loop(0, place, one, state)


def prompt_marks(positions, offsets):
    before = offsets[None, :] <= positions[:, None]
    prompt_first = jnp.max(jnp.where(before, offsets[None, :], 0), axis=1)
    return (prompt_first, (prompt_first == positions).astype(jnp.float32))


def short_conv(raw_rows, before_rows, weight, positions, prompt_first):
    tap_count = weight.shape[0]
    extended = jnp.concatenate([before_rows, raw_rows], axis=0)
    summed = jnp.zeros(raw_rows.shape, jnp.float32)
    for tap_index in range(tap_count):
        lag_rows = tap_count - 1 - tap_index
        inside_prompt = (positions - lag_rows >= prompt_first).astype(jnp.float32)
        window = lax.slice_in_dim(extended, tap_index, tap_index + raw_rows.shape[0], axis=0)
        summed = (
            summed
            + weight[tap_index].astype(jnp.float32)[None, :]
            * window.astype(jnp.float32)
            * inside_prompt[:, None]
        )
    return jax.nn.silu(summed).astype(jnp.bfloat16)


def span_parts(head_keys, head_values, decays, starts):
    cumulative = jnp.cumsum(decays, axis=0)
    groups = jnp.cumsum(starts)
    intact = (groups == 0.0).astype(jnp.float32)
    final_log = cumulative[-1]
    in_tail = (groups == groups[-1]).astype(jnp.float32)
    weighted = (
        head_keys.astype(jnp.float32) * jnp.exp(final_log[None, :] - cumulative) * in_tail[:, None]
    ).astype(jnp.bfloat16)
    update = lax.dot_general(
        weighted, head_values, (((0,), (0,)), ((), ())), preferred_element_type=jnp.float32
    )
    step_decay = jnp.exp(final_log) * intact[-1]
    return (cumulative, groups, intact, update, step_decay)


def state_step(carried, pieces):
    memory, product = carried
    head_keys, head_values, decays, starts = pieces
    _, _, _, update, step_decay = span_parts(head_keys, head_values, decays, starts)
    return ((step_decay[:, None] * memory + update, product * step_decay), None)


def span_step(carried, pieces):
    memory, product = carried
    queries, head_keys, head_values, decays, starts = pieces
    cumulative, groups, intact, update, step_decay = span_parts(
        head_keys, head_values, decays, starts
    )
    index_rows = jnp.arange(queries.shape[0])
    allowed = (groups[:, None] == groups[None, :]) & (index_rows[:, None] >= index_rows[None, :])
    lifted = queries.astype(jnp.float32) * jnp.exp(cumulative)
    lowered = (head_keys.astype(jnp.float32) * jnp.exp(-cumulative)).astype(jnp.bfloat16)
    raw_scores = lax.dot_general(
        lifted.astype(jnp.bfloat16),
        lowered,
        (((1,), (1,)), ((), ())),
        preferred_element_type=jnp.float32,
    )
    scores = jnp.where(allowed, raw_scores, 0.0).astype(jnp.bfloat16)
    inside = jnp.dot(scores, head_values, preferred_element_type=jnp.float32)
    outside = jnp.dot(lifted * intact[:, None], memory, precision=HIGHEST_PRECISION)
    reaches = product[None, :] * jnp.exp(cumulative) * intact[:, None]
    return (
        (step_decay[:, None] * memory + update, product * step_decay),
        (inside + outside, reaches),
    )


def blocked(array_in):
    return array_in.reshape((array_in.shape[0] // SPAN, SPAN) + array_in.shape[1:])


def sweep(queries, head_keys, head_values, decays, starts, memory):
    initial = (memory, jnp.ones((decays.shape[1],), jnp.float32))
    (closing, product), (outputs, reaches) = lax.scan(
        span_step,
        initial,
        (
            blocked(queries),
            blocked(head_keys),
            blocked(head_values),
            blocked(decays),
            blocked(starts),
        ),
    )
    row_count = queries.shape[0]
    return (
        outputs.reshape((row_count, head_values.shape[1])),
        reaches.reshape((row_count, decays.shape[1])),
        closing,
        product,
    )


def combine(earlier, following):
    return (earlier[0] * following[0], following[0][:, None] * earlier[1] + following[1])


def shards(
    tokens,
    prompt_lengths,
    query_weight,
    key_weight,
    value_weight,
    query_conv,
    key_conv,
    value_conv,
    decay_down,
    decay_up,
    decay_bias,
    gate_weight,
    norm_gain,
    out_weight,
):
    gathered = lax.all_gather(tokens, "hv", axis=0, tiled=True)

    def project(weight):
        return jnp.dot(gathered, weight, preferred_element_type=jnp.float32).astype(jnp.bfloat16)

    raw_query = project(query_weight)
    raw_key = project(key_weight)
    raw_value = project(value_weight)
    gate_values = project(gate_weight)
    low_rank = project(decay_down)
    row_count = raw_query.shape[0]
    key_width = raw_query.shape[1]
    value_width = raw_value.shape[1]
    positions = lax.axis_index("tok") * row_count + jnp.arange(row_count, dtype=jnp.int32)
    offsets = jnp.cumsum(prompt_lengths) - prompt_lengths
    prompt_first, starts = prompt_marks(positions, offsets)
    rim_rows = query_conv.shape[0] - 1
    joined = jnp.concatenate([raw_query, raw_key, raw_value], axis=1)
    before_rows = shifted(joined[row_count - rim_rows :], "tok", 1)
    conv_query = short_conv(
        raw_query, before_rows[:, :key_width], query_conv, positions, prompt_first
    )
    conv_key = short_conv(
        raw_key, before_rows[:, key_width : 2 * key_width], key_conv, positions, prompt_first
    )
    conv_value = short_conv(
        raw_value, before_rows[:, 2 * key_width :], value_conv, positions, prompt_first
    )
    decays = (
        jax.nn.log_sigmoid(
            jnp.dot(low_rank, decay_up, preferred_element_type=jnp.float32) + decay_bias
        )
        / 16.0
    )
    empty_memory = jnp.zeros((key_width, value_width), jnp.float32)
    ones_decay = jnp.ones((key_width,), jnp.float32)
    (local_memory, local_decay), _ = lax.scan(
        state_step,
        (empty_memory, ones_decay),
        (blocked(conv_key), blocked(conv_value), blocked(decays), blocked(starts)),
    )
    entering_decay, entering = carried_in(
        (local_decay, local_memory), "tok", combine, (ones_decay, empty_memory)
    )
    heads_out, _, closing, _ = sweep(conv_query, conv_key, conv_value, decays, starts, entering)
    gate_float = gate_values.astype(jnp.float32)
    rescale = lax.rsqrt(jnp.mean(heads_out * heads_out, axis=1, keepdims=True) + 1e-05)
    gated_out = (
        heads_out * rescale * norm_gain[None, :] * gate_float * jax.nn.sigmoid(gate_float)
    ).astype(jnp.bfloat16)
    mixed = lax.psum_scatter(
        jnp.dot(gated_out, out_weight, preferred_element_type=jnp.float32).astype(jnp.bfloat16),
        "hv",
        scatter_dimension=0,
        tiled=True,
    )
    segment_states = closing[None, None]
    in_prompt = positions[row_count - rim_rows :] >= prompt_first[row_count - 1]
    tail_rows = joined[row_count - rim_rows :]
    conv_edges = jnp.where(in_prompt[:, None], tail_rows, jnp.zeros_like(tail_rows))
    conv_edges = conv_edges.reshape((1, rim_rows, 1, joined.shape[1]))
    return (mixed, segment_states, conv_edges)


def solution(mesh):
    in_specs = (
        P(("tok", "hv"), None),
        P(),
        P(None, "hv"),
        P(None, "hv"),
        P(None, "hv"),
        P(None, "hv"),
        P(None, "hv"),
        P(None, "hv"),
        P(),
        P(None, "hv"),
        P("hv"),
        P(None, "hv"),
        P(),
        P("hv", None),
    )
    out_specs = (P(("tok", "hv"), None), P("tok", "hv", None, None), P("tok", None, "hv", None))
    return jax.shard_map(shards, mesh=mesh, in_specs=in_specs, out_specs=out_specs, check_vma=False)
```

profile of v0, /device:TPU:24, one launch (start us, length us, event | category | flops | bytes accessed | tf_op | source)
XLA Modules:
  0.0 200.0 jit_solution(11787991160110611997)
XLA Ops:
  7.2 0.7 all-gather.6.cloned.1.call-update
  8.0 0.8 reduce-window.15
  10.2 0.7 slice_compare_fusion
  11.5 1.4 slice_convert_fusion.11
  13.0 0.8 slice_convert_fusion.3
  13.8 13.4 %all-gather.6.cloned.1.call-done = bf16[256,2048]{1,0:T(8,128)(2,1)} async-done(((bf16[64,2048]{1,0:T(8,128)(2,1)}), bf16[256,2048]{1,0:T(8,128)(2,1)}) %all-gather.6.cloned.1.call-update) | async-done | bytes 1048592 | tf_op jit(solution)/shard_map/all_gather | solution.py:149
  27.3 2.8 %convolution_convert_fusion.2 = bf16[256,512]{1,0:T(8,128)(2,1)S(1)} fusion(bf16[256,2048]{1,0:T(8,128)(2,1)} %all-gather.6.cloned.1.call-done, bf16[2048,512]{1,0:T(8,128)(2,1)} %param.24), kind=kOutput, calls=%fused_computation.77 | convolution fusion | flops 537001984 | bytes 3407872 | tf_op jit(solution)/shard_map/dot_general | solution.py:152
  31.7 3.4 %collective-permute-start = (bf16[3,1024]{1,0:T(4,128)(2,1)S(1)}, bf16[3,1024]{1,0:T(4,128)(2,1)S(1)}, u32[]{:S(2)}, u32[]{:S(2)}) collective-permute-start(bf16[3,1024]{1,0:T(4,128)(2,1)S(1)} %get-tuple-element.200), channel_id=1, source_target_pairs={{0,4},{4,8},{8,12},{12,16},{16,20},{20,24},{24,28},{1,5},{5,9},{9,... | collective-permute-start | bytes 18440 | tf_op jit(solution)/shard_map/ppermute | solution.py:15
  35.1 2.0 %fusion.69 = f32[256,256]{1,0:T(8,128)S(1)} fusion(bf16[16,256]{1,0:T(8,128)(2,1)S(1)} %copy-done.10, bf16[256,2048]{1,0:T(8,128)(2,1)} %all-gather.6.cloned.1.call-done, bf16[2048,16]{0,1:T(8,128)(2,1)S(1)} %copy-done.9, f32[256]{0:T(256)S(1)} %copy-done.12), kind=kOutput, calls=%fused_computation.97 | convolution fusion | flops 19533824 | bytes 1385472 | tf_op jit(solution)/shard_map/dot_general | solution.py:179
  37.1 1.0 collective-permute-done
  38.1 2.0 multiply_convert_fusion
  40.7 0.9 multiply_convert_fusion.2
  41.6 13.3 %while.39 = (s32[]{:T(128)}, f32[256,512]{1,0:T(8,128)S(1)}, f32[256]{0:T(256)S(1)}, f32[4,64,256]{2,1,0:T(8,128)S(1)}, f32[4,64]{1,0:T(4,128)}, /*index=5*/bf16...) while((s32[]{:T(128)}, f32[256,512]{1,0:T(8,128)S(1)}, ...), condition=%wide.region_5.6_spmd.clone, body=%wide.region_2.5_spmd.clone.sunk | while | flops 18289476 | bytes 1486494 | solution.py:185
  41.8 0.7 fusion.115
  43.8 0.8 convert_reduce_fusion.2
  45.1 0.7 fusion.115
  47.2 0.8 convert_reduce_fusion.2
  48.4 0.7 fusion.115
  50.5 0.8 convert_reduce_fusion.2
  51.7 0.7 fusion.115
  53.8 0.8 convert_reduce_fusion.2
  54.9 0.8 copy-done.2
  55.8 0.8 slice_convert_fusion.7
  56.6 15.5 %all-gather.2 = f32[8,1,256]{2,1,0:T(1,128)S(1)} all-gather(f32[1,1,256]{2,1,0:T(1,128)S(1)} %bitcast.206), channel_id=2, replica_groups=mesh['tok'=8,'hv'=4] {'tok'}, dimensions={0}, use_global_device_ids=true | all-gather | bytes 9216 | tf_op jit(solution)/shard_map/all_gather | solution.py:20
  72.1 1.7 multiply_convert_fusion.1
  73.8 52.6 %all-gather.8.cloned.1.call-done = f32[2048,512]{1,0:T(8,128)} async-done(((f32[256,512]{1,0:T(8,128)}), f32[2048,512]{1,0:T(8,128)}) %all-gather.8.cloned.1.call-update) | async-done | bytes 4194320 | tf_op jit(solution)/shard_map/all_gather | solution.py:20
  126.4 7.4 %while.37 = (s32[]{:T(128)}, f32[256,512]{1,0:T(8,128)S(1)}, s32[]{:T(128)}, f32[8,256]{1,0:T(8,128)S(1)}, f32[8,256,512]{2,1,0:T(8,128)}, /*index=5*/s32[]{:T(128)}, s32[]{:T(128)}, s32[]{:T(128)}) while((s32[]{:T(128)}, f32[256,512]{1,0:T(8,128)S(1)}, s32[]{:T(128)}, f32[8,256]{1,0:T(8,128)S(1)}, f32[8,256,512]{2,1,0:T(8,128)}, ...), condition=%wide.region_7.8_spmd, body=%wide.region_6.7_spmd.sunk | while | flops 262149 | bytes 1576063 | solution.py:28
  126.4 1.2 bitcast_add_fusion.2
  127.7 1.2 bitcast_add_fusion.2
  128.9 1.2 bitcast_add_fusion.2
  130.1 1.2 bitcast_add_fusion.2
  131.4 1.2 bitcast_add_fusion.2
  132.6 1.2 bitcast_add_fusion.2
  133.8 27.4 %while.38 = (s32[]{:T(128)}, f32[256,512]{1,0:T(8,128)S(1)}, f32[4,64,512]{2,1,0:T(8,128)}, f32[4,64,256]{2,1,0:T(8,128)S(1)}, f32[4,64]{1,0:T(4,128)}, /*index=...) while((s32[]{:T(128)}, f32[256,512]{1,0:T(8,128)S(1)}, ...), condition=%wide.region_11.12_spmd, body=%wide.region_8.11_spmd.sunk | while | flops 125329856 | bytes 2767001 | solution.py:109
  134.0 0.7 fusion.110
  134.9 1.0 fusion.111
  137.2 1.9 fusion.112
  140.8 0.7 fusion.110
  141.8 1.0 fusion.111
  144.0 1.9 fusion.112
  148.7 1.0 fusion.111
  150.9 1.9 fusion.112
  155.5 1.0 fusion.111
  157.7 1.9 fusion.112
  161.3 1.3 multiply_reduce_fusion
  162.7 2.8 %fusion.65 = bf16[256,512]{1,0:T(8,128)(2,1)S(1)} fusion(f32[4,64,512]{2,1,0:T(8,128)} %get-tuple-element.131, bf16[256,2048]{1,0:T(8,128)(2,1)} %all-gather.6.cloned.1.call-done, bf16[2048,512]{1,0:T(8,128)(2,1)} %param.31, f32[512]{0:T(512)S(1)} %copy-done.11, f32[256]{0:T(256)S(1)} %rsqrt.12), kind=kOutput, calls=%fused_computation.89 | convolution fusion | flops 538181632 | bytes 3935232 | tf_op jit(solution)/shard_map/dot_general | solution.py:152
  165.5 1.7 convolution_convert_fusion
  167.2 26.2 %reduce-scatter.2.cloned.1.call-done = bf16[64,2048]{1,0:T(8,128)(2,1)} async-done(((bf16[256,2048]{1,0:T(8,128)(2,1)}), bf16[64,2048]{1,0:T(8,128)(2,1)}) %reduce-scatter.2.cloned.1.call-update) | async-done | bytes 262160 | tf_op jit(solution)/shard_map/reduce_scatter | solution.py:199
  (133 shorter events, 23.4 us)
Async XLA Ops:
  7.2 158.4 %copy-start = (bf16[512,2048]{1,0:T(8,128)(2,1)S(1)}, bf16[512,2048]{1,0:T(8,128)(2,1)}, u32[]{:S(2)}) copy-start(bf16[512,2048]{1,0:T(8,128)(2,1)} %param.33) | copy-start | bytes 6291460
  7.2 20.1 %all-gather.6.cloned.1.call-start = ((), (), s32[]{:S(2)}) async-start(), calls=%async_computation.1 | async-start | bytes 1310720 | tf_op jit(solution)/shard_map/all_gather | solution.py:149
  7.9 118.4 %all-gather.8.cloned.1.call-start = ((), (), s32[]{:S(2)}) async-start(), calls=%async_computation.3 | async-start | bytes 4718592 | tf_op jit(solution)/shard_map/all_gather | solution.py:20
  11.5 26.6 %copy-start.8 = (f32[256]{0:T(256)}, f32[256]{0:T(256)S(1)}, u32[]{:S(2)}) copy-start(f32[256]{0:T(256)S(1)} %get-tuple-element.220) | copy-start | bytes 3076
  11.5 29.2 %copy-start.7 = (f32[256]{0:T(256)}, f32[256]{0:T(256)S(1)}, u32[]{:S(2)}) copy-start(f32[256]{0:T(256)S(1)} %get-tuple-element.219) | copy-start | bytes 3076
  27.3 2.8 %copy-start.3 = (bf16[256,2048]{1,0:T(8,128)(2,1)S(1)}, bf16[256,2048]{1,0:T(8,128)(2,1)}, u32[]{:S(2)}) copy-start(bf16[256,2048]{1,0:T(8,128)(2,1)} %all-gather.6.cloned.1.call-done) | copy-start | bytes 3145732
  27.3 2.8 %copy-start.5 = (bf16[2048,256]{1,0:T(8,128)(2,1)S(1)}, bf16[2048,256]{1,0:T(8,128)(2,1)}, u32[]{:S(2)}) copy-start(bf16[2048,256]{1,0:T(8,128)(2,1)} %param.23) | copy-start | bytes 3145732
  27.3 3.3 %copy-start.6 = (bf16[2048,256]{1,0:T(8,128)(2,1)S(1)}, bf16[2048,256]{1,0:T(8,128)(2,1)}, u32[]{:S(2)}) copy-start(bf16[2048,256]{1,0:T(8,128)(2,1)} %param.22) | copy-start | bytes 3145732
  30.0 1.0 copy-start.4
  30.1 5.0 %copy-start.9 = (bf16[2048,16]{0,1:T(8,128)(2,1)S(1)}, bf16[2048,16]{0,1:T(8,128)(2,1)}, u32[]{:S(2)}) copy-start(bf16[2048,16]{0,1:T(8,128)(2,1)} %param.28) | copy-start | bytes 196612
  30.1 5.0 %copy-start.10 = (bf16[16,256]{1,0:T(8,128)(2,1)S(1)}, bf16[16,256]{1,0:T(8,128)(2,1)}, u32[]{:S(2)}) copy-start(bf16[16,256]{1,0:T(8,128)(2,1)} %param.29) | copy-start | bytes 24580
  30.1 5.0 %copy-start.12 = (f32[256]{0:T(256)S(1)}, f32[256]{0:T(256)}, u32[]{:S(2)}) copy-start(f32[256]{0:T(256)} %param.30) | copy-start | bytes 3076
  31.7 6.4 %collective-permute-start = (bf16[3,1024]{1,0:T(4,128)(2,1)S(1)}, bf16[3,1024]{1,0:T(4,128)(2,1)S(1)}, u32[]{:S(2)}, u32[]{:S(2)}) collective-permute-start(bf16[3,1024]{1,0:T(4,128)(2,1)S(1)} %get-tuple-element.200), channel_id=1, source_target_pairs={{0,4},{4,8},{8,12},{12,16},{16,20},{20,24},{24,28},{1,5},{5,9},{9,... | collective-permute-start | bytes 18440 | tf_op jit(solution)/shard_map/ppermute | solution.py:15
  54.9 0.8 copy-start.2
  55.7 137.7 %reduce-scatter.2.cloned.1.call-start = ((), (), s32[]{:S(2)}) async-start(), calls=%async_computation.2 | async-start | bytes 1310720 | tf_op jit(solution)/shard_map/reduce_scatter | solution.py:199
  133.8 28.9 %copy-start.11 = (f32[512]{0:T(512)S(1)}, f32[512]{0:T(512)}, u32[]{:S(2)}) copy-start(f32[512]{0:T(512)} %param.32) | copy-start | bytes 6148
  161.3 4.2 %copy-start.1 = (f32[256,512]{1,0:T(8,128)}, f32[256,512]{1,0:T(8,128)S(1)}, u32[]{:S(2)}) copy-start(f32[256,512]{1,0:T(8,128)S(1)} %get-tuple-element.132) | copy-start | bytes 1572868
Sparse Core Ops, SparseCore 0:
  9.5 17.6 all-gather.5
  55.8 70.4 all-gather.7
  167.4 26.0 reduce-scatter.1
where the time goes:
time: 203 us; the launch traced here: 200 us
  waiting for transfers between devices  93.9 us (46%)
  other arithmetic  30 us (15%)
  matrix products  24.7 us (12%)
  blocking collectives  15.5 us (8%)
  local copies, waits for them, and re-layouts  15.1 us (7%)
  between operations  14 us (7%)
  starting transfers between devices  3.48 us (2%)
  loops' own time  3.26 us (2%)
    all_gather x1, waiting for transfers between devices, carried_in(): gathered = jax.tree.map(lambda a: lax.all_gather(a, axis), part)  52.6 us
    reduce_scatter x1, waiting for transfers between devices, shards(): lax.psum_scatter(jnp.dot(gated_out, out_weight, preferred_element_type=jn...  26.2 us
    all_gather x1, blocking collectives, carried_in(): gathered = jax.tree.map(lambda a: lax.all_gather(a, axis), part)  15.5 us
    all_gather x1, waiting for transfers between devices, shards(): gathered = lax.all_gather(tokens, 'hv', axis=0, tiled=True)  13.4 us
    dot_general x4, matrix products, span_step(): jnp.dot(lifted * intact[:, None], memory, precision=HIGHEST_PRECISION)  7.54 us
    add x6, other arithmetic, combine(): following[0][:, None] * earlier[1] + following[1]  7.13 us
    dot_general x4, matrix products, project(): jnp.dot(gathered, weight, preferred_element_type=jnp.float32)  6.41 us
    convert_element_type x8, other arithmetic, span_parts(): in_tail = (groups == groups[-1]).astype(jnp.float32)  5.59 us
  transfers between devices with their start and end apart: 4, of which 4 were waited for; matrix products, arithmetic and copies ran while one was open for 5% of the time, Pallas kernels for 0%

commit v1 on v0

v1 whole, which is shorter than its diff:
```python
import jax
import jax.numpy as jnp
from jax import lax
from jax.sharding import PartitionSpec as P

SPAN = 64


HIGHEST_PRECISION = lax.Precision.HIGHEST


def shifted(value, axis, steps):
    count = lax.axis_size(axis)
    initial, last = (max(0, -steps), min(count, count - steps))
    return lax.ppermute(value, axis, [(source, source + steps) for source in range(initial, last)])


def prompt_marks(positions, offsets):
    before = offsets[None, :] <= positions[:, None]
    prompt_first = jnp.max(jnp.where(before, offsets[None, :], 0), axis=1)
    return (prompt_first, (prompt_first == positions).astype(jnp.float32))


def short_conv(raw_rows, before_rows, weight, positions, prompt_first):
    tap_count = weight.shape[0]
    extended = jnp.concatenate([before_rows, raw_rows], axis=0)
    summed = jnp.zeros(raw_rows.shape, jnp.float32)
    for tap_index in range(tap_count):
        lag_rows = tap_count - 1 - tap_index
        inside_prompt = (positions - lag_rows >= prompt_first).astype(jnp.float32)
        window = lax.slice_in_dim(extended, tap_index, tap_index + raw_rows.shape[0], axis=0)
        summed = (
            summed
            + weight[tap_index].astype(jnp.float32)[None, :]
            * window.astype(jnp.float32)
            * inside_prompt[:, None]
        )
    return jax.nn.silu(summed).astype(jnp.bfloat16)


def blocked(array_in):
    return array_in.reshape((array_in.shape[0] // SPAN, SPAN) + array_in.shape[1:])


def segment_parts(queries, head_keys, head_values, decays, starts):
    cumulative = jnp.cumsum(decays, axis=1)
    groups = jnp.cumsum(starts, axis=1)
    intact = (groups == 0.0).astype(jnp.float32)
    final_log = cumulative[:, -1]
    in_tail = (groups == groups[:, -1:]).astype(jnp.float32)
    weighted = (
        head_keys.astype(jnp.float32)
        * jnp.exp(final_log[:, None, :] - cumulative)
        * in_tail[:, :, None]
    ).astype(jnp.bfloat16)
    update = jnp.einsum("bsk,bsv->bkv", weighted, head_values, preferred_element_type=jnp.float32)
    step_decay = jnp.exp(final_log) * intact[:, -1:]
    index_rows = jnp.arange(queries.shape[1])
    allowed = (groups[:, :, None] == groups[:, None, :]) & (
        index_rows[None, :, None] >= index_rows[None, None, :]
    )
    lifted = queries.astype(jnp.float32) * jnp.exp(cumulative)
    lowered = (head_keys.astype(jnp.float32) * jnp.exp(-cumulative)).astype(jnp.bfloat16)
    raw_scores = jnp.einsum(
        "bak,bck->bac", lifted.astype(jnp.bfloat16), lowered, preferred_element_type=jnp.float32
    )
    scores = jnp.where(allowed, raw_scores, 0.0).astype(jnp.bfloat16)
    inside = jnp.einsum("bac,bcv->bav", scores, head_values, preferred_element_type=jnp.float32)
    lifted_intact = lifted * intact[:, :, None]
    block_count = queries.shape[0]
    memory = jnp.zeros(update.shape[1:], jnp.float32)
    product = jnp.ones(step_decay.shape[1:], jnp.float32)
    local_outs = [jnp.zeros(inside.shape[1:], jnp.float32)]
    products = [product]
    for block in range(block_count):
        if block > 0:
            local_outs.append(jnp.dot(lifted_intact[block], memory, precision=HIGHEST_PRECISION))
            products.append(product)
        memory = step_decay[block][:, None] * memory + update[block]
        product = product * step_decay[block]
    local_out = inside + jnp.stack(local_outs)
    carry_lift = lifted_intact * jnp.stack(products)[:, None, :]
    return (local_out, carry_lift, memory, product)


def prefix_states(decay, memory, axis):
    count = lax.axis_size(axis)
    place = lax.axis_index(axis)
    steps = 1
    while steps < count:
        earlier_decay, earlier_memory = shifted((decay, memory), axis, steps)
        valid = place >= steps
        memory = jnp.where(valid, decay[:, None] * earlier_memory + memory, memory)
        decay = jnp.where(valid, earlier_decay * decay, decay)
        steps *= 2
    entering = shifted(memory, axis, 1)
    return (memory, entering)


def shards(
    tokens,
    prompt_lengths,
    query_weight,
    key_weight,
    value_weight,
    query_conv,
    key_conv,
    value_conv,
    decay_down,
    decay_up,
    decay_bias,
    gate_weight,
    norm_gain,
    out_weight,
):
    gathered = lax.all_gather(tokens, "hv", axis=0, tiled=True)

    def project(weight):
        return jnp.dot(gathered, weight, preferred_element_type=jnp.float32).astype(jnp.bfloat16)

    raw_query = project(query_weight)
    raw_key = project(key_weight)
    raw_value = project(value_weight)
    gate_values = project(gate_weight)
    low_rank = project(decay_down)
    row_count = raw_query.shape[0]
    key_width = raw_query.shape[1]
    value_width = raw_value.shape[1]
    positions = lax.axis_index("tok") * row_count + jnp.arange(row_count, dtype=jnp.int32)
    offsets = jnp.cumsum(prompt_lengths) - prompt_lengths
    prompt_first, starts = prompt_marks(positions, offsets)
    rim_rows = query_conv.shape[0] - 1
    joined = jnp.concatenate([raw_query, raw_key, raw_value], axis=1)
    before_rows = shifted(joined[row_count - rim_rows :], "tok", 1)
    conv_query = short_conv(
        raw_query, before_rows[:, :key_width], query_conv, positions, prompt_first
    )
    conv_key = short_conv(
        raw_key, before_rows[:, key_width : 2 * key_width], key_conv, positions, prompt_first
    )
    conv_value = short_conv(
        raw_value, before_rows[:, 2 * key_width :], value_conv, positions, prompt_first
    )
    decays = (
        jax.nn.log_sigmoid(
            jnp.dot(low_rank, decay_up, preferred_element_type=jnp.float32) + decay_bias
        )
        / 16.0
    )
    local_out, carry_lift, local_memory, local_decay = segment_parts(
        blocked(conv_query), blocked(conv_key), blocked(conv_value), blocked(decays), blocked(starts)
    )
    closing, entering = prefix_states(local_decay, local_memory, "tok")
    heads_out = local_out.reshape((row_count, value_width)) + jnp.dot(
        carry_lift.reshape((row_count, key_width)), entering, precision=HIGHEST_PRECISION
    )
    gate_float = gate_values.astype(jnp.float32)
    rescale = lax.rsqrt(jnp.mean(heads_out * heads_out, axis=1, keepdims=True) + 1e-05)
    gated_out = (
        heads_out * rescale * norm_gain[None, :] * gate_float * jax.nn.sigmoid(gate_float)
    ).astype(jnp.bfloat16)
    mixed = lax.psum_scatter(
        jnp.dot(gated_out, out_weight, preferred_element_type=jnp.float32).astype(jnp.bfloat16),
        "hv",
        scatter_dimension=0,
        tiled=True,
    )
    segment_states = closing[None, None]
    in_prompt = positions[row_count - rim_rows :] >= prompt_first[row_count - 1]
    tail_rows = joined[row_count - rim_rows :]
    conv_edges = jnp.where(in_prompt[:, None], tail_rows, jnp.zeros_like(tail_rows))
    conv_edges = conv_edges.reshape((1, rim_rows, 1, joined.shape[1]))
    return (mixed, segment_states, conv_edges)


def solution(mesh):
    in_specs = (
        P(("tok", "hv"), None),
        P(),
        P(None, "hv"),
        P(None, "hv"),
        P(None, "hv"),
        P(None, "hv"),
        P(None, "hv"),
        P(None, "hv"),
        P(),
        P(None, "hv"),
        P("hv"),
        P(None, "hv"),
        P(),
        P("hv", None),
    )
    out_specs = (P(("tok", "hv"), None), P("tok", "hv", None, None), P("tok", None, "hv", None))
    return jax.shard_map(shards, mesh=mesh, in_specs=in_specs, out_specs=out_specs, check_vma=False)
```

time: 203 us -> 165 us (0.81)
  blocking collectives: 15.5 us -> 0 us
  other arithmetic: 30 us -> 19.5 us
  starting transfers between devices: 3.48 us -> 13.2 us
  local copies, waits for them, and re-layouts: 15.1 us -> 5.68 us
  matrix products: 24.7 us -> 19.2 us
  waiting for transfers between devices: 93.9 us -> 90.1 us
  loops' own time: 3.26 us -> 0 us
    all_gather x1 -> x0, waiting for transfers between devices: 52.6 us -> none  [carried_in(): gathered = jax.tree.map(lambda a: lax.all_gather(a, axis), part)]
    ppermute x1 -> x7, waiting for transfers between devices: 1 us -> 52.6 us  [shifted(): lax.ppermute(value, axis, [(source, source + steps) for source in range(i...]
    all_gather x1 -> x0, blocking collectives: 15.5 us -> none  [carried_in(): gathered = jax.tree.map(lambda a: lax.all_gather(a, axis), part)]
    ppermute x1 -> x7, starting transfers between devices: 3.37 us -> 13.1 us  [shifted(): lax.ppermute(value, axis, [(source, source + steps) for source in range(i...]
    add x6 -> x1, other arithmetic: 7.13 us -> 1 us  [segment_parts(): memory = step_decay[block][:, None] * memory + update[block]]
    slice x20 -> x3, local copies, waits for them, and re-layouts: 6.5 us -> 0.38 us  [the longest x1 0.19 us: segment_parts(): in_tail = (groups == groups[:, -1:]).astype(jnp.float32)]
    convert_element_type x8 -> x1, other arithmetic: 5.59 us -> 0.66 us  [segment_parts(): intact = (groups == 0.0).astype(jnp.float32)]
    dot_general x16 -> x6, matrix products: 14.6 us -> 9.95 us  [the longest x3 3.65 us: segment_parts(): jnp.dot(lifted_intact[block], memory, precision=HIGHEST_PRECISION)]
  transfers between devices with their start and end apart: 4 -> 9, of which waited for: 4 -> 7; matrix products, arithmetic and copies ran while one was open for 5% -> 13% of each run, Pallas kernels for 0% -> 0%
where the time goes in v1:
time: 165 us; the launch traced here: 162 us
  waiting for transfers between devices  90.1 us (55%)
  other arithmetic  19.5 us (12%)
  matrix products  19.2 us (12%)
  between operations  14.6 us (9%)
  starting transfers between devices  13.2 us (8%)
  local copies, waits for them, and re-layouts  5.68 us (3%)
    ppermute x7, waiting for transfers between devices, shifted(): lax.ppermute(value, axis, [(source, source + steps) for source in range(i...  52.6 us
    reduce_scatter x1, waiting for transfers between devices, shards(): lax.psum_scatter(jnp.dot(gated_out, out_weight, preferred_element_type=jn...  24.1 us
    ppermute x7, starting transfers between devices, shifted(): lax.ppermute(value, axis, [(source, source + steps) for source in range(i...  13.1 us
    all_gather x1, waiting for transfers between devices, shards(): gathered = lax.all_gather(tokens, 'hv', axis=0, tiled=True)  12.8 us
    dot_general x1, matrix products, shards(): jnp.dot(gated_out, out_weight, preferred_element_type=jnp.float32)  4.17 us
    dot_general x3, matrix products, segment_parts(): jnp.dot(lifted_intact[block], memory, precision=HIGHEST_PRECISION)  3.65 us
    dot_general x3, matrix products, project(): jnp.dot(gathered, weight, preferred_element_type=jnp.float32)  3.63 us
    convert_element_type x2, other arithmetic, short_conv(): return jax.nn.silu(summed).astype(jnp.bfloat16)  3.61 us
  transfers between devices with their start and end apart: 9, of which 7 were waited for; matrix products, arithmetic and copies ran while one was open for 13% of the time, Pallas kernels for 0%

profile of v1, /device:TPU:24, one launch (start us, length us, event | category | flops | bytes accessed | tf_op | source)
XLA Modules:
  0.0 162.3 jit_solution(2460254521028870375)
XLA Ops:
  7.2 0.7 all-gather.2.cloned.1.call-update
  8.0 0.8 reduce-window.9
  8.8 0.7 bitcast_subtract_fusion
  9.6 0.6 slice.177
  10.7 0.7 compare_convert_fusion.1
  11.5 0.7 slice_compare_fusion
  12.3 1.4 slice_convert_fusion.7
  13.7 0.8 slice_convert_fusion.3
  14.5 12.8 %all-gather.2.cloned.1.call-done = bf16[256,2048]{1,0:T(8,128)(2,1)} async-done(((bf16[64,2048]{1,0:T(8,128)(2,1)}), bf16[256,2048]{1,0:T(8,128)(2,1)}) %all-gather.2.cloned.1.call-update) | async-done | bytes 1048592 | tf_op jit(solution)/shard_map/all_gather | solution.py:116
  27.3 2.8 %convolution_convert_fusion.2 = bf16[256,512]{1,0:T(8,128)(2,1)S(1)} fusion(bf16[256,2048]{1,0:T(8,128)(2,1)} %all-gather.2.cloned.1.call-done, bf16[2048,512]{1,0:T(8,128)(2,1)} %param.18), kind=kOutput, calls=%fused_computation.4 | convolution fusion | flops 537001984 | bytes 3407872 | tf_op jit(solution)/shard_map/dot_general | solution.py:119
  31.2 0.7 select_bitcast_fusion
  31.9 3.4 %collective-permute-start = (bf16[3,1024]{1,0:T(4,128)(2,1)S(1)}, bf16[3,1024]{1,0:T(4,128)(2,1)S(1)}, u32[]{:S(2)}, u32[]{:S(2)}) collective-permute-start(bf16[3,1024]{1,0:T(4,128)(2,1)S(1)} %get-tuple-element.4), channel_id=1, source_target_pairs={{0,4},{4,8},{8,12},{12,16},{16,20},{20,24},{24,28},{1,5},{5,9},{9,... | collective-permute-start | bytes 18440 | tf_op jit(solution)/shard_map/ppermute | solution.py:15
  35.3 1.5 fusion.19
  36.8 1.2 reduce_window_sum.30
  38.1 0.6 slice_multiply_fusion
  38.7 0.6 multiply_multiply_fusion
  39.3 2.1 %multiply_convert_fusion.1 = bf16[256,512]{1,0:T(8,128)(2,1)S(1)} fusion(bf16[256,512]{1,0:T(8,128)(2,1)} %copy-done.9, bf16[3,512]{1,0:T(4,128)(2,1)S(1)} %slice.188, f32[256]{0:T(256)S(1)} %get-tuple-element.32, f32[512]{0:T(512)S(1)} %bitcast.138, f32[256]{0:T(256)S(1)} %get-tuple-element.33, f32[512]{0:T(512)S(1)} %bitcast.139, ...), kind=kLoop, calls=%fused_computation.36 | loop fusion | flops 3801088 | bytes 539648 | tf_op jit(solution)/shard_map/convert_element_type | solution.py:38
  41.5 0.6 fusion.53
  42.1 1.5 multiply_convert_fusion.3
  43.6 1.3 fusion.30
  44.9 1.3 copy-done.1
  46.2 1.0 fusion.3
  47.2 1.9 %collective-permute-start.3 = (f32[256,512]{1,0:T(8,128)}, f32[256,512]{1,0:T(8,128)}, u32[]{:S(2)}, u32[]{:S(2)}) collective-permute-start(f32[256,512]{1,0:T(8,128)} %fusion.3), channel_id=1, source_target_pairs={{0,4},{4,8},{8,12},{12,16},{16,20},{20,24},{24,28},{1,5},{5,9},{9,... | collective-permute-start | bytes 1572872 | tf_op jit(solution)/shard_map/ppermute | solution.py:15
  49.2 0.6 reshape.227
  50.8 0.8 slice_convert_fusion.11
  51.6 12.5 %collective-permute-done.3 = f32[256,512]{1,0:T(8,128)} collective-permute-done((f32[256,512]{1,0:T(8,128)}, f32[256,512]{1,0:T(8,128)}, u32[]{:S(2)}, u32[]{:S(2)}) %collective-permute-start.3) | collective-permute-done | bytes 524320 | tf_op jit(solution)/shard_map/ppermute | solution.py:15
  64.2 2.0 %add_select_fusion.2 = f32[256,512]{1,0:T(8,128)S(1)} fusion(f32[256,512]{1,0:T(8,128)} %collective-permute-done.3, f32[256]{0:T(256)} %get-tuple-element.29, pred[]{:T(512)S(6)} %ge.78, f32[4,256,512]{2,1,0:T(8,128)} %copy-done.1, f32[256]{0:T(256)S(1)} %get-tuple-element.30, f32[256]{0:T(256)S(1)} %bitcast.124, f32[256]{0:T(256)} %bitcast.129, f32[256]{0:T(256)} %bitcast.133), kind=kLoop, calls=%fused_computation.18 | loop fusion | flops 1310720 | bytes 3150849 | tf_op jit(solution)/shard_map/jit(_where)/select_n | solution.py:93
  66.2 1.4 collective-permute-start.4
  67.6 1.9 %collective-permute-start.1 = (f32[256]{0:T(256)}, f32[256]{0:T(256)S(1)}, u32[]{:S(2)}, u32[]{:S(2)}) collective-permute-start(f32[256]{0:T(256)} %get-tuple-element.29), channel_id=1, source_target_pairs={{0,4},{4,8},{8,12},{12,16},{16,20},{20,24},{24,28},{1,5},{5,9},{9,... | collective-permute-start | bytes 3080 | tf_op jit(solution)/shard_map/ppermute | solution.py:15
  69.6 0.8 pad_maximum_fusion.5
  70.4 9.9 %collective-permute-done.1 = f32[256]{0:T(256)S(1)} collective-permute-done((f32[256]{0:T(256)}, f32[256]{0:T(256)S(1)}, u32[]{:S(2)}, u32[]{:S(2)}) %collective-permute-start.1) | collective-permute-done | bytes 1056 | tf_op jit(solution)/shard_map/ppermute | solution.py:15
  80.2 0.6 multiply_select_fusion.1
  80.9 1.3 collective-permute-start.2
  82.3 1.3 collective-permute-start.5
  83.6 2.8 %collective-permute-done.2 = f32[256]{0:T(256)S(1)} collective-permute-done((f32[256]{0:T(256)S(1)}, f32[256]{0:T(256)S(1)}, u32[]{:S(2)}, u32[]{:S(2)}) %collective-permute-start.2) | collective-permute-done | bytes 1056 | tf_op jit(solution)/shard_map/ppermute | solution.py:15
  86.5 1.0 bitcast_multiply_fusion
  87.5 0.7 copy-done.4
  88.4 1.2 convolution_bitcast_fusion.1
  89.6 18.8 %collective-permute-done.5 = f32[256,512]{1,0:T(8,128)S(1)} collective-permute-done((f32[256,512]{1,0:T(8,128)S(1)}, f32[256,512]{1,0:T(8,128)S(1)}, u32[]{:S(2)}, u32[]{:S(2)}) %collective-permute-start.5) | collective-permute-done | bytes 524320 | tf_op jit(solution)/shard_map/ppermute | solution.py:15
  108.4 0.9 add_select_fusion
  109.3 1.9 %collective-permute-start.6 = (f32[256,512]{1,0:T(8,128)}, f32[256,512]{1,0:T(8,128)}, u32[]{:S(2)}, u32[]{:S(2)}) collective-permute-start(f32[256,512]{1,0:T(8,128)} %add_select_fusion), channel_id=1, source_target_pairs={{0,4},{4,8},{8,12},{12,16},{16,20},{20,24},{24,28},{1,5},{5,9},{9,... | collective-permute-start | bytes 1572872 | tf_op jit(solution)/shard_map/ppermute | solution.py:15
  111.2 1.2 convolution_bitcast_fusion.2
  112.4 1.2 convolution_bitcast_fusion
  113.7 2.3 %convolution_add_fusion = f32[4,64,512]{2,1,0:T(8,128)} fusion(bf16[4,64,512]{2,1,0:T(8,128)(2,1)} %bitcast.117, f32[1,64,512]{2,1,0:T(8,128)} %convolution_bitcast_fusion, f32[1,64,512]{2,1,0:T(8,128)} %convolution_bitcast_fusion.1, f32[1,64,512]{2,1,0:T(8,128)} %convolution_bitcast_fusion.2, f32[4]{0:T(128)S(1)} %copy-done.30, ...), kind=kOutput, calls=%fused_computation.1 | convolution fusion | flops 26148864 | bytes 1840144 | tf_op jit(solution)/shard_map/bac,bcv->bav/dot_general | solution.py:68
  116.0 8.5 %collective-permute-done.6 = f32[256,512]{1,0:T(8,128)} collective-permute-done((f32[256,512]{1,0:T(8,128)}, f32[256,512]{1,0:T(8,128)}, u32[]{:S(2)}, u32[]{:S(2)}) %collective-permute-start.6) | collective-permute-done | bytes 524320 | tf_op jit(solution)/shard_map/ppermute | solution.py:15
  124.5 2.7 %multiply_reduce_fusion = (f32[256]{0:T(256)S(1)}, f32[256,512]{1,0:T(8,128)}) fusion(f32[256,512]{1,0:T(8,128)} %bitcast.118, f32[256,256]{1,0:T(8,128)} %get-tuple-element.5, f32[256,512]{1,0:T(8,128)} %collective-permute-done.6), kind=kOutput, calls=%fused_computation.32 | convolution fusion | flops 403046144 | bytes 1836032 | tf_op jit(solution)/shard_map/dot_general | solution.py:154
  127.2 4.2 %convolution_convert_fusion = bf16[256,2048]{1,0:T(8,128)(2,1)} fusion(bf16[512,2048]{1,0:T(8,128)(2,1)S(1)} %copy-done, f32[256,512]{1,0:T(8,128)} %get-tuple-element.36, bf16[256,2048]{1,0:T(8,128)(2,1)S(1)} %copy-done.3, bf16[2048,512]{1,0:T(8,128)(2,1)} %param.25, f32[512]{0:T(512)} %param.26, f32[256]{0:T(256)S(1)} %add_rsqrt_fusion), kind=kOutput, calls=%fused_computation | convolution fusion | flops 1075576832 | bytes 6818816 | tf_op jit(solution)/shard_map/dot_general | solution.py:163
  131.4 24.1 %reduce-scatter.2.cloned.1.call-done = bf16[64,2048]{1,0:T(8,128)(2,1)} async-done(((bf16[256,2048]{1,0:T(8,128)(2,1)}), bf16[64,2048]{1,0:T(8,128)(2,1)}) %reduce-scatter.2.cloned.1.call-update) | async-done | bytes 262160 | tf_op jit(solution)/shard_map/reduce_scatter | solution.py:162
  (95 shorter events, 3.5 us)
Async XLA Ops:
  7.2 120.0 %copy-start = (bf16[512,2048]{1,0:T(8,128)(2,1)S(1)}, bf16[512,2048]{1,0:T(8,128)(2,1)}, u32[]{:S(2)}) copy-start(bf16[512,2048]{1,0:T(8,128)(2,1)} %param.27) | copy-start | bytes 6291460
  7.2 20.1 %all-gather.2.cloned.1.call-start = ((), (), s32[]{:S(2)}) async-start(), calls=%async_computation.1 | async-start | bytes 1310720 | tf_op jit(solution)/shard_map/all_gather | solution.py:116
  7.9 147.5 %reduce-scatter.2.cloned.1.call-start = ((), (), s32[]{:S(2)}) async-start(), calls=%async_computation.2 | async-start | bytes 1310720 | tf_op jit(solution)/shard_map/reduce_scatter | solution.py:162
  12.2 27.1 %copy-start.19 = (f32[256]{0:T(256)}, f32[256]{0:T(256)S(1)}, u32[]{:S(2)}) copy-start(f32[256]{0:T(256)S(1)} %get-tuple-element.31) | copy-start | bytes 3076
  12.2 27.1 %copy-start.21 = (f32[256]{0:T(256)}, f32[256]{0:T(256)S(1)}, u32[]{:S(2)}) copy-start(f32[256]{0:T(256)S(1)} %get-tuple-element.32) | copy-start | bytes 3076
  12.2 27.1 %copy-start.23 = (f32[256]{0:T(256)}, f32[256]{0:T(256)S(1)}, u32[]{:S(2)}) copy-start(f32[256]{0:T(256)S(1)} %get-tuple-element.33) | copy-start | bytes 3076
  12.3 27.1 %copy-start.25 = (f32[256]{0:T(256)}, f32[256]{0:T(256)S(1)}, u32[]{:S(2)}) copy-start(f32[256]{0:T(256)S(1)} %get-tuple-element.34) | copy-start | bytes 3076
  27.3 2.8 %copy-start.3 = (bf16[256,2048]{1,0:T(8,128)(2,1)S(1)}, bf16[256,2048]{1,0:T(8,128)(2,1)}, u32[]{:S(2)}) copy-start(bf16[256,2048]{1,0:T(8,128)(2,1)} %all-gather.2.cloned.1.call-done) | copy-start | bytes 3145732
  27.3 2.8 %copy-start.10 = (bf16[2048,256]{1,0:T(8,128)(2,1)S(1)}, bf16[2048,256]{1,0:T(8,128)(2,1)}, u32[]{:S(2)}) copy-start(bf16[2048,256]{1,0:T(8,128)(2,1)} %param.17) | copy-start | bytes 3145732
  27.3 3.3 %copy-start.11 = (bf16[2048,256]{1,0:T(8,128)(2,1)S(1)}, bf16[2048,256]{1,0:T(8,128)(2,1)}, u32[]{:S(2)}) copy-start(bf16[2048,256]{1,0:T(8,128)(2,1)} %param.16) | copy-start | bytes 3145732
  30.1 1.0 copy-start.9
  30.1 5.2 %copy-start.32 = (bf16[2048,16]{0,1:T(8,128)(2,1)S(1)}, bf16[2048,16]{0,1:T(8,128)(2,1)}, u32[]{:S(2)}) copy-start(bf16[2048,16]{0,1:T(8,128)(2,1)} %param.22) | copy-start | bytes 196612
  30.1 5.2 %copy-start.33 = (bf16[16,256]{1,0:T(8,128)(2,1)S(1)}, bf16[16,256]{1,0:T(8,128)(2,1)}, u32[]{:S(2)}) copy-start(bf16[16,256]{1,0:T(8,128)(2,1)} %param.23) | copy-start | bytes 24580
  30.1 5.2 %copy-start.34 = (f32[256]{0:T(256)S(1)}, f32[256]{0:T(256)}, u32[]{:S(2)}) copy-start(f32[256]{0:T(256)} %param.24) | copy-start | bytes 3076
  30.6 0.6 copy-start.6
  31.2 0.7 copy-start.7
  31.9 7.4 %collective-permute-start = (bf16[3,1024]{1,0:T(4,128)(2,1)S(1)}, bf16[3,1024]{1,0:T(4,128)(2,1)S(1)}, u32[]{:S(2)}, u32[]{:S(2)}) collective-permute-start(bf16[3,1024]{1,0:T(4,128)(2,1)S(1)} %get-tuple-element.4), channel_id=1, source_target_pairs={{0,4},{4,8},{8,12},{12,16},{16,20},{20,24},{24,28},{1,5},{5,9},{9,... | collective-permute-start | bytes 18440 | tf_op jit(solution)/shard_map/ppermute | solution.py:15
  38.7 3.4 %copy-start.27 = (f32[1,256]{1,0:T(1,128)}, f32[1,256]{1,0:T(1,128)S(1)}, u32[]{:S(2)}) copy-start(f32[1,256]{1,0:T(1,128)S(1)} %get-tuple-element.13) | copy-start | bytes 3076
  38.7 8.5 %copy-start.16 = (f32[1,256]{1,0:T(1,128)}, f32[1,256]{1,0:T(1,128)S(1)}, u32[]{:S(2)}) copy-start(f32[1,256]{1,0:T(1,128)S(1)} %get-tuple-element.14) | copy-start | bytes 3076
  38.7 8.5 %copy-start.18 = (f32[1,256]{1,0:T(1,128)}, f32[1,256]{1,0:T(1,128)S(1)}, u32[]{:S(2)}) copy-start(f32[1,256]{1,0:T(1,128)S(1)} %get-tuple-element.11) | copy-start | bytes 3076
  38.7 25.4 %copy-start.14 = (f32[1,256]{1,0:T(1,128)}, f32[1,256]{1,0:T(1,128)S(1)}, u32[]{:S(2)}) copy-start(f32[1,256]{1,0:T(1,128)S(1)} %get-tuple-element.12) | copy-start | bytes 3076
  39.3 24.8 %copy-start.12 = (f32[256]{0:T(256)}, f32[256]{0:T(256)S(1)}, u32[]{:S(2)}) copy-start(f32[256]{0:T(256)S(1)} %get-tuple-element.30) | copy-start | bytes 3076
  41.5 2.1 %copy-start.5 = (bf16[256,512]{1,0:T(8,128)(2,1)}, bf16[256,512]{1,0:T(8,128)(2,1)S(1)}, u32[]{:S(2)}) copy-start(bf16[256,512]{1,0:T(8,128)(2,1)S(1)} %multiply_convert_fusion.1) | copy-start | bytes 786436
  44.9 1.3 copy-start.1
  47.2 16.9 %collective-permute-start.3 = (f32[256,512]{1,0:T(8,128)}, f32[256,512]{1,0:T(8,128)}, u32[]{:S(2)}, u32[]{:S(2)}) collective-permute-start(f32[256,512]{1,0:T(8,128)} %fusion.3), channel_id=1, source_target_pairs={{0,4},{4,8},{8,12},{12,16},{16,20},{20,24},{24,28},{1,5},{5,9},{9,... | collective-permute-start | bytes 1572872 | tf_op jit(solution)/shard_map/ppermute | solution.py:15
  50.7 18.8 %copy-start.31 = (f32[4]{0:T(128)S(1)}, f32[4]{0:T(128)}, u32[]{:S(2)}) copy-start(f32[4]{0:T(128)} %pad.clone) | copy-start | bytes 52
  64.1 22.3 %copy-start.8 = (bf16[256,256]{1,0:T(8,128)(2,1)S(1)}, bf16[256,256]{1,0:T(8,128)(2,1)}, u32[]{:S(2)}) copy-start(bf16[256,256]{1,0:T(8,128)(2,1)} %copy-done.7) | copy-start | bytes 393220
  64.1 22.3 %copy-start.20 = (f32[256]{0:T(256)S(1)}, f32[256]{0:T(256)}, u32[]{:S(2)}) copy-start(f32[256]{0:T(256)} %copy-done.19) | copy-start | bytes 3076
  64.1 22.3 %copy-start.22 = (f32[256]{0:T(256)S(1)}, f32[256]{0:T(256)}, u32[]{:S(2)}) copy-start(f32[256]{0:T(256)} %copy-done.21) | copy-start | bytes 3076
  64.1 22.3 %copy-start.24 = (f32[256]{0:T(256)S(1)}, f32[256]{0:T(256)}, u32[]{:S(2)}) copy-start(f32[256]{0:T(256)} %copy-done.23) | copy-start | bytes 3076
  64.1 22.3 %copy-start.26 = (f32[256]{0:T(256)S(1)}, f32[256]{0:T(256)}, u32[]{:S(2)}) copy-start(f32[256]{0:T(256)} %copy-done.25) | copy-start | bytes 3076
  64.2 22.3 %copy-start.28 = (bf16[3,256]{1,0:T(4,128)(2,1)S(1)}, bf16[3,256]{1,0:T(4,128)(2,1)}, u32[]{:S(2)}) copy-start(bf16[3,256]{1,0:T(4,128)(2,1)} %get-tuple-element.9) | copy-start | bytes 4612
  64.2 22.3 %copy-start.29 = (f32[256]{0:T(256)S(1)}, f32[256]{0:T(256)}, u32[]{:S(2)}) copy-start(f32[256]{0:T(256)} %reshape.227) | copy-start | bytes 3076
  66.1 22.2 %copy-start.2 = (f32[4,256,512]{2,1,0:T(8,128)S(1)}, f32[4,256,512]{2,1,0:T(8,128)}, u32[]{:S(2)}) copy-start(f32[4,256,512]{2,1,0:T(8,128)} %copy-done.1) | copy-start | bytes 6291460
  66.1 22.2 %copy-start.13 = (f32[256]{0:T(256)S(1)}, f32[256]{0:T(256)}, u32[]{:S(2)}) copy-start(f32[256]{0:T(256)} %copy-done.12) | copy-start | bytes 3076
  66.2 22.2 %copy-start.15 = (f32[1,256]{1,0:T(1,128)S(1)}, f32[1,256]{1,0:T(1,128)}, u32[]{:S(2)}) copy-start(f32[1,256]{1,0:T(1,128)} %copy-done.14) | copy-start | bytes 3076
  66.2 16.0 %collective-permute-start.4 = (f32[256,512]{1,0:T(8,128)S(1)}, f32[256,512]{1,0:T(8,128)S(1)}, u32[]{:S(2)}, u32[]{:S(2)}) collective-permute-start(f32[256,512]{1,0:T(8,128)S(1)} %add_select_fusion.2), channel_id=1, source_target_pairs={{0,8},{4,12},{8,16},{12,20},{16,24},{20,28},{1,9},{5,13},{9,17},{1... | collective-permute-start | bytes 1572872 | tf_op jit(solution)/shard_map/ppermute | solution.py:15
  67.6 12.6 %collective-permute-start.1 = (f32[256]{0:T(256)}, f32[256]{0:T(256)S(1)}, u32[]{:S(2)}, u32[]{:S(2)}) collective-permute-start(f32[256]{0:T(256)} %get-tuple-element.29), channel_id=1, source_target_pairs={{0,4},{4,8},{8,12},{12,16},{16,20},{20,24},{24,28},{1,5},{5,9},{9,... | collective-permute-start | bytes 3080 | tf_op jit(solution)/shard_map/ppermute | solution.py:15
  80.9 5.6 %collective-permute-start.2 = (f32[256]{0:T(256)S(1)}, f32[256]{0:T(256)S(1)}, u32[]{:S(2)}, u32[]{:S(2)}) collective-permute-start(f32[256]{0:T(256)S(1)} %multiply_select_fusion.1), channel_id=1, source_target_pairs={{0,8},{4,12},{8,16},{12,20},{16,24},{20,28},{1,9},{5,13},{9,17},{1... | collective-permute-start | bytes 3080 | tf_op jit(solution)/shard_map/ppermute | solution.py:15
  82.3 26.1 %collective-permute-start.5 = (f32[256,512]{1,0:T(8,128)S(1)}, f32[256,512]{1,0:T(8,128)S(1)}, u32[]{:S(2)}, u32[]{:S(2)}) collective-permute-start(f32[256,512]{1,0:T(8,128)S(1)} %add_select_fusion.1), channel_id=1, source_target_pairs={{0,16},{4,20},{8,24},{12,28},{1,17},{5,21},{9,25},{13,29},{2,18},{... | collective-permute-start | bytes 1572872 | tf_op jit(solution)/shard_map/ppermute | solution.py:15
  87.5 0.7 copy-start.4
  87.5 24.9 %copy-start.17 = (f32[1,256]{1,0:T(1,128)S(1)}, f32[1,256]{1,0:T(1,128)}, u32[]{:S(2)}) copy-start(f32[1,256]{1,0:T(1,128)} %copy-done.16) | copy-start | bytes 3076
  88.3 25.3 %copy-start.30 = (f32[4]{0:T(128)S(1)}, f32[4]{0:T(128)}, u32[]{:S(2)}) copy-start(f32[4]{0:T(128)} %pad.4.clone) | copy-start | bytes 52
  109.3 15.2 %collective-permute-start.6 = (f32[256,512]{1,0:T(8,128)}, f32[256,512]{1,0:T(8,128)}, u32[]{:S(2)}, u32[]{:S(2)}) collective-permute-start(f32[256,512]{1,0:T(8,128)} %add_select_fusion), channel_id=1, source_target_pairs={{0,4},{4,8},{8,12},{12,16},{16,20},{20,24},{24,28},{1,5},{5,9},{9,... | collective-permute-start | bytes 1572872 | tf_op jit(solution)/shard_map/ppermute | solution.py:15
Sparse Core Ops, SparseCore 0:
  9.5 17.7 all-gather.1
  131.5 23.9 reduce-scatter.1

commit v2 on v1

--- a/solution.py
+++ b/solution.py
@@ -86,15 +86,48 @@
 def prefix_states(decay, memory, axis):
     count = lax.axis_size(axis)
     place = lax.axis_index(axis)
+    entering_decay = jnp.ones_like(decay)
+    entering = jnp.zeros_like(memory)
     steps = 1
     while steps < count:
         earlier_decay, earlier_memory = shifted((decay, memory), axis, steps)
         valid = place >= steps
         memory = jnp.where(valid, decay[:, None] * earlier_memory + memory, memory)
         decay = jnp.where(valid, earlier_decay * decay, decay)
+        if steps == 1:
+            entering = earlier_memory
+            entering_decay = earlier_decay
+        else:
+            entering = jnp.where(valid, entering_decay[:, None] * earlier_memory + entering, entering)
+            entering_decay = jnp.where(valid, earlier_decay * entering_decay, entering_decay)
         steps *= 2
-    entering = shifted(memory, axis, 1)
     return (memory, entering)
+
+
+def rotations(axis):
+    count = lax.axis_size(axis)
+    return [[(source, (source + step) % count) for source in range(count)] for step in range(1, count)]
+
+
+def gather_rows(rows, axis):
+    count = lax.axis_size(axis)
+    place = lax.axis_index(axis)
+    received = [rows] + [lax.ppermute(rows, axis, pairs) for pairs in rotations(axis)]
+    reverse = [received[(-index) % count] for index in range(count)]
+    doubled = jnp.stack(reverse + reverse)
+    ordered = lax.dynamic_slice_in_dim(doubled, (count - place) % count, count, axis=0)
+    return ordered.reshape((count * rows.shape[0],) + rows.shape[1:])
+
+
+def scatter_sum(terms, axis):
+    count = lax.axis_size(axis)
+    place = lax.axis_index(axis)
+    chunks = terms.reshape((count, terms.shape[0] // count) + terms.shape[1:])
+    total = lax.dynamic_index_in_dim(chunks, place, 0, False).astype(jnp.float32)
+    for step, pairs in enumerate(rotations(axis), start=1):
+        outgoing = lax.dynamic_index_in_dim(chunks, (place + step) % count, 0, False)
+        total = total + lax.ppermute(outgoing, axis, pairs).astype(jnp.float32)
+    return total.astype(jnp.bfloat16)
 
 
 def shards(
@@ -113,7 +146,7 @@
     norm_gain,
     out_weight,
 ):
-    gathered = lax.all_gather(tokens, "hv", axis=0, tiled=True)
+    gathered = gather_rows(tokens, "hv")
 
     def project(weight):
         return jnp.dot(gathered, weight, preferred_element_type=jnp.float32).astype(jnp.bfloat16)
@@ -159,11 +192,9 @@
     gated_out = (
         heads_out * rescale * norm_gain[None, :] * gate_float * jax.nn.sigmoid(gate_float)
     ).astype(jnp.bfloat16)
-    mixed = lax.psum_scatter(
+    mixed = scatter_sum(
         jnp.dot(gated_out, out_weight, preferred_element_type=jnp.float32).astype(jnp.bfloat16),
         "hv",
-        scatter_dimension=0,
-        tiled=True,
     )
     segment_states = closing[None, None]
     in_prompt = positions[row_count - rim_rows :] >= prompt_first[row_count - 1]

time: 165 us -> 122 us (0.74); the launches traced: 162 us -> 122 us
  waiting for transfers between devices: 90.1 us -> 55.4 us
  between operations: 14.6 us -> 1.19 us
  local copies, waits for them, and re-layouts: 5.68 us -> 13.6 us
    reduce_scatter x1 -> x0, waiting for transfers between devices: 24.1 us -> none  [shards(): lax.psum_scatter(jnp.dot(gated_out, out_weight, preferred_element_type=jn...]
    all_gather x1 -> x0, waiting for transfers between devices: 12.8 us -> none  [shards(): gathered = lax.all_gather(tokens, 'hv', axis=0, tiled=True)]
    ppermute x0 -> x6, waiting for transfers between devices: none -> 11.2 us  [the longest x3 10.6 us: scatter_sum(): total = total + lax.ppermute(outgoing, axis, pairs).astype(jnp.float32)]
    ppermute x7 -> x6, waiting for transfers between devices: 52.6 us -> 44.2 us  [shifted(): lax.ppermute(value, axis, [(source, source + steps) for source in range(i...]
    unnamed x71 -> x76, local copies, waits for them, and re-layouts: 2.38 us -> 7.5 us
    ppermute x0 -> x6, starting transfers between devices: none -> 2.6 us  [the longest x3 1.8 us: gather_rows(): lax.ppermute(rows, axis, pairs)]
    broadcast_in_dim x0 -> x1, other arithmetic: none -> 2.12 us  [shards(): segment_states = closing[None, None]]
    dot_general x3, matrix products: 3.63 us -> 1.58 us  [project(): jnp.dot(gathered, weight, preferred_element_type=jnp.float32)]
  transfers between devices with their start and end apart: 9 -> 12, of which waited for: 7 -> 9; matrix products, arithmetic and copies ran while one was open for 13% -> 21% of each run, Pallas kernels for 0% -> 0%
where the time goes in v2:
time: 122 us
  waiting for transfers between devices  55.4 us (45%)
  other arithmetic  19.5 us (16%)
  matrix products  17.6 us (14%)
  starting transfers between devices  14.4 us (12%)
  local copies, waits for them, and re-layouts  13.6 us (11%)
    ppermute x6, waiting for transfers between devices, shifted(): lax.ppermute(value, axis, [(source, source + steps) for source in range(i...  44.2 us
    ppermute x6, starting transfers between devices, shifted(): lax.ppermute(value, axis, [(source, source + steps) for source in range(i...  11.8 us
    ppermute x3, waiting for transfers between devices, scatter_sum(): total = total + lax.ppermute(outgoing, axis, pairs).astype(jnp.float32)  10.6 us
    unnamed x76, local copies, waits for them, and re-layouts  7.5 us
    dot_general x1, matrix products, shards(): jnp.dot(gated_out, out_weight, preferred_element_type=jnp.float32)  4.06 us
    mul x3, other arithmetic, short_conv(): weight[tap_index].astype(jnp.float32)[None, :] * window.astype(jnp.float32)  3.68 us
    dot_general x3, matrix products, segment_parts(): jnp.dot(lifted_intact[block], memory, precision=HIGHEST_PRECISION)  3.65 us
    convert_element_type x2, other arithmetic, short_conv(): return jax.nn.silu(summed).astype(jnp.bfloat16)  3.48 us
  transfers between devices with their start and end apart: 12, of which 9 were waited for; matrix products, arithmetic and copies ran while one was open for 21% of the time, Pallas kernels for 0%

profile of v2, /device:TPU:24, one launch (start us, length us, event | category | flops | bytes accessed | tf_op | source)
XLA Modules:
  0.0 121.7 jit_solution(2988543917810232325)
XLA Ops:
  0.7 1.0 collective-permute-start
  2.5 1.7 %bitcast_dynamic-update-slice_fusion.6 = bf16[8,64,2048]{2,1,0:T(8,128)(2,1)} fusion(bf16[64,2048]{1,0:T(8,128)(2,1)} %param.14), kind=kLoop, calls=%fused_computation.71 | loop fusion | bytes 524288
  4.1 0.8 reduce-window.9
  6.4 0.7 slice_compare_fusion
  7.1 1.4 %slice_convert_fusion.7 = (f32[1,256]{1,0:T(1,128)}, f32[1,256]{1,0:T(1,128)}, f32[1,256]{1,0:T(1,128)}, f32[1,256]{1,0:T(1,128)}) fusion(bf16[4,256]{1,0:T(4,128)(2,1)} %param.20), kind=kLoop, calls=%fused_computation.145 | loop fusion | flops 1024 | bytes 6144 | tf_op jit(solution)/shard_map/mul | solution.py:34
  9.7 1.4 %slice_convert_fusion.11 = (f32[1,256]{1,0:T(1,128)}, f32[1,256]{1,0:T(1,128)}, f32[1,256]{1,0:T(1,128)}, f32[1,256]{1,0:T(1,128)}) fusion(bf16[4,256]{1,0:T(4,128)(2,1)} %param.19), kind=kLoop, calls=%fused_computation.149 | loop fusion | flops 1024 | bytes 6144 | tf_op jit(solution)/shard_map/mul | solution.py:34
  13.0 0.8 slice_convert_fusion.3
  13.9 0.7 bitcast_dynamic-update-slice_fusion.4
  15.2 0.7 bitcast_dynamic-update-slice_fusion.2
  15.9 0.7 bitcast_dynamic-update-slice_fusion
  16.6 0.7 bitcast_dynamic-update-slice_fusion.7
  17.3 0.7 bitcast_dynamic-update-slice_fusion.5
  18.1 0.7 bitcast_dynamic-update-slice_fusion.3
  18.8 0.7 bitcast_dynamic-update-slice_fusion.1
  19.5 1.3 %constant_dynamic-slice_fusion = bf16[4,64,2048]{2,1,0:T(8,128)(2,1)S(1)} fusion(bf16[8,64,2048]{2,1,0:T(8,128)(2,1)} %bitcast_dynamic-update-slice_fusion.1, s32[]{:T(128)S(6)} %select_n.100), kind=kLoop, calls=%fused_computation.139 | loop fusion | bytes 2097156 | tf_op jit(solution)/shard_map/dynamic_slice | solution.py:118
  20.8 0.7 convolution_convert_fusion.2
  23.1 0.7 select_bitcast_fusion
  23.8 3.4 %collective-permute-start.3 = (bf16[3,1024]{1,0:T(4,128)(2,1)S(1)}, bf16[3,1024]{1,0:T(4,128)(2,1)S(1)}, u32[]{:S(2)}, u32[]{:S(2)}) collective-permute-start(bf16[3,1024]{1,0:T(4,128)(2,1)S(1)} %get-tuple-element.4), channel_id=1, source_target_pairs={{0,4},{4,8},{8,12},{12,16},{16,20},{20,24},{24,28},{1,5},{5,9},{9,... | collective-permute-start | bytes 18440 | tf_op jit(solution)/shard_map/ppermute | solution.py:15
  27.2 1.5 %fusion.27 = f32[256,256]{1,0:T(8,128)} fusion(bf16[16,256]{1,0:T(8,128)(2,1)S(1)} %copy-done.31, bf16[256,2048]{1,0:T(8,128)(2,1)S(1)} %bitcast.140, bf16[2048,16]{0,1:T(8,128)(2,1)S(1)} %copy-done.30, f32[256]{0:T(256)S(1)} %copy-done.33), kind=kOutput, calls=%fused_computation.60 | convolution fusion | flops 19533824 | bytes 1385472 | tf_op jit(solution)/shard_map/dot_general | solution.py:179
  28.7 1.2 reduce_window_sum.30
  30.3 2.0 %multiply_convert_fusion.1 = bf16[256,512]{1,0:T(8,128)(2,1)S(1)} fusion(bf16[256,512]{1,0:T(8,128)(2,1)} %copy-done.8, bf16[3,512]{1,0:T(4,128)(2,1)S(1)} %slice.188, f32[256]{0:T(256)S(1)} %get-tuple-element.37, f32[512]{0:T(512)S(1)} %bitcast.168, f32[256]{0:T(256)S(1)} %get-tuple-element.38, f32[512]{0:T(512)S(1)} %bitcast.169, ...), kind=kLoop, calls=%fused_computation.47 | loop fusion | flops 3801088 | bytes 539648 | tf_op jit(solution)/shard_map/convert_element_type | solution.py:38
  32.3 1.5 %multiply_convert_fusion.2 = bf16[256,256]{1,0:T(8,128)(2,1)S(1)} fusion(bf16[256,256]{1,0:T(8,128)(2,1)} %copy-done.5, bf16[3,256]{1,0:T(4,128)(2,1)S(1)} %get-tuple-element.13, f32[256]{0:T(256)} %bitcast.172, f32[256]{0:T(256)} %bitcast.173, f32[256]{0:T(256)} %bitcast.171, f32[256]{0:T(256)} %bitcast.170, f32[256]{0:T(256)} %copy-done.14, ...), kind=kLoop, calls=%fused_computation.83 | loop fusion | flops 1900544 | bytes 271872 | tf_op jit(solution)/shard_map/convert_element_type | solution.py:38
  33.8 1.3 %fusion.42 = f32[4,256,512]{2,1,0:T(8,128)S(1)} fusion(bf16[4,64,512]{2,1,0:T(8,128)(2,1)S(1)} %bitcast.144, bf16[4,64,256]{2,1,0:T(8,128)(2,1)S(1)} %bitcast.147, f32[4,64,256]{2,1,0:T(8,128)S(1)} %reduce_window_sum.30, f32[4,64]{1,0:T(4,128)} %get-tuple-element.27, f32[4,256]{1,0:T(4,128)S(1)} %bitcast.164), kind=kOutput, calls=%fused_computation.95 | convolution fusion | flops 67436544 | bytes 2757632 | tf_op jit(solution)/shard_map/bsk,bsv->bkv/dot_general | solution.py:56
  35.4 2.5 %collective-permute-start.6 = (f32[256,512]{1,0:T(8,128)S(1)}, f32[256,512]{1,0:T(8,128)S(1)}, u32[]{:S(2)}, u32[]{:S(2)}) collective-permute-start(f32[256,512]{1,0:T(8,128)S(1)} %fusion.4), channel_id=1, source_target_pairs={{0,4},{4,8},{8,12},{12,16},{16,20},{20,24},{24,28},{1,5},{5,9},{9,... | collective-permute-start | bytes 1572872 | tf_op jit(solution)/shard_map/ppermute | solution.py:15
  38.0 1.9 %collective-permute-start.4 = (f32[256]{0:T(256)S(1)}, f32[256]{0:T(256)S(1)}, u32[]{:S(2)}, u32[]{:S(2)}) collective-permute-start(f32[256]{0:T(256)S(1)} %get-tuple-element.34), channel_id=1, source_target_pairs={{0,4},{4,8},{8,12},{12,16},{16,20},{20,24},{24,28},{1,5},{5,9},{9,... | collective-permute-start | bytes 3080 | tf_op jit(solution)/shard_map/ppermute | solution.py:15
  40.0 12.5 %collective-permute-done.4 = f32[256]{0:T(256)S(1)} collective-permute-done((f32[256]{0:T(256)S(1)}, f32[256]{0:T(256)S(1)}, u32[]{:S(2)}, u32[]{:S(2)}) %collective-permute-start.4) | collective-permute-done | bytes 1056 | tf_op jit(solution)/shard_map/ppermute | solution.py:15
  52.5 1.3 %collective-permute-start.5 = (f32[256]{0:T(256)S(1)}, f32[256]{0:T(256)S(1)}, u32[]{:S(2)}, u32[]{:S(2)}) collective-permute-start(f32[256]{0:T(256)S(1)} %multiply_select_fusion.2), channel_id=1, source_target_pairs={{0,8},{4,12},{8,16},{12,20},{16,24},{20,28},{1,9},{5,13},{9,17},{1... | collective-permute-start | bytes 3080 | tf_op jit(solution)/shard_map/ppermute | solution.py:15
  54.1 1.3 %collective-permute-start.7 = (f32[256,512]{1,0:T(8,128)S(1)}, f32[256,512]{1,0:T(8,128)S(1)}, u32[]{:S(2)}, u32[]{:S(2)}) collective-permute-start(f32[256,512]{1,0:T(8,128)S(1)} %add_select_fusion.4), channel_id=1, source_target_pairs={{0,8},{4,12},{8,16},{12,20},{16,24},{20,28},{1,9},{5,13},{9,17},{1... | collective-permute-start | bytes 1572872 | tf_op jit(solution)/shard_map/ppermute | solution.py:15
  55.4 2.6 %collective-permute-done.5 = f32[256]{0:T(256)S(1)} collective-permute-done((f32[256]{0:T(256)S(1)}, f32[256]{0:T(256)S(1)}, u32[]{:S(2)}, u32[]{:S(2)}) %collective-permute-start.5) | collective-permute-done | bytes 1056 | tf_op jit(solution)/shard_map/ppermute | solution.py:15
  58.6 1.0 bitcast_multiply_fusion
  59.6 0.7 copy-done.1
  60.4 1.2 convolution_bitcast_fusion.1
  61.7 8.2 %collective-permute-done.7 = f32[256,512]{1,0:T(8,128)S(1)} collective-permute-done((f32[256,512]{1,0:T(8,128)S(1)}, f32[256,512]{1,0:T(8,128)S(1)}, u32[]{:S(2)}, u32[]{:S(2)}) %collective-permute-start.7) | collective-permute-done | bytes 524320 | tf_op jit(solution)/shard_map/ppermute | solution.py:15
  69.9 1.0 add_select_fusion.3
  70.9 1.4 %collective-permute-start.8 = (f32[256,512]{1,0:T(8,128)}, f32[256,512]{1,0:T(8,128)}, u32[]{:S(2)}, u32[]{:S(2)}) collective-permute-start(f32[256,512]{1,0:T(8,128)} %add_select_fusion.3), channel_id=1, source_target_pairs={{0,16},{4,20},{8,24},{12,28},{1,17},{5,21},{9,25},{13,29},{2,18},{... | collective-permute-start | bytes 1572872 | tf_op jit(solution)/shard_map/ppermute | solution.py:15
  72.3 1.2 convolution_bitcast_fusion.2
  73.5 1.3 %convolution_bitcast_fusion = f32[1,64,512]{2,1,0:T(8,128)} fusion(f32[4,256,512]{2,1,0:T(8,128)S(1)} %fusion.42, f32[256]{0:T(256)S(1)} %bitcast.160, f32[4,64,256]{2,1,0:T(8,128)S(1)} %broadcast_multiply_fusion, f32[256]{0:T(256)S(1)} %bitcast.156, f32[256]{0:T(256)S(1)} %get-tuple-element.35), kind=kOutput, calls=%fused_computation.10 | convolution fusion | flops 101318656 | bytes 1772544 | tf_op jit(solution)/shard_map/dot_general | solution.py:77
  74.8 2.3 %convolution_add_fusion = f32[4,64,512]{2,1,0:T(8,128)} fusion(bf16[4,64,512]{2,1,0:T(8,128)(2,1)} %bitcast.145, f32[1,64,512]{2,1,0:T(8,128)} %convolution_bitcast_fusion, f32[1,64,512]{2,1,0:T(8,128)} %convolution_bitcast_fusion.1, f32[1,64,512]{2,1,0:T(8,128)} %convolution_bitcast_fusion.2, f32[4]{0:T(128)} %pad.4.clone, ...), kind=kOutput, calls=%fused_computation.1 | convolution fusion | flops 26148864 | bytes 1840144 | tf_op jit(solution)/shard_map/bac,bcv->bav/dot_general | solution.py:68
  77.1 20.7 %collective-permute-done.8 = f32[256,512]{1,0:T(8,128)} collective-permute-done((f32[256,512]{1,0:T(8,128)}, f32[256,512]{1,0:T(8,128)}, u32[]{:S(2)}, u32[]{:S(2)}) %collective-permute-start.8) | collective-permute-done | bytes 524320 | tf_op jit(solution)/shard_map/ppermute | solution.py:15
  97.8 3.2 %multiply_reduce_fusion = (f32[256]{0:T(256)S(1)}, f32[256,512]{1,0:T(8,128)}) fusion(f32[256,512]{1,0:T(8,128)} %bitcast.146, f32[256,256]{1,0:T(8,128)} %get-tuple-element.5, f32[256,512]{1,0:T(8,128)} %copy-done.3, f32[256,512]{1,0:T(8,128)} %copy-done.4, f32[256,512]{1,0:T(8,128)} %collective-permute-done.8, f32[256]{0:T(256)S(1)} %copy-done.21, ...), kind=kOutput, calls=%fused_computation.41 | convolution fusion | flops 403832576 | bytes 2886658 | tf_op jit(solution)/shard_map/dot_general | solution.py:187
  101.1 4.1 %convolution_convert_fusion = bf16[256,2048]{1,0:T(8,128)(2,1)} fusion(bf16[512,2048]{1,0:T(8,128)(2,1)S(1)} %copy-done, bf16[256,2048]{1,0:T(8,128)(2,1)S(1)} %bitcast.141, bf16[2048,512]{1,0:T(8,128)(2,1)} %param.25, f32[256,512]{1,0:T(8,128)} %get-tuple-element.41, f32[512]{0:T(512)S(1)} %copy-done.32, f32[256]{0:T(256)S(1)} %add_rsqrt_fusion), kind=kOutput, calls=%fused_computation | convolution fusion | flops 1075576832 | bytes 6818816 | tf_op jit(solution)/shard_map/dot_general | solution.py:196
  105.1 1.2 dynamic-slice_bitcast_fusion.2
  106.4 0.7 collective-permute-start.10
  107.1 2.1 %fusion.3 = f32[1,1,256,512]{3,2,1,0:T(8,128)} fusion(f32[256,512]{1,0:T(8,128)} %add_select_fusion.3, f32[256,512]{1,0:T(8,128)} %collective-permute-done.8, f32[256]{0:T(256)S(1)} %copy-done.22, pred[]{:T(512)S(6)} %ge.76), kind=kLoop, calls=%fused_computation.22 | loop fusion | flops 393216 | bytes 1573889 | tf_op jit(solution)/shard_map/broadcast_in_dim | solution.py:199
  109.2 3.8 %collective-permute-done.11 = bf16[64,2048]{1,0:T(8,128)(2,1)S(1)} collective-permute-done((bf16[64,2048]{1,0:T(8,128)(2,1)S(1)}, bf16[64,2048]{1,0:T(8,128)(2,1)S(1)}, u32[]{:S(2)}, u32[]{:S(2)}) %collective-permute-start.11) | collective-permute-done | bytes 262176 | tf_op jit(solution)/shard_map/ppermute | solution.py:129
  113.1 6.0 %collective-permute-done.10 = bf16[64,2048]{1,0:T(8,128)(2,1)S(1)} collective-permute-done((bf16[64,2048]{1,0:T(8,128)(2,1)S(1)}, bf16[64,2048]{1,0:T(8,128)(2,1)S(1)}, u32[]{:S(2)}, u32[]{:S(2)}) %collective-permute-start.10) | collective-permute-done | bytes 262176 | tf_op jit(solution)/shard_map/ppermute | solution.py:129
  119.1 0.8 collective-permute-done.9
  119.9 1.8 %fusion.7 = bf16[64,2048]{1,0:T(8,128)(2,1)} fusion(bf16[64,2048]{1,0:T(8,128)(2,1)S(1)} %collective-permute-done.11, bf16[64,2048]{1,0:T(8,128)(2,1)S(1)} %collective-permute-done.10, bf16[64,2048]{1,0:T(8,128)(2,1)S(1)} %collective-permute-done.9, bf16[4,64,2048]{2,1,0:T(8,128)(2,1)} %bitcast.150, s32[]{:T(128)S(6)} %select_n.114), kind=kLoop, calls=%fused_computation.28 | loop fusion | flops 1048576 | bytes 1310724 | tf_op jit(solution)/shard_map/convert_element_type | solution.py:130
  (108 shorter events, 9.2 us)
Async XLA Ops:
  0.6 100.4 %copy-start = (bf16[512,2048]{1,0:T(8,128)(2,1)S(1)}, bf16[512,2048]{1,0:T(8,128)(2,1)}, u32[]{:S(2)}) copy-start(bf16[512,2048]{1,0:T(8,128)(2,1)} %param.27) | copy-start | bytes 6291460
  0.6 16.0 %copy-start.11 = (bf16[64,2048]{1,0:T(8,128)(2,1)S(1)}, bf16[64,2048]{1,0:T(8,128)(2,1)}, u32[]{:S(2)}) copy-start(bf16[64,2048]{1,0:T(8,128)(2,1)} %param.14) | copy-start | bytes 786436
  0.7 13.2 %collective-permute-start = (bf16[64,2048]{1,0:T(8,128)(2,1)}, bf16[64,2048]{1,0:T(8,128)(2,1)S(1)}, u32[]{:S(2)}, u32[]{:S(2)}) collective-permute-start(bf16[64,2048]{1,0:T(8,128)(2,1)} %param.14), channel_id=1, source_target_pairs={{0,3},{1,0},{2,1},{3,2},{4,7},{5,4},{6,5},{7,6},{8,11},{9,8},{10,9... | collective-permute-start | bytes 786440 | tf_op jit(solution)/shard_map/ppermute | solution.py:115
  1.7 13.5 %collective-permute-start.1 = (bf16[64,2048]{1,0:T(8,128)(2,1)}, bf16[64,2048]{1,0:T(8,128)(2,1)S(1)}, u32[]{:S(2)}, u32[]{:S(2)}) collective-permute-start(bf16[64,2048]{1,0:T(8,128)(2,1)} %param.14), channel_id=1, source_target_pairs={{0,2},{1,3},{2,0},{3,1},{4,6},{5,7},{6,4},{7,5},{8,10},{9,11},{10,... | collective-permute-start | bytes 786440 | tf_op jit(solution)/shard_map/ppermute | solution.py:115
  2.3 13.6 %collective-permute-start.2 = (bf16[64,2048]{1,0:T(8,128)(2,1)}, bf16[64,2048]{1,0:T(8,128)(2,1)S(1)}, u32[]{:S(2)}, u32[]{:S(2)}) collective-permute-start(bf16[64,2048]{1,0:T(8,128)(2,1)} %param.14), channel_id=1, source_target_pairs={{0,1},{1,2},{2,3},{3,0},{4,5},{5,6},{6,7},{7,4},{8,9},{9,10},{10,1... | collective-permute-start | bytes 786440 | tf_op jit(solution)/shard_map/ppermute | solution.py:115
  6.3 24.0 %copy-start.12 = (f32[256]{0:T(256)}, f32[256]{0:T(256)S(1)}, u32[]{:S(2)}) copy-start(f32[256]{0:T(256)S(1)} %get-tuple-element.36) | copy-start | bytes 3076
  6.3 24.0 %copy-start.14 = (f32[256]{0:T(256)}, f32[256]{0:T(256)S(1)}, u32[]{:S(2)}) copy-start(f32[256]{0:T(256)S(1)} %get-tuple-element.37) | copy-start | bytes 3076
  6.3 24.0 %copy-start.16 = (f32[256]{0:T(256)}, f32[256]{0:T(256)S(1)}, u32[]{:S(2)}) copy-start(f32[256]{0:T(256)S(1)} %get-tuple-element.38) | copy-start | bytes 3076
  6.3 24.0 %copy-start.18 = (f32[256]{0:T(256)}, f32[256]{0:T(256)S(1)}, u32[]{:S(2)}) copy-start(f32[256]{0:T(256)S(1)} %get-tuple-element.39) | copy-start | bytes 3076
  16.6 4.2 %copy-start.29 = (bf16[2048,512]{1,0:T(8,128)(2,1)S(1)}, bf16[2048,512]{1,0:T(8,128)(2,1)}, u32[]{:S(2)}) copy-start(bf16[2048,512]{1,0:T(8,128)(2,1)} %param.18) | copy-start | bytes 6291460
  20.8 1.2 %copy-start.9 = (bf16[2048,256]{1,0:T(8,128)(2,1)S(1)}, bf16[2048,256]{1,0:T(8,128)(2,1)}, u32[]{:S(2)}) copy-start(bf16[2048,256]{1,0:T(8,128)(2,1)} %param.17) | copy-start | bytes 3145732
  20.8 1.7 %copy-start.10 = (bf16[2048,256]{1,0:T(8,128)(2,1)S(1)}, bf16[2048,256]{1,0:T(8,128)(2,1)}, u32[]{:S(2)}) copy-start(bf16[2048,256]{1,0:T(8,128)(2,1)} %param.16) | copy-start | bytes 3145732
  22.0 0.9 copy-start.8
  22.0 5.2 %copy-start.30 = (bf16[2048,16]{0,1:T(8,128)(2,1)S(1)}, bf16[2048,16]{0,1:T(8,128)(2,1)}, u32[]{:S(2)}) copy-start(bf16[2048,16]{0,1:T(8,128)(2,1)} %param.22) | copy-start | bytes 196612
  22.0 5.2 %copy-start.31 = (bf16[16,256]{1,0:T(8,128)(2,1)S(1)}, bf16[16,256]{1,0:T(8,128)(2,1)}, u32[]{:S(2)}) copy-start(bf16[16,256]{1,0:T(8,128)(2,1)} %param.23) | copy-start | bytes 24580
  22.0 5.2 %copy-start.33 = (f32[256]{0:T(256)S(1)}, f32[256]{0:T(256)}, u32[]{:S(2)}) copy-start(f32[256]{0:T(256)} %param.24) | copy-start | bytes 3076
  22.5 0.6 copy-start.5
  23.1 0.7 copy-start.6
  23.8 6.4 %collective-permute-start.3 = (bf16[3,1024]{1,0:T(4,128)(2,1)S(1)}, bf16[3,1024]{1,0:T(4,128)(2,1)S(1)}, u32[]{:S(2)}, u32[]{:S(2)}) collective-permute-start(bf16[3,1024]{1,0:T(4,128)(2,1)S(1)} %get-tuple-element.4), channel_id=1, source_target_pairs={{0,4},{4,8},{8,12},{12,16},{16,20},{20,24},{24,28},{1,5},{5,9},{9,... | collective-permute-start | bytes 18440 | tf_op jit(solution)/shard_map/ppermute | solution.py:15
  32.3 1.5 %copy-start.2 = (bf16[256,512]{1,0:T(8,128)(2,1)}, bf16[256,512]{1,0:T(8,128)(2,1)S(1)}, u32[]{:S(2)}) copy-start(bf16[256,512]{1,0:T(8,128)(2,1)S(1)} %multiply_convert_fusion.1) | copy-start | bytes 786436
  33.8 6.1 %copy-start.28 = (f32[4]{0:T(128)S(1)}, f32[4]{0:T(128)}, u32[]{:S(2)}) copy-start(f32[4]{0:T(128)} %pad.clone) | copy-start | bytes 52
  35.3 23.2 %copy-start.7 = (bf16[256,256]{1,0:T(8,128)(2,1)S(1)}, bf16[256,256]{1,0:T(8,128)(2,1)}, u32[]{:S(2)}) copy-start(bf16[256,256]{1,0:T(8,128)(2,1)} %copy-done.6) | copy-start | bytes 393220
  35.3 23.2 %copy-start.13 = (f32[256]{0:T(256)S(1)}, f32[256]{0:T(256)}, u32[]{:S(2)}) copy-start(f32[256]{0:T(256)} %copy-done.12) | copy-start | bytes 3076
  35.3 23.2 %copy-start.15 = (f32[256]{0:T(256)S(1)}, f32[256]{0:T(256)}, u32[]{:S(2)}) copy-start(f32[256]{0:T(256)} %copy-done.14) | copy-start | bytes 3076
  35.4 23.2 %copy-start.17 = (f32[256]{0:T(256)S(1)}, f32[256]{0:T(256)}, u32[]{:S(2)}) copy-start(f32[256]{0:T(256)} %copy-done.16) | copy-start | bytes 3076
  35.4 23.2 %copy-start.19 = (f32[256]{0:T(256)S(1)}, f32[256]{0:T(256)}, u32[]{:S(2)}) copy-start(f32[256]{0:T(256)} %copy-done.18) | copy-start | bytes 3076
  35.4 23.2 %copy-start.23 = (f32[256]{0:T(256)S(1)}, f32[256]{0:T(256)}, u32[]{:S(2)}) copy-start(f32[256]{0:T(256)} %reshape.239) | copy-start | bytes 3076
  35.4 23.2 %copy-start.24 = (f32[1,256]{1,0:T(1,128)S(1)}, f32[1,256]{1,0:T(1,128)}, u32[]{:S(2)}) copy-start(f32[1,256]{1,0:T(1,128)} %get-tuple-element.22) | copy-start | bytes 3076
  35.4 23.2 %copy-start.25 = (f32[1,256]{1,0:T(1,128)S(1)}, f32[1,256]{1,0:T(1,128)}, u32[]{:S(2)}) copy-start(f32[1,256]{1,0:T(1,128)} %get-tuple-element.23) | copy-start | bytes 3076
  35.4 23.2 %copy-start.26 = (f32[1,256]{1,0:T(1,128)S(1)}, f32[1,256]{1,0:T(1,128)}, u32[]{:S(2)}) copy-start(f32[1,256]{1,0:T(1,128)} %get-tuple-element.24) | copy-start | bytes 3076
  35.4 23.2 %copy-start.27 = (f32[1,256]{1,0:T(1,128)S(1)}, f32[1,256]{1,0:T(1,128)}, u32[]{:S(2)}) copy-start(f32[1,256]{1,0:T(1,128)} %get-tuple-element.25) | copy-start | bytes 3076
  35.4 18.4 %collective-permute-start.6 = (f32[256,512]{1,0:T(8,128)S(1)}, f32[256,512]{1,0:T(8,128)S(1)}, u32[]{:S(2)}, u32[]{:S(2)}) collective-permute-start(f32[256,512]{1,0:T(8,128)S(1)} %fusion.4), channel_id=1, source_target_pairs={{0,4},{4,8},{8,12},{12,16},{16,20},{20,24},{24,28},{1,5},{5,9},{9,... | collective-permute-start | bytes 1572872 | tf_op jit(solution)/shard_map/ppermute | solution.py:15
  38.0 14.5 %collective-permute-start.4 = (f32[256]{0:T(256)S(1)}, f32[256]{0:T(256)S(1)}, u32[]{:S(2)}, u32[]{:S(2)}) collective-permute-start(f32[256]{0:T(256)S(1)} %get-tuple-element.34), channel_id=1, source_target_pairs={{0,4},{4,8},{8,12},{12,16},{16,20},{20,24},{24,28},{1,5},{5,9},{9,... | collective-permute-start | bytes 3080 | tf_op jit(solution)/shard_map/ppermute | solution.py:15
  52.5 7.9 %copy-start.20 = (f32[256]{0:T(256)}, f32[256]{0:T(256)S(1)}, u32[]{:S(2)}) copy-start(f32[256]{0:T(256)S(1)} %collective-permute-done.4) | copy-start | bytes 3076
  52.5 5.5 %collective-permute-start.5 = (f32[256]{0:T(256)S(1)}, f32[256]{0:T(256)S(1)}, u32[]{:S(2)}, u32[]{:S(2)}) collective-permute-start(f32[256]{0:T(256)S(1)} %multiply_select_fusion.2), channel_id=1, source_target_pairs={{0,8},{4,12},{8,16},{12,20},{16,24},{20,28},{1,9},{5,13},{9,17},{1... | collective-permute-start | bytes 3080 | tf_op jit(solution)/shard_map/ppermute | solution.py:15
  53.8 6.7 %copy-start.3 = (f32[256,512]{1,0:T(8,128)}, f32[256,512]{1,0:T(8,128)S(1)}, u32[]{:S(2)}) copy-start(f32[256,512]{1,0:T(8,128)S(1)} %collective-permute-done.6) | copy-start | bytes 1572868
  54.1 15.8 %collective-permute-start.7 = (f32[256,512]{1,0:T(8,128)S(1)}, f32[256,512]{1,0:T(8,128)S(1)}, u32[]{:S(2)}, u32[]{:S(2)}) collective-permute-start(f32[256,512]{1,0:T(8,128)S(1)} %add_select_fusion.4), channel_id=1, source_target_pairs={{0,8},{4,12},{8,16},{12,20},{16,24},{20,28},{1,9},{5,13},{9,17},{1... | collective-permute-start | bytes 1572872 | tf_op jit(solution)/shard_map/ppermute | solution.py:15
  59.6 0.7 copy-start.1
  69.9 1.0 copy-start.4
  70.9 26.9 %copy-start.21 = (f32[256]{0:T(256)S(1)}, f32[256]{0:T(256)}, u32[]{:S(2)}) copy-start(f32[256]{0:T(256)} %copy-done.20) | copy-start | bytes 3076
  70.9 26.9 %collective-permute-start.8 = (f32[256,512]{1,0:T(8,128)}, f32[256,512]{1,0:T(8,128)}, u32[]{:S(2)}, u32[]{:S(2)}) collective-permute-start(f32[256,512]{1,0:T(8,128)} %add_select_fusion.3), channel_id=1, source_target_pairs={{0,16},{4,20},{8,24},{12,28},{1,17},{5,21},{9,25},{13,29},{2,18},{... | collective-permute-start | bytes 1572872 | tf_op jit(solution)/shard_map/ppermute | solution.py:15
  77.1 24.0 %copy-start.32 = (f32[512]{0:T(512)S(1)}, f32[512]{0:T(512)}, u32[]{:S(2)}) copy-start(f32[512]{0:T(512)} %param.26) | copy-start | bytes 6148
  101.1 6.1 %copy-start.22 = (f32[256]{0:T(256)S(1)}, f32[256]{0:T(256)}, u32[]{:S(2)}) copy-start(f32[256]{0:T(256)} %get-tuple-element.32) | copy-start | bytes 3076
  106.3 6.8 %collective-permute-start.11 = (bf16[64,2048]{1,0:T(8,128)(2,1)S(1)}, bf16[64,2048]{1,0:T(8,128)(2,1)S(1)}, u32[]{:S(2)}, u32[]{:S(2)}) collective-permute-start(bf16[64,2048]{1,0:T(8,128)(2,1)S(1)} %get-tuple-element.10), channel_id=1, source_target_pairs={{0,3},{1,0},{2,1},{3,2},{4,7},{5,4},{6,5},{7,6},{8,11},{9,8},{10,9... | collective-permute-start | bytes 786440 | tf_op jit(solution)/shard_map/ppermute | solution.py:129
  106.4 12.7 %collective-permute-start.10 = (bf16[64,2048]{1,0:T(8,128)(2,1)S(1)}, bf16[64,2048]{1,0:T(8,128)(2,1)S(1)}, u32[]{:S(2)}, u32[]{:S(2)}) collective-permute-start(bf16[64,2048]{1,0:T(8,128)(2,1)S(1)} %get-tuple-element.11), channel_id=1, source_target_pairs={{0,2},{1,3},{2,0},{3,1},{4,6},{5,7},{6,4},{7,5},{8,10},{9,11},{10,... | collective-permute-start | bytes 786440 | tf_op jit(solution)/shard_map/ppermute | solution.py:129
  107.1 12.8 %collective-permute-start.9 = (bf16[64,2048]{1,0:T(8,128)(2,1)S(1)}, bf16[64,2048]{1,0:T(8,128)(2,1)S(1)}, u32[]{:S(2)}, u32[]{:S(2)}) collective-permute-start(bf16[64,2048]{1,0:T(8,128)(2,1)S(1)} %get-tuple-element.9), channel_id=1, source_target_pairs={{0,1},{1,2},{2,3},{3,0},{4,5},{5,6},{6,7},{7,4},{8,9},{9,10},{10,1... | collective-permute-start | bytes 786440 | tf_op jit(solution)/shard_map/ppermute | solution.py:129

commit v3 on v2

--- a/solution.py
+++ b/solution.py
@@ -1,3 +1,5 @@
+import functools
+
 import jax
 import jax.numpy as jnp
 from jax import lax
@@ -113,10 +115,11 @@
     count = lax.axis_size(axis)
     place = lax.axis_index(axis)
     received = [rows] + [lax.ppermute(rows, axis, pairs) for pairs in rotations(axis)]
-    reverse = [received[(-index) % count] for index in range(count)]
-    doubled = jnp.stack(reverse + reverse)
-    ordered = lax.dynamic_slice_in_dim(doubled, (count - place) % count, count, axis=0)
-    return ordered.reshape((count * rows.shape[0],) + rows.shape[1:])
+
+    def ordered(shift):
+        return jnp.concatenate([received[(shift - index) % count] for index in range(count)])
+
+    return lax.switch(place, [functools.partial(ordered, shift) for shift in range(count)])
 
 
 def scatter_sum(terms, axis):

time: 122 us -> 114 us (0.934)
  local copies, waits for them, and re-layouts: 13.6 us -> 5.09 us
  waiting for transfers between devices: 55.4 us -> 52.7 us
  matrix products: 17.6 us -> 19.4 us
    unnamed x76 -> x65, local copies, waits for them, and re-layouts: 7.5 us -> 1.04 us
    ppermute x6, waiting for transfers between devices: 44.2 us -> 39 us  [shifted(): lax.ppermute(value, axis, [(source, source + steps) for source in range(i...]
    ppermute x3, waiting for transfers between devices: 0.58 us -> 3.11 us  [gather_rows(): lax.ppermute(rows, axis, pairs)]
    dot_general x3, matrix products: 1.58 us -> 3.32 us  [project(): jnp.dot(gathered, weight, preferred_element_type=jnp.float32)]
    dynamic_slice x1 -> x0, local copies, waits for them, and re-layouts: 1.29 us -> none  [gather_rows(): lax.dynamic_slice_in_dim(doubled, (count - place) % count, count, axis=0)]
  transfers between devices with their start and end apart: 12 -> 12, of which waited for: 9 -> 9; matrix products, arithmetic and copies ran while one was open for 21% -> 20% of each run, Pallas kernels for 0% -> 0%
where the time goes in v3:
time: 114 us; the launch traced here: 113 us
  waiting for transfers between devices  52.7 us (46%)
  other arithmetic  20.6 us (18%)
  matrix products  19.4 us (17%)
  starting transfers between devices  14.4 us (13%)
  local copies, waits for them, and re-layouts  5.09 us (4%)
  between operations  1.19 us (1%)
    ppermute x6, waiting for transfers between devices, shifted(): lax.ppermute(value, axis, [(source, source + steps) for source in range(i...  39 us
    ppermute x6, starting transfers between devices, shifted(): lax.ppermute(value, axis, [(source, source + steps) for source in range(i...  11.8 us
    ppermute x3, waiting for transfers between devices, scatter_sum(): total = total + lax.ppermute(outgoing, axis, pairs).astype(jnp.float32)  10.6 us
    dot_general x1, matrix products, shards(): jnp.dot(gated_out, out_weight, preferred_element_type=jnp.float32)  4.08 us
    mul x3, other arithmetic, short_conv(): weight[tap_index].astype(jnp.float32)[None, :] * window.astype(jnp.float32)  3.68 us
    dot_general x3, matrix products, segment_parts(): jnp.dot(lifted_intact[block], memory, precision=HIGHEST_PRECISION)  3.65 us
    convert_element_type x2, other arithmetic, short_conv(): return jax.nn.silu(summed).astype(jnp.bfloat16)  3.44 us
    dot_general x3, matrix products, project(): jnp.dot(gathered, weight, preferred_element_type=jnp.float32)  3.32 us
  transfers between devices with their start and end apart: 12, of which 9 were waited for; matrix products, arithmetic and copies ran while one was open for 20% of the time, Pallas kernels for 0%

profile of v3, /device:TPU:24, one launch (start us, length us, event | category | flops | bytes accessed | tf_op | source)
XLA Modules:
  0.0 113.5 jit_solution(7095246871404871548)
XLA Ops:
  0.6 1.0 collective-permute-start
  1.7 0.6 collective-permute-start.1
  2.5 0.8 reduce-window.9
  3.3 0.7 bitcast_subtract_fusion
  4.7 0.7 slice_compare_fusion
  5.4 1.4 %slice_convert_fusion.7 = (f32[1,256]{1,0:T(1,128)}, f32[1,256]{1,0:T(1,128)}, f32[1,256]{1,0:T(1,128)}, f32[1,256]{1,0:T(1,128)}) fusion(bf16[4,256]{1,0:T(4,128)(2,1)} %param.24), kind=kLoop, calls=%fused_computation.140 | loop fusion | flops 1024 | bytes 6144 | tf_op jit(solution)/shard_map/mul | solution.py:36
  7.3 0.7 compare_convert_fusion.1
  8.0 1.4 %slice_convert_fusion.11 = (f32[1,256]{1,0:T(1,128)}, f32[1,256]{1,0:T(1,128)}, f32[1,256]{1,0:T(1,128)}, f32[1,256]{1,0:T(1,128)}) fusion(bf16[4,256]{1,0:T(4,128)(2,1)} %param.23), kind=kLoop, calls=%fused_computation.144 | loop fusion | flops 1024 | bytes 6144 | tf_op jit(solution)/shard_map/mul | solution.py:36
  9.6 0.7 reshape.235
  10.8 0.6 pad.20.clone
  11.4 0.8 slice_convert_fusion.3
  12.2 3.1 %collective-permute-done.1 = bf16[64,2048]{1,0:T(8,128)(2,1)} collective-permute-done((bf16[64,2048]{1,0:T(8,128)(2,1)}, bf16[64,2048]{1,0:T(8,128)(2,1)}, u32[]{:S(2)}, u32[]{:S(2)}) %collective-permute-start.1) | collective-permute-done | bytes 262176 | tf_op jit(solution)/shard_map/ppermute | solution.py:117
  15.3 1.2 %conditional.1 = (bf16[256,2048]{1,0:T(8,128)(2,1)S(1)}) conditional(s32[]{:T(128)} %clamp.3, (bf16[64,2048]{1,0:T(8,128)(2,1)}, bf16[64,2048]{1,0:T(8,128)(2,1)S(1)}, bf16[64,2048]{1,0:T(8,128)(2,1)}, bf16[64,2048]{1,0:T(8,128)(2,1)}) %tuple.20, (bf16[64,2048]{1,0:T(8,128)(2,1)}, bf16[64,2048]{1,0:T(8,128)(2,1)}, ...), branch_computations={%region_3.0_spmd, %region_4.0_spmd, %region_5.6_spmd, %region_6.7_... | conditional | flops 4194304 | bytes 2097160 | solution.py:122
  15.3 1.2 %pad_maximum_fusion = bf16[256,2048]{1,0:T(8,128)(2,1)S(1)} fusion(bf16[64,2048]{1,0:T(8,128)(2,1)} %get-tuple-element.40, bf16[64,2048]{1,0:T(8,128)(2,1)} %get-tuple-element.34, bf16[64,2048]{1,0:T(8,128)(2,1)S(1)} %get-tuple-element.33, bf16[64,2048]{1,0:T(8,128)(2,1)} %get-tuple-element.32), kind=kLoop, calls=%fused_computation | loop fusion | flops 4194304 | bytes 2097152 | tf_op jit(solution)/shard_map/cond/branch_0_fun/concatenate | solution.py:120
  16.5 2.4 %convolution_convert_fusion.2 = bf16[256,512]{1,0:T(8,128)(2,1)S(1)} fusion(bf16[256,2048]{1,0:T(8,128)(2,1)S(1)} %get-tuple-element.95, bf16[2048,512]{1,0:T(8,128)(2,1)} %param.22), kind=kOutput, calls=%fused_computation.8 | convolution fusion | flops 537001984 | bytes 3407872 | tf_op jit(solution)/shard_map/dot_general | solution.py:155
  20.2 0.7 select_bitcast_fusion
  20.8 3.4 %collective-permute-start.3 = (bf16[3,1024]{1,0:T(4,128)(2,1)S(1)}, bf16[3,1024]{1,0:T(4,128)(2,1)S(1)}, u32[]{:S(2)}, u32[]{:S(2)}) collective-permute-start(bf16[3,1024]{1,0:T(4,128)(2,1)S(1)} %get-tuple-element.57), channel_id=1, source_target_pairs={{0,4},{4,8},{8,12},{12,16},{16,20},{20,24},{24,28},{1,5},{5,9},{9,... | collective-permute-start | bytes 18440 | tf_op jit(solution)/shard_map/ppermute | solution.py:17
  24.3 1.5 %fusion.27 = f32[256,256]{1,0:T(8,128)} fusion(bf16[16,256]{1,0:T(8,128)(2,1)S(1)} %copy-done.29, bf16[256,2048]{1,0:T(8,128)(2,1)S(1)} %get-tuple-element.95, bf16[2048,16]{0,1:T(8,128)(2,1)S(1)} %copy-done.28, f32[256]{0:T(256)S(1)} %copy-done.31), kind=kOutput, calls=%fused_computation.64 | convolution fusion | flops 19533824 | bytes 1385472 | tf_op jit(solution)/shard_map/dot_general | solution.py:182
  25.8 1.2 %reduce_window_sum.30 = f32[4,64,256]{2,1,0:T(8,128)S(1)} reduce-window(f32[4,64,256]{2,1,0:T(8,128)} %bitcast.133, f32[]{:T(128)} %constant.82.clone.1), window={size=1x64x1 pad=0_0x63_0x0_0}, to_apply=%region_7.8 | reduce-window | flops 4128768 | bytes 524292 | tf_op jit(solution)/shard_map/jit(cumsum)/reduce_window_sum | solution.py:48
  27.3 2.0 %multiply_convert_fusion.1 = bf16[256,512]{1,0:T(8,128)(2,1)S(1)} fusion(bf16[256,512]{1,0:T(8,128)(2,1)} %copy-done.8, bf16[3,512]{1,0:T(4,128)(2,1)S(1)} %slice.188, f32[256]{0:T(256)S(1)} %get-tuple-element.90, f32[512]{0:T(512)S(1)} %bitcast.150, f32[256]{0:T(256)S(1)} %get-tuple-element.91, f32[512]{0:T(512)S(1)} %bitcast.151, ...), kind=kLoop, calls=%fused_computation.51 | loop fusion | flops 3801088 | bytes 539648 | tf_op jit(solution)/shard_map/convert_element_type | solution.py:40
  29.3 1.5 %multiply_convert_fusion.2 = bf16[256,256]{1,0:T(8,128)(2,1)S(1)} fusion(bf16[256,256]{1,0:T(8,128)(2,1)} %copy-done.5, bf16[3,256]{1,0:T(4,128)(2,1)S(1)} %get-tuple-element.66, f32[256]{0:T(256)} %bitcast.154, f32[256]{0:T(256)} %bitcast.155, f32[256]{0:T(256)} %bitcast.153, f32[256]{0:T(256)} %bitcast.152, f32[256]{0:T(256)} %copy-done.13, ...), kind=kLoop, calls=%fused_computation.79 | loop fusion | flops 1900544 | bytes 271872 | tf_op jit(solution)/shard_map/convert_element_type | solution.py:40
  30.8 1.3 %fusion.42 = f32[4,256,512]{2,1,0:T(8,128)S(1)} fusion(bf16[4,64,512]{2,1,0:T(8,128)(2,1)S(1)} %bitcast.126, bf16[4,64,256]{2,1,0:T(8,128)(2,1)S(1)} %bitcast.129, f32[4,64,256]{2,1,0:T(8,128)S(1)} %reduce_window_sum.30, f32[4,64]{1,0:T(4,128)} %get-tuple-element.80, f32[4,256]{1,0:T(4,128)S(1)} %bitcast.146), kind=kOutput, calls=%fused_computation.91 | convolution fusion | flops 67436544 | bytes 2757632 | tf_op jit(solution)/shard_map/bsk,bsv->bkv/dot_general | solution.py:58
  32.4 2.5 %collective-permute-start.6 = (f32[256,512]{1,0:T(8,128)S(1)}, f32[256,512]{1,0:T(8,128)S(1)}, u32[]{:S(2)}, u32[]{:S(2)}) collective-permute-start(f32[256,512]{1,0:T(8,128)S(1)} %fusion.4), channel_id=1, source_target_pairs={{0,4},{4,8},{8,12},{12,16},{16,20},{20,24},{24,28},{1,5},{5,9},{9,... | collective-permute-start | bytes 1572872 | tf_op jit(solution)/shard_map/ppermute | solution.py:17
  34.9 1.9 %collective-permute-start.4 = (f32[256]{0:T(256)S(1)}, f32[256]{0:T(256)S(1)}, u32[]{:S(2)}, u32[]{:S(2)}) collective-permute-start(f32[256]{0:T(256)S(1)} %get-tuple-element.87), channel_id=1, source_target_pairs={{0,4},{4,8},{8,12},{12,16},{16,20},{20,24},{24,28},{1,5},{5,9},{9,... | collective-permute-start | bytes 3080 | tf_op jit(solution)/shard_map/ppermute | solution.py:17
  37.0 10.7 %collective-permute-done.4 = f32[256]{0:T(256)S(1)} collective-permute-done((f32[256]{0:T(256)S(1)}, f32[256]{0:T(256)S(1)}, u32[]{:S(2)}, u32[]{:S(2)}) %collective-permute-start.4) | collective-permute-done | bytes 1056 | tf_op jit(solution)/shard_map/ppermute | solution.py:17
  47.7 1.3 %collective-permute-start.5 = (f32[256]{0:T(256)S(1)}, f32[256]{0:T(256)S(1)}, u32[]{:S(2)}, u32[]{:S(2)}) collective-permute-start(f32[256]{0:T(256)S(1)} %multiply_select_fusion.2), channel_id=1, source_target_pairs={{0,8},{4,12},{8,16},{12,20},{16,24},{20,28},{1,9},{5,13},{9,17},{1... | collective-permute-start | bytes 3080 | tf_op jit(solution)/shard_map/ppermute | solution.py:17
  49.3 1.3 %collective-permute-start.7 = (f32[256,512]{1,0:T(8,128)S(1)}, f32[256,512]{1,0:T(8,128)S(1)}, u32[]{:S(2)}, u32[]{:S(2)}) collective-permute-start(f32[256,512]{1,0:T(8,128)S(1)} %add_select_fusion.4), channel_id=1, source_target_pairs={{0,8},{4,12},{8,16},{12,20},{16,24},{20,28},{1,9},{5,13},{9,17},{1... | collective-permute-start | bytes 1572872 | tf_op jit(solution)/shard_map/ppermute | solution.py:17
  50.6 2.6 %collective-permute-done.5 = f32[256]{0:T(256)S(1)} collective-permute-done((f32[256]{0:T(256)S(1)}, f32[256]{0:T(256)S(1)}, u32[]{:S(2)}, u32[]{:S(2)}) %collective-permute-start.5) | collective-permute-done | bytes 1056 | tf_op jit(solution)/shard_map/ppermute | solution.py:17
  53.2 0.6 multiply_select_fusion
  53.9 1.0 bitcast_multiply_fusion
  54.9 0.7 copy-done.1
  55.7 1.2 %convolution_bitcast_fusion.1 = f32[1,64,512]{2,1,0:T(8,128)} fusion(f32[4,64,256]{2,1,0:T(8,128)S(1)} %broadcast_multiply_fusion, f32[4,256,512]{2,1,0:T(8,128)S(1)} %fusion.42, f32[256]{0:T(256)S(1)} %bitcast.137, f32[256]{0:T(256)S(1)} %get-tuple-element.88), kind=kOutput, calls=%fused_computation.15 | convolution fusion | flops 101056512 | bytes 1247232 | tf_op jit(solution)/shard_map/dot_general | solution.py:79
  56.9 6.5 %collective-permute-done.7 = f32[256,512]{1,0:T(8,128)S(1)} collective-permute-done((f32[256,512]{1,0:T(8,128)S(1)}, f32[256,512]{1,0:T(8,128)S(1)}, u32[]{:S(2)}, u32[]{:S(2)}) %collective-permute-start.7) | collective-permute-done | bytes 524320 | tf_op jit(solution)/shard_map/ppermute | solution.py:17
  63.4 1.0 add_select_fusion.3
  64.4 1.4 %collective-permute-start.8 = (f32[256,512]{1,0:T(8,128)}, f32[256,512]{1,0:T(8,128)}, u32[]{:S(2)}, u32[]{:S(2)}) collective-permute-start(f32[256,512]{1,0:T(8,128)} %add_select_fusion.3), channel_id=1, source_target_pairs={{0,16},{4,20},{8,24},{12,28},{1,17},{5,21},{9,25},{13,29},{2,18},{... | collective-permute-start | bytes 1572872 | tf_op jit(solution)/shard_map/ppermute | solution.py:17
  65.8 1.2 %convolution_bitcast_fusion.2 = f32[1,64,512]{2,1,0:T(8,128)} fusion(f32[4,256,512]{2,1,0:T(8,128)S(1)} %fusion.42, f32[256]{0:T(256)S(1)} %get-tuple-element.88, f32[4,64,256]{2,1,0:T(8,128)S(1)} %broadcast_multiply_fusion), kind=kOutput, calls=%fused_computation.16 | convolution fusion | flops 100794368 | bytes 721920 | tf_op jit(solution)/shard_map/dot_general | solution.py:79
  67.0 1.3 %convolution_bitcast_fusion = f32[1,64,512]{2,1,0:T(8,128)} fusion(f32[4,256,512]{2,1,0:T(8,128)S(1)} %fusion.42, f32[256]{0:T(256)S(1)} %bitcast.142, f32[4,64,256]{2,1,0:T(8,128)S(1)} %broadcast_multiply_fusion, f32[256]{0:T(256)S(1)} %bitcast.138, f32[256]{0:T(256)S(1)} %get-tuple-element.88), kind=kOutput, calls=%fused_computation.14 | convolution fusion | flops 101318656 | bytes 1772544 | tf_op jit(solution)/shard_map/dot_general | solution.py:79
  68.3 2.3 %convolution_add_fusion = f32[4,64,512]{2,1,0:T(8,128)} fusion(bf16[4,64,512]{2,1,0:T(8,128)(2,1)} %bitcast.127, f32[1,64,512]{2,1,0:T(8,128)} %convolution_bitcast_fusion, f32[1,64,512]{2,1,0:T(8,128)} %convolution_bitcast_fusion.1, f32[1,64,512]{2,1,0:T(8,128)} %convolution_bitcast_fusion.2, f32[4]{0:T(128)} %pad.20.clone, ...), kind=kOutput, calls=%fused_computation.5 | convolution fusion | flops 26148864 | bytes 1840144 | tf_op jit(solution)/shard_map/bac,bcv->bav/dot_general | solution.py:70
  70.6 19.0 %collective-permute-done.8 = f32[256,512]{1,0:T(8,128)} collective-permute-done((f32[256,512]{1,0:T(8,128)}, f32[256,512]{1,0:T(8,128)}, u32[]{:S(2)}, u32[]{:S(2)}) %collective-permute-start.8) | collective-permute-done | bytes 524320 | tf_op jit(solution)/shard_map/ppermute | solution.py:17
  89.6 3.2 %multiply_reduce_fusion = (f32[256]{0:T(256)S(1)}, f32[256,512]{1,0:T(8,128)}) fusion(f32[256,512]{1,0:T(8,128)} %bitcast.128, f32[256,256]{1,0:T(8,128)} %get-tuple-element.58, f32[256,512]{1,0:T(8,128)} %copy-done.3, f32[256,512]{1,0:T(8,128)} %copy-done.4, f32[256,512]{1,0:T(8,128)} %collective-permute-done.8, f32[256]{0:T(256)S(1)} %copy-done.20, ...), kind=kOutput, calls=%fused_computation.45 | convolution fusion | flops 403832576 | bytes 2886658 | tf_op jit(solution)/shard_map/dot_general | solution.py:190
  92.8 4.1 %convolution_convert_fusion = bf16[256,2048]{1,0:T(8,128)(2,1)} fusion(bf16[512,2048]{1,0:T(8,128)(2,1)S(1)} %copy-done, bf16[256,2048]{1,0:T(8,128)(2,1)S(1)} %get-tuple-element.95, bf16[2048,512]{1,0:T(8,128)(2,1)} %param.29, f32[256,512]{1,0:T(8,128)} %get-tuple-element.94, f32[512]{0:T(512)S(1)} %copy-done.30, f32[256]{0:T(256)S(1)} %add_rsqrt_fusion), kind=kOutput, calls=%fused_computation.4 | convolution fusion | flops 1075576832 | bytes 6818816 | tf_op jit(solution)/shard_map/dot_general | solution.py:199
  96.9 1.2 %dynamic-slice_bitcast_fusion.2 = (bf16[64,2048]{1,0:T(8,128)(2,1)S(1)}, bf16[64,2048]{1,0:T(8,128)(2,1)S(1)}, bf16[64,2048]{1,0:T(8,128)(2,1)S(1)}) fusion(bf16[4,64,2048]{2,1,0:T(8,128)(2,1)} %bitcast.131, s32[]{:T(128)S(6)} %select_n.107, s32[]{:T(128)S(6)} %select_n.111, s32[]{:T(128)S(6)} %select_n.109), kind=kLoop, calls=%fused_computation.71 | loop fusion | bytes 1572876 | tf_op jit(solution)/shard_map/jit(dynamic_index_in_dim)/squeeze | solution.py:131
  98.1 0.8 collective-permute-start.10
  98.9 2.1 %fusion.3 = f32[1,1,256,512]{3,2,1,0:T(8,128)} fusion(f32[256,512]{1,0:T(8,128)} %add_select_fusion.3, f32[256,512]{1,0:T(8,128)} %collective-permute-done.8, f32[256]{0:T(256)S(1)} %copy-done.21, pred[]{:T(512)S(6)} %ge.76), kind=kLoop, calls=%fused_computation.26 | loop fusion | flops 393216 | bytes 1573889 | tf_op jit(solution)/shard_map/broadcast_in_dim | solution.py:202
  101.0 3.8 %collective-permute-done.11 = bf16[64,2048]{1,0:T(8,128)(2,1)S(1)} collective-permute-done((bf16[64,2048]{1,0:T(8,128)(2,1)S(1)}, bf16[64,2048]{1,0:T(8,128)(2,1)S(1)}, u32[]{:S(2)}, u32[]{:S(2)}) %collective-permute-start.11) | collective-permute-done | bytes 262176 | tf_op jit(solution)/shard_map/ppermute | solution.py:132
  104.8 6.1 %collective-permute-done.10 = bf16[64,2048]{1,0:T(8,128)(2,1)S(1)} collective-permute-done((bf16[64,2048]{1,0:T(8,128)(2,1)S(1)}, bf16[64,2048]{1,0:T(8,128)(2,1)S(1)}, u32[]{:S(2)}, u32[]{:S(2)}) %collective-permute-start.10) | collective-permute-done | bytes 262176 | tf_op jit(solution)/shard_map/ppermute | solution.py:132
  110.9 0.8 collective-permute-done.9
  111.7 1.8 %fusion.7 = bf16[64,2048]{1,0:T(8,128)(2,1)} fusion(bf16[64,2048]{1,0:T(8,128)(2,1)S(1)} %collective-permute-done.11, bf16[64,2048]{1,0:T(8,128)(2,1)S(1)} %collective-permute-done.10, bf16[64,2048]{1,0:T(8,128)(2,1)S(1)} %collective-permute-done.9, bf16[4,64,2048]{2,1,0:T(8,128)(2,1)} %bitcast.132, s32[]{:T(128)S(6)} %select_n.105), kind=kLoop, calls=%fused_computation.32 | loop fusion | flops 1048576 | bytes 1310724 | tf_op jit(solution)/shard_map/convert_element_type | solution.py:133
  (97 shorter events, 4.4 us)
Async XLA Ops:
  0.6 92.2 %copy-start = (bf16[512,2048]{1,0:T(8,128)(2,1)S(1)}, bf16[512,2048]{1,0:T(8,128)(2,1)}, u32[]{:S(2)}) copy-start(bf16[512,2048]{1,0:T(8,128)(2,1)} %param.31) | copy-start | bytes 6291460
  0.6 11.6 %collective-permute-start = (bf16[64,2048]{1,0:T(8,128)(2,1)}, bf16[64,2048]{1,0:T(8,128)(2,1)S(1)}, u32[]{:S(2)}, u32[]{:S(2)}) collective-permute-start(bf16[64,2048]{1,0:T(8,128)(2,1)} %param.18), channel_id=1, source_target_pairs={{0,3},{1,0},{2,1},{3,2},{4,7},{5,4},{6,5},{7,6},{8,11},{9,8},{10,9... | collective-permute-start | bytes 786440 | tf_op jit(solution)/shard_map/ppermute | solution.py:117
  1.7 13.6 %collective-permute-start.1 = (bf16[64,2048]{1,0:T(8,128)(2,1)}, bf16[64,2048]{1,0:T(8,128)(2,1)}, u32[]{:S(2)}, u32[]{:S(2)}) collective-permute-start(bf16[64,2048]{1,0:T(8,128)(2,1)} %param.18), channel_id=1, source_target_pairs={{0,2},{1,3},{2,0},{3,1},{4,6},{5,7},{6,4},{7,5},{8,10},{9,11},{10,... | collective-permute-start | bytes 786440 | tf_op jit(solution)/shard_map/ppermute | solution.py:117
  2.3 13.0 %collective-permute-start.2 = (bf16[64,2048]{1,0:T(8,128)(2,1)}, bf16[64,2048]{1,0:T(8,128)(2,1)}, u32[]{:S(2)}, u32[]{:S(2)}) collective-permute-start(bf16[64,2048]{1,0:T(8,128)(2,1)} %param.18), channel_id=1, source_target_pairs={{0,1},{1,2},{2,3},{3,0},{4,5},{5,6},{6,7},{7,4},{8,9},{9,10},{10,1... | collective-permute-start | bytes 786440 | tf_op jit(solution)/shard_map/ppermute | solution.py:117
  4.6 22.7 %copy-start.11 = (f32[256]{0:T(256)}, f32[256]{0:T(256)S(1)}, u32[]{:S(2)}) copy-start(f32[256]{0:T(256)S(1)} %get-tuple-element.89) | copy-start | bytes 3076
  4.6 22.7 %copy-start.13 = (f32[256]{0:T(256)}, f32[256]{0:T(256)S(1)}, u32[]{:S(2)}) copy-start(f32[256]{0:T(256)S(1)} %get-tuple-element.90) | copy-start | bytes 3076
  4.6 22.7 %copy-start.15 = (f32[256]{0:T(256)}, f32[256]{0:T(256)S(1)}, u32[]{:S(2)}) copy-start(f32[256]{0:T(256)S(1)} %get-tuple-element.91) | copy-start | bytes 3076
  4.6 22.7 %copy-start.17 = (f32[256]{0:T(256)}, f32[256]{0:T(256)S(1)}, u32[]{:S(2)}) copy-start(f32[256]{0:T(256)S(1)} %get-tuple-element.92) | copy-start | bytes 3076
  16.5 2.5 %copy-start.9 = (bf16[2048,256]{1,0:T(8,128)(2,1)S(1)}, bf16[2048,256]{1,0:T(8,128)(2,1)}, u32[]{:S(2)}) copy-start(bf16[2048,256]{1,0:T(8,128)(2,1)} %param.21) | copy-start | bytes 3145732
  16.5 3.0 %copy-start.10 = (bf16[2048,256]{1,0:T(8,128)(2,1)S(1)}, bf16[2048,256]{1,0:T(8,128)(2,1)}, u32[]{:S(2)}) copy-start(bf16[2048,256]{1,0:T(8,128)(2,1)} %param.20) | copy-start | bytes 3145732
  19.0 1.0 copy-start.8
  19.0 5.2 %copy-start.28 = (bf16[2048,16]{0,1:T(8,128)(2,1)S(1)}, bf16[2048,16]{0,1:T(8,128)(2,1)}, u32[]{:S(2)}) copy-start(bf16[2048,16]{0,1:T(8,128)(2,1)} %param.26) | copy-start | bytes 196612
  19.0 5.2 %copy-start.29 = (bf16[16,256]{1,0:T(8,128)(2,1)S(1)}, bf16[16,256]{1,0:T(8,128)(2,1)}, u32[]{:S(2)}) copy-start(bf16[16,256]{1,0:T(8,128)(2,1)} %param.27) | copy-start | bytes 24580
  19.0 5.2 %copy-start.31 = (f32[256]{0:T(256)S(1)}, f32[256]{0:T(256)}, u32[]{:S(2)}) copy-start(f32[256]{0:T(256)} %param.28) | copy-start | bytes 3076
  19.5 0.6 copy-start.5
  20.2 0.7 copy-start.6
  20.8 6.4 %collective-permute-start.3 = (bf16[3,1024]{1,0:T(4,128)(2,1)S(1)}, bf16[3,1024]{1,0:T(4,128)(2,1)S(1)}, u32[]{:S(2)}, u32[]{:S(2)}) collective-permute-start(bf16[3,1024]{1,0:T(4,128)(2,1)S(1)} %get-tuple-element.57), channel_id=1, source_target_pairs={{0,4},{4,8},{8,12},{12,16},{16,20},{20,24},{24,28},{1,5},{5,9},{9,... | collective-permute-start | bytes 18440 | tf_op jit(solution)/shard_map/ppermute | solution.py:17
  29.3 1.5 %copy-start.2 = (bf16[256,512]{1,0:T(8,128)(2,1)}, bf16[256,512]{1,0:T(8,128)(2,1)S(1)}, u32[]{:S(2)}) copy-start(bf16[256,512]{1,0:T(8,128)(2,1)S(1)} %multiply_convert_fusion.1) | copy-start | bytes 786436
  30.8 6.1 %copy-start.27 = (f32[4]{0:T(128)S(1)}, f32[4]{0:T(128)}, u32[]{:S(2)}) copy-start(f32[4]{0:T(128)} %pad.16.clone) | copy-start | bytes 52
  32.3 21.5 %copy-start.7 = (bf16[256,256]{1,0:T(8,128)(2,1)S(1)}, bf16[256,256]{1,0:T(8,128)(2,1)}, u32[]{:S(2)}) copy-start(bf16[256,256]{1,0:T(8,128)(2,1)} %copy-done.6) | copy-start | bytes 393220
  32.3 21.5 %copy-start.12 = (f32[256]{0:T(256)S(1)}, f32[256]{0:T(256)}, u32[]{:S(2)}) copy-start(f32[256]{0:T(256)} %copy-done.11) | copy-start | bytes 3076
  32.3 21.5 %copy-start.14 = (f32[256]{0:T(256)S(1)}, f32[256]{0:T(256)}, u32[]{:S(2)}) copy-start(f32[256]{0:T(256)} %copy-done.13) | copy-start | bytes 3076
  32.4 21.5 %copy-start.16 = (f32[256]{0:T(256)S(1)}, f32[256]{0:T(256)}, u32[]{:S(2)}) copy-start(f32[256]{0:T(256)} %copy-done.15) | copy-start | bytes 3076
  32.4 21.5 %copy-start.18 = (f32[256]{0:T(256)S(1)}, f32[256]{0:T(256)}, u32[]{:S(2)}) copy-start(f32[256]{0:T(256)} %copy-done.17) | copy-start | bytes 3076
  32.4 21.5 %copy-start.22 = (f32[256]{0:T(256)S(1)}, f32[256]{0:T(256)}, u32[]{:S(2)}) copy-start(f32[256]{0:T(256)} %reshape.235) | copy-start | bytes 3076
  32.4 21.5 %copy-start.23 = (f32[1,256]{1,0:T(1,128)S(1)}, f32[1,256]{1,0:T(1,128)}, u32[]{:S(2)}) copy-start(f32[1,256]{1,0:T(1,128)} %get-tuple-element.75) | copy-start | bytes 3076
  32.4 21.5 %copy-start.24 = (f32[1,256]{1,0:T(1,128)S(1)}, f32[1,256]{1,0:T(1,128)}, u32[]{:S(2)}) copy-start(f32[1,256]{1,0:T(1,128)} %get-tuple-element.76) | copy-start | bytes 3076
  32.4 21.5 %copy-start.25 = (f32[1,256]{1,0:T(1,128)S(1)}, f32[1,256]{1,0:T(1,128)}, u32[]{:S(2)}) copy-start(f32[1,256]{1,0:T(1,128)} %get-tuple-element.77) | copy-start | bytes 3076
  32.4 21.5 %copy-start.26 = (f32[1,256]{1,0:T(1,128)S(1)}, f32[1,256]{1,0:T(1,128)}, u32[]{:S(2)}) copy-start(f32[1,256]{1,0:T(1,128)} %get-tuple-element.78) | copy-start | bytes 3076
  32.4 16.6 %collective-permute-start.6 = (f32[256,512]{1,0:T(8,128)S(1)}, f32[256,512]{1,0:T(8,128)S(1)}, u32[]{:S(2)}, u32[]{:S(2)}) collective-permute-start(f32[256,512]{1,0:T(8,128)S(1)} %fusion.4), channel_id=1, source_target_pairs={{0,4},{4,8},{8,12},{12,16},{16,20},{20,24},{24,28},{1,5},{5,9},{9,... | collective-permute-start | bytes 1572872 | tf_op jit(solution)/shard_map/ppermute | solution.py:17
  34.9 12.8 %collective-permute-start.4 = (f32[256]{0:T(256)S(1)}, f32[256]{0:T(256)S(1)}, u32[]{:S(2)}, u32[]{:S(2)}) collective-permute-start(f32[256]{0:T(256)S(1)} %get-tuple-element.87), channel_id=1, source_target_pairs={{0,4},{4,8},{8,12},{12,16},{16,20},{20,24},{24,28},{1,5},{5,9},{9,... | collective-permute-start | bytes 3080 | tf_op jit(solution)/shard_map/ppermute | solution.py:17
  47.7 8.0 %copy-start.19 = (f32[256]{0:T(256)}, f32[256]{0:T(256)S(1)}, u32[]{:S(2)}) copy-start(f32[256]{0:T(256)S(1)} %collective-permute-done.4) | copy-start | bytes 3076
  47.7 5.5 %collective-permute-start.5 = (f32[256]{0:T(256)S(1)}, f32[256]{0:T(256)S(1)}, u32[]{:S(2)}, u32[]{:S(2)}) collective-permute-start(f32[256]{0:T(256)S(1)} %multiply_select_fusion.2), channel_id=1, source_target_pairs={{0,8},{4,12},{8,16},{12,20},{16,24},{20,28},{1,9},{5,13},{9,17},{1... | collective-permute-start | bytes 3080 | tf_op jit(solution)/shard_map/ppermute | solution.py:17
  49.0 6.7 %copy-start.3 = (f32[256,512]{1,0:T(8,128)}, f32[256,512]{1,0:T(8,128)S(1)}, u32[]{:S(2)}) copy-start(f32[256,512]{1,0:T(8,128)S(1)} %collective-permute-done.6) | copy-start | bytes 1572868
  49.3 14.1 %collective-permute-start.7 = (f32[256,512]{1,0:T(8,128)S(1)}, f32[256,512]{1,0:T(8,128)S(1)}, u32[]{:S(2)}, u32[]{:S(2)}) collective-permute-start(f32[256,512]{1,0:T(8,128)S(1)} %add_select_fusion.4), channel_id=1, source_target_pairs={{0,8},{4,12},{8,16},{12,20},{16,24},{20,28},{1,9},{5,13},{9,17},{1... | collective-permute-start | bytes 1572872 | tf_op jit(solution)/shard_map/ppermute | solution.py:17
  54.9 0.7 copy-start.1
  63.4 1.0 copy-start.4
  64.4 25.2 %copy-start.20 = (f32[256]{0:T(256)S(1)}, f32[256]{0:T(256)}, u32[]{:S(2)}) copy-start(f32[256]{0:T(256)} %copy-done.19) | copy-start | bytes 3076
  64.4 25.2 %collective-permute-start.8 = (f32[256,512]{1,0:T(8,128)}, f32[256,512]{1,0:T(8,128)}, u32[]{:S(2)}, u32[]{:S(2)}) collective-permute-start(f32[256,512]{1,0:T(8,128)} %add_select_fusion.3), channel_id=1, source_target_pairs={{0,16},{4,20},{8,24},{12,28},{1,17},{5,21},{9,25},{13,29},{2,18},{... | collective-permute-start | bytes 1572872 | tf_op jit(solution)/shard_map/ppermute | solution.py:17
  70.6 22.2 %copy-start.30 = (f32[512]{0:T(512)S(1)}, f32[512]{0:T(512)}, u32[]{:S(2)}) copy-start(f32[512]{0:T(512)} %param.30) | copy-start | bytes 6148
  92.8 6.1 %copy-start.21 = (f32[256]{0:T(256)S(1)}, f32[256]{0:T(256)}, u32[]{:S(2)}) copy-start(f32[256]{0:T(256)} %get-tuple-element.85) | copy-start | bytes 3076
  98.1 6.8 %collective-permute-start.11 = (bf16[64,2048]{1,0:T(8,128)(2,1)S(1)}, bf16[64,2048]{1,0:T(8,128)(2,1)S(1)}, u32[]{:S(2)}, u32[]{:S(2)}) collective-permute-start(bf16[64,2048]{1,0:T(8,128)(2,1)S(1)} %get-tuple-element.63), channel_id=1, source_target_pairs={{0,3},{1,0},{2,1},{3,2},{4,7},{5,4},{6,5},{7,6},{8,11},{9,8},{10,9... | collective-permute-start | bytes 786440 | tf_op jit(solution)/shard_map/ppermute | solution.py:132
  98.1 12.7 %collective-permute-start.10 = (bf16[64,2048]{1,0:T(8,128)(2,1)S(1)}, bf16[64,2048]{1,0:T(8,128)(2,1)S(1)}, u32[]{:S(2)}, u32[]{:S(2)}) collective-permute-start(bf16[64,2048]{1,0:T(8,128)(2,1)S(1)} %get-tuple-element.64), channel_id=1, source_target_pairs={{0,2},{1,3},{2,0},{3,1},{4,6},{5,7},{6,4},{7,5},{8,10},{9,11},{10,... | collective-permute-start | bytes 786440 | tf_op jit(solution)/shard_map/ppermute | solution.py:132
  98.9 12.8 %collective-permute-start.9 = (bf16[64,2048]{1,0:T(8,128)(2,1)S(1)}, bf16[64,2048]{1,0:T(8,128)(2,1)S(1)}, u32[]{:S(2)}, u32[]{:S(2)}) collective-permute-start(bf16[64,2048]{1,0:T(8,128)(2,1)S(1)} %get-tuple-element.62), channel_id=1, source_target_pairs={{0,1},{1,2},{2,3},{3,0},{4,5},{5,6},{6,7},{7,4},{8,9},{9,10},{10,1... | collective-permute-start | bytes 786440 | tf_op jit(solution)/shard_map/ppermute | solution.py:132

commit v4 on v3

--- a/solution.py
+++ b/solution.py
@@ -92,7 +92,8 @@
     entering = jnp.zeros_like(memory)
     steps = 1
     while steps < count:
-        earlier_decay, earlier_memory = shifted((decay, memory), axis, steps)
+        earlier_decay, earlier_memory = shifted((decay, memory.astype(jnp.bfloat16)), axis, steps)
+        earlier_memory = earlier_memory.astype(jnp.float32)
         valid = place >= steps
         memory = jnp.where(valid, decay[:, None] * earlier_memory + memory, memory)
         decay = jnp.where(valid, earlier_decay * decay, decay)

time: 114 us -> 101 us (0.89)
  waiting for transfers between devices: 52.7 us -> 34.5 us
  other arithmetic: 20.6 us -> 24 us
  matrix products: 19.4 us -> 20.6 us
    ppermute x6, waiting for transfers between devices: 39 us -> 23.2 us  [shifted(): lax.ppermute(value, axis, [(source, source + steps) for source in range(i...]
    ppermute x3, waiting for transfers between devices: 3.11 us -> 0.99 us  [gather_rows(): lax.ppermute(rows, axis, pairs)]
    dot_general x3, matrix products: 3.32 us -> 4.67 us  [project(): jnp.dot(gathered, weight, preferred_element_type=jnp.float32)]
    convert_element_type x0 -> x3, other arithmetic: none -> 1.28 us  [prefix_states(): memory.astype(jnp.bfloat16)]
    select_n x2 -> x0, other arithmetic: 1.27 us -> none  [prefix_states(): memory = jnp.where(valid, decay[:, None] * earlier_memory + memory, memory)]
  transfers between devices with their start and end apart: 12 -> 12, of which waited for: 9 -> 8; matrix products, arithmetic and copies ran while one was open for 20% -> 24% of each run, Pallas kernels for 0% -> 0%
where the time goes in v4:
time: 101 us; the launch traced here: 100 us
  waiting for transfers between devices  34.5 us (34%)
  other arithmetic  24 us (24%)
  matrix products  20.6 us (20%)
  starting transfers between devices  15.4 us (15%)
  local copies, waits for them, and re-layouts  4.63 us (5%)
  between operations  1.14 us (1%)
    ppermute x6, waiting for transfers between devices, shifted(): lax.ppermute(value, axis, [(source, source + steps) for source in range(i...  23.2 us
    ppermute x6, starting transfers between devices, shifted(): lax.ppermute(value, axis, [(source, source + steps) for source in range(i...  12.6 us
    ppermute x3, waiting for transfers between devices, scatter_sum(): total = total + lax.ppermute(outgoing, axis, pairs).astype(jnp.float32)  10.3 us
    dot_general x3, matrix products, project(): jnp.dot(gathered, weight, preferred_element_type=jnp.float32)  4.67 us
    mul x3, other arithmetic, short_conv(): weight[tap_index].astype(jnp.float32)[None, :] * window.astype(jnp.float32)  4.3 us
    dot_general x1, matrix products, shards(): jnp.dot(gated_out, out_weight, preferred_element_type=jnp.float32)  4.2 us
    dot_general x3, matrix products, segment_parts(): jnp.dot(lifted_intact[block], memory, precision=HIGHEST_PRECISION)  3.64 us
    convert_element_type x2, other arithmetic, short_conv(): return jax.nn.silu(summed).astype(jnp.bfloat16)  3.03 us
  transfers between devices with their start and end apart: 12, of which 8 were waited for; matrix products, arithmetic and copies ran while one was open for 24% of the time, Pallas kernels for 0%

profile of v4, /device:TPU:24, one launch (start us, length us, event | category | flops | bytes accessed | tf_op | source)
XLA Modules:
  0.0 100.3 jit_solution(1011419290713384864)
XLA Ops:
  0.6 1.0 %collective-permute-start = (bf16[64,2048]{1,0:T(8,128)(2,1)}, bf16[64,2048]{1,0:T(8,128)(2,1)S(1)}, u32[]{:S(2)}, u32[]{:S(2)}) collective-permute-start(bf16[64,2048]{1,0:T(8,128)(2,1)} %param.18), channel_id=1, source_target_pairs={{0,3},{1,0},{2,1},{3,2},{4,7},{5,4},{6,5},{7,6},{8,11},{9,8},{10,9... | collective-permute-start | bytes 786440 | tf_op jit(solution)/shard_map/ppermute | solution.py:118
  1.7 0.6 collective-permute-start.1
  2.5 0.8 reduce-window.9
  3.3 0.7 bitcast_subtract_fusion
  5.3 1.2 %slice_compare_fusion = pred[3]{0:T(512)(128)(4,1)} fusion(s32[256]{0:T(256)S(1)} %iota_add_fusion, s32[]{:T(128)} %bitcast.45), kind=kLoop, calls=%fused_computation.151 | loop fusion | flops 3 | bytes 19 | tf_op jit(solution)/shard_map/ge | solution.py:204
  6.5 1.4 %slice_convert_fusion.7 = (f32[1,256]{1,0:T(1,128)}, f32[1,256]{1,0:T(1,128)}, f32[1,256]{1,0:T(1,128)}, f32[1,256]{1,0:T(1,128)}) fusion(bf16[4,256]{1,0:T(4,128)(2,1)} %param.24), kind=kLoop, calls=%fused_computation.144 | loop fusion | flops 1024 | bytes 6144 | tf_op jit(solution)/shard_map/mul | solution.py:36
  8.4 0.6 compare_convert_fusion.1
  9.0 1.4 %slice_convert_fusion.11 = (f32[1,256]{1,0:T(1,128)}, f32[1,256]{1,0:T(1,128)}, f32[1,256]{1,0:T(1,128)}, f32[1,256]{1,0:T(1,128)}) fusion(bf16[4,256]{1,0:T(4,128)(2,1)} %param.23), kind=kLoop, calls=%fused_computation.148 | loop fusion | flops 1024 | bytes 6144 | tf_op jit(solution)/shard_map/mul | solution.py:36
  10.5 0.8 slice_reduce_fusion.1
  11.2 0.7 reshape.235
  12.9 1.4 %slice_convert_fusion.3 = (f32[1,512]{1,0:T(1,128)}, f32[1,512]{1,0:T(1,128)}, f32[1,512]{1,0:T(1,128)}, f32[1,512]{1,0:T(1,128)}) fusion(bf16[4,512]{1,0:T(4,128)(2,1)} %param.25), kind=kLoop, calls=%fused_computation.127 | loop fusion | flops 2048 | bytes 12288 | tf_op jit(solution)/shard_map/mul | solution.py:36
  14.3 0.9 collective-permute-done.1
  15.3 1.2 %conditional.1 = (bf16[256,2048]{1,0:T(8,128)(2,1)S(1)}) conditional(s32[]{:T(128)} %clamp.3, (bf16[64,2048]{1,0:T(8,128)(2,1)}, bf16[64,2048]{1,0:T(8,128)(2,1)S(1)}, bf16[64,2048]{1,0:T(8,128)(2,1)}, bf16[64,2048]{1,0:T(8,128)(2,1)}) %tuple.20, (bf16[64,2048]{1,0:T(8,128)(2,1)}, bf16[64,2048]{1,0:T(8,128)(2,1)}, ...), branch_computations={%region_3.0_spmd, %region_4.0_spmd, %region_5.6_spmd, %region_6.7_... | conditional | flops 4194304 | bytes 2097160 | solution.py:123
  15.3 1.2 %pad_maximum_fusion = bf16[256,2048]{1,0:T(8,128)(2,1)S(1)} fusion(bf16[64,2048]{1,0:T(8,128)(2,1)} %get-tuple-element.40, bf16[64,2048]{1,0:T(8,128)(2,1)} %get-tuple-element.34, bf16[64,2048]{1,0:T(8,128)(2,1)S(1)} %get-tuple-element.33, bf16[64,2048]{1,0:T(8,128)(2,1)} %get-tuple-element.32), kind=kLoop, calls=%fused_computation | loop fusion | flops 4194304 | bytes 2097152 | tf_op jit(solution)/shard_map/cond/branch_0_fun/concatenate | solution.py:121
  16.5 3.1 %convolution_convert_fusion.2 = bf16[256,512]{1,0:T(8,128)(2,1)} fusion(bf16[256,2048]{1,0:T(8,128)(2,1)S(1)} %get-tuple-element.97, bf16[2048,512]{1,0:T(8,128)(2,1)} %param.22), kind=kOutput, calls=%fused_computation.8 | convolution fusion | flops 537001984 | bytes 3407872 | tf_op jit(solution)/shard_map/dot_general | solution.py:156
  20.2 1.1 %convolution_convert_fusion.4 = bf16[256,256]{1,0:T(8,128)(2,1)} fusion(bf16[256,2048]{1,0:T(8,128)(2,1)S(1)} %get-tuple-element.97, bf16[2048,256]{1,0:T(8,128)(2,1)S(1)} %copy-done.11), kind=kOutput, calls=%fused_computation.13 | convolution fusion | flops 268500992 | bytes 2228224 | tf_op jit(solution)/shard_map/dot_general | solution.py:156
  21.3 1.5 %fusion.26 = f32[256,256]{1,0:T(8,128)} fusion(bf16[16,256]{1,0:T(8,128)(2,1)S(1)} %copy-done.29, bf16[256,2048]{1,0:T(8,128)(2,1)S(1)} %get-tuple-element.97, bf16[2048,16]{0,1:T(8,128)(2,1)S(1)} %copy-done.28, f32[256]{0:T(256)S(1)} %copy-done.30), kind=kOutput, calls=%fused_computation.68 | convolution fusion | flops 19533824 | bytes 1385472 | tf_op jit(solution)/shard_map/dot_general | solution.py:183
  22.8 1.2 %reduce_window_sum.30 = f32[4,64,256]{2,1,0:T(8,128)S(1)} reduce-window(f32[4,64,256]{2,1,0:T(8,128)} %bitcast.129, f32[]{:T(128)} %constant.82.clone.1), window={size=1x64x1 pad=0_0x63_0x0_0}, to_apply=%region_7.8 | reduce-window | flops 4128768 | bytes 524292 | tf_op jit(solution)/shard_map/jit(cumsum)/reduce_window_sum | solution.py:48
  24.0 0.7 exponential_multiply_fusion
  24.7 3.4 %collective-permute-start.4 = (f32[256]{0:T(256)S(1)}, f32[256]{0:T(256)S(1)}, u32[]{:S(2)}, u32[]{:S(2)}) collective-permute-start(f32[256]{0:T(256)S(1)} %get-tuple-element.89), channel_id=1, source_target_pairs={{0,4},{4,8},{8,12},{12,16},{16,20},{20,24},{24,28},{1,5},{5,9},{9,... | collective-permute-start | bytes 3080 | tf_op jit(solution)/shard_map/ppermute | solution.py:17
  28.1 1.4 %select_bitcast_fusion = (bf16[1,3,1,1024]{3,1,2,0:T(4,128)(2,1)}, bf16[3,1024]{1,0:T(4,128)(2,1)S(1)}) fusion(pred[3]{0:T(512)(128)(4,1)} %slice_compare_fusion, bf16[256,512]{1,0:T(8,128)(2,1)} %convolution_convert_fusion.2, bf16[256,256]{1,0:T(8,128)(2,1)S(1)} %convolution_convert_fusion.3, bf16[256,256]{1,0:T(8,128)(2,1)} %convolution_convert_fusion.4), kind=kLoop, calls=%fused_computation.117 | loop fusion | flops 21504 | bytes 536579 | tf_op jit(solution)/shard_map/reshape | solution.py:207
  29.6 1.9 %collective-permute-start.3 = (bf16[3,1024]{1,0:T(4,128)(2,1)S(1)}, bf16[3,1024]{1,0:T(4,128)(2,1)S(1)}, u32[]{:S(2)}, u32[]{:S(2)}) collective-permute-start(bf16[3,1024]{1,0:T(4,128)(2,1)S(1)} %get-tuple-element.57), channel_id=1, source_target_pairs={{0,4},{4,8},{8,12},{12,16},{16,20},{20,24},{24,28},{1,5},{5,9},{9,... | collective-permute-start | bytes 18440 | tf_op jit(solution)/shard_map/ppermute | solution.py:17
  31.5 1.3 %collective-permute-start.5 = (f32[256]{0:T(256)S(1)}, f32[256]{0:T(256)S(1)}, u32[]{:S(2)}, u32[]{:S(2)}) collective-permute-start(f32[256]{0:T(256)S(1)} %multiply_select_fusion.2), channel_id=1, source_target_pairs={{0,8},{4,12},{8,16},{12,20},{16,24},{20,28},{1,9},{5,13},{9,17},{1... | collective-permute-start | bytes 3080 | tf_op jit(solution)/shard_map/ppermute | solution.py:17
  32.8 0.6 pad_maximum_fusion.9
  33.5 3.5 %collective-permute-done.5 = f32[256]{0:T(256)S(1)} collective-permute-done((f32[256]{0:T(256)S(1)}, f32[256]{0:T(256)S(1)}, u32[]{:S(2)}, u32[]{:S(2)}) %collective-permute-start.5) | collective-permute-done | bytes 1056 | tf_op jit(solution)/shard_map/ppermute | solution.py:17
  37.6 2.0 %multiply_convert_fusion.1 = bf16[256,512]{1,0:T(8,128)(2,1)S(1)} fusion(bf16[256,512]{1,0:T(8,128)(2,1)} %convolution_convert_fusion.2, bf16[3,512]{1,0:T(4,128)(2,1)S(1)} %slice.188, f32[256]{0:T(256)} %get-tuple-element.92, f32[512]{0:T(512)} %bitcast.143, f32[256]{0:T(256)} %get-tuple-element.93, f32[512]{0:T(512)} %bitcast.144, ...), kind=kLoop, calls=%fused_computation.54 | loop fusion | flops 3801088 | bytes 539648 | tf_op jit(solution)/shard_map/convert_element_type | solution.py:40
  39.6 1.0 %multiply_convert_fusion.2 = bf16[256,256]{1,0:T(8,128)(2,1)S(1)} fusion(bf16[256,256]{1,0:T(8,128)(2,1)S(1)} %convolution_convert_fusion.3, bf16[3,256]{1,0:T(4,128)(2,1)S(1)} %get-tuple-element.68, f32[256]{0:T(256)} %bitcast.147, f32[256]{0:T(256)} %bitcast.148, f32[256]{0:T(256)} %bitcast.146, f32[256]{0:T(256)} %bitcast.145, f32[256]{0:T(256)} %get-tuple-element.92, ...), kind=kLoop, calls=%fused_computation.83 | loop fusion | flops 1900544 | bytes 271872 | tf_op jit(solution)/shard_map/convert_element_type | solution.py:40
  40.7 1.3 %fusion.41 = f32[4,256,512]{2,1,0:T(8,128)S(1)} fusion(bf16[4,64,512]{2,1,0:T(8,128)(2,1)S(1)} %bitcast.122, bf16[4,64,256]{2,1,0:T(8,128)(2,1)S(1)} %bitcast.125, f32[4,64,256]{2,1,0:T(8,128)S(1)} %reduce_window_sum.30, f32[4,64]{1,0:T(4,128)} %get-tuple-element.82, f32[4,256]{1,0:T(4,128)S(1)} %bitcast.130), kind=kOutput, calls=%fused_computation.95 | convolution fusion | flops 67436544 | bytes 2757632 | tf_op jit(solution)/shard_map/bsk,bsv->bkv/dot_general | solution.py:58
  42.3 3.4 %collective-permute-start.6 = (bf16[256,512]{1,0:T(8,128)(2,1)S(1)}, bf16[256,512]{1,0:T(8,128)(2,1)S(1)}, u32[]{:S(2)}, u32[]{:S(2)}) collective-permute-start(bf16[256,512]{1,0:T(8,128)(2,1)S(1)} %get-tuple-element.58), channel_id=1, source_target_pairs={{0,4},{4,8},{8,12},{12,16},{16,20},{20,24},{24,28},{1,5},{5,9},{9,... | collective-permute-start | bytes 786440 | tf_op jit(solution)/shard_map/ppermute | solution.py:17
  45.8 1.0 bitcast_multiply_fusion
  46.9 1.2 %convolution_bitcast_fusion.1 = f32[1,64,512]{2,1,0:T(8,128)} fusion(f32[4,64,256]{2,1,0:T(8,128)S(1)} %broadcast_multiply_fusion, f32[4,256,512]{2,1,0:T(8,128)S(1)} %fusion.41, f32[256]{0:T(256)S(1)} %bitcast.133, f32[256]{0:T(256)S(1)} %get-tuple-element.90), kind=kOutput, calls=%fused_computation.15 | convolution fusion | flops 101056512 | bytes 1247232 | tf_op jit(solution)/shard_map/dot_general | solution.py:79
  48.1 4.3 %collective-permute-done.6 = bf16[256,512]{1,0:T(8,128)(2,1)S(1)} collective-permute-done((bf16[256,512]{1,0:T(8,128)(2,1)S(1)}, bf16[256,512]{1,0:T(8,128)(2,1)S(1)}, u32[]{:S(2)}, u32[]{:S(2)}) %collective-permute-start.6) | collective-permute-done | bytes 262176 | tf_op jit(solution)/shard_map/ppermute | solution.py:17
  52.6 1.3 %collective-permute-start.7 = (bf16[256,512]{1,0:T(8,128)(2,1)S(1)}, bf16[256,512]{1,0:T(8,128)(2,1)S(1)}, u32[]{:S(2)}, u32[]{:S(2)}) collective-permute-start(bf16[256,512]{1,0:T(8,128)(2,1)S(1)} %fusion.19), channel_id=1, source_target_pairs={{0,8},{4,12},{8,16},{12,20},{16,24},{20,28},{1,9},{5,13},{9,17},{1... | collective-permute-start | bytes 786440 | tf_op jit(solution)/shard_map/ppermute | solution.py:17
  53.9 1.2 %convolution_bitcast_fusion.2 = f32[1,64,512]{2,1,0:T(8,128)} fusion(f32[4,256,512]{2,1,0:T(8,128)S(1)} %fusion.41, f32[256]{0:T(256)S(1)} %get-tuple-element.90, f32[4,64,256]{2,1,0:T(8,128)S(1)} %broadcast_multiply_fusion), kind=kOutput, calls=%fused_computation.16 | convolution fusion | flops 100794368 | bytes 721920 | tf_op jit(solution)/shard_map/dot_general | solution.py:79
  55.1 1.2 %convolution_bitcast_fusion = f32[1,64,512]{2,1,0:T(8,128)} fusion(f32[4,256,512]{2,1,0:T(8,128)S(1)} %fusion.41, f32[256]{0:T(256)S(1)} %bitcast.137, f32[4,64,256]{2,1,0:T(8,128)S(1)} %broadcast_multiply_fusion, f32[256]{0:T(256)S(1)} %bitcast.134, f32[256]{0:T(256)S(1)} %get-tuple-element.90), kind=kOutput, calls=%fused_computation.14 | convolution fusion | flops 101318656 | bytes 1772544 | tf_op jit(solution)/shard_map/dot_general | solution.py:79
  56.3 4.6 %collective-permute-done.7 = bf16[256,512]{1,0:T(8,128)(2,1)S(1)} collective-permute-done((bf16[256,512]{1,0:T(8,128)(2,1)S(1)}, bf16[256,512]{1,0:T(8,128)(2,1)S(1)}, u32[]{:S(2)}, u32[]{:S(2)}) %collective-permute-start.7) | collective-permute-done | bytes 262176 | tf_op jit(solution)/shard_map/ppermute | solution.py:17
  61.0 0.9 fusion.63
  61.9 1.3 %collective-permute-start.8 = (bf16[256,512]{1,0:T(8,128)(2,1)}, bf16[256,512]{1,0:T(8,128)(2,1)}, u32[]{:S(2)}, u32[]{:S(2)}) collective-permute-start(bf16[256,512]{1,0:T(8,128)(2,1)} %fusion.63), channel_id=1, source_target_pairs={{0,16},{4,20},{8,24},{12,28},{1,17},{5,21},{9,25},{13,29},{2,18},{... | collective-permute-start | bytes 786440 | tf_op jit(solution)/shard_map/ppermute | solution.py:17
  63.2 2.3 %convolution_add_fusion = f32[4,64,512]{2,1,0:T(8,128)} fusion(bf16[4,64,512]{2,1,0:T(8,128)(2,1)} %bitcast.123, f32[1,64,512]{2,1,0:T(8,128)} %convolution_bitcast_fusion, f32[1,64,512]{2,1,0:T(8,128)} %convolution_bitcast_fusion.1, f32[1,64,512]{2,1,0:T(8,128)} %convolution_bitcast_fusion.2, f32[4]{0:T(128)} %pad.20.clone, ...), kind=kOutput, calls=%fused_computation.5 | convolution fusion | flops 26148864 | bytes 1840144 | tf_op jit(solution)/shard_map/bac,bcv->bav/dot_general | solution.py:70
  65.5 10.7 %collective-permute-done.8 = bf16[256,512]{1,0:T(8,128)(2,1)} collective-permute-done((bf16[256,512]{1,0:T(8,128)(2,1)}, bf16[256,512]{1,0:T(8,128)(2,1)}, u32[]{:S(2)}, u32[]{:S(2)}) %collective-permute-start.8) | collective-permute-done | bytes 262176 | tf_op jit(solution)/shard_map/ppermute | solution.py:17
  76.3 3.0 %multiply_reduce_fusion = (f32[256]{0:T(256)S(1)}, f32[256,512]{1,0:T(8,128)}) fusion(f32[256,512]{1,0:T(8,128)} %bitcast.124, f32[256,256]{1,0:T(8,128)} %get-tuple-element.60, bf16[256,512]{1,0:T(8,128)(2,1)} %collective-permute-done.8, bf16[256,512]{1,0:T(8,128)(2,1)} %copy-done.2, bf16[256,512]{1,0:T(8,128)(2,1)} %copy-done.6, f32[256]{0:T(256)S(1)} %copy-done.21, ...), kind=kOutput, calls=%fused_computation.50 | convolution fusion | flops 404225792 | bytes 2100226 | tf_op jit(solution)/shard_map/dot_general | solution.py:191
  79.3 4.2 %convolution_convert_fusion = bf16[256,2048]{1,0:T(8,128)(2,1)} fusion(bf16[512,2048]{1,0:T(8,128)(2,1)S(1)} %copy-done, bf16[256,2048]{1,0:T(8,128)(2,1)S(1)} %get-tuple-element.97, bf16[2048,512]{1,0:T(8,128)(2,1)} %param.29, f32[256,512]{1,0:T(8,128)} %get-tuple-element.96, f32[512]{0:T(512)} %param.30, f32[256]{0:T(256)S(1)} %add_rsqrt_fusion), kind=kOutput, calls=%fused_computation.4 | convolution fusion | flops 1075576832 | bytes 6818816 | tf_op jit(solution)/shard_map/dot_general | solution.py:200
  83.5 1.2 %dynamic-slice_bitcast_fusion.2 = (bf16[64,2048]{1,0:T(8,128)(2,1)S(1)}, bf16[64,2048]{1,0:T(8,128)(2,1)S(1)}, bf16[64,2048]{1,0:T(8,128)(2,1)S(1)}) fusion(bf16[4,64,2048]{2,1,0:T(8,128)(2,1)} %bitcast.127, s32[]{:T(128)S(6)} %select_n.107, s32[]{:T(128)S(6)} %select_n.111, s32[]{:T(128)S(6)} %select_n.109), kind=kLoop, calls=%fused_computation.75 | loop fusion | bytes 1572876 | tf_op jit(solution)/shard_map/jit(dynamic_index_in_dim)/squeeze | solution.py:132
  84.8 1.0 collective-permute-start.10
  85.8 2.5 %fusion.3 = f32[1,1,256,512]{3,2,1,0:T(8,128)} fusion(bf16[256,512]{1,0:T(8,128)(2,1)} %collective-permute-done.8, f32[256]{0:T(256)S(1)} %copy-done.22, pred[]{:T(512)S(6)} %ge.76, f32[256,512]{1,0:T(8,128)} %copy-done.1, bf16[256,512]{1,0:T(8,128)(2,1)S(1)} %copy-done.3, f32[256]{0:T(256)S(1)} %copy-done.13, pred[]{:T(512)S(6)} %ge.78, ...), kind=kLoop, calls=%fused_computation.31 | loop fusion | flops 1572864 | bytes 1838083 | tf_op jit(solution)/shard_map/broadcast_in_dim | solution.py:203
  88.2 3.2 %collective-permute-done.11 = bf16[64,2048]{1,0:T(8,128)(2,1)S(1)} collective-permute-done((bf16[64,2048]{1,0:T(8,128)(2,1)S(1)}, bf16[64,2048]{1,0:T(8,128)(2,1)S(1)}, u32[]{:S(2)}, u32[]{:S(2)}) %collective-permute-start.11) | collective-permute-done | bytes 262176 | tf_op jit(solution)/shard_map/ppermute | solution.py:133
  91.5 6.5 %collective-permute-done.10 = bf16[64,2048]{1,0:T(8,128)(2,1)S(1)} collective-permute-done((bf16[64,2048]{1,0:T(8,128)(2,1)S(1)}, bf16[64,2048]{1,0:T(8,128)(2,1)S(1)}, u32[]{:S(2)}, u32[]{:S(2)}) %collective-permute-start.10) | collective-permute-done | bytes 262176 | tf_op jit(solution)/shard_map/ppermute | solution.py:133
  98.5 1.8 %fusion.7 = bf16[64,2048]{1,0:T(8,128)(2,1)} fusion(bf16[64,2048]{1,0:T(8,128)(2,1)S(1)} %collective-permute-done.11, bf16[64,2048]{1,0:T(8,128)(2,1)S(1)} %collective-permute-done.10, bf16[64,2048]{1,0:T(8,128)(2,1)S(1)} %collective-permute-done.9, bf16[4,64,2048]{2,1,0:T(8,128)(2,1)} %bitcast.128, s32[]{:T(128)S(6)} %select_n.105), kind=kLoop, calls=%fused_computation.37 | loop fusion | flops 1048576 | bytes 1310724 | tf_op jit(solution)/shard_map/convert_element_type | solution.py:134
  (95 shorter events, 5.4 us)
Async XLA Ops:
  0.6 78.7 %copy-start = (bf16[512,2048]{1,0:T(8,128)(2,1)S(1)}, bf16[512,2048]{1,0:T(8,128)(2,1)}, u32[]{:S(2)}) copy-start(bf16[512,2048]{1,0:T(8,128)(2,1)} %param.31) | copy-start | bytes 6291460
  0.6 13.7 %collective-permute-start = (bf16[64,2048]{1,0:T(8,128)(2,1)}, bf16[64,2048]{1,0:T(8,128)(2,1)S(1)}, u32[]{:S(2)}, u32[]{:S(2)}) collective-permute-start(bf16[64,2048]{1,0:T(8,128)(2,1)} %param.18), channel_id=1, source_target_pairs={{0,3},{1,0},{2,1},{3,2},{4,7},{5,4},{6,5},{7,6},{8,11},{9,8},{10,9... | collective-permute-start | bytes 786440 | tf_op jit(solution)/shard_map/ppermute | solution.py:118
  1.7 13.6 %collective-permute-start.1 = (bf16[64,2048]{1,0:T(8,128)(2,1)}, bf16[64,2048]{1,0:T(8,128)(2,1)}, u32[]{:S(2)}, u32[]{:S(2)}) collective-permute-start(bf16[64,2048]{1,0:T(8,128)(2,1)} %param.18), channel_id=1, source_target_pairs={{0,2},{1,3},{2,0},{3,1},{4,6},{5,7},{6,4},{7,5},{8,10},{9,11},{10,... | collective-permute-start | bytes 786440 | tf_op jit(solution)/shard_map/ppermute | solution.py:118
  2.3 13.0 %collective-permute-start.2 = (bf16[64,2048]{1,0:T(8,128)(2,1)}, bf16[64,2048]{1,0:T(8,128)(2,1)}, u32[]{:S(2)}, u32[]{:S(2)}) collective-permute-start(bf16[64,2048]{1,0:T(8,128)(2,1)} %param.18), channel_id=1, source_target_pairs={{0,1},{1,2},{2,3},{3,0},{4,5},{5,6},{6,7},{7,4},{8,9},{9,10},{10,1... | collective-permute-start | bytes 786440 | tf_op jit(solution)/shard_map/ppermute | solution.py:118
  16.5 3.2 %copy-start.10 = (bf16[2048,256]{1,0:T(8,128)(2,1)S(1)}, bf16[2048,256]{1,0:T(8,128)(2,1)}, u32[]{:S(2)}) copy-start(bf16[2048,256]{1,0:T(8,128)(2,1)} %param.21) | copy-start | bytes 3145732
  16.5 3.6 %copy-start.11 = (bf16[2048,256]{1,0:T(8,128)(2,1)S(1)}, bf16[2048,256]{1,0:T(8,128)(2,1)}, u32[]{:S(2)}) copy-start(bf16[2048,256]{1,0:T(8,128)(2,1)} %param.20) | copy-start | bytes 3145732
  19.7 1.6 %copy-start.28 = (bf16[2048,16]{0,1:T(8,128)(2,1)S(1)}, bf16[2048,16]{0,1:T(8,128)(2,1)}, u32[]{:S(2)}) copy-start(bf16[2048,16]{0,1:T(8,128)(2,1)} %param.26) | copy-start | bytes 196612
  19.7 1.6 %copy-start.29 = (bf16[16,256]{1,0:T(8,128)(2,1)S(1)}, bf16[16,256]{1,0:T(8,128)(2,1)}, u32[]{:S(2)}) copy-start(bf16[16,256]{1,0:T(8,128)(2,1)} %param.27) | copy-start | bytes 24580
  19.7 1.6 %copy-start.30 = (f32[256]{0:T(256)S(1)}, f32[256]{0:T(256)}, u32[]{:S(2)}) copy-start(f32[256]{0:T(256)} %param.28) | copy-start | bytes 3076
  24.7 36.3 %copy-start.12 = (f32[256]{0:T(256)}, f32[256]{0:T(256)S(1)}, u32[]{:S(2)}) copy-start(f32[256]{0:T(256)S(1)} %get-tuple-element.89) | copy-start | bytes 3076
  24.7 6.8 %collective-permute-start.4 = (f32[256]{0:T(256)S(1)}, f32[256]{0:T(256)S(1)}, u32[]{:S(2)}, u32[]{:S(2)}) collective-permute-start(f32[256]{0:T(256)S(1)} %get-tuple-element.89), channel_id=1, source_target_pairs={{0,4},{4,8},{8,12},{12,16},{16,20},{20,24},{24,28},{1,5},{5,9},{9,... | collective-permute-start | bytes 3080 | tf_op jit(solution)/shard_map/ppermute | solution.py:17
  29.6 8.0 %collective-permute-start.3 = (bf16[3,1024]{1,0:T(4,128)(2,1)S(1)}, bf16[3,1024]{1,0:T(4,128)(2,1)S(1)}, u32[]{:S(2)}, u32[]{:S(2)}) collective-permute-start(bf16[3,1024]{1,0:T(4,128)(2,1)S(1)} %get-tuple-element.57), channel_id=1, source_target_pairs={{0,4},{4,8},{8,12},{12,16},{16,20},{20,24},{24,28},{1,5},{5,9},{9,... | collective-permute-start | bytes 18440 | tf_op jit(solution)/shard_map/ppermute | solution.py:17
  31.5 6.1 %copy-start.20 = (f32[256]{0:T(256)}, f32[256]{0:T(256)S(1)}, u32[]{:S(2)}) copy-start(f32[256]{0:T(256)S(1)} %collective-permute-done.4) | copy-start | bytes 3076
  31.5 29.4 %copy-start.18 = (f32[256]{0:T(256)}, f32[256]{0:T(256)S(1)}, u32[]{:S(2)}) copy-start(f32[256]{0:T(256)S(1)} %multiply_select_fusion.2) | copy-start | bytes 3076
  31.5 5.5 %collective-permute-start.5 = (f32[256]{0:T(256)S(1)}, f32[256]{0:T(256)S(1)}, u32[]{:S(2)}, u32[]{:S(2)}) collective-permute-start(f32[256]{0:T(256)S(1)} %multiply_select_fusion.2), channel_id=1, source_target_pairs={{0,8},{4,12},{8,16},{12,20},{16,24},{20,28},{1,9},{5,13},{9,17},{1... | collective-permute-start | bytes 3080 | tf_op jit(solution)/shard_map/ppermute | solution.py:17
  39.6 2.4 %copy-start.5 = (bf16[256,512]{1,0:T(8,128)(2,1)}, bf16[256,512]{1,0:T(8,128)(2,1)S(1)}, u32[]{:S(2)}) copy-start(bf16[256,512]{1,0:T(8,128)(2,1)S(1)} %multiply_convert_fusion.1) | copy-start | bytes 786436
  40.7 1.3 %copy-start.7 = (bf16[256,256]{1,0:T(8,128)(2,1)}, bf16[256,256]{1,0:T(8,128)(2,1)S(1)}, u32[]{:S(2)}) copy-start(bf16[256,256]{1,0:T(8,128)(2,1)S(1)} %multiply_convert_fusion.2) | copy-start | bytes 393220
  42.0 3.7 %copy-start.9 = (bf16[256,256]{1,0:T(8,128)(2,1)S(1)}, bf16[256,256]{1,0:T(8,128)(2,1)}, u32[]{:S(2)}) copy-start(bf16[256,256]{1,0:T(8,128)(2,1)} %convolution_convert_fusion.4) | copy-start | bytes 393220
  42.0 3.7 %copy-start.14 = (f32[256]{0:T(256)S(1)}, f32[256]{0:T(256)}, u32[]{:S(2)}) copy-start(f32[256]{0:T(256)} %get-tuple-element.91) | copy-start | bytes 3076
  42.0 3.7 %copy-start.15 = (f32[256]{0:T(256)S(1)}, f32[256]{0:T(256)}, u32[]{:S(2)}) copy-start(f32[256]{0:T(256)} %get-tuple-element.92) | copy-start | bytes 3076
  42.0 3.7 %copy-start.16 = (f32[256]{0:T(256)S(1)}, f32[256]{0:T(256)}, u32[]{:S(2)}) copy-start(f32[256]{0:T(256)} %get-tuple-element.93) | copy-start | bytes 3076
  42.0 3.7 %copy-start.17 = (f32[256]{0:T(256)S(1)}, f32[256]{0:T(256)}, u32[]{:S(2)}) copy-start(f32[256]{0:T(256)} %get-tuple-element.94) | copy-start | bytes 3076
  42.0 3.7 %copy-start.23 = (f32[256]{0:T(256)S(1)}, f32[256]{0:T(256)}, u32[]{:S(2)}) copy-start(f32[256]{0:T(256)} %reshape.235) | copy-start | bytes 3076
  42.0 3.7 %copy-start.24 = (f32[1,256]{1,0:T(1,128)S(1)}, f32[1,256]{1,0:T(1,128)}, u32[]{:S(2)}) copy-start(f32[1,256]{1,0:T(1,128)} %get-tuple-element.77) | copy-start | bytes 3076
  42.1 3.7 %copy-start.25 = (f32[1,256]{1,0:T(1,128)S(1)}, f32[1,256]{1,0:T(1,128)}, u32[]{:S(2)}) copy-start(f32[1,256]{1,0:T(1,128)} %get-tuple-element.78) | copy-start | bytes 3076
  42.1 3.7 %copy-start.26 = (f32[1,256]{1,0:T(1,128)S(1)}, f32[1,256]{1,0:T(1,128)}, u32[]{:S(2)}) copy-start(f32[1,256]{1,0:T(1,128)} %get-tuple-element.79) | copy-start | bytes 3076
  42.1 3.7 %copy-start.27 = (f32[1,256]{1,0:T(1,128)S(1)}, f32[1,256]{1,0:T(1,128)}, u32[]{:S(2)}) copy-start(f32[1,256]{1,0:T(1,128)} %get-tuple-element.80) | copy-start | bytes 3076
  42.3 18.7 %copy-start.1 = (f32[256,512]{1,0:T(8,128)}, f32[256,512]{1,0:T(8,128)S(1)}, u32[]{:S(2)}) copy-start(f32[256,512]{1,0:T(8,128)S(1)} %get-tuple-element.59) | copy-start | bytes 1572868
  42.3 10.1 %collective-permute-start.6 = (bf16[256,512]{1,0:T(8,128)(2,1)S(1)}, bf16[256,512]{1,0:T(8,128)(2,1)S(1)}, u32[]{:S(2)}, u32[]{:S(2)}) collective-permute-start(bf16[256,512]{1,0:T(8,128)(2,1)S(1)} %get-tuple-element.58), channel_id=1, source_target_pairs={{0,4},{4,8},{8,12},{12,16},{16,20},{20,24},{24,28},{1,5},{5,9},{9,... | collective-permute-start | bytes 786440 | tf_op jit(solution)/shard_map/ppermute | solution.py:17
  46.8 9.5 %copy-start.4 = (f32[256,256]{1,0:T(8,128)}, f32[256,256]{1,0:T(8,128)S(1)}, u32[]{:S(2)}) copy-start(f32[256,256]{1,0:T(8,128)S(1)} %get-tuple-element.61) | copy-start | bytes 786436
  48.1 15.1 %copy-start.8 = (bf16[256,256]{1,0:T(8,128)(2,1)S(1)}, bf16[256,256]{1,0:T(8,128)(2,1)}, u32[]{:S(2)}) copy-start(bf16[256,256]{1,0:T(8,128)(2,1)} %copy-done.7) | copy-start | bytes 393220
  52.4 9.5 %copy-start.2 = (bf16[256,512]{1,0:T(8,128)(2,1)}, bf16[256,512]{1,0:T(8,128)(2,1)S(1)}, u32[]{:S(2)}) copy-start(bf16[256,512]{1,0:T(8,128)(2,1)S(1)} %collective-permute-done.6) | copy-start | bytes 786436
  52.6 8.4 %collective-permute-start.7 = (bf16[256,512]{1,0:T(8,128)(2,1)S(1)}, bf16[256,512]{1,0:T(8,128)(2,1)S(1)}, u32[]{:S(2)}, u32[]{:S(2)}) collective-permute-start(bf16[256,512]{1,0:T(8,128)(2,1)S(1)} %fusion.19), channel_id=1, source_target_pairs={{0,8},{4,12},{8,16},{12,20},{16,24},{20,28},{1,9},{5,13},{9,17},{1... | collective-permute-start | bytes 786440 | tf_op jit(solution)/shard_map/ppermute | solution.py:17
  55.1 21.2 %copy-start.21 = (f32[256]{0:T(256)S(1)}, f32[256]{0:T(256)}, u32[]{:S(2)}) copy-start(f32[256]{0:T(256)} %copy-done.20) | copy-start | bytes 3076
  61.0 0.9 copy-start.6
  61.9 14.3 %collective-permute-start.8 = (bf16[256,512]{1,0:T(8,128)(2,1)}, bf16[256,512]{1,0:T(8,128)(2,1)}, u32[]{:S(2)}, u32[]{:S(2)}) collective-permute-start(bf16[256,512]{1,0:T(8,128)(2,1)} %fusion.63), channel_id=1, source_target_pairs={{0,16},{4,20},{8,24},{12,28},{1,17},{5,21},{9,25},{13,29},{2,18},{... | collective-permute-start | bytes 786440 | tf_op jit(solution)/shard_map/ppermute | solution.py:17
  79.3 6.5 %copy-start.3 = (bf16[256,512]{1,0:T(8,128)(2,1)S(1)}, bf16[256,512]{1,0:T(8,128)(2,1)}, u32[]{:S(2)}) copy-start(bf16[256,512]{1,0:T(8,128)(2,1)} %copy-done.2) | copy-start | bytes 786436
  79.3 6.5 %copy-start.13 = (f32[256]{0:T(256)S(1)}, f32[256]{0:T(256)}, u32[]{:S(2)}) copy-start(f32[256]{0:T(256)} %copy-done.12) | copy-start | bytes 3076
  79.3 6.5 %copy-start.19 = (f32[256]{0:T(256)S(1)}, f32[256]{0:T(256)}, u32[]{:S(2)}) copy-start(f32[256]{0:T(256)} %copy-done.18) | copy-start | bytes 3076
  79.3 6.5 %copy-start.22 = (f32[256]{0:T(256)S(1)}, f32[256]{0:T(256)}, u32[]{:S(2)}) copy-start(f32[256]{0:T(256)} %get-tuple-element.87) | copy-start | bytes 3076
  84.7 6.8 %collective-permute-start.11 = (bf16[64,2048]{1,0:T(8,128)(2,1)S(1)}, bf16[64,2048]{1,0:T(8,128)(2,1)S(1)}, u32[]{:S(2)}, u32[]{:S(2)}) collective-permute-start(bf16[64,2048]{1,0:T(8,128)(2,1)S(1)} %get-tuple-element.65), channel_id=1, source_target_pairs={{0,3},{1,0},{2,1},{3,2},{4,7},{5,4},{6,5},{7,6},{8,11},{9,8},{10,9... | collective-permute-start | bytes 786440 | tf_op jit(solution)/shard_map/ppermute | solution.py:133
  84.8 13.2 %collective-permute-start.10 = (bf16[64,2048]{1,0:T(8,128)(2,1)S(1)}, bf16[64,2048]{1,0:T(8,128)(2,1)S(1)}, u32[]{:S(2)}, u32[]{:S(2)}) collective-permute-start(bf16[64,2048]{1,0:T(8,128)(2,1)S(1)} %get-tuple-element.66), channel_id=1, source_target_pairs={{0,2},{1,3},{2,0},{3,1},{4,6},{5,7},{6,4},{7,5},{8,10},{9,11},{10,... | collective-permute-start | bytes 786440 | tf_op jit(solution)/shard_map/ppermute | solution.py:133
  85.7 12.8 %collective-permute-start.9 = (bf16[64,2048]{1,0:T(8,128)(2,1)S(1)}, bf16[64,2048]{1,0:T(8,128)(2,1)S(1)}, u32[]{:S(2)}, u32[]{:S(2)}) collective-permute-start(bf16[64,2048]{1,0:T(8,128)(2,1)S(1)} %get-tuple-element.64), channel_id=1, source_target_pairs={{0,1},{1,2},{2,3},{3,0},{4,5},{5,6},{6,7},{7,4},{8,9},{9,10},{10,1... | collective-permute-start | bytes 786440 | tf_op jit(solution)/shard_map/ppermute | solution.py:133

commit v5 on v3

--- a/solution.py
+++ b/solution.py
@@ -85,23 +85,47 @@
     return (local_out, carry_lift, memory, product)
 
 
+def packed_state(decay, memory):
+    high = decay.astype(jnp.bfloat16)
+    low = (decay - high.astype(jnp.float32)).astype(jnp.bfloat16)
+    width = memory.shape[1]
+    flat = jnp.concatenate([high, low])
+    flat = jnp.pad(flat, (0, -flat.shape[0] % width))
+    return jnp.concatenate([memory.astype(jnp.bfloat16), flat.reshape((-1, width))], axis=0)
+
+
+def unpacked_state(packed, key_width):
+    memory = packed[:key_width].astype(jnp.float32)
+    flat = packed[key_width:].reshape((-1,)).astype(jnp.float32)
+    return (flat[:key_width] + flat[key_width : 2 * key_width], memory)
+
+
 def prefix_states(decay, memory, axis):
     count = lax.axis_size(axis)
     place = lax.axis_index(axis)
+    key_width = memory.shape[0]
     entering_decay = jnp.ones_like(decay)
     entering = jnp.zeros_like(memory)
     steps = 1
     while steps < count:
-        earlier_decay, earlier_memory = shifted((decay, memory), axis, steps)
         valid = place >= steps
+        if steps * 2 < count:
+            earlier_decay, earlier_memory = unpacked_state(
+                shifted(packed_state(decay, memory), axis, steps), key_width
+            )
+        else:
+            earlier_decay = None
+            earlier_memory = shifted(memory.astype(jnp.bfloat16), axis, steps).astype(jnp.float32)
         memory = jnp.where(valid, decay[:, None] * earlier_memory + memory, memory)
-        decay = jnp.where(valid, earlier_decay * decay, decay)
         if steps == 1:
             entering = earlier_memory
             entering_decay = earlier_decay
         else:
             entering = jnp.where(valid, entering_decay[:, None] * earlier_memory + entering, entering)
-            entering_decay = jnp.where(valid, earlier_decay * entering_decay, entering_decay)
+        if earlier_decay is not None:
+            decay = jnp.where(valid, earlier_decay * decay, decay)
+            if steps > 1:
+                entering_decay = jnp.where(valid, earlier_decay * entering_decay, entering_decay)
         steps *= 2
     return (memory, entering)
 
@@ -114,10 +138,27 @@
 def gather_rows(rows, axis):
     count = lax.axis_size(axis)
     place = lax.axis_index(axis)
-    received = [rows] + [lax.ppermute(rows, axis, pairs) for pairs in rotations(axis)]
+    if count & (count - 1):
+        received = [rows] + [lax.ppermute(rows, axis, pairs) for pairs in rotations(axis)]
+        order = [(-step) % count for step in range(count)]
+    else:
+        received = [rows]
+        order = [0]
+        mask = count // 2
+        while mask >= 1:
+            incoming = lax.ppermute(
+                jnp.concatenate(received), axis, [(source, source ^ mask) for source in range(count)]
+            )
+            received = received + list(jnp.split(incoming, len(received)))
+            order = order + [flip ^ mask for flip in order]
+            mask //= 2
 
     def ordered(shift):
-        return jnp.concatenate([received[(shift - index) % count] for index in range(count)])
+        if count & (count - 1):
+            picks = [order.index((index - shift) % count) for index in range(count)]
+        else:
+            picks = [order.index(shift ^ index) for index in range(count)]
+        return jnp.concatenate([received[pick] for pick in picks])
 
     return lax.switch(place, [functools.partial(ordered, shift) for shift in range(count)])
 

time: 114 us -> 102 us (0.89)
  waiting for transfers between devices: 52.7 us -> 36 us
  other arithmetic: 20.6 us -> 27.1 us
  starting transfers between devices: 14.4 us -> 11.4 us
  local copies, waits for them, and re-layouts: 5.09 us -> 6.76 us
    ppermute x6 -> x4, waiting for transfers between devices: 39 us -> 25.7 us  [shifted(): lax.ppermute(value, axis, [(source, source + steps) for source in range(i...]
    ppermute x6 -> x4, starting transfers between devices: 11.8 us -> 8.01 us  [shifted(): lax.ppermute(value, axis, [(source, source + steps) for source in range(i...]
    ppermute x3 -> x2, waiting for transfers between devices: 3.11 us -> 0.01 us  [gather_rows(): lax.ppermute(jnp.concatenate(received), axis, [(source, source ^ mask) fo...]
    convert_element_type x0 -> x7, other arithmetic: none -> 3.09 us  [the longest x1 1.41 us: prefix_states(): memory.astype(jnp.bfloat16)]
    concatenate x1 -> x6, other arithmetic: 1.18 us -> 2.78 us  [the longest x1 1.04 us: ordered(): return jnp.concatenate([received[pick] for pick in picks])]
    convert_element_type x2, other arithmetic: 3.44 us -> 2.15 us  [short_conv(): return jax.nn.silu(summed).astype(jnp.bfloat16)]
    select_n x2 -> x0, other arithmetic: 1.27 us -> none  [prefix_states(): memory = jnp.where(valid, decay[:, None] * earlier_memory + memory, memory)]
    mul x1, other arithmetic: 0.98 us -> 2.15 us  [segment_parts(): carry_lift = lifted_intact * jnp.stack(products)[:, None, :]]
  transfers between devices with their start and end apart: 12 -> 9, of which waited for: 9 -> 5; matrix products, arithmetic and copies ran while one was open for 20% -> 24% of each run, Pallas kernels for 0% -> 0%
where the time goes in v5:
time: 102 us
  waiting for transfers between devices  36 us (35%)
  other arithmetic  27.1 us (27%)
  matrix products  19.2 us (19%)
  starting transfers between devices  11.4 us (11%)
  local copies, waits for them, and re-layouts  6.76 us (7%)
  between operations  1.15 us (1%)
    ppermute x4, waiting for transfers between devices, shifted(): lax.ppermute(value, axis, [(source, source + steps) for source in range(i...  25.7 us
    ppermute x3, waiting for transfers between devices, scatter_sum(): total = total + lax.ppermute(outgoing, axis, pairs).astype(jnp.float32)  10.2 us
    ppermute x4, starting transfers between devices, shifted(): lax.ppermute(value, axis, [(source, source + steps) for source in range(i...  8.01 us
    mul x3, other arithmetic, short_conv(): weight[tap_index].astype(jnp.float32)[None, :] * window.astype(jnp.float32)  4.27 us
    dot_general x1, matrix products, shards(): jnp.dot(gated_out, out_weight, preferred_element_type=jnp.float32)  4.1 us
    dot_general x3, matrix products, segment_parts(): jnp.dot(lifted_intact[block], memory, precision=HIGHEST_PRECISION)  3.66 us
    dot_general x3, matrix products, project(): jnp.dot(gathered, weight, preferred_element_type=jnp.float32)  3.31 us
    dot_general x1, matrix products, shards(): jnp.dot(carry_lift.reshape((row_count, key_width)), entering, precision=H...  3.03 us
  transfers between devices with their start and end apart: 9, of which 5 were waited for; matrix products, arithmetic and copies ran while one was open for 24% of the time, Pallas kernels for 0%

profile of v5, /device:TPU:24, one launch (start us, length us, event | category | flops | bytes accessed | tf_op | source)
XLA Modules:
  0.0 101.6 jit_solution(6958016284951148803)
XLA Ops:
  0.7 1.6 %collective-permute-start = (bf16[64,2048]{1,0:T(8,128)(2,1)}, bf16[64,2048]{1,0:T(8,128)(2,1)S(1)}, u32[]{:S(2)}, u32[]{:S(2)}) collective-permute-start(bf16[64,2048]{1,0:T(8,128)(2,1)} %param.18), channel_id=1, source_target_pairs={{0,2},{1,3},{2,0},{3,1},{4,6},{5,7},{6,4},{7,5},{8,10},{9,11},{10,... | collective-permute-start | bytes 786440 | tf_op jit(solution)/shard_map/ppermute | solution.py:149
  2.2 0.8 reduce-window.9
  3.1 0.7 bitcast_subtract_fusion
  5.1 1.2 %slice_compare_fusion = pred[3]{0:T(512)(128)(4,1)} fusion(s32[256]{0:T(256)S(1)} %iota_add_fusion, s32[]{:T(128)} %bitcast.47), kind=kLoop, calls=%fused_computation.164 | loop fusion | flops 3 | bytes 19 | tf_op jit(solution)/shard_map/ge | solution.py:244
  6.7 0.7 compare_convert_fusion.1
  9.2 1.4 %slice_convert_fusion.9 = (f32[1,256]{1,0:T(1,128)}, f32[1,256]{1,0:T(1,128)}, f32[1,256]{1,0:T(1,128)}, f32[1,256]{1,0:T(1,128)}) fusion(bf16[4,256]{1,0:T(4,128)(2,1)} %param.24), kind=kLoop, calls=%fused_computation.157 | loop fusion | flops 1024 | bytes 6144 | tf_op jit(solution)/shard_map/mul | solution.py:36
  10.6 1.0 pad_maximum_fusion.4
  11.7 0.7 slice_reduce_fusion.1
  12.4 1.4 %slice_convert_fusion.13 = (f32[1,256]{1,0:T(1,128)}, f32[1,256]{1,0:T(1,128)}, f32[1,256]{1,0:T(1,128)}, f32[1,256]{1,0:T(1,128)}) fusion(bf16[4,256]{1,0:T(4,128)(2,1)} %param.23), kind=kLoop, calls=%fused_computation.161 | loop fusion | flops 1024 | bytes 6144 | tf_op jit(solution)/shard_map/mul | solution.py:36
  13.8 1.4 %slice_convert_fusion.5 = (f32[1,512]{1,0:T(1,128)}, f32[1,512]{1,0:T(1,128)}, f32[1,512]{1,0:T(1,128)}, f32[1,512]{1,0:T(1,128)}) fusion(bf16[4,512]{1,0:T(4,128)(2,1)} %param.25), kind=kLoop, calls=%fused_computation.134 | loop fusion | flops 2048 | bytes 12288 | tf_op jit(solution)/shard_map/mul | solution.py:36
  15.3 1.8 %conditional.1 = (bf16[256,2048]{1,0:T(8,128)(2,1)S(1)}) conditional(s32[]{:T(128)} %clamp.3, (bf16[64,2048]{1,0:T(8,128)(2,1)S(1)}, bf16[64,2048]{1,0:T(8,128)(2,1)S(1)}, bf16[64,2048]{1,0:T(8,128)(2,1)S(1)}, bf16[64,2048]{1,0:T(8,128)(2,1)S(1)}) %tuple.61, (bf16[64,2048]{1,0:T(8,128)(2,1)S(1)}, ...), branch_computations={%region_3.0_spmd, %region_4.0_spmd, %region_5.6_spmd, %region_6.7_... | conditional | flops 4194304 | bytes 3145764 | solution.py:163
  15.3 0.7 copy-done.3
  16.0 1.0 %pad_maximum_fusion = bf16[256,2048]{1,0:T(8,128)(2,1)S(1)} fusion(bf16[64,2048]{1,0:T(8,128)(2,1)S(1)} %get-tuple-element.40, bf16[64,2048]{1,0:T(8,128)(2,1)} %copy-done.3, bf16[64,2048]{1,0:T(8,128)(2,1)S(1)} %get-tuple-element.33, bf16[64,2048]{1,0:T(8,128)(2,1)S(1)} %get-tuple-element.32), kind=kLoop, calls=%fused_computation | loop fusion | flops 4194304 | bytes 2097152 | tf_op jit(solution)/shard_map/cond/branch_0_fun/concatenate | solution.py:161
  17.1 2.4 %convolution_convert_fusion.2 = bf16[256,512]{1,0:T(8,128)(2,1)S(1)} fusion(bf16[256,2048]{1,0:T(8,128)(2,1)S(1)} %get-tuple-element.104, bf16[2048,512]{1,0:T(8,128)(2,1)} %param.22), kind=kOutput, calls=%fused_computation.8 | convolution fusion | flops 537001984 | bytes 3407872 | tf_op jit(solution)/shard_map/dot_general | solution.py:196
  20.6 0.7 select_bitcast_fusion
  21.2 3.4 %collective-permute-start.2 = (bf16[3,1024]{1,0:T(4,128)(2,1)}, bf16[3,1024]{1,0:T(4,128)(2,1)}, u32[]{:S(2)}, u32[]{:S(2)}) collective-permute-start(bf16[3,1024]{1,0:T(4,128)(2,1)} %get-tuple-element.57), channel_id=1, source_target_pairs={{0,4},{4,8},{8,12},{12,16},{16,20},{20,24},{24,28},{1,5},{5,9},{9,... | collective-permute-start | bytes 18440 | tf_op jit(solution)/shard_map/ppermute | solution.py:17
  24.7 1.5 %fusion.26 = f32[256,256]{1,0:T(8,128)} fusion(bf16[16,256]{1,0:T(8,128)(2,1)S(1)} %copy-done.25, bf16[256,2048]{1,0:T(8,128)(2,1)S(1)} %get-tuple-element.104, bf16[2048,16]{0,1:T(8,128)(2,1)S(1)} %copy-done.24, f32[256]{0:T(256)S(1)} %copy-done.27), kind=kOutput, calls=%fused_computation.71 | convolution fusion | flops 19533824 | bytes 1385472 | tf_op jit(solution)/shard_map/dot_general | solution.py:223
  26.2 1.2 %reduce_window_sum.30 = f32[4,64,256]{2,1,0:T(8,128)S(1)} reduce-window(f32[4,64,256]{2,1,0:T(8,128)} %bitcast.131, f32[]{:T(128)} %constant.82.clone.1), window={size=1x64x1 pad=0_0x63_0x0_0}, to_apply=%region_7.8 | reduce-window | flops 4128768 | bytes 524292 | tf_op jit(solution)/shard_map/jit(cumsum)/reduce_window_sum | solution.py:48
  27.4 0.7 exponential_multiply_fusion
  28.1 0.7 pad_maximum_fusion.12
  28.9 0.7 fusion.70
  29.6 2.1 %bitcast_multiply_fusion = (f32[256,256]{1,0:T(8,128)}, f32[256,256]{1,0:T(8,128)S(1)}) fusion(f32[4,64,256]{2,1,0:T(8,128)S(1)} %exp.37, f32[4,256]{1,0:T(4,128)S(1)} %pad_maximum_fusion.12, f32[256]{0:T(256)} %reshape.253, f32[256]{0:T(256)} %get-tuple-element.99, bf16[256,256]{1,0:T(8,128)(2,1)} %copy-done.13, f32[256]{0:T(256)} %bitcast.157, ...), kind=kLoop, calls=%fused_computation.73 | loop fusion | flops 2162688 | bytes 932352 | tf_op jit(solution)/shard_map/mul | solution.py:84
  31.9 0.7 slice.224
  32.5 1.2 %multiply_convert_fusion.1 = bf16[256,512]{1,0:T(8,128)(2,1)S(1)} fusion(bf16[256,512]{1,0:T(8,128)(2,1)S(1)} %copy-done.15, bf16[3,512]{1,0:T(4,128)(2,1)S(1)} %slice.224, f32[256]{0:T(256)} %get-tuple-element.99, f32[512]{0:T(512)} %bitcast.148, f32[256]{0:T(256)} %get-tuple-element.100, f32[512]{0:T(512)} %bitcast.149, f32[256]{0:T(256)} %get-tuple-element.101, ...), kind=kLoop, calls=%fused_computation.55 | loop fusion | flops 3801088 | bytes 539648 | tf_op jit(solution)/shard_map/convert_element_type | solution.py:40
  33.7 1.0 multiply_convert_fusion.2
  34.7 1.3 %fusion.43 = f32[4,256,512]{2,1,0:T(8,128)S(1)} fusion(bf16[4,64,512]{2,1,0:T(8,128)(2,1)S(1)} %bitcast.124, bf16[4,64,256]{2,1,0:T(8,128)(2,1)S(1)} %bitcast.126, f32[4,64,256]{2,1,0:T(8,128)S(1)} %reduce_window_sum.30, f32[4,64]{1,0:T(4,128)} %get-tuple-element.90, f32[4,256]{1,0:T(4,128)S(1)} %bitcast.136), kind=kOutput, calls=%fused_computation.100 | convolution fusion | flops 67436544 | bytes 2757632 | tf_op jit(solution)/shard_map/bsk,bsv->bkv/dot_general | solution.py:58
  36.3 1.2 %convolution_bitcast_fusion.1 = f32[1,64,512]{2,1,0:T(8,128)} fusion(f32[4,64,256]{2,1,0:T(8,128)S(1)} %broadcast_multiply_fusion, f32[4,256,512]{2,1,0:T(8,128)S(1)} %fusion.43, f32[256]{0:T(256)S(1)} %bitcast.134, f32[256]{0:T(256)S(1)} %get-tuple-element.97), kind=kOutput, calls=%fused_computation.15 | convolution fusion | flops 101056512 | bytes 1247232 | tf_op jit(solution)/shard_map/dot_general | solution.py:79
  37.5 2.1 %collective-permute-start.3 = (bf16[257,512]{1,0:T(8,128)(2,1)S(1)}, bf16[257,512]{1,0:T(8,128)(2,1)S(1)}, u32[]{:S(2)}, u32[]{:S(2)}) collective-permute-start(bf16[257,512]{1,0:T(8,128)(2,1)S(1)} %pad_maximum_fusion.5), channel_id=1, source_target_pairs={{0,4},{4,8},{8,12},{12,16},{16,20},{20,24},{24,28},{1,5},{5,9},{9,... | collective-permute-start | bytes 789512 | tf_op jit(solution)/shard_map/ppermute | solution.py:17
  39.6 1.2 %convolution_bitcast_fusion.2 = f32[1,64,512]{2,1,0:T(8,128)} fusion(f32[4,256,512]{2,1,0:T(8,128)S(1)} %fusion.43, f32[256]{0:T(256)S(1)} %get-tuple-element.97, f32[4,64,256]{2,1,0:T(8,128)S(1)} %broadcast_multiply_fusion), kind=kOutput, calls=%fused_computation.16 | convolution fusion | flops 100794368 | bytes 721920 | tf_op jit(solution)/shard_map/dot_general | solution.py:79
  40.8 1.3 %convolution_bitcast_fusion = f32[1,64,512]{2,1,0:T(8,128)} fusion(f32[4,256,512]{2,1,0:T(8,128)S(1)} %fusion.43, f32[256]{0:T(256)S(1)} %bitcast.139, f32[4,64,256]{2,1,0:T(8,128)S(1)} %broadcast_multiply_fusion, f32[256]{0:T(256)S(1)} %bitcast.135, f32[256]{0:T(256)S(1)} %get-tuple-element.97), kind=kOutput, calls=%fused_computation.14 | convolution fusion | flops 101318656 | bytes 1772544 | tf_op jit(solution)/shard_map/dot_general | solution.py:79
  42.0 7.0 %collective-permute-done.3 = bf16[257,512]{1,0:T(8,128)(2,1)S(1)} collective-permute-done((bf16[257,512]{1,0:T(8,128)(2,1)S(1)}, bf16[257,512]{1,0:T(8,128)(2,1)S(1)}, u32[]{:S(2)}, u32[]{:S(2)}) %collective-permute-start.3) | collective-permute-done | bytes 263200 | tf_op jit(solution)/shard_map/ppermute | solution.py:17
  49.9 0.7 pad_maximum_fusion.6
  50.7 1.3 %collective-permute-start.4 = (bf16[257,512]{1,0:T(8,128)(2,1)}, bf16[257,512]{1,0:T(8,128)(2,1)}, u32[]{:S(2)}, u32[]{:S(2)}) collective-permute-start(bf16[257,512]{1,0:T(8,128)(2,1)} %pad_maximum_fusion.6), channel_id=1, source_target_pairs={{0,8},{4,12},{8,16},{12,20},{16,24},{20,28},{1,9},{5,13},{9,17},{1... | collective-permute-start | bytes 789512 | tf_op jit(solution)/shard_map/ppermute | solution.py:17
  51.9 2.3 %convolution_add_fusion = f32[4,64,512]{2,1,0:T(8,128)} fusion(bf16[4,64,512]{2,1,0:T(8,128)(2,1)} %bitcast.125, f32[1,64,512]{2,1,0:T(8,128)} %convolution_bitcast_fusion, f32[1,64,512]{2,1,0:T(8,128)} %convolution_bitcast_fusion.1, f32[1,64,512]{2,1,0:T(8,128)} %convolution_bitcast_fusion.2, f32[4]{0:T(128)} %pad.28.clone, ...), kind=kOutput, calls=%fused_computation.5 | convolution fusion | flops 26148864 | bytes 1840144 | tf_op jit(solution)/shard_map/bac,bcv->bav/dot_general | solution.py:70
  54.3 6.3 %collective-permute-done.4 = bf16[257,512]{1,0:T(8,128)(2,1)} collective-permute-done((bf16[257,512]{1,0:T(8,128)(2,1)}, bf16[257,512]{1,0:T(8,128)(2,1)}, u32[]{:S(2)}, u32[]{:S(2)}) %collective-permute-start.4) | collective-permute-done | bytes 263200 | tf_op jit(solution)/shard_map/ppermute | solution.py:17
  60.6 1.4 %fusion.65 = bf16[256,512]{1,0:T(8,128)(2,1)S(1)} fusion(f32[256,512]{1,0:T(8,128)} %copy-done.1, bf16[257,512]{1,0:T(8,128)(2,1)} %copy-done.9, f32[256]{0:T(256)S(1)} %copy-done.20, pred[]{:T(512)S(6)} %ge.78, bf16[257,512]{1,0:T(8,128)(2,1)} %collective-permute-done.4, f32[256]{0:T(256)} %get-tuple-element.60, pred[]{:T(512)S(6)} %ge.77), kind=kLoop, calls=%fused_computation.170 | loop fusion | flops 1179648 | bytes 1312770 | tf_op jit(solution)/shard_map/convert_element_type | solution.py:118
  62.0 1.3 %collective-permute-start.5 = (bf16[256,512]{1,0:T(8,128)(2,1)S(1)}, bf16[256,512]{1,0:T(8,128)(2,1)S(1)}, u32[]{:S(2)}, u32[]{:S(2)}) collective-permute-start(bf16[256,512]{1,0:T(8,128)(2,1)S(1)} %fusion.65), channel_id=1, source_target_pairs={{0,16},{4,20},{8,24},{12,28},{1,17},{5,21},{9,25},{13,29},{2,18},{... | collective-permute-start | bytes 786440 | tf_op jit(solution)/shard_map/ppermute | solution.py:17
  63.3 0.7 slice_convert_fusion
  64.0 0.7 multiply_select_fusion
  64.7 12.4 %collective-permute-done.5 = bf16[256,512]{1,0:T(8,128)(2,1)S(1)} collective-permute-done((bf16[256,512]{1,0:T(8,128)(2,1)S(1)}, bf16[256,512]{1,0:T(8,128)(2,1)S(1)}, u32[]{:S(2)}, u32[]{:S(2)}) %collective-permute-start.5) | collective-permute-done | bytes 262176 | tf_op jit(solution)/shard_map/ppermute | solution.py:17
  77.1 3.0 %multiply_reduce_fusion = (f32[256]{0:T(256)S(1)}, f32[256,512]{1,0:T(8,128)}) fusion(f32[256,512]{1,0:T(8,128)} %bitcast.130, f32[256,256]{1,0:T(8,128)} %get-tuple-element.66, bf16[256,512]{1,0:T(8,128)(2,1)S(1)} %collective-permute-done.5, f32[256]{0:T(256)} %bitcast.145, f32[256]{0:T(256)S(1)} %get-tuple-element.96, pred[]{:T(512)S(6)} %ge.77, ...), kind=kOutput, calls=%fused_computation.51 | convolution fusion | flops 404225792 | bytes 2100226 | tf_op jit(solution)/shard_map/dot_general | solution.py:231
  80.1 4.1 %convolution_convert_fusion = bf16[256,2048]{1,0:T(8,128)(2,1)} fusion(bf16[512,2048]{1,0:T(8,128)(2,1)S(1)} %copy-done, bf16[256,2048]{1,0:T(8,128)(2,1)S(1)} %get-tuple-element.104, bf16[2048,512]{1,0:T(8,128)(2,1)} %param.29, f32[256,512]{1,0:T(8,128)} %get-tuple-element.103, f32[512]{0:T(512)S(1)} %copy-done.26, f32[256]{0:T(256)S(1)} %add_rsqrt_fusion), kind=kOutput, calls=%fused_computation.4 | convolution fusion | flops 1075576832 | bytes 6818816 | tf_op jit(solution)/shard_map/dot_general | solution.py:240
  84.2 1.2 %dynamic-slice_bitcast_fusion.2 = (bf16[64,2048]{1,0:T(8,128)(2,1)S(1)}, bf16[64,2048]{1,0:T(8,128)(2,1)S(1)}, bf16[64,2048]{1,0:T(8,128)(2,1)S(1)}) fusion(bf16[4,64,2048]{2,1,0:T(8,128)(2,1)} %bitcast.128, s32[]{:T(128)S(6)} %select_n.107, s32[]{:T(128)S(6)} %select_n.111, s32[]{:T(128)S(6)} %select_n.109), kind=kLoop, calls=%fused_computation.78 | loop fusion | bytes 1572876 | tf_op jit(solution)/shard_map/jit(dynamic_index_in_dim)/squeeze | solution.py:172
  85.6 1.6 %collective-permute-start.7 = (bf16[64,2048]{1,0:T(8,128)(2,1)S(1)}, bf16[64,2048]{1,0:T(8,128)(2,1)S(1)}, u32[]{:S(2)}, u32[]{:S(2)}) collective-permute-start(bf16[64,2048]{1,0:T(8,128)(2,1)S(1)} %get-tuple-element.72), channel_id=1, source_target_pairs={{0,2},{1,3},{2,0},{3,1},{4,6},{5,7},{6,4},{7,5},{8,10},{9,11},{10,... | collective-permute-start | bytes 786440 | tf_op jit(solution)/shard_map/ppermute | solution.py:173
  87.1 2.5 %fusion.3 = f32[1,1,256,512]{3,2,1,0:T(8,128)} fusion(bf16[256,512]{1,0:T(8,128)(2,1)} %copy-done.18, f32[256]{0:T(256)S(1)} %get-tuple-element.95, pred[]{:T(512)S(6)} %ge.76, f32[256,512]{1,0:T(8,128)} %copy-done.1, bf16[257,512]{1,0:T(8,128)(2,1)S(1)} %copy-done.10, f32[256]{0:T(256)S(1)} %copy-done.20, pred[]{:T(512)S(6)} %ge.78, ...), kind=kLoop, calls=%fused_computation.31 | loop fusion | flops 1572864 | bytes 1838083 | tf_op jit(solution)/shard_map/broadcast_in_dim | solution.py:243
  89.6 2.7 %collective-permute-done.8 = bf16[64,2048]{1,0:T(8,128)(2,1)S(1)} collective-permute-done((bf16[64,2048]{1,0:T(8,128)(2,1)S(1)}, bf16[64,2048]{1,0:T(8,128)(2,1)S(1)}, u32[]{:S(2)}, u32[]{:S(2)}) %collective-permute-start.8) | collective-permute-done | bytes 262176 | tf_op jit(solution)/shard_map/ppermute | solution.py:173
  92.3 7.6 %collective-permute-done.7 = bf16[64,2048]{1,0:T(8,128)(2,1)S(1)} collective-permute-done((bf16[64,2048]{1,0:T(8,128)(2,1)S(1)}, bf16[64,2048]{1,0:T(8,128)(2,1)S(1)}, u32[]{:S(2)}, u32[]{:S(2)}) %collective-permute-start.7) | collective-permute-done | bytes 262176 | tf_op jit(solution)/shard_map/ppermute | solution.py:173
  99.8 1.8 %fusion.7 = bf16[64,2048]{1,0:T(8,128)(2,1)} fusion(bf16[64,2048]{1,0:T(8,128)(2,1)S(1)} %collective-permute-done.8, bf16[64,2048]{1,0:T(8,128)(2,1)S(1)} %collective-permute-done.7, bf16[64,2048]{1,0:T(8,128)(2,1)S(1)} %collective-permute-done.6, bf16[4,64,2048]{2,1,0:T(8,128)(2,1)} %bitcast.129, s32[]{:T(128)S(6)} %select_n.105), kind=kLoop, calls=%fused_computation.38 | loop fusion | flops 1048576 | bytes 1310724 | tf_op jit(solution)/shard_map/convert_element_type | solution.py:174
  (89 shorter events, 6.0 us)
Async XLA Ops:
  0.6 79.5 %copy-start = (bf16[512,2048]{1,0:T(8,128)(2,1)S(1)}, bf16[512,2048]{1,0:T(8,128)(2,1)}, u32[]{:S(2)}) copy-start(bf16[512,2048]{1,0:T(8,128)(2,1)} %param.31) | copy-start | bytes 6291460
  0.6 14.7 %copy-start.2 = (bf16[64,2048]{1,0:T(8,128)(2,1)S(1)}, bf16[64,2048]{1,0:T(8,128)(2,1)}, u32[]{:S(2)}) copy-start(bf16[64,2048]{1,0:T(8,128)(2,1)} %param.18) | copy-start | bytes 786436
  0.7 10.0 %collective-permute-start = (bf16[64,2048]{1,0:T(8,128)(2,1)}, bf16[64,2048]{1,0:T(8,128)(2,1)S(1)}, u32[]{:S(2)}, u32[]{:S(2)}) collective-permute-start(bf16[64,2048]{1,0:T(8,128)(2,1)} %param.18), channel_id=1, source_target_pairs={{0,2},{1,3},{2,0},{3,1},{4,6},{5,7},{6,4},{7,5},{8,10},{9,11},{10,... | collective-permute-start | bytes 786440 | tf_op jit(solution)/shard_map/ppermute | solution.py:149
  11.6 3.7 %collective-permute-start.1 = (bf16[128,2048]{1,0:T(8,128)(2,1)S(1)}, bf16[128,2048]{1,0:T(8,128)(2,1)S(1)}, u32[]{:S(2)}, u32[]{:S(2)}) collective-permute-start(bf16[128,2048]{1,0:T(8,128)(2,1)S(1)} %pad_maximum_fusion.4), channel_id=1, source_target_pairs={{0,1},{1,0},{2,3},{3,2},{4,5},{5,4},{6,7},{7,6},{8,9},{9,8},{10,11... | collective-permute-start | bytes 1572872 | tf_op jit(solution)/shard_map/ppermute | solution.py:149
  15.3 0.7 copy-start.3
  17.1 2.5 %copy-start.16 = (bf16[2048,256]{1,0:T(8,128)(2,1)S(1)}, bf16[2048,256]{1,0:T(8,128)(2,1)}, u32[]{:S(2)}) copy-start(bf16[2048,256]{1,0:T(8,128)(2,1)} %param.21) | copy-start | bytes 3145732
  17.1 3.0 %copy-start.17 = (bf16[2048,256]{1,0:T(8,128)(2,1)S(1)}, bf16[2048,256]{1,0:T(8,128)(2,1)}, u32[]{:S(2)}) copy-start(bf16[2048,256]{1,0:T(8,128)(2,1)} %param.20) | copy-start | bytes 3145732
  19.6 1.0 copy-start.14
  19.6 1.0 copy-start.23
  19.6 5.0 %copy-start.24 = (bf16[2048,16]{0,1:T(8,128)(2,1)S(1)}, bf16[2048,16]{0,1:T(8,128)(2,1)}, u32[]{:S(2)}) copy-start(bf16[2048,16]{0,1:T(8,128)(2,1)} %param.26) | copy-start | bytes 196612
  19.6 5.0 %copy-start.25 = (bf16[16,256]{1,0:T(8,128)(2,1)S(1)}, bf16[16,256]{1,0:T(8,128)(2,1)}, u32[]{:S(2)}) copy-start(bf16[16,256]{1,0:T(8,128)(2,1)} %param.27) | copy-start | bytes 24580
  19.6 5.0 %copy-start.27 = (f32[256]{0:T(256)S(1)}, f32[256]{0:T(256)}, u32[]{:S(2)}) copy-start(f32[256]{0:T(256)} %param.28) | copy-start | bytes 3076
  20.6 5.6 %copy-start.13 = (bf16[256,256]{1,0:T(8,128)(2,1)}, bf16[256,256]{1,0:T(8,128)(2,1)S(1)}, u32[]{:S(2)}) copy-start(bf16[256,256]{1,0:T(8,128)(2,1)S(1)} %convolution_convert_fusion.4) | copy-start | bytes 393220
  21.2 7.7 %collective-permute-start.2 = (bf16[3,1024]{1,0:T(4,128)(2,1)}, bf16[3,1024]{1,0:T(4,128)(2,1)}, u32[]{:S(2)}, u32[]{:S(2)}) collective-permute-start(bf16[3,1024]{1,0:T(4,128)(2,1)} %get-tuple-element.57), channel_id=1, source_target_pairs={{0,4},{4,8},{8,12},{12,16},{16,20},{20,24},{24,28},{1,5},{5,9},{9,... | collective-permute-start | bytes 18440 | tf_op jit(solution)/shard_map/ppermute | solution.py:17
  27.4 5.1 %copy-start.15 = (bf16[256,512]{1,0:T(8,128)(2,1)S(1)}, bf16[256,512]{1,0:T(8,128)(2,1)}, u32[]{:S(2)}) copy-start(bf16[256,512]{1,0:T(8,128)(2,1)} %copy-done.14) | copy-start | bytes 786436
  28.8 20.9 %copy-start.19 = (f32[256]{0:T(256)}, f32[256]{0:T(256)S(1)}, u32[]{:S(2)}) copy-start(f32[256]{0:T(256)S(1)} %get-tuple-element.65) | copy-start | bytes 3076
  31.7 4.3 %copy-start.7 = (f32[256,256]{1,0:T(8,128)}, f32[256,256]{1,0:T(8,128)S(1)}, u32[]{:S(2)}) copy-start(f32[256,256]{1,0:T(8,128)S(1)} %get-tuple-element.67) | copy-start | bytes 786436
  33.7 2.3 %copy-start.8 = (bf16[256,512]{1,0:T(8,128)(2,1)}, bf16[256,512]{1,0:T(8,128)(2,1)S(1)}, u32[]{:S(2)}) copy-start(bf16[256,512]{1,0:T(8,128)(2,1)S(1)} %multiply_convert_fusion.1) | copy-start | bytes 786436
  34.7 1.3 %copy-start.11 = (bf16[256,256]{1,0:T(8,128)(2,1)}, bf16[256,256]{1,0:T(8,128)(2,1)S(1)}, u32[]{:S(2)}) copy-start(bf16[256,256]{1,0:T(8,128)(2,1)S(1)} %multiply_convert_fusion.2) | copy-start | bytes 393220
  36.3 14.4 %copy-start.1 = (f32[256,512]{1,0:T(8,128)}, f32[256,512]{1,0:T(8,128)S(1)}, u32[]{:S(2)}) copy-start(f32[256,512]{1,0:T(8,128)S(1)} %get-tuple-element.62) | copy-start | bytes 1572868
  37.5 14.4 %copy-start.12 = (bf16[256,256]{1,0:T(8,128)(2,1)S(1)}, bf16[256,256]{1,0:T(8,128)(2,1)}, u32[]{:S(2)}) copy-start(bf16[256,256]{1,0:T(8,128)(2,1)} %copy-done.11) | copy-start | bytes 393220
  37.5 11.5 %collective-permute-start.3 = (bf16[257,512]{1,0:T(8,128)(2,1)S(1)}, bf16[257,512]{1,0:T(8,128)(2,1)S(1)}, u32[]{:S(2)}, u32[]{:S(2)}) collective-permute-start(bf16[257,512]{1,0:T(8,128)(2,1)S(1)} %pad_maximum_fusion.5), channel_id=1, source_target_pairs={{0,4},{4,8},{8,12},{12,16},{16,20},{20,24},{24,28},{1,5},{5,9},{9,... | collective-permute-start | bytes 789512 | tf_op jit(solution)/shard_map/ppermute | solution.py:17
  49.1 0.7 copy-start.9
  49.1 0.7 copy-start.22
  49.9 10.7 %copy-start.20 = (f32[256]{0:T(256)S(1)}, f32[256]{0:T(256)}, u32[]{:S(2)}) copy-start(f32[256]{0:T(256)} %copy-done.19) | copy-start | bytes 3076
  50.7 10.0 %collective-permute-start.4 = (bf16[257,512]{1,0:T(8,128)(2,1)}, bf16[257,512]{1,0:T(8,128)(2,1)}, u32[]{:S(2)}, u32[]{:S(2)}) collective-permute-start(bf16[257,512]{1,0:T(8,128)(2,1)} %pad_maximum_fusion.6), channel_id=1, source_target_pairs={{0,8},{4,12},{8,16},{12,20},{16,24},{20,28},{1,9},{5,13},{9,17},{1... | collective-permute-start | bytes 789512 | tf_op jit(solution)/shard_map/ppermute | solution.py:17
  54.3 25.9 %copy-start.26 = (f32[512]{0:T(512)S(1)}, f32[512]{0:T(512)}, u32[]{:S(2)}) copy-start(f32[512]{0:T(512)} %param.30) | copy-start | bytes 6148
  62.0 15.0 %collective-permute-start.5 = (bf16[256,512]{1,0:T(8,128)(2,1)S(1)}, bf16[256,512]{1,0:T(8,128)(2,1)S(1)}, u32[]{:S(2)}, u32[]{:S(2)}) collective-permute-start(bf16[256,512]{1,0:T(8,128)(2,1)S(1)} %fusion.65), channel_id=1, source_target_pairs={{0,16},{4,20},{8,24},{12,28},{1,17},{5,21},{9,25},{13,29},{2,18},{... | collective-permute-start | bytes 786440 | tf_op jit(solution)/shard_map/ppermute | solution.py:17
  77.1 3.0 %copy-start.18 = (bf16[256,512]{1,0:T(8,128)(2,1)}, bf16[256,512]{1,0:T(8,128)(2,1)S(1)}, u32[]{:S(2)}) copy-start(bf16[256,512]{1,0:T(8,128)(2,1)S(1)} %collective-permute-done.5) | copy-start | bytes 786436
  80.1 7.0 %copy-start.10 = (bf16[257,512]{1,0:T(8,128)(2,1)S(1)}, bf16[257,512]{1,0:T(8,128)(2,1)}, u32[]{:S(2)}) copy-start(bf16[257,512]{1,0:T(8,128)(2,1)} %copy-done.9) | copy-start | bytes 789508
  80.1 7.0 %copy-start.21 = (f32[256]{0:T(256)S(1)}, f32[256]{0:T(256)}, u32[]{:S(2)}) copy-start(f32[256]{0:T(256)} %get-tuple-element.60) | copy-start | bytes 3076
  85.4 6.8 %collective-permute-start.8 = (bf16[64,2048]{1,0:T(8,128)(2,1)S(1)}, bf16[64,2048]{1,0:T(8,128)(2,1)S(1)}, u32[]{:S(2)}, u32[]{:S(2)}) collective-permute-start(bf16[64,2048]{1,0:T(8,128)(2,1)S(1)} %get-tuple-element.71), channel_id=1, source_target_pairs={{0,3},{1,0},{2,1},{3,2},{4,7},{5,4},{6,5},{7,6},{8,11},{9,8},{10,9... | collective-permute-start | bytes 786440 | tf_op jit(solution)/shard_map/ppermute | solution.py:173
  85.6 14.3 %collective-permute-start.7 = (bf16[64,2048]{1,0:T(8,128)(2,1)S(1)}, bf16[64,2048]{1,0:T(8,128)(2,1)S(1)}, u32[]{:S(2)}, u32[]{:S(2)}) collective-permute-start(bf16[64,2048]{1,0:T(8,128)(2,1)S(1)} %get-tuple-element.72), channel_id=1, source_target_pairs={{0,2},{1,3},{2,0},{3,1},{4,6},{5,7},{6,4},{7,5},{8,10},{9,11},{10,... | collective-permute-start | bytes 786440 | tf_op jit(solution)/shard_map/ppermute | solution.py:173
  87.1 12.7 %collective-permute-start.6 = (bf16[64,2048]{1,0:T(8,128)(2,1)S(1)}, bf16[64,2048]{1,0:T(8,128)(2,1)S(1)}, u32[]{:S(2)}, u32[]{:S(2)}) collective-permute-start(bf16[64,2048]{1,0:T(8,128)(2,1)S(1)} %get-tuple-element.70), channel_id=1, source_target_pairs={{0,1},{1,2},{2,3},{3,0},{4,5},{5,6},{6,7},{7,4},{8,9},{9,10},{10,1... | collective-permute-start | bytes 786440 | tf_op jit(solution)/shard_map/ppermute | solution.py:173

commit v6 on v5

--- a/solution.py
+++ b/solution.py
@@ -8,7 +8,7 @@
 SPAN = 64
 
 
-HIGHEST_PRECISION = lax.Precision.HIGHEST
+HIGH_PRECISION = lax.Precision.HIGH
 
 
 def shifted(value, axis, steps):
@@ -76,7 +76,7 @@
     products = [product]
     for block in range(block_count):
         if block > 0:
-            local_outs.append(jnp.dot(lifted_intact[block], memory, precision=HIGHEST_PRECISION))
+            local_outs.append(jnp.dot(lifted_intact[block], memory, precision=HIGH_PRECISION))
             products.append(product)
         memory = step_decay[block][:, None] * memory + update[block]
         product = product * step_decay[block]
@@ -163,15 +163,36 @@
     return lax.switch(place, [functools.partial(ordered, shift) for shift in range(count)])
 
 
-def scatter_sum(terms, axis):
+def scatter_sum(gated, weight, axis):
     count = lax.axis_size(axis)
     place = lax.axis_index(axis)
-    chunks = terms.reshape((count, terms.shape[0] // count) + terms.shape[1:])
-    total = lax.dynamic_index_in_dim(chunks, place, 0, False).astype(jnp.float32)
-    for step, pairs in enumerate(rotations(axis), start=1):
-        outgoing = lax.dynamic_index_in_dim(chunks, (place + step) % count, 0, False)
-        total = total + lax.ppermute(outgoing, axis, pairs).astype(jnp.float32)
-    return total.astype(jnp.bfloat16)
+    chunk = gated.shape[0] // count
+
+    def term(index):
+        rows = lax.slice_in_dim(gated, index * chunk, (index + 1) * chunk, axis=0)
+        return jnp.dot(rows, weight, preferred_element_type=jnp.float32).astype(jnp.bfloat16)
+
+    if count & (count - 1):
+        chunks = jnp.stack([term(index) for index in range(count)])
+        total = lax.dynamic_index_in_dim(chunks, place, 0, False).astype(jnp.float32)
+        for step, pairs in enumerate(rotations(axis), start=1):
+            outgoing = lax.dynamic_index_in_dim(chunks, (place + step) % count, 0, False)
+            total = total + lax.ppermute(outgoing, axis, pairs).astype(jnp.float32)
+        return total.astype(jnp.bfloat16)
+    held = [term(index) for index in range(count)]
+    mask = 1
+    while mask < count:
+        odd = (place // mask) % 2 == 1
+        pairs = list(zip(held[0::2], held[1::2]))
+        keep = [jnp.where(odd, high, low) for low, high in pairs]
+        outgoing = jnp.stack([jnp.where(odd, low, high).astype(jnp.bfloat16) for low, high in pairs])
+        incoming = lax.ppermute(outgoing, axis, [(source, source ^ mask) for source in range(count)])
+        held = [
+            kept.astype(jnp.float32) + incoming[index].astype(jnp.float32)
+            for index, kept in enumerate(keep)
+        ]
+        mask *= 2
+    return held[0].astype(jnp.bfloat16)
 
 
 def shards(
@@ -229,17 +250,14 @@
     )
     closing, entering = prefix_states(local_decay, local_memory, "tok")
     heads_out = local_out.reshape((row_count, value_width)) + jnp.dot(
-        carry_lift.reshape((row_count, key_width)), entering, precision=HIGHEST_PRECISION
+        carry_lift.reshape((row_count, key_width)), entering, precision=HIGH_PRECISION
     )
     gate_float = gate_values.astype(jnp.float32)
     rescale = lax.rsqrt(jnp.mean(heads_out * heads_out, axis=1, keepdims=True) + 1e-05)
     gated_out = (
         heads_out * rescale * norm_gain[None, :] * gate_float * jax.nn.sigmoid(gate_float)
     ).astype(jnp.bfloat16)
-    mixed = scatter_sum(
-        jnp.dot(gated_out, out_weight, preferred_element_type=jnp.float32).astype(jnp.bfloat16),
-        "hv",
-    )
+    mixed = scatter_sum(gated_out, out_weight, "hv")
     segment_states = closing[None, None]
     in_prompt = positions[row_count - rim_rows :] >= prompt_first[row_count - 1]
     tail_rows = joined[row_count - rim_rows :]

time: 102 us -> 98.3 us (0.964)
  matrix products: 19.2 us -> 16.3 us
  other arithmetic: 27.1 us -> 29.5 us
  waiting for transfers between devices: 36 us -> 33.9 us
  starting transfers between devices: 11.4 us -> 10.2 us
    dot_general x4 -> x7, matrix products: 7.76 us -> 5.09 us  [the longest x3 3.16 us: segment_parts(): jnp.dot(lifted_intact[block], memory, precision=HIGH_PRECISION)]
    ppermute x3 -> x2, waiting for transfers between devices: 10.2 us -> 7.8 us  [scatter_sum(): lax.ppermute(outgoing, axis, [(source, source ^ mask) for source in range...]
    another operation x1 -> x4, other arithmetic: 0.83 us -> 2.97 us  [the longest x3 2.15 us: scatter_sum(): jnp.stack([jnp.where(odd, low, high).astype(jnp.bfloat16) for low, high i...]
    squeeze x1 -> x0, local copies, waits for them, and re-layouts: 1.17 us -> none  [scatter_sum(): lax.dynamic_index_in_dim(chunks, (place + step) % count, 0, False)]
    ppermute x3 -> x2, starting transfers between devices: 1.7 us -> 0.55 us  [scatter_sum(): lax.ppermute(outgoing, axis, [(source, source ^ mask) for source in range...]
    dot_general x3 -> x4, matrix products: 3.31 us -> 4.1 us  [project(): jnp.dot(gathered, weight, preferred_element_type=jnp.float32)]
  transfers between devices with their start and end apart: 9 -> 8, of which waited for: 5 -> 5; matrix products, arithmetic and copies ran while one was open for 24% -> 25% of each run, Pallas kernels for 0% -> 0%
where the time goes in v6:
time: 98.3 us; the launch traced here: 97.5 us
  waiting for transfers between devices  33.9 us (34%)
  other arithmetic  29.5 us (30%)
  matrix products  16.3 us (17%)
  starting transfers between devices  10.2 us (10%)
  local copies, waits for them, and re-layouts  6.35 us (6%)
  between operations  1.16 us (1%)
    ppermute x4, waiting for transfers between devices, shifted(): lax.ppermute(value, axis, [(source, source + steps) for source in range(i...  26.1 us
    ppermute x4, starting transfers between devices, shifted(): lax.ppermute(value, axis, [(source, source + steps) for source in range(i...  8.01 us
    ppermute x2, waiting for transfers between devices, scatter_sum(): lax.ppermute(outgoing, axis, [(source, source ^ mask) for source in range...  7.8 us
    mul x3, other arithmetic, short_conv(): weight[tap_index].astype(jnp.float32)[None, :] * window.astype(jnp.float32)  4.3 us
    dot_general x4, matrix products, project(): jnp.dot(gathered, weight, preferred_element_type=jnp.float32)  4.1 us
    dot_general x3, matrix products, segment_parts(): jnp.dot(lifted_intact[block], memory, precision=HIGH_PRECISION)  3.16 us
    broadcast_in_dim x1, other arithmetic, shards(): segment_states = closing[None, None]  2.39 us
    dot_general x1, matrix products, segment_parts(): jnp.einsum('bac,bcv->bav', scores, head_values, preferred_element_type=jn...  2.31 us
  transfers between devices with their start and end apart: 8, of which 5 were waited for; matrix products, arithmetic and copies ran while one was open for 25% of the time, Pallas kernels for 0%

profile of v6, /device:TPU:24, one launch (start us, length us, event | category | flops | bytes accessed | tf_op | source)
XLA Modules:
  0.0 97.5 jit_solution(12793571774363275494)
XLA Ops:
  0.7 1.6 %collective-permute-start = (bf16[64,2048]{1,0:T(8,128)(2,1)}, bf16[64,2048]{1,0:T(8,128)(2,1)S(1)}, u32[]{:S(2)}, u32[]{:S(2)}) collective-permute-start(bf16[64,2048]{1,0:T(8,128)(2,1)} %param.18), channel_id=1, source_target_pairs={{0,2},{1,3},{2,0},{3,1},{4,6},{5,7},{6,4},{7,5},{8,10},{9,11},{10,... | collective-permute-start | bytes 786440 | tf_op jit(solution)/shard_map/ppermute | solution.py:149
  2.2 0.8 reduce-window.9
  3.1 0.7 bitcast_subtract_fusion
  5.1 1.2 %slice_compare_fusion = pred[3]{0:T(512)(128)(4,1)} fusion(s32[256]{0:T(256)S(1)} %iota_add_fusion, s32[]{:T(128)} %bitcast.48), kind=kLoop, calls=%fused_computation.172 | loop fusion | flops 3 | bytes 19 | tf_op jit(solution)/shard_map/ge | solution.py:262
  7.4 0.7 reshape.253
  9.2 1.4 %slice_convert_fusion.9 = (f32[1,256]{1,0:T(1,128)}, f32[1,256]{1,0:T(1,128)}, f32[1,256]{1,0:T(1,128)}, f32[1,256]{1,0:T(1,128)}) fusion(bf16[4,256]{1,0:T(4,128)(2,1)} %param.24), kind=kLoop, calls=%fused_computation.165 | loop fusion | flops 1024 | bytes 6144 | tf_op jit(solution)/shard_map/mul | solution.py:36
  10.6 1.0 %pad_maximum_fusion.4 = bf16[128,2048]{1,0:T(8,128)(2,1)S(1)} fusion(bf16[64,2048]{1,0:T(8,128)(2,1)S(1)} %collective-permute-done, bf16[64,2048]{1,0:T(8,128)(2,1)} %param.18), kind=kLoop, calls=%fused_computation.37 | loop fusion | flops 1048576 | bytes 1048576 | tf_op jit(solution)/shard_map/concatenate | solution.py:150
  11.7 0.8 slice_reduce_fusion.1
  12.4 1.4 %slice_convert_fusion.13 = (f32[1,256]{1,0:T(1,128)}, f32[1,256]{1,0:T(1,128)}, f32[1,256]{1,0:T(1,128)}, f32[1,256]{1,0:T(1,128)}) fusion(bf16[4,256]{1,0:T(4,128)(2,1)} %param.23), kind=kLoop, calls=%fused_computation.169 | loop fusion | flops 1024 | bytes 6144 | tf_op jit(solution)/shard_map/mul | solution.py:36
  13.8 1.4 %slice_convert_fusion.5 = (f32[1,512]{1,0:T(1,128)}, f32[1,512]{1,0:T(1,128)}, f32[1,512]{1,0:T(1,128)}, f32[1,512]{1,0:T(1,128)}) fusion(bf16[4,512]{1,0:T(4,128)(2,1)} %param.25), kind=kLoop, calls=%fused_computation.142 | loop fusion | flops 2048 | bytes 12288 | tf_op jit(solution)/shard_map/mul | solution.py:36
  15.3 1.8 %conditional.1 = (bf16[256,2048]{1,0:T(8,128)(2,1)S(1)}) conditional(s32[]{:T(128)} %clamp.3, (bf16[64,2048]{1,0:T(8,128)(2,1)S(1)}, bf16[64,2048]{1,0:T(8,128)(2,1)S(1)}, bf16[64,2048]{1,0:T(8,128)(2,1)S(1)}, bf16[64,2048]{1,0:T(8,128)(2,1)S(1)}) %tuple.60, (bf16[64,2048]{1,0:T(8,128)(2,1)S(1)}, ...), branch_computations={%region_3.0_spmd, %region_4.0_spmd, %region_5.6_spmd, %region_6.7_... | conditional | flops 4194304 | bytes 3145764 | solution.py:163
  15.4 0.7 copy-done.4
  16.1 1.0 %pad_maximum_fusion = bf16[256,2048]{1,0:T(8,128)(2,1)S(1)} fusion(bf16[64,2048]{1,0:T(8,128)(2,1)S(1)} %get-tuple-element.40, bf16[64,2048]{1,0:T(8,128)(2,1)} %copy-done.4, bf16[64,2048]{1,0:T(8,128)(2,1)S(1)} %get-tuple-element.33, bf16[64,2048]{1,0:T(8,128)(2,1)S(1)} %get-tuple-element.32), kind=kLoop, calls=%fused_computation | loop fusion | flops 4194304 | bytes 2097152 | tf_op jit(solution)/shard_map/cond/branch_0_fun/concatenate | solution.py:161
  17.2 2.4 %convolution_convert_fusion.5 = bf16[256,512]{1,0:T(8,128)(2,1)S(1)} fusion(bf16[256,2048]{1,0:T(8,128)(2,1)S(1)} %get-tuple-element.103, bf16[2048,512]{1,0:T(8,128)(2,1)} %param.22), kind=kOutput, calls=%fused_computation.11 | convolution fusion | flops 537001984 | bytes 3407872 | tf_op jit(solution)/shard_map/dot_general | solution.py:217
  20.6 0.7 select_bitcast_fusion.2
  21.3 3.4 %collective-permute-start.2 = (bf16[3,1024]{1,0:T(4,128)(2,1)}, bf16[3,1024]{1,0:T(4,128)(2,1)}, u32[]{:S(2)}, u32[]{:S(2)}) collective-permute-start(bf16[3,1024]{1,0:T(4,128)(2,1)} %get-tuple-element.57), channel_id=1, source_target_pairs={{0,4},{4,8},{8,12},{12,16},{16,20},{20,24},{24,28},{1,5},{5,9},{9,... | collective-permute-start | bytes 18440 | tf_op jit(solution)/shard_map/ppermute | solution.py:17
  24.7 1.5 %fusion.23 = f32[256,256]{1,0:T(8,128)} fusion(bf16[16,256]{1,0:T(8,128)(2,1)S(1)} %copy-done.28, bf16[256,2048]{1,0:T(8,128)(2,1)S(1)} %get-tuple-element.103, bf16[2048,16]{0,1:T(8,128)(2,1)S(1)} %copy-done.27, f32[256]{0:T(256)S(1)} %copy-done.30), kind=kOutput, calls=%fused_computation.75 | convolution fusion | flops 19533824 | bytes 1385472 | tf_op jit(solution)/shard_map/dot_general | solution.py:244
  26.2 1.2 %reduce_window_sum.30 = f32[4,64,256]{2,1,0:T(8,128)S(1)} reduce-window(f32[4,64,256]{2,1,0:T(8,128)} %bitcast.145, f32[]{:T(128)} %constant.90.clone.1), window={size=1x64x1 pad=0_0x63_0x0_0}, to_apply=%region_7.8 | reduce-window | flops 4128768 | bytes 524292 | tf_op jit(solution)/shard_map/jit(cumsum)/reduce_window_sum | solution.py:48
  27.4 0.8 exponential_multiply_fusion
  29.0 0.7 fusion.67
  29.7 2.2 %bitcast_multiply_fusion = (f32[256,256]{1,0:T(8,128)}, f32[256,256]{1,0:T(8,128)S(1)}) fusion(f32[4,64,256]{2,1,0:T(8,128)S(1)} %exp.37, f32[4,256]{1,0:T(4,128)S(1)} %pad_maximum_fusion.13, f32[256]{0:T(256)} %reshape.253, f32[256]{0:T(256)} %get-tuple-element.96, bf16[256,256]{1,0:T(8,128)(2,1)} %copy-done.15, f32[256]{0:T(256)} %bitcast.171, ...), kind=kLoop, calls=%fused_computation.79 | loop fusion | flops 2162688 | bytes 932352 | tf_op jit(solution)/shard_map/mul | solution.py:84
  32.0 0.7 slice.248
  32.7 1.1 %multiply_convert_fusion.1 = bf16[256,512]{1,0:T(8,128)(2,1)S(1)} fusion(bf16[256,512]{1,0:T(8,128)(2,1)S(1)} %copy-done.17, bf16[3,512]{1,0:T(4,128)(2,1)S(1)} %slice.248, f32[256]{0:T(256)} %get-tuple-element.96, f32[512]{0:T(512)} %bitcast.162, f32[256]{0:T(256)} %get-tuple-element.97, f32[512]{0:T(512)} %bitcast.163, f32[256]{0:T(256)} %get-tuple-element.98, ...), kind=kLoop, calls=%fused_computation.58 | loop fusion | flops 3801088 | bytes 539648 | tf_op jit(solution)/shard_map/convert_element_type | solution.py:40
  33.8 1.0 %multiply_convert_fusion.2 = bf16[256,256]{1,0:T(8,128)(2,1)S(1)} fusion(bf16[256,256]{1,0:T(8,128)(2,1)S(1)} %convolution_convert_fusion.6, bf16[3,256]{1,0:T(4,128)(2,1)S(1)} %get-tuple-element.73, f32[256]{0:T(256)} %bitcast.166, f32[256]{0:T(256)} %bitcast.167, f32[256]{0:T(256)} %bitcast.165, f32[256]{0:T(256)} %bitcast.164, f32[256]{0:T(256)} %get-tuple-element.96, ...), kind=kLoop, calls=%fused_computation.88 | loop fusion | flops 1900544 | bytes 271872 | tf_op jit(solution)/shard_map/convert_element_type | solution.py:40
  34.9 1.3 %fusion.37 = f32[4,256,512]{2,1,0:T(8,128)S(1)} fusion(bf16[4,64,512]{2,1,0:T(8,128)(2,1)S(1)} %bitcast.140, bf16[4,64,256]{2,1,0:T(8,128)(2,1)S(1)} %bitcast.142, f32[4,64,256]{2,1,0:T(8,128)S(1)} %reduce_window_sum.30, f32[4,64]{1,0:T(4,128)} %get-tuple-element.87, f32[4,256]{1,0:T(4,128)S(1)} %bitcast.150), kind=kOutput, calls=%fused_computation.104 | convolution fusion | flops 67436544 | bytes 2757632 | tf_op jit(solution)/shard_map/bsk,bsv->bkv/dot_general | solution.py:58
  36.4 1.1 %convolution_bitcast_fusion.1 = f32[1,64,512]{2,1,0:T(8,128)} fusion(f32[4,64,256]{2,1,0:T(8,128)S(1)} %broadcast_multiply_fusion, f32[4,256,512]{2,1,0:T(8,128)S(1)} %fusion.37, f32[256]{0:T(256)S(1)} %bitcast.148, f32[256]{0:T(256)S(1)} %get-tuple-element.94), kind=kOutput, calls=%fused_computation.18 | convolution fusion | flops 50724864 | bytes 1247232 | tf_op jit(solution)/shard_map/dot_general | solution.py:79
  37.5 2.1 %collective-permute-start.3 = (bf16[257,512]{1,0:T(8,128)(2,1)S(1)}, bf16[257,512]{1,0:T(8,128)(2,1)S(1)}, u32[]{:S(2)}, u32[]{:S(2)}) collective-permute-start(bf16[257,512]{1,0:T(8,128)(2,1)S(1)} %pad_maximum_fusion.6), channel_id=1, source_target_pairs={{0,4},{4,8},{8,12},{12,16},{16,20},{20,24},{24,28},{1,5},{5,9},{9,... | collective-permute-start | bytes 789512 | tf_op jit(solution)/shard_map/ppermute | solution.py:17
  39.5 1.0 %convolution_bitcast_fusion.2 = f32[1,64,512]{2,1,0:T(8,128)} fusion(f32[4,256,512]{2,1,0:T(8,128)S(1)} %fusion.37, f32[256]{0:T(256)S(1)} %get-tuple-element.94, f32[4,64,256]{2,1,0:T(8,128)S(1)} %broadcast_multiply_fusion), kind=kOutput, calls=%fused_computation.19 | convolution fusion | flops 50462720 | bytes 721920 | tf_op jit(solution)/shard_map/dot_general | solution.py:79
  40.6 1.1 %convolution_bitcast_fusion = f32[1,64,512]{2,1,0:T(8,128)} fusion(f32[4,256,512]{2,1,0:T(8,128)S(1)} %fusion.37, f32[256]{0:T(256)S(1)} %bitcast.153, f32[4,64,256]{2,1,0:T(8,128)S(1)} %broadcast_multiply_fusion, f32[256]{0:T(256)S(1)} %bitcast.149, f32[256]{0:T(256)S(1)} %get-tuple-element.94), kind=kOutput, calls=%fused_computation.17 | convolution fusion | flops 50987008 | bytes 1772544 | tf_op jit(solution)/shard_map/dot_general | solution.py:79
  41.6 7.4 %collective-permute-done.3 = bf16[257,512]{1,0:T(8,128)(2,1)S(1)} collective-permute-done((bf16[257,512]{1,0:T(8,128)(2,1)S(1)}, bf16[257,512]{1,0:T(8,128)(2,1)S(1)}, u32[]{:S(2)}, u32[]{:S(2)}) %collective-permute-start.3) | collective-permute-done | bytes 263200 | tf_op jit(solution)/shard_map/ppermute | solution.py:17
  49.9 0.7 pad_maximum_fusion.7
  50.6 1.3 %collective-permute-start.4 = (bf16[257,512]{1,0:T(8,128)(2,1)}, bf16[257,512]{1,0:T(8,128)(2,1)}, u32[]{:S(2)}, u32[]{:S(2)}) collective-permute-start(bf16[257,512]{1,0:T(8,128)(2,1)} %pad_maximum_fusion.7), channel_id=1, source_target_pairs={{0,8},{4,12},{8,16},{12,20},{16,24},{20,28},{1,9},{5,13},{9,17},{1... | collective-permute-start | bytes 789512 | tf_op jit(solution)/shard_map/ppermute | solution.py:17
  51.9 2.3 %convolution_add_fusion = f32[4,64,512]{2,1,0:T(8,128)} fusion(bf16[4,64,512]{2,1,0:T(8,128)(2,1)} %bitcast.141, f32[1,64,512]{2,1,0:T(8,128)} %convolution_bitcast_fusion, f32[1,64,512]{2,1,0:T(8,128)} %convolution_bitcast_fusion.1, f32[1,64,512]{2,1,0:T(8,128)} %convolution_bitcast_fusion.2, f32[4]{0:T(128)} %pad.30.clone, ...), kind=kOutput, calls=%fused_computation.8 | convolution fusion | flops 26148864 | bytes 1840144 | tf_op jit(solution)/shard_map/bac,bcv->bav/dot_general | solution.py:70
  54.2 6.3 %collective-permute-done.4 = bf16[257,512]{1,0:T(8,128)(2,1)} collective-permute-done((bf16[257,512]{1,0:T(8,128)(2,1)}, bf16[257,512]{1,0:T(8,128)(2,1)}, u32[]{:S(2)}, u32[]{:S(2)}) %collective-permute-start.4) | collective-permute-done | bytes 263200 | tf_op jit(solution)/shard_map/ppermute | solution.py:17
  60.5 1.4 %fusion.62 = bf16[256,512]{1,0:T(8,128)(2,1)S(1)} fusion(f32[256,512]{1,0:T(8,128)} %copy-done.1, bf16[257,512]{1,0:T(8,128)(2,1)} %copy-done.12, f32[256]{0:T(256)S(1)} %copy-done.22, pred[]{:T(512)S(6)} %ge.78, bf16[257,512]{1,0:T(8,128)(2,1)} %collective-permute-done.4, f32[256]{0:T(256)} %get-tuple-element.60, pred[]{:T(512)S(6)} %ge.77), kind=kLoop, calls=%fused_computation.177 | loop fusion | flops 1179648 | bytes 1312770 | tf_op jit(solution)/shard_map/convert_element_type | solution.py:118
  62.0 1.3 %collective-permute-start.5 = (bf16[256,512]{1,0:T(8,128)(2,1)S(1)}, bf16[256,512]{1,0:T(8,128)(2,1)S(1)}, u32[]{:S(2)}, u32[]{:S(2)}) collective-permute-start(bf16[256,512]{1,0:T(8,128)(2,1)S(1)} %fusion.62), channel_id=1, source_target_pairs={{0,16},{4,20},{8,24},{12,28},{1,17},{5,21},{9,25},{13,29},{2,18},{... | collective-permute-start | bytes 786440 | tf_op jit(solution)/shard_map/ppermute | solution.py:17
  63.3 0.7 slice_convert_fusion
  64.0 0.7 multiply_select_fusion
  64.6 12.4 %collective-permute-done.5 = bf16[256,512]{1,0:T(8,128)(2,1)S(1)} collective-permute-done((bf16[256,512]{1,0:T(8,128)(2,1)S(1)}, bf16[256,512]{1,0:T(8,128)(2,1)S(1)}, u32[]{:S(2)}, u32[]{:S(2)}) %collective-permute-start.5) | collective-permute-done | bytes 262176 | tf_op jit(solution)/shard_map/ppermute | solution.py:17
  77.0 2.1 %multiply_reduce_fusion = (f32[256]{0:T(256)S(1)}, f32[256,512]{1,0:T(8,128)S(1)}) fusion(f32[256,512]{1,0:T(8,128)} %bitcast.144, f32[256,256]{1,0:T(8,128)} %get-tuple-element.66, bf16[256,512]{1,0:T(8,128)(2,1)S(1)} %collective-permute-done.5, f32[256]{0:T(256)} %bitcast.159, f32[256]{0:T(256)S(1)} %get-tuple-element.93, pred[]{:T(512)S(6)} %ge.77, ...), kind=kOutput, calls=%fused_computation.54 | convolution fusion | flops 202899200 | bytes 2100226 | tf_op jit(solution)/shard_map/dot_general | solution.py:252
  79.1 0.8 multiply_convert_fusion
  81.9 0.7 copy-done.8
  82.6 0.8 pad_maximum_fusion.5
  83.5 2.2 %collective-permute-done.6 = bf16[2,64,2048]{2,1,0:T(8,128)(2,1)} collective-permute-done((bf16[2,64,2048]{2,1,0:T(8,128)(2,1)}, bf16[2,64,2048]{2,1,0:T(8,128)(2,1)}, u32[]{:S(2)}, u32[]{:S(2)}) %collective-permute-start.6) | collective-permute-done | bytes 524320 | tf_op jit(solution)/shard_map/ppermute | solution.py:189
  85.7 1.3 %fusion.21 = bf16[1,64,2048]{2,1,0:T(8,128)(2,1)S(1)} fusion(pred[]{:T(512)S(6)} %eq.50, bf16[2,64,2048]{2,1,0:T(8,128)(2,1)} %collective-permute-done.6, bf16[64,2048]{1,0:T(8,128)(2,1)S(1)} %convolution_convert_fusion.3, bf16[64,2048]{1,0:T(8,128)(2,1)S(1)} %convolution_convert_fusion.2, pred[]{:T(512)S(6)} %eq.51, bf16[64,2048]{1,0:T(8,128)(2,1)} %copy-done.8, ...), kind=kLoop, calls=%fused_computation.73 | loop fusion | flops 1310720 | bytes 1835010 | tf_op jit(solution)/shard_map/stack | solution.py:188
  87.5 2.4 %fusion.3 = f32[1,1,256,512]{3,2,1,0:T(8,128)} fusion(bf16[256,512]{1,0:T(8,128)(2,1)} %copy-done.20, f32[256]{0:T(256)S(1)} %get-tuple-element.92, pred[]{:T(512)S(6)} %ge.76, f32[256,512]{1,0:T(8,128)S(1)} %copy-done.2, bf16[257,512]{1,0:T(8,128)(2,1)} %copy-done.12, f32[256]{0:T(256)S(1)} %copy-done.22, pred[]{:T(512)S(6)} %ge.78, ...), kind=kLoop, calls=%fused_computation.34 | loop fusion | flops 1572864 | bytes 1838083 | tf_op jit(solution)/shard_map/broadcast_in_dim | solution.py:261
  89.9 5.6 %collective-permute-done.7 = bf16[1,64,2048]{2,1,0:T(8,128)(2,1)S(1)} collective-permute-done((bf16[1,64,2048]{2,1,0:T(8,128)(2,1)S(1)}, bf16[1,64,2048]{2,1,0:T(8,128)(2,1)S(1)}, u32[]{:S(2)}, u32[]{:S(2)}) %collective-permute-start.7) | collective-permute-done | bytes 262176 | tf_op jit(solution)/shard_map/ppermute | solution.py:189
  95.5 2.0 %fusion.5 = bf16[64,2048]{1,0:T(8,128)(2,1)} fusion(bf16[1,64,2048]{2,1,0:T(8,128)(2,1)S(1)} %collective-permute-done.7, pred[]{:T(512)S(6)} %eq.50, bf16[2,64,2048]{2,1,0:T(8,128)(2,1)} %collective-permute-done.6, bf16[64,2048]{1,0:T(8,128)(2,1)S(1)} %convolution_convert_fusion.3, bf16[64,2048]{1,0:T(8,128)(2,1)S(1)} %convolution_convert_fusion.2, ...), kind=kLoop, calls=%fused_computation.40 | loop fusion | flops 1572864 | bytes 2097154 | tf_op jit(solution)/shard_map/convert_element_type | solution.py:195
  (99 shorter events, 9.0 us)
Async XLA Ops:
  0.6 79.3 %copy-start = (bf16[512,2048]{1,0:T(8,128)(2,1)S(1)}, bf16[512,2048]{1,0:T(8,128)(2,1)}, u32[]{:S(2)}) copy-start(bf16[512,2048]{1,0:T(8,128)(2,1)} %param.31) | copy-start | bytes 6291460
  0.6 14.7 %copy-start.3 = (bf16[64,2048]{1,0:T(8,128)(2,1)S(1)}, bf16[64,2048]{1,0:T(8,128)(2,1)}, u32[]{:S(2)}) copy-start(bf16[64,2048]{1,0:T(8,128)(2,1)} %param.18) | copy-start | bytes 786436
  0.7 9.9 %collective-permute-start = (bf16[64,2048]{1,0:T(8,128)(2,1)}, bf16[64,2048]{1,0:T(8,128)(2,1)S(1)}, u32[]{:S(2)}, u32[]{:S(2)}) collective-permute-start(bf16[64,2048]{1,0:T(8,128)(2,1)} %param.18), channel_id=1, source_target_pairs={{0,2},{1,3},{2,0},{3,1},{4,6},{5,7},{6,4},{7,5},{8,10},{9,11},{10,... | collective-permute-start | bytes 786440 | tf_op jit(solution)/shard_map/ppermute | solution.py:149
  11.6 3.7 %collective-permute-start.1 = (bf16[128,2048]{1,0:T(8,128)(2,1)S(1)}, bf16[128,2048]{1,0:T(8,128)(2,1)S(1)}, u32[]{:S(2)}, u32[]{:S(2)}) collective-permute-start(bf16[128,2048]{1,0:T(8,128)(2,1)S(1)} %pad_maximum_fusion.4), channel_id=1, source_target_pairs={{0,1},{1,0},{2,3},{3,2},{4,5},{5,4},{6,7},{7,6},{8,9},{9,8},{10,11... | collective-permute-start | bytes 1572872 | tf_op jit(solution)/shard_map/ppermute | solution.py:149
  15.4 0.7 copy-start.4
  17.1 2.5 %copy-start.18 = (bf16[2048,256]{1,0:T(8,128)(2,1)S(1)}, bf16[2048,256]{1,0:T(8,128)(2,1)}, u32[]{:S(2)}) copy-start(bf16[2048,256]{1,0:T(8,128)(2,1)} %param.21) | copy-start | bytes 3145732
  17.1 3.0 %copy-start.19 = (bf16[2048,256]{1,0:T(8,128)(2,1)S(1)}, bf16[2048,256]{1,0:T(8,128)(2,1)}, u32[]{:S(2)}) copy-start(bf16[2048,256]{1,0:T(8,128)(2,1)} %param.20) | copy-start | bytes 3145732
  19.6 1.0 copy-start.16
  19.6 1.0 copy-start.25
  19.6 5.0 %copy-start.27 = (bf16[2048,16]{0,1:T(8,128)(2,1)S(1)}, bf16[2048,16]{0,1:T(8,128)(2,1)}, u32[]{:S(2)}) copy-start(bf16[2048,16]{0,1:T(8,128)(2,1)} %param.26) | copy-start | bytes 196612
  19.6 5.0 %copy-start.28 = (bf16[16,256]{1,0:T(8,128)(2,1)S(1)}, bf16[16,256]{1,0:T(8,128)(2,1)}, u32[]{:S(2)}) copy-start(bf16[16,256]{1,0:T(8,128)(2,1)} %param.27) | copy-start | bytes 24580
  19.7 5.0 %copy-start.30 = (f32[256]{0:T(256)S(1)}, f32[256]{0:T(256)}, u32[]{:S(2)}) copy-start(f32[256]{0:T(256)} %param.28) | copy-start | bytes 3076
  20.6 5.6 %copy-start.15 = (bf16[256,256]{1,0:T(8,128)(2,1)}, bf16[256,256]{1,0:T(8,128)(2,1)S(1)}, u32[]{:S(2)}) copy-start(bf16[256,256]{1,0:T(8,128)(2,1)S(1)} %convolution_convert_fusion.7) | copy-start | bytes 393220
  21.3 7.7 %collective-permute-start.2 = (bf16[3,1024]{1,0:T(4,128)(2,1)}, bf16[3,1024]{1,0:T(4,128)(2,1)}, u32[]{:S(2)}, u32[]{:S(2)}) collective-permute-start(bf16[3,1024]{1,0:T(4,128)(2,1)} %get-tuple-element.57), channel_id=1, source_target_pairs={{0,4},{4,8},{8,12},{12,16},{16,20},{20,24},{24,28},{1,5},{5,9},{9,... | collective-permute-start | bytes 18440 | tf_op jit(solution)/shard_map/ppermute | solution.py:17
  27.4 5.3 %copy-start.17 = (bf16[256,512]{1,0:T(8,128)(2,1)S(1)}, bf16[256,512]{1,0:T(8,128)(2,1)}, u32[]{:S(2)}) copy-start(bf16[256,512]{1,0:T(8,128)(2,1)} %copy-done.16) | copy-start | bytes 786436
  28.9 20.8 %copy-start.21 = (f32[256]{0:T(256)}, f32[256]{0:T(256)S(1)}, u32[]{:S(2)}) copy-start(f32[256]{0:T(256)S(1)} %get-tuple-element.65) | copy-start | bytes 3076
  31.9 4.3 %copy-start.10 = (f32[256,256]{1,0:T(8,128)}, f32[256,256]{1,0:T(8,128)S(1)}, u32[]{:S(2)}) copy-start(f32[256,256]{1,0:T(8,128)S(1)} %get-tuple-element.67) | copy-start | bytes 786436
  33.8 2.3 %copy-start.11 = (bf16[256,512]{1,0:T(8,128)(2,1)}, bf16[256,512]{1,0:T(8,128)(2,1)S(1)}, u32[]{:S(2)}) copy-start(bf16[256,512]{1,0:T(8,128)(2,1)S(1)} %multiply_convert_fusion.1) | copy-start | bytes 786436
  34.8 1.3 %copy-start.13 = (bf16[256,256]{1,0:T(8,128)(2,1)}, bf16[256,256]{1,0:T(8,128)(2,1)S(1)}, u32[]{:S(2)}) copy-start(bf16[256,256]{1,0:T(8,128)(2,1)S(1)} %multiply_convert_fusion.2) | copy-start | bytes 393220
  36.4 14.2 %copy-start.1 = (f32[256,512]{1,0:T(8,128)}, f32[256,512]{1,0:T(8,128)S(1)}, u32[]{:S(2)}) copy-start(f32[256,512]{1,0:T(8,128)S(1)} %get-tuple-element.62) | copy-start | bytes 1572868
  37.5 14.4 %copy-start.14 = (bf16[256,256]{1,0:T(8,128)(2,1)S(1)}, bf16[256,256]{1,0:T(8,128)(2,1)}, u32[]{:S(2)}) copy-start(bf16[256,256]{1,0:T(8,128)(2,1)} %copy-done.13) | copy-start | bytes 393220
  37.5 11.5 %collective-permute-start.3 = (bf16[257,512]{1,0:T(8,128)(2,1)S(1)}, bf16[257,512]{1,0:T(8,128)(2,1)S(1)}, u32[]{:S(2)}, u32[]{:S(2)}) collective-permute-start(bf16[257,512]{1,0:T(8,128)(2,1)S(1)} %pad_maximum_fusion.6), channel_id=1, source_target_pairs={{0,4},{4,8},{8,12},{12,16},{16,20},{20,24},{24,28},{1,5},{5,9},{9,... | collective-permute-start | bytes 789512 | tf_op jit(solution)/shard_map/ppermute | solution.py:17
  49.0 0.7 copy-start.12
  49.0 0.7 copy-start.24
  49.9 10.7 %copy-start.22 = (f32[256]{0:T(256)S(1)}, f32[256]{0:T(256)}, u32[]{:S(2)}) copy-start(f32[256]{0:T(256)} %copy-done.21) | copy-start | bytes 3076
  50.6 9.9 %collective-permute-start.4 = (bf16[257,512]{1,0:T(8,128)(2,1)}, bf16[257,512]{1,0:T(8,128)(2,1)}, u32[]{:S(2)}, u32[]{:S(2)}) collective-permute-start(bf16[257,512]{1,0:T(8,128)(2,1)} %pad_maximum_fusion.7), channel_id=1, source_target_pairs={{0,8},{4,12},{8,16},{12,20},{16,24},{20,28},{1,9},{5,13},{9,17},{1... | collective-permute-start | bytes 789512 | tf_op jit(solution)/shard_map/ppermute | solution.py:17
  54.2 24.9 %copy-start.26 = (bf16[2048,512]{1,0:T(8,128)(2,1)S(1)}, bf16[2048,512]{1,0:T(8,128)(2,1)}, u32[]{:S(2)}) copy-start(bf16[2048,512]{1,0:T(8,128)(2,1)} %param.29) | copy-start | bytes 6291460
  54.2 24.9 %copy-start.29 = (f32[512]{0:T(512)S(1)}, f32[512]{0:T(512)}, u32[]{:S(2)}) copy-start(f32[512]{0:T(512)} %param.30) | copy-start | bytes 6148
  62.0 15.0 %collective-permute-start.5 = (bf16[256,512]{1,0:T(8,128)(2,1)S(1)}, bf16[256,512]{1,0:T(8,128)(2,1)S(1)}, u32[]{:S(2)}, u32[]{:S(2)}) collective-permute-start(bf16[256,512]{1,0:T(8,128)(2,1)S(1)} %fusion.62), channel_id=1, source_target_pairs={{0,16},{4,20},{8,24},{12,28},{1,17},{5,21},{9,25},{13,29},{2,18},{... | collective-permute-start | bytes 786440 | tf_op jit(solution)/shard_map/ppermute | solution.py:17
  77.0 2.1 %copy-start.20 = (bf16[256,512]{1,0:T(8,128)(2,1)}, bf16[256,512]{1,0:T(8,128)(2,1)S(1)}, u32[]{:S(2)}) copy-start(bf16[256,512]{1,0:T(8,128)(2,1)S(1)} %collective-permute-done.5) | copy-start | bytes 786436
  81.9 0.7 copy-start.8
  82.6 4.9 %copy-start.2 = (f32[256,512]{1,0:T(8,128)S(1)}, f32[256,512]{1,0:T(8,128)}, u32[]{:S(2)}) copy-start(f32[256,512]{1,0:T(8,128)} %copy-done.1) | copy-start | bytes 1572868
  82.6 4.9 %copy-start.23 = (f32[256]{0:T(256)S(1)}, f32[256]{0:T(256)}, u32[]{:S(2)}) copy-start(f32[256]{0:T(256)} %get-tuple-element.60) | copy-start | bytes 3076
  83.5 2.3 %collective-permute-start.6 = (bf16[2,64,2048]{2,1,0:T(8,128)(2,1)}, bf16[2,64,2048]{2,1,0:T(8,128)(2,1)}, u32[]{:S(2)}, u32[]{:S(2)}) collective-permute-start(bf16[2,64,2048]{2,1,0:T(8,128)(2,1)} %pad_maximum_fusion.5), channel_id=1, source_target_pairs={{0,1},{1,0},{2,3},{3,2},{4,5},{5,4},{6,7},{7,6},{8,9},{9,8},{10,11... | collective-permute-start | bytes 1572872 | tf_op jit(solution)/shard_map/ppermute | solution.py:189
  83.5 12.0 %copy-start.9 = (bf16[64,2048]{1,0:T(8,128)(2,1)S(1)}, bf16[64,2048]{1,0:T(8,128)(2,1)}, u32[]{:S(2)}) copy-start(bf16[64,2048]{1,0:T(8,128)(2,1)} %copy-done.8) | copy-start | bytes 786436
  87.0 8.5 %collective-permute-start.7 = (bf16[1,64,2048]{2,1,0:T(8,128)(2,1)S(1)}, bf16[1,64,2048]{2,1,0:T(8,128)(2,1)S(1)}, u32[]{:S(2)}, u32[]{:S(2)}) collective-permute-start(bf16[1,64,2048]{2,1,0:T(8,128)(2,1)S(1)} %fusion.21), channel_id=1, source_target_pairs={{0,2},{1,3},{2,0},{3,1},{4,6},{5,7},{6,4},{7,5},{8,10},{9,11},{10,... | collective-permute-start | bytes 786440 | tf_op jit(solution)/shard_map/ppermute | solution.py:189

commit v7 on v5

--- a/solution.py
+++ b/solution.py
@@ -8,7 +8,7 @@
 SPAN = 64
 
 
-HIGHEST_PRECISION = lax.Precision.HIGHEST
+HIGH_PRECISION = lax.Precision.HIGH
 
 
 def shifted(value, axis, steps):
@@ -76,7 +76,7 @@
     products = [product]
     for block in range(block_count):
         if block > 0:
-            local_outs.append(jnp.dot(lifted_intact[block], memory, precision=HIGHEST_PRECISION))
+            local_outs.append(jnp.dot(lifted_intact[block], memory, precision=HIGH_PRECISION))
             products.append(product)
         memory = step_decay[block][:, None] * memory + update[block]
         product = product * step_decay[block]
@@ -163,15 +163,11 @@
     return lax.switch(place, [functools.partial(ordered, shift) for shift in range(count)])
 
 
-def scatter_sum(terms, axis):
-    count = lax.axis_size(axis)
-    place = lax.axis_index(axis)
-    chunks = terms.reshape((count, terms.shape[0] // count) + terms.shape[1:])
-    total = lax.dynamic_index_in_dim(chunks, place, 0, False).astype(jnp.float32)
-    for step, pairs in enumerate(rotations(axis), start=1):
-        outgoing = lax.dynamic_index_in_dim(chunks, (place + step) % count, 0, False)
-        total = total + lax.ppermute(outgoing, axis, pairs).astype(jnp.float32)
-    return total.astype(jnp.bfloat16)
+def scatter_sum(gated, weight, axis):
+    count = lax.axis_size(axis)
+    terms = jnp.dot(gated, weight, preferred_element_type=jnp.float32).astype(jnp.bfloat16)
+    parts = lax.all_to_all(terms.reshape((count, -1) + terms.shape[1:]), axis, 0, 0, tiled=True)
+    return jnp.sum(parts.astype(jnp.float32), axis=0).astype(jnp.bfloat16)
 
 
 def shards(
@@ -190,7 +186,9 @@
     norm_gain,
     out_weight,
 ):
-    gathered = gather_rows(tokens, "hv")
+    gathered = lax.all_to_all(
+        jnp.broadcast_to(tokens[None], (lax.axis_size("hv"),) + tokens.shape), "hv", 0, 0, tiled=True
+    ).reshape((-1, tokens.shape[1]))
 
     def project(weight):
         return jnp.dot(gathered, weight, preferred_element_type=jnp.float32).astype(jnp.bfloat16)
@@ -229,17 +227,14 @@
     )
     closing, entering = prefix_states(local_decay, local_memory, "tok")
     heads_out = local_out.reshape((row_count, value_width)) + jnp.dot(
-        carry_lift.reshape((row_count, key_width)), entering, precision=HIGHEST_PRECISION
+        carry_lift.reshape((row_count, key_width)), entering, precision=HIGH_PRECISION
     )
     gate_float = gate_values.astype(jnp.float32)
     rescale = lax.rsqrt(jnp.mean(heads_out * heads_out, axis=1, keepdims=True) + 1e-05)
     gated_out = (
         heads_out * rescale * norm_gain[None, :] * gate_float * jax.nn.sigmoid(gate_float)
     ).astype(jnp.bfloat16)
-    mixed = scatter_sum(
-        jnp.dot(gated_out, out_weight, preferred_element_type=jnp.float32).astype(jnp.bfloat16),
-        "hv",
-    )
+    mixed = scatter_sum(gated_out, out_weight, "hv")
     segment_states = closing[None, None]
     in_prompt = positions[row_count - rim_rows :] >= prompt_first[row_count - 1]
     tail_rows = joined[row_count - rim_rows :]

time: 102 us -> 107 us (1.049)
  waiting for transfers between devices: 36 us -> 42.1 us
  other arithmetic: 27.1 us -> 21.1 us
  starting transfers between devices: 11.4 us -> 15.9 us
    all_to_all x0 -> x2, waiting for transfers between devices: none -> 19 us  [the longest x1 12.2 us: scatter_sum(): lax.all_to_all(terms.reshape((count, -1) + terms.shape[1:]), axis, 0, 0,...]
    ppermute x5 -> x0, waiting for transfers between devices: 10.2 us -> none  [the longest x3 10.2 us: scatter_sum(): total = total + lax.ppermute(outgoing, axis, pairs).astype(jnp.float32)]
    all_to_all x0 -> x2, starting transfers between devices: none -> 7.9 us  [the longest x1 4.39 us: scatter_sum(): lax.all_to_all(terms.reshape((count, -1) + terms.shape[1:]), axis, 0, 0,...]
    ppermute x5 -> x0, starting transfers between devices: 3.36 us -> none  [the longest x3 1.7 us: scatter_sum(): total = total + lax.ppermute(outgoing, axis, pairs).astype(jnp.float32)]
    ppermute x4, waiting for transfers between devices: 25.7 us -> 23.1 us  [shifted(): lax.ppermute(value, axis, [(source, source + steps) for source in range(i...]
    mul x3, other arithmetic: 4.27 us -> 1.8 us  [short_conv(): weight[tap_index].astype(jnp.float32)[None, :] * window.astype(jnp.float32)]
    broadcast_in_dim x0 -> x1, local copies, waits for them, and re-layouts: none -> 2.2 us  [shards(): jnp.broadcast_to(tokens[None], (lax.axis_size('hv'),) + tokens.shape)]
    reduce_sum x0 -> x1, other arithmetic: none -> 2.16 us  [scatter_sum(): return jnp.sum(parts.astype(jnp.float32), axis=0).astype(jnp.bfloat16)]
  transfers between devices with their start and end apart: 9 -> 6, of which waited for: 5 -> 5; matrix products, arithmetic and copies ran while one was open for 24% -> 19% of each run, Pallas kernels for 0% -> 0%
where the time goes in v7:
time: 107 us; the launch traced here: 106 us
  waiting for transfers between devices  42.1 us (39%)
  other arithmetic  21.1 us (20%)
  matrix products  18.3 us (17%)
  starting transfers between devices  15.9 us (15%)
  local copies, waits for them, and re-layouts  7.69 us (7%)
  between operations  1.09 us (1%)
    ppermute x4, waiting for transfers between devices, shifted(): lax.ppermute(value, axis, [(source, source + steps) for source in range(i...  23.1 us
    all_to_all x1, waiting for transfers between devices, scatter_sum(): lax.all_to_all(terms.reshape((count, -1) + terms.shape[1:]), axis, 0, 0,...  12.2 us
    ppermute x4, starting transfers between devices, shifted(): lax.ppermute(value, axis, [(source, source + steps) for source in range(i...  8.01 us
    all_to_all x1, waiting for transfers between devices, shards(): lax.all_to_all(jnp.broadcast_to(tokens[None], (lax.axis_size('hv'),) + to...  6.74 us
    all_to_all x1, starting transfers between devices, scatter_sum(): lax.all_to_all(terms.reshape((count, -1) + terms.shape[1:]), axis, 0, 0,...  4.39 us
    dot_general x1, matrix products, scatter_sum(): jnp.dot(gated, weight, preferred_element_type=jnp.float32)  4.06 us
    all_to_all x1, starting transfers between devices, shards(): lax.all_to_all(jnp.broadcast_to(tokens[None], (lax.axis_size('hv'),) + to...  3.51 us
    dot_general x3, matrix products, project(): jnp.dot(gathered, weight, preferred_element_type=jnp.float32)  3.32 us
  transfers between devices with their start and end apart: 6, of which 5 were waited for; matrix products, arithmetic and copies ran while one was open for 19% of the time, Pallas kernels for 0%

profile of v7, /device:TPU:24, one launch (start us, length us, event | category | flops | bytes accessed | tf_op | source)
XLA Modules:
  0.0 106.2 jit_solution(6907778009512684624)
XLA Ops:
  0.7 2.2 %broadcast_in_dim.27 = bf16[4,64,2048]{2,1,0:T(8,128)(2,1)} broadcast(bf16[64,2048]{1,0:T(8,128)(2,1)} %param.14), dimensions={1,2} | broadcast | bytes 1310720 | tf_op jit(solution)/shard_map/broadcast_in_dim | solution.py:190
  2.9 3.5 %all-to-all-start = ((bf16[4,64,2048]{2,1,0:T(8,128)(2,1)}), bf16[4,64,2048]{2,1,0:T(8,128)(2,1)S(1)}, u32[]{:S(2)}, u32[]{:S(2)}) async-start(bf16[4,64,2048]{2,1,0:T(8,128)(2,1)} %broadcast_in_dim.27), calls=%async_computation | async-start | bytes 2097152 | tf_op jit(solution)/shard_map/all_to_all | solution.py:189
  6.7 0.6 slice.213
  7.3 0.6 compare_convert_fusion.5
  8.0 0.7 slice_compare_fusion
  9.1 0.7 compare_convert_fusion.1
  9.8 0.7 slice_reduce_fusion.1
  10.5 0.7 reshape.256
  11.2 0.5 pad.8.clone
  12.3 0.6 slice_convert_fusion.9
  12.9 0.6 slice_convert_fusion.13
  13.5 0.6 slice_convert_fusion.5
  14.1 6.7 %all-to-all-done = bf16[4,64,2048]{2,1,0:T(8,128)(2,1)S(1)} async-done(((bf16[4,64,2048]{2,1,0:T(8,128)(2,1)}), bf16[4,64,2048]{2,1,0:T(8,128)(2,1)S(1)}, u32[]{:S(2)}, u32[]{:S(2)}) %all-to-all-start) | async-done | bytes 1048608 | tf_op jit(solution)/shard_map/all_to_all | solution.py:189
  20.8 2.4 %convolution_convert_fusion.2 = bf16[256,512]{1,0:T(8,128)(2,1)S(1)} fusion(bf16[256,2048]{1,0:T(8,128)(2,1)S(1)} %bitcast.114, bf16[2048,512]{1,0:T(8,128)(2,1)} %param.18), kind=kOutput, calls=%fused_computation.4 | convolution fusion | flops 537001984 | bytes 3407872 | tf_op jit(solution)/shard_map/dot_general | solution.py:194
  24.2 0.6 copy-done.9
  24.9 0.7 select_bitcast_fusion
  25.5 3.4 %collective-permute-start = (bf16[3,1024]{1,0:T(4,128)(2,1)}, bf16[3,1024]{1,0:T(4,128)(2,1)}, u32[]{:S(2)}, u32[]{:S(2)}) collective-permute-start(bf16[3,1024]{1,0:T(4,128)(2,1)} %get-tuple-element.4), channel_id=1, source_target_pairs={{0,4},{4,8},{8,12},{12,16},{16,20},{20,24},{24,28},{1,5},{5,9},{9,... | collective-permute-start | bytes 18440 | tf_op jit(solution)/shard_map/ppermute | solution.py:17
  29.0 1.5 %fusion.21 = f32[256,256]{1,0:T(8,128)} fusion(bf16[16,256]{1,0:T(8,128)(2,1)S(1)} %copy-done.22, bf16[256,2048]{1,0:T(8,128)(2,1)S(1)} %bitcast.117, bf16[2048,16]{0,1:T(8,128)(2,1)S(1)} %copy-done.21, f32[256]{0:T(256)S(1)} %copy-done.24), kind=kOutput, calls=%fused_computation.60 | convolution fusion | flops 19533824 | bytes 1385472 | tf_op jit(solution)/shard_map/dot_general | solution.py:221
  30.5 1.2 %reduce_window_sum.30 = f32[4,64,256]{2,1,0:T(8,128)S(1)} reduce-window(f32[4,64,256]{2,1,0:T(8,128)} %bitcast.127, f32[]{:T(128)} %constant.31.clone.1), window={size=1x64x1 pad=0_0x63_0x0_0}, to_apply=%region_3.4 | reduce-window | flops 4128768 | bytes 524292 | tf_op jit(solution)/shard_map/jit(cumsum)/reduce_window_sum | solution.py:48
  31.7 0.7 exponential_multiply_fusion
  32.4 0.7 pad_maximum_fusion.7
  33.2 0.7 fusion.64
  33.9 2.2 %bitcast_multiply_fusion = (f32[256,256]{1,0:T(8,128)}, f32[256,256]{1,0:T(8,128)S(1)}) fusion(f32[4,64,256]{2,1,0:T(8,128)S(1)} %exp.37, f32[4,256]{1,0:T(4,128)S(1)} %pad_maximum_fusion.7, f32[256]{0:T(256)} %reshape.256, f32[256]{0:T(256)} %get-tuple-element.41, bf16[256,256]{1,0:T(8,128)(2,1)} %copy-done.9, f32[256]{0:T(256)} %bitcast.153, ...), kind=kLoop, calls=%fused_computation.62 | loop fusion | flops 2162688 | bytes 932352 | tf_op jit(solution)/shard_map/mul | solution.py:84
  36.2 0.7 slice.224
  36.9 1.1 %multiply_convert_fusion.1 = bf16[256,512]{1,0:T(8,128)(2,1)S(1)} fusion(bf16[256,512]{1,0:T(8,128)(2,1)S(1)} %copy-done.11, bf16[3,512]{1,0:T(4,128)(2,1)S(1)} %slice.224, f32[256]{0:T(256)} %get-tuple-element.41, f32[512]{0:T(512)} %bitcast.144, f32[256]{0:T(256)} %get-tuple-element.42, f32[512]{0:T(512)} %bitcast.145, f32[256]{0:T(256)} %get-tuple-element.43, ...), kind=kLoop, calls=%fused_computation.44 | loop fusion | flops 3801088 | bytes 539648 | tf_op jit(solution)/shard_map/convert_element_type | solution.py:40
  38.1 1.0 multiply_convert_fusion.3
  39.1 1.3 %fusion.38 = f32[4,256,512]{2,1,0:T(8,128)S(1)} fusion(bf16[4,64,512]{2,1,0:T(8,128)(2,1)S(1)} %bitcast.121, bf16[4,64,256]{2,1,0:T(8,128)(2,1)S(1)} %bitcast.123, f32[4,64,256]{2,1,0:T(8,128)S(1)} %reduce_window_sum.30, f32[4,64]{1,0:T(4,128)} %get-tuple-element.32, f32[4,256]{1,0:T(4,128)S(1)} %bitcast.132), kind=kOutput, calls=%fused_computation.86 | convolution fusion | flops 67436544 | bytes 2757632 | tf_op jit(solution)/shard_map/bsk,bsv->bkv/dot_general | solution.py:58
  40.7 1.0 convolution_bitcast_fusion.1
  41.7 2.1 %collective-permute-start.1 = (bf16[257,512]{1,0:T(8,128)(2,1)S(1)}, bf16[257,512]{1,0:T(8,128)(2,1)S(1)}, u32[]{:S(2)}, u32[]{:S(2)}) collective-permute-start(bf16[257,512]{1,0:T(8,128)(2,1)S(1)} %pad_maximum_fusion), channel_id=1, source_target_pairs={{0,4},{4,8},{8,12},{12,16},{16,20},{20,24},{24,28},{1,5},{5,9},{9,... | collective-permute-start | bytes 789512 | tf_op jit(solution)/shard_map/ppermute | solution.py:17
  43.8 1.0 convolution_bitcast_fusion.2
  44.8 1.1 %convolution_bitcast_fusion = f32[1,64,512]{2,1,0:T(8,128)} fusion(f32[4,256,512]{2,1,0:T(8,128)S(1)} %fusion.38, f32[256]{0:T(256)S(1)} %bitcast.135, f32[4,64,256]{2,1,0:T(8,128)S(1)} %broadcast_multiply_fusion, f32[256]{0:T(256)S(1)} %bitcast.131, f32[256]{0:T(256)S(1)} %get-tuple-element.39), kind=kOutput, calls=%fused_computation.10 | convolution fusion | flops 50987008 | bytes 1772544 | tf_op jit(solution)/shard_map/dot_general | solution.py:79
  45.9 6.4 %collective-permute-done.1 = bf16[257,512]{1,0:T(8,128)(2,1)S(1)} collective-permute-done((bf16[257,512]{1,0:T(8,128)(2,1)S(1)}, bf16[257,512]{1,0:T(8,128)(2,1)S(1)}, u32[]{:S(2)}, u32[]{:S(2)}) %collective-permute-start.1) | collective-permute-done | bytes 263200 | tf_op jit(solution)/shard_map/ppermute | solution.py:17
  52.3 0.7 subtract_convert_fusion
  53.2 0.7 pad_maximum_fusion.1
  53.9 1.3 %collective-permute-start.2 = (bf16[257,512]{1,0:T(8,128)(2,1)}, bf16[257,512]{1,0:T(8,128)(2,1)}, u32[]{:S(2)}, u32[]{:S(2)}) collective-permute-start(bf16[257,512]{1,0:T(8,128)(2,1)} %pad_maximum_fusion.1), channel_id=1, source_target_pairs={{0,8},{4,12},{8,16},{12,20},{16,24},{20,28},{1,9},{5,13},{9,17},{1... | collective-permute-start | bytes 789512 | tf_op jit(solution)/shard_map/ppermute | solution.py:17
  55.2 2.3 %convolution_add_fusion = f32[4,64,512]{2,1,0:T(8,128)} fusion(bf16[4,64,512]{2,1,0:T(8,128)(2,1)} %bitcast.122, f32[1,64,512]{2,1,0:T(8,128)} %convolution_bitcast_fusion, f32[1,64,512]{2,1,0:T(8,128)} %convolution_bitcast_fusion.1, f32[1,64,512]{2,1,0:T(8,128)} %convolution_bitcast_fusion.2, f32[4]{0:T(128)} %pad.12.clone, ...), kind=kOutput, calls=%fused_computation.1 | convolution fusion | flops 26148864 | bytes 1840144 | tf_op jit(solution)/shard_map/bac,bcv->bav/dot_general | solution.py:70
  57.5 5.4 %collective-permute-done.2 = bf16[257,512]{1,0:T(8,128)(2,1)} collective-permute-done((bf16[257,512]{1,0:T(8,128)(2,1)}, bf16[257,512]{1,0:T(8,128)(2,1)}, u32[]{:S(2)}, u32[]{:S(2)}) %collective-permute-start.2) | collective-permute-done | bytes 263200 | tf_op jit(solution)/shard_map/ppermute | solution.py:17
  62.9 1.4 %fusion.60 = bf16[256,512]{1,0:T(8,128)(2,1)S(1)} fusion(f32[256,512]{1,0:T(8,128)} %copy-done.1, bf16[257,512]{1,0:T(8,128)(2,1)} %copy-done.5, f32[256]{0:T(256)S(1)} %copy-done.15, pred[]{:T(512)S(6)} %ge.78, bf16[257,512]{1,0:T(8,128)(2,1)} %collective-permute-done.2, f32[256]{0:T(256)} %get-tuple-element.7, pred[]{:T(512)S(6)} %ge.77), kind=kLoop, calls=%fused_computation.156 | loop fusion | flops 1179648 | bytes 1312770 | tf_op jit(solution)/shard_map/convert_element_type | solution.py:118
  64.3 1.3 %collective-permute-start.3 = (bf16[256,512]{1,0:T(8,128)(2,1)S(1)}, bf16[256,512]{1,0:T(8,128)(2,1)S(1)}, u32[]{:S(2)}, u32[]{:S(2)}) collective-permute-start(bf16[256,512]{1,0:T(8,128)(2,1)S(1)} %fusion.60), channel_id=1, source_target_pairs={{0,16},{4,20},{8,24},{12,28},{1,17},{5,21},{9,25},{13,29},{2,18},{... | collective-permute-start | bytes 786440 | tf_op jit(solution)/shard_map/ppermute | solution.py:17
  65.6 0.7 slice_convert_fusion
  66.3 0.7 multiply_select_fusion
  67.0 11.4 %collective-permute-done.3 = bf16[256,512]{1,0:T(8,128)(2,1)S(1)} collective-permute-done((bf16[256,512]{1,0:T(8,128)(2,1)S(1)}, bf16[256,512]{1,0:T(8,128)(2,1)S(1)}, u32[]{:S(2)}, u32[]{:S(2)}) %collective-permute-start.3) | collective-permute-done | bytes 262176 | tf_op jit(solution)/shard_map/ppermute | solution.py:17
  78.4 2.7 %multiply_reduce_fusion = (f32[256]{0:T(256)S(1)}, f32[256,512]{1,0:T(8,128)}) fusion(f32[256,512]{1,0:T(8,128)} %bitcast.126, f32[256,256]{1,0:T(8,128)} %get-tuple-element.13, bf16[256,512]{1,0:T(8,128)(2,1)S(1)} %collective-permute-done.3, f32[256]{0:T(256)} %bitcast.141, f32[256]{0:T(256)S(1)} %get-tuple-element.38, pred[]{:T(512)S(6)} %ge.77, ...), kind=kOutput, calls=%fused_computation.40 | convolution fusion | flops 202899200 | bytes 2100226 | tf_op jit(solution)/shard_map/dot_general | solution.py:229
  81.1 4.1 %convolution_convert_fusion = bf16[256,2048]{1,0:T(8,128)(2,1)} fusion(bf16[512,2048]{1,0:T(8,128)(2,1)S(1)} %copy-done, f32[256,512]{1,0:T(8,128)} %get-tuple-element.45, bf16[256,2048]{1,0:T(8,128)(2,1)S(1)} %bitcast.118, bf16[2048,512]{1,0:T(8,128)(2,1)} %param.25, f32[512]{0:T(512)S(1)} %copy-done.23, f32[256]{0:T(256)S(1)} %add_rsqrt_fusion), kind=kOutput, calls=%fused_computation | convolution fusion | flops 1075576832 | bytes 6818816 | tf_op jit(solution)/shard_map/dot_general | solution.py:168
  85.2 4.4 %all-to-all-start.1 = ((bf16[4,64,2048]{2,1,0:T(8,128)(2,1)}), bf16[4,64,2048]{2,1,0:T(8,128)(2,1)}, u32[]{:S(2)}, u32[]{:S(2)}) async-start(bf16[4,64,2048]{2,1,0:T(8,128)(2,1)} %bitcast.125), calls=%async_computation.1 | async-start | bytes 2097152 | tf_op jit(solution)/shard_map/all_to_all | solution.py:169
  89.6 2.2 %fusion.3 = f32[1,1,256,512]{3,2,1,0:T(8,128)} fusion(bf16[256,512]{1,0:T(8,128)(2,1)S(1)} %collective-permute-done.3, f32[256]{0:T(256)S(1)} %get-tuple-element.37, pred[]{:T(512)S(6)} %ge.76, f32[256,512]{1,0:T(8,128)S(1)} %copy-done.2, bf16[257,512]{1,0:T(8,128)(2,1)S(1)} %copy-done.6, f32[256]{0:T(256)S(1)} %copy-done.15, pred[]{:T(512)S(6)} %ge.78, ...), kind=kLoop, calls=%fused_computation.27 | loop fusion | flops 1572864 | bytes 1838083 | tf_op jit(solution)/shard_map/broadcast_in_dim | solution.py:238
  91.8 12.2 %all-to-all-done.1 = bf16[4,64,2048]{2,1,0:T(8,128)(2,1)} async-done(((bf16[4,64,2048]{2,1,0:T(8,128)(2,1)}), bf16[4,64,2048]{2,1,0:T(8,128)(2,1)}, u32[]{:S(2)}, u32[]{:S(2)}) %all-to-all-start.1) | async-done | bytes 1048608 | tf_op jit(solution)/shard_map/all_to_all | solution.py:169
  104.0 2.2 %reduce_sum.22 = bf16[64,2048]{1,0:T(8,128)(2,1)} reduce(bf16[4,64,2048]{2,1,0:T(8,128)(2,1)} %all-to-all-done.1, bf16[]{:T(256)} %constant.64.clone.1), dimensions={0}, to_apply=%region_5.6 | reduce | flops 393216 | bytes 1310722 | tf_op jit(solution)/shard_map/reduce_sum | solution.py:170
  (81 shorter events, 2.9 us)
Async XLA Ops:
  0.6 80.4 %copy-start = (bf16[512,2048]{1,0:T(8,128)(2,1)S(1)}, bf16[512,2048]{1,0:T(8,128)(2,1)}, u32[]{:S(2)}) copy-start(bf16[512,2048]{1,0:T(8,128)(2,1)} %param.27) | copy-start | bytes 6291460
  0.6 5.8 %copy-start.25 = (s32[5]{0:T(128)S(1)}, s32[5]{0:T(128)}, u32[]{:S(2)}) copy-start(s32[5]{0:T(128)} %param.15) | copy-start | bytes 64
  0.7 11.6 %copy-start.19 = (bf16[4,256]{1,0:T(4,128)(2,1)S(1)}, bf16[4,256]{1,0:T(4,128)(2,1)}, u32[]{:S(2)}) copy-start(bf16[4,256]{1,0:T(4,128)(2,1)} %param.20) | copy-start | bytes 6148
  0.7 12.2 %copy-start.20 = (bf16[4,256]{1,0:T(4,128)(2,1)S(1)}, bf16[4,256]{1,0:T(4,128)(2,1)}, u32[]{:S(2)}) copy-start(bf16[4,256]{1,0:T(4,128)(2,1)} %param.19) | copy-start | bytes 6148
  0.7 12.8 %copy-start.16 = (bf16[4,512]{1,0:T(4,128)(2,1)S(1)}, bf16[4,512]{1,0:T(4,128)(2,1)}, u32[]{:S(2)}) copy-start(bf16[4,512]{1,0:T(4,128)(2,1)} %param.21) | copy-start | bytes 12292
  2.9 17.9 %all-to-all-start = ((bf16[4,64,2048]{2,1,0:T(8,128)(2,1)}), bf16[4,64,2048]{2,1,0:T(8,128)(2,1)S(1)}, u32[]{:S(2)}, u32[]{:S(2)}) async-start(bf16[4,64,2048]{2,1,0:T(8,128)(2,1)} %broadcast_in_dim.27), calls=%async_computation | async-start | bytes 2097152 | tf_op jit(solution)/shard_map/all_to_all | solution.py:189
  20.8 2.5 %copy-start.12 = (bf16[2048,256]{1,0:T(8,128)(2,1)S(1)}, bf16[2048,256]{1,0:T(8,128)(2,1)}, u32[]{:S(2)}) copy-start(bf16[2048,256]{1,0:T(8,128)(2,1)} %param.17) | copy-start | bytes 3145732
  20.8 3.0 %copy-start.13 = (bf16[2048,256]{1,0:T(8,128)(2,1)S(1)}, bf16[2048,256]{1,0:T(8,128)(2,1)}, u32[]{:S(2)}) copy-start(bf16[2048,256]{1,0:T(8,128)(2,1)} %param.16) | copy-start | bytes 3145732
  23.3 0.9 copy-start.10
  23.3 5.7 %copy-start.21 = (bf16[2048,16]{0,1:T(8,128)(2,1)S(1)}, bf16[2048,16]{0,1:T(8,128)(2,1)}, u32[]{:S(2)}) copy-start(bf16[2048,16]{0,1:T(8,128)(2,1)} %param.22) | copy-start | bytes 196612
  23.3 5.7 %copy-start.22 = (bf16[16,256]{1,0:T(8,128)(2,1)S(1)}, bf16[16,256]{1,0:T(8,128)(2,1)}, u32[]{:S(2)}) copy-start(bf16[16,256]{1,0:T(8,128)(2,1)} %param.23) | copy-start | bytes 24580
  23.3 5.7 %copy-start.24 = (f32[256]{0:T(256)S(1)}, f32[256]{0:T(256)}, u32[]{:S(2)}) copy-start(f32[256]{0:T(256)} %param.24) | copy-start | bytes 3076
  24.2 0.6 copy-start.9
  25.5 7.7 %collective-permute-start = (bf16[3,1024]{1,0:T(4,128)(2,1)}, bf16[3,1024]{1,0:T(4,128)(2,1)}, u32[]{:S(2)}, u32[]{:S(2)}) collective-permute-start(bf16[3,1024]{1,0:T(4,128)(2,1)} %get-tuple-element.4), channel_id=1, source_target_pairs={{0,4},{4,8},{8,12},{12,16},{16,20},{20,24},{24,28},{1,5},{5,9},{9,... | collective-permute-start | bytes 18440 | tf_op jit(solution)/shard_map/ppermute | solution.py:17
  31.7 5.2 %copy-start.11 = (bf16[256,512]{1,0:T(8,128)(2,1)S(1)}, bf16[256,512]{1,0:T(8,128)(2,1)}, u32[]{:S(2)}) copy-start(bf16[256,512]{1,0:T(8,128)(2,1)} %copy-done.10) | copy-start | bytes 786436
  33.1 19.9 %copy-start.14 = (f32[256]{0:T(256)}, f32[256]{0:T(256)S(1)}, u32[]{:S(2)}) copy-start(f32[256]{0:T(256)S(1)} %get-tuple-element.12) | copy-start | bytes 3076
  36.1 4.3 %copy-start.3 = (f32[256,256]{1,0:T(8,128)}, f32[256,256]{1,0:T(8,128)S(1)}, u32[]{:S(2)}) copy-start(f32[256,256]{1,0:T(8,128)S(1)} %get-tuple-element.14) | copy-start | bytes 786436
  38.1 2.3 %copy-start.4 = (bf16[256,512]{1,0:T(8,128)(2,1)}, bf16[256,512]{1,0:T(8,128)(2,1)S(1)}, u32[]{:S(2)}) copy-start(bf16[256,512]{1,0:T(8,128)(2,1)S(1)} %multiply_convert_fusion.1) | copy-start | bytes 786436
  39.1 1.3 %copy-start.7 = (bf16[256,256]{1,0:T(8,128)(2,1)}, bf16[256,256]{1,0:T(8,128)(2,1)S(1)}, u32[]{:S(2)}) copy-start(bf16[256,256]{1,0:T(8,128)(2,1)S(1)} %multiply_convert_fusion.3) | copy-start | bytes 393220
  40.7 13.3 %copy-start.1 = (f32[256,512]{1,0:T(8,128)}, f32[256,512]{1,0:T(8,128)S(1)}, u32[]{:S(2)}) copy-start(f32[256,512]{1,0:T(8,128)S(1)} %get-tuple-element.9) | copy-start | bytes 1572868
  41.7 13.5 %copy-start.8 = (bf16[256,256]{1,0:T(8,128)(2,1)S(1)}, bf16[256,256]{1,0:T(8,128)(2,1)}, u32[]{:S(2)}) copy-start(bf16[256,256]{1,0:T(8,128)(2,1)} %copy-done.7) | copy-start | bytes 393220
  41.7 10.6 %collective-permute-start.1 = (bf16[257,512]{1,0:T(8,128)(2,1)S(1)}, bf16[257,512]{1,0:T(8,128)(2,1)S(1)}, u32[]{:S(2)}, u32[]{:S(2)}) collective-permute-start(bf16[257,512]{1,0:T(8,128)(2,1)S(1)} %pad_maximum_fusion), channel_id=1, source_target_pairs={{0,4},{4,8},{8,12},{12,16},{16,20},{20,24},{24,28},{1,5},{5,9},{9,... | collective-permute-start | bytes 789512 | tf_op jit(solution)/shard_map/ppermute | solution.py:17
  52.3 0.7 copy-start.5
  52.3 0.7 copy-start.18
  53.2 9.7 %copy-start.15 = (f32[256]{0:T(256)S(1)}, f32[256]{0:T(256)}, u32[]{:S(2)}) copy-start(f32[256]{0:T(256)} %copy-done.14) | copy-start | bytes 3076
  53.9 9.0 %collective-permute-start.2 = (bf16[257,512]{1,0:T(8,128)(2,1)}, bf16[257,512]{1,0:T(8,128)(2,1)}, u32[]{:S(2)}, u32[]{:S(2)}) collective-permute-start(bf16[257,512]{1,0:T(8,128)(2,1)} %pad_maximum_fusion.1), channel_id=1, source_target_pairs={{0,8},{4,12},{8,16},{12,20},{16,24},{20,28},{1,9},{5,13},{9,17},{1... | collective-permute-start | bytes 789512 | tf_op jit(solution)/shard_map/ppermute | solution.py:17
  57.5 23.5 %copy-start.23 = (f32[512]{0:T(512)S(1)}, f32[512]{0:T(512)}, u32[]{:S(2)}) copy-start(f32[512]{0:T(512)} %param.26) | copy-start | bytes 6148
  64.3 14.0 %collective-permute-start.3 = (bf16[256,512]{1,0:T(8,128)(2,1)S(1)}, bf16[256,512]{1,0:T(8,128)(2,1)S(1)}, u32[]{:S(2)}, u32[]{:S(2)}) collective-permute-start(bf16[256,512]{1,0:T(8,128)(2,1)S(1)} %fusion.60), channel_id=1, source_target_pairs={{0,16},{4,20},{8,24},{12,28},{1,17},{5,21},{9,25},{13,29},{2,18},{... | collective-permute-start | bytes 786440 | tf_op jit(solution)/shard_map/ppermute | solution.py:17
  85.1 4.4 %copy-start.2 = (f32[256,512]{1,0:T(8,128)S(1)}, f32[256,512]{1,0:T(8,128)}, u32[]{:S(2)}) copy-start(f32[256,512]{1,0:T(8,128)} %copy-done.1) | copy-start | bytes 1572868
  85.1 4.4 %copy-start.6 = (bf16[257,512]{1,0:T(8,128)(2,1)S(1)}, bf16[257,512]{1,0:T(8,128)(2,1)}, u32[]{:S(2)}) copy-start(bf16[257,512]{1,0:T(8,128)(2,1)} %copy-done.5) | copy-start | bytes 789508
  85.2 4.4 %copy-start.17 = (f32[256]{0:T(256)S(1)}, f32[256]{0:T(256)}, u32[]{:S(2)}) copy-start(f32[256]{0:T(256)} %get-tuple-element.7) | copy-start | bytes 3076
  85.2 18.9 %all-to-all-start.1 = ((bf16[4,64,2048]{2,1,0:T(8,128)(2,1)}), bf16[4,64,2048]{2,1,0:T(8,128)(2,1)}, u32[]{:S(2)}, u32[]{:S(2)}) async-start(bf16[4,64,2048]{2,1,0:T(8,128)(2,1)} %bitcast.125), calls=%async_computation.1 | async-start | bytes 2097152 | tf_op jit(solution)/shard_map/all_to_all | solution.py:169

commit v8 on v6

--- a/solution.py
+++ b/solution.py
@@ -25,18 +25,19 @@
 
 def short_conv(raw_rows, before_rows, weight, positions, prompt_first):
     tap_count = weight.shape[0]
+    row_count = raw_rows.shape[0]
     extended = jnp.concatenate([before_rows, raw_rows], axis=0)
-    summed = jnp.zeros(raw_rows.shape, jnp.float32)
-    for tap_index in range(tap_count):
-        lag_rows = tap_count - 1 - tap_index
-        inside_prompt = (positions - lag_rows >= prompt_first).astype(jnp.float32)
-        window = lax.slice_in_dim(extended, tap_index, tap_index + raw_rows.shape[0], axis=0)
-        summed = (
-            summed
-            + weight[tap_index].astype(jnp.float32)[None, :]
-            * window.astype(jnp.float32)
-            * inside_prompt[:, None]
-        )
+    lags = tap_count - 1 - jnp.arange(tap_count)
+    inside_prompt = (positions[None, :] - lags[:, None] >= prompt_first[None, :]).astype(jnp.float32)
+    windows = jnp.stack(
+        [lax.slice_in_dim(extended, tap, tap + row_count, axis=0) for tap in range(tap_count)]
+    )
+    summed = jnp.sum(
+        weight.astype(jnp.float32)[:, None, :]
+        * windows.astype(jnp.float32)
+        * inside_prompt[:, :, None],
+        axis=0,
+    )
     return jax.nn.silu(summed).astype(jnp.bfloat16)
 
 
@@ -225,7 +226,10 @@
     key_width = raw_query.shape[1]
     value_width = raw_value.shape[1]
     positions = lax.axis_index("tok") * row_count + jnp.arange(row_count, dtype=jnp.int32)
-    offsets = jnp.cumsum(prompt_lengths) - prompt_lengths
+    prompt_index = jnp.arange(prompt_lengths.shape[0])
+    offsets = jnp.sum(
+        jnp.where(prompt_index[None, :] < prompt_index[:, None], prompt_lengths[None, :], 0), axis=1
+    )
     prompt_first, starts = prompt_marks(positions, offsets)
     rim_rows = query_conv.shape[0] - 1
     joined = jnp.concatenate([raw_query, raw_key, raw_value], axis=1)

time: 98.3 us -> 86 us (0.87)
  other arithmetic: 29.5 us -> 20.4 us
  local copies, waits for them, and re-layouts: 6.35 us -> 3.81 us
  starting transfers between devices: 10.2 us -> 11.7 us
  matrix products: 16.3 us -> 15.1 us
    mul x4 -> x0, other arithmetic: 4.4 us -> none  [the longest x3 4.3 us: short_conv(): weight[tap_index].astype(jnp.float32)[None, :] * window.astype(jnp.float32)]
    ppermute x2, waiting for transfers between devices: 0.01 us -> 2.33 us  [gather_rows(): lax.ppermute(jnp.concatenate(received), axis, [(source, source ^ mask) fo...]
    ppermute x4, waiting for transfers between devices: 26.1 us -> 24.1 us  [shifted(): lax.ppermute(value, axis, [(source, source + steps) for source in range(i...]
    mul x1, other arithmetic: 2.23 us -> 0.8 us  [segment_parts(): carry_lift = lifted_intact * jnp.stack(products)[:, None, :]]
    reduce_sum x0 -> x3, other arithmetic: none -> 1.41 us  [the longest x1 0.77 us: shards(): jnp.sum(jnp.where(prompt_index[None, :] < prompt_index[:, None], prompt_l...]
    ppermute x2, starting transfers between devices: 0.55 us -> 1.63 us  [scatter_sum(): lax.ppermute(outgoing, axis, [(source, source ^ mask) for source in range...]
    ppermute x2, waiting for transfers between devices: 7.8 us -> 6.72 us  [scatter_sum(): lax.ppermute(outgoing, axis, [(source, source ^ mask) for source in range...]
    convert_element_type x3 -> x4, other arithmetic: 2.74 us -> 2.13 us  [the longest x3 2.06 us: short_conv(): weight.astype(jnp.float32)[:, None, :] * windows.astype(jnp.float32)]
  transfers between devices with their start and end apart: 8 -> 8, of which waited for: 5 -> 8; matrix products, arithmetic and copies ran while one was open for 25% -> 18% of each run, Pallas kernels for 0% -> 0%
where the time goes in v8:
time: 86 us; the launch traced here: 85.3 us
  waiting for transfers between devices  33.2 us (39%)
  other arithmetic  20.4 us (24%)
  matrix products  15.1 us (18%)
  starting transfers between devices  11.7 us (14%)
  local copies, waits for them, and re-layouts  3.81 us (4%)
  between operations  1.12 us (1%)
    ppermute x4, waiting for transfers between devices, shifted(): lax.ppermute(value, axis, [(source, source + steps) for source in range(i...  24.1 us
    ppermute x4, starting transfers between devices, shifted(): lax.ppermute(value, axis, [(source, source + steps) for source in range(i...  8.46 us
    ppermute x2, waiting for transfers between devices, scatter_sum(): lax.ppermute(outgoing, axis, [(source, source ^ mask) for source in range...  6.72 us
    dot_general x4, matrix products, project(): jnp.dot(gathered, weight, preferred_element_type=jnp.float32)  3.77 us
    dot_general x1, matrix products, segment_parts(): jnp.einsum('bac,bcv->bav', scores, head_values, preferred_element_type=jn...  2.69 us
    dot_general x3, matrix products, segment_parts(): jnp.dot(lifted_intact[block], memory, precision=HIGH_PRECISION)  2.48 us
    broadcast_in_dim x1, other arithmetic, shards(): segment_states = closing[None, None]  2.38 us
    ppermute x2, waiting for transfers between devices, gather_rows(): lax.ppermute(jnp.concatenate(received), axis, [(source, source ^ mask) fo...  2.33 us
  transfers between devices with their start and end apart: 8, of which 8 were waited for; matrix products, arithmetic and copies ran while one was open for 18% of the time, Pallas kernels for 0%

profile of v8, /device:TPU:24, one launch (start us, length us, event | category | flops | bytes accessed | tf_op | source)
XLA Modules:
  0.0 85.3 jit_solution(12210877273109400014)
XLA Ops:
  0.7 1.6 %collective-permute-start = (bf16[64,2048]{1,0:T(8,128)(2,1)}, bf16[64,2048]{1,0:T(8,128)(2,1)S(1)}, u32[]{:S(2)}, u32[]{:S(2)}) collective-permute-start(bf16[64,2048]{1,0:T(8,128)(2,1)} %param.18), channel_id=1, source_target_pairs={{0,2},{1,3},{2,0},{3,1},{4,6},{5,7},{6,4},{7,5},{8,10},{9,11},{10,... | collective-permute-start | bytes 786440 | tf_op jit(solution)/shard_map/ppermute | solution.py:150
  2.2 0.8 select_reduce_fusion.1
  3.7 0.6 slice.189
  4.3 0.7 convert_element_type.196
  5.0 0.7 convert_element_type.206
  5.7 0.7 convert_element_type.212
  6.4 0.5 pad.30.clone
  7.1 0.6 iota_compare_fusion
  7.7 1.2 %collective-permute-done = bf16[64,2048]{1,0:T(8,128)(2,1)S(1)} collective-permute-done((bf16[64,2048]{1,0:T(8,128)(2,1)}, bf16[64,2048]{1,0:T(8,128)(2,1)S(1)}, u32[]{:S(2)}, u32[]{:S(2)}) %collective-permute-start) | collective-permute-done | bytes 262176 | tf_op jit(solution)/shard_map/ppermute | solution.py:150
  9.0 1.0 %pad_maximum_fusion.4 = bf16[128,2048]{1,0:T(8,128)(2,1)S(1)} fusion(bf16[64,2048]{1,0:T(8,128)(2,1)S(1)} %collective-permute-done, bf16[64,2048]{1,0:T(8,128)(2,1)} %param.18), kind=kLoop, calls=%fused_computation.40 | loop fusion | flops 1048576 | bytes 1048576 | tf_op jit(solution)/shard_map/concatenate | solution.py:151
  10.1 0.7 slice_compare_fusion
  10.9 1.1 %collective-permute-done.1 = bf16[128,2048]{1,0:T(8,128)(2,1)S(1)} collective-permute-done((bf16[128,2048]{1,0:T(8,128)(2,1)S(1)}, bf16[128,2048]{1,0:T(8,128)(2,1)S(1)}, u32[]{:S(2)}, u32[]{:S(2)}) %collective-permute-start.1) | collective-permute-done | bytes 524320 | tf_op jit(solution)/shard_map/ppermute | solution.py:150
  12.0 1.8 %conditional.1 = (bf16[256,2048]{1,0:T(8,128)(2,1)S(1)}) conditional(s32[]{:T(128)} %clamp.3, (bf16[64,2048]{1,0:T(8,128)(2,1)S(1)}, bf16[64,2048]{1,0:T(8,128)(2,1)S(1)}, bf16[64,2048]{1,0:T(8,128)(2,1)S(1)}, bf16[64,2048]{1,0:T(8,128)(2,1)S(1)}) %tuple.57, (bf16[64,2048]{1,0:T(8,128)(2,1)S(1)}, ...), branch_computations={%region_3.0_spmd, %region_4.5_spmd, %region_5.6_spmd, %region_6.7_... | conditional | flops 4194304 | bytes 3145764 | solution.py:164
  12.1 0.7 copy-done.4
  12.8 1.0 %pad_maximum_fusion = bf16[256,2048]{1,0:T(8,128)(2,1)S(1)} fusion(bf16[64,2048]{1,0:T(8,128)(2,1)S(1)} %get-tuple-element.40, bf16[64,2048]{1,0:T(8,128)(2,1)} %copy-done.4, bf16[64,2048]{1,0:T(8,128)(2,1)S(1)} %get-tuple-element.33, bf16[64,2048]{1,0:T(8,128)(2,1)S(1)} %get-tuple-element.32), kind=kLoop, calls=%fused_computation | loop fusion | flops 4194304 | bytes 2097152 | tf_op jit(solution)/shard_map/cond/branch_0_fun/concatenate | solution.py:162
  13.8 1.5 %fusion.25 = f32[256,256]{1,0:T(8,128)} fusion(bf16[16,256]{1,0:T(8,128)(2,1)S(1)} %copy-done.20, bf16[256,2048]{1,0:T(8,128)(2,1)S(1)} %get-tuple-element.99, bf16[2048,16]{0,1:T(8,128)(2,1)S(1)} %copy-done.19, f32[256]{0:T(256)S(1)} %copy-done.22), kind=kOutput, calls=%fused_computation.80 | convolution fusion | flops 19533824 | bytes 1385472 | tf_op jit(solution)/shard_map/dot_general | solution.py:248
  15.3 1.2 %reduce_window_sum.23 = f32[4,64,256]{2,1,0:T(8,128)S(1)} reduce-window(f32[4,64,256]{2,1,0:T(8,128)} %bitcast.148, f32[]{:T(128)} %constant.82.clone.1), window={size=1x64x1 pad=0_0x63_0x0_0}, to_apply=%region_8.9 | reduce-window | flops 4128768 | bytes 524292 | tf_op jit(solution)/shard_map/jit(cumsum)/reduce_window_sum | solution.py:49
  16.6 1.8 %convolution_convert_fusion.7 = bf16[256,256]{1,0:T(8,128)(2,1)S(1)} fusion(bf16[256,2048]{1,0:T(8,128)(2,1)S(1)} %get-tuple-element.99, bf16[2048,256]{1,0:T(8,128)(2,1)} %param.20), kind=kOutput, calls=%fused_computation.17 | convolution fusion | flops 268500992 | bytes 2228224 | tf_op jit(solution)/shard_map/dot_general | solution.py:218
  18.6 0.7 convolution_convert_fusion.5
  19.3 0.5 copy-done.13
  20.2 0.7 select_bitcast_fusion.2
  20.9 3.4 %collective-permute-start.2 = (bf16[3,1024]{1,0:T(4,128)(2,1)S(1)}, bf16[3,1024]{1,0:T(4,128)(2,1)S(1)}, u32[]{:S(2)}, u32[]{:S(2)}) collective-permute-start(bf16[3,1024]{1,0:T(4,128)(2,1)S(1)} %get-tuple-element.59), channel_id=1, source_target_pairs={{0,4},{4,8},{8,12},{12,16},{16,20},{20,24},{24,28},{1,5},{5,9},{9,... | collective-permute-start | bytes 18440 | tf_op jit(solution)/shard_map/ppermute | solution.py:17
  24.5 2.8 %collective-permute-done.2 = bf16[3,1024]{1,0:T(4,128)(2,1)S(1)} collective-permute-done((bf16[3,1024]{1,0:T(4,128)(2,1)S(1)}, bf16[3,1024]{1,0:T(4,128)(2,1)S(1)}, u32[]{:S(2)}, u32[]{:S(2)}) %collective-permute-start.2) | collective-permute-done | bytes 6176 | tf_op jit(solution)/shard_map/ppermute | solution.py:17
  28.5 0.6 fusion.48
  29.8 2.5 %collective-permute-start.3 = (bf16[257,512]{1,0:T(8,128)(2,1)S(1)}, bf16[257,512]{1,0:T(8,128)(2,1)S(1)}, u32[]{:S(2)}, u32[]{:S(2)}) collective-permute-start(bf16[257,512]{1,0:T(8,128)(2,1)S(1)} %pad_maximum_fusion.6), channel_id=1, source_target_pairs={{0,4},{4,8},{8,12},{12,16},{16,20},{20,24},{24,28},{1,5},{5,9},{9,... | collective-permute-start | bytes 789512 | tf_op jit(solution)/shard_map/ppermute | solution.py:17
  32.3 0.8 bitcast_multiply_fusion
  33.1 1.0 %convolution_bitcast_fusion.2 = f32[1,64,512]{2,1,0:T(8,128)} fusion(f32[4,256,512]{2,1,0:T(8,128)S(1)} %fusion.48, f32[256]{0:T(256)S(1)} %get-tuple-element.93, f32[4,64,256]{2,1,0:T(8,128)S(1)} %get-tuple-element.76), kind=kOutput, calls=%fused_computation.20 | convolution fusion | flops 50462720 | bytes 721920 | tf_op jit(solution)/shard_map/dot_general | solution.py:80
  34.1 1.1 %convolution_bitcast_fusion = f32[1,64,512]{2,1,0:T(8,128)} fusion(f32[4,256,512]{2,1,0:T(8,128)S(1)} %fusion.48, f32[256]{0:T(256)S(1)} %bitcast.157, f32[4,64,256]{2,1,0:T(8,128)S(1)} %get-tuple-element.76, f32[256]{0:T(256)S(1)} %bitcast.154, f32[256]{0:T(256)S(1)} %get-tuple-element.93), kind=kOutput, calls=%fused_computation.18 | convolution fusion | flops 50987008 | bytes 1772544 | tf_op jit(solution)/shard_map/dot_general | solution.py:80
  35.2 4.8 %collective-permute-done.3 = bf16[257,512]{1,0:T(8,128)(2,1)S(1)} collective-permute-done((bf16[257,512]{1,0:T(8,128)(2,1)S(1)}, bf16[257,512]{1,0:T(8,128)(2,1)S(1)}, u32[]{:S(2)}, u32[]{:S(2)}) %collective-permute-start.3) | collective-permute-done | bytes 263200 | tf_op jit(solution)/shard_map/ppermute | solution.py:17
  40.2 0.7 pad_maximum_fusion.7
  40.9 1.3 %collective-permute-start.4 = (bf16[257,512]{1,0:T(8,128)(2,1)}, bf16[257,512]{1,0:T(8,128)(2,1)}, u32[]{:S(2)}, u32[]{:S(2)}) collective-permute-start(bf16[257,512]{1,0:T(8,128)(2,1)} %pad_maximum_fusion.7), channel_id=1, source_target_pairs={{0,8},{4,12},{8,16},{12,20},{16,24},{20,28},{1,9},{5,13},{9,17},{1... | collective-permute-start | bytes 789512 | tf_op jit(solution)/shard_map/ppermute | solution.py:17
  42.2 2.7 %convolution_add_fusion = f32[4,64,512]{2,1,0:T(8,128)} fusion(f32[1,64,512]{2,1,0:T(8,128)} %convolution_bitcast_fusion, f32[1,64,512]{2,1,0:T(8,128)S(1)} %convolution_bitcast_fusion.1, f32[1,64,512]{2,1,0:T(8,128)} %convolution_bitcast_fusion.2, f32[4]{0:T(128)} %pad.30.clone, f32[4,64,256]{2,1,0:T(8,128)} %copy-done.11, ...), kind=kOutput, calls=%fused_computation.9 | convolution fusion | flops 27525120 | bytes 2233360 | tf_op jit(solution)/shard_map/bac,bcv->bav/dot_general | solution.py:71
  44.9 4.7 %collective-permute-done.4 = bf16[257,512]{1,0:T(8,128)(2,1)} collective-permute-done((bf16[257,512]{1,0:T(8,128)(2,1)}, bf16[257,512]{1,0:T(8,128)(2,1)}, u32[]{:S(2)}, u32[]{:S(2)}) %collective-permute-start.4) | collective-permute-done | bytes 263200 | tf_op jit(solution)/shard_map/ppermute | solution.py:17
  49.6 1.4 %fusion.71 = bf16[256,512]{1,0:T(8,128)(2,1)S(1)} fusion(f32[256,512]{1,0:T(8,128)} %copy-done.1, bf16[257,512]{1,0:T(8,128)(2,1)} %copy-done.10, f32[256]{0:T(256)S(1)} %get-tuple-element.67, pred[]{:T(512)S(6)} %ge.60, bf16[257,512]{1,0:T(8,128)(2,1)} %collective-permute-done.4, f32[256]{0:T(256)S(1)} %get-tuple-element.62, pred[]{:T(512)S(6)} %ge.59), kind=kLoop, calls=%fused_computation.177 | loop fusion | flops 1179648 | bytes 1312770 | tf_op jit(solution)/shard_map/convert_element_type | solution.py:119
  51.0 1.3 %collective-permute-start.5 = (bf16[256,512]{1,0:T(8,128)(2,1)S(1)}, bf16[256,512]{1,0:T(8,128)(2,1)S(1)}, u32[]{:S(2)}, u32[]{:S(2)}) collective-permute-start(bf16[256,512]{1,0:T(8,128)(2,1)S(1)} %fusion.71), channel_id=1, source_target_pairs={{0,16},{4,20},{8,24},{12,28},{1,17},{5,21},{9,25},{13,29},{2,18},{... | collective-permute-start | bytes 786440 | tf_op jit(solution)/shard_map/ppermute | solution.py:17
  52.3 0.7 slice_convert_fusion
  53.1 11.8 %collective-permute-done.5 = bf16[256,512]{1,0:T(8,128)(2,1)S(1)} collective-permute-done((bf16[256,512]{1,0:T(8,128)(2,1)S(1)}, bf16[256,512]{1,0:T(8,128)(2,1)S(1)}, u32[]{:S(2)}, u32[]{:S(2)}) %collective-permute-start.5) | collective-permute-done | bytes 262176 | tf_op jit(solution)/shard_map/ppermute | solution.py:17
  64.8 2.1 %multiply_reduce_fusion.3 = (f32[256]{0:T(256)S(1)}, f32[256,512]{1,0:T(8,128)S(1)}) fusion(f32[256,512]{1,0:T(8,128)} %bitcast.166, f32[256,256]{1,0:T(8,128)} %bitcast_multiply_fusion, bf16[256,512]{1,0:T(8,128)(2,1)S(1)} %collective-permute-done.5, f32[256]{0:T(256)S(1)} %bitcast.163, f32[256]{0:T(256)S(1)} %get-tuple-element.92, pred[]{:T(512)S(6)} %ge.59, ...), kind=kOutput, calls=%fused_computation.57 | convolution fusion | flops 202899200 | bytes 2100226 | tf_op jit(solution)/shard_map/dot_general | solution.py:256
  66.9 0.8 multiply_convert_fusion
  67.8 0.5 convolution_convert_fusion.2
  69.8 0.6 copy-done.8
  70.5 0.8 pad_maximum_fusion.5
  71.3 2.2 %collective-permute-done.6 = bf16[2,64,2048]{2,1,0:T(8,128)(2,1)} collective-permute-done((bf16[2,64,2048]{2,1,0:T(8,128)(2,1)}, bf16[2,64,2048]{2,1,0:T(8,128)(2,1)}, u32[]{:S(2)}, u32[]{:S(2)}) %collective-permute-start.6) | collective-permute-done | bytes 524320 | tf_op jit(solution)/shard_map/ppermute | solution.py:190
  73.6 1.3 %fusion.23 = bf16[1,64,2048]{2,1,0:T(8,128)(2,1)S(1)} fusion(pred[]{:T(512)S(6)} %eq.50, bf16[2,64,2048]{2,1,0:T(8,128)(2,1)} %collective-permute-done.6, bf16[64,2048]{1,0:T(8,128)(2,1)S(1)} %convolution_convert_fusion.3, bf16[64,2048]{1,0:T(8,128)(2,1)S(1)} %convolution_convert_fusion.2, pred[]{:T(512)S(6)} %eq.51, bf16[64,2048]{1,0:T(8,128)(2,1)} %copy-done.8, ...), kind=kLoop, calls=%fused_computation.78 | loop fusion | flops 1310720 | bytes 1835010 | tf_op jit(solution)/shard_map/stack | solution.py:189
  74.8 1.6 %collective-permute-start.7 = (bf16[1,64,2048]{2,1,0:T(8,128)(2,1)S(1)}, bf16[1,64,2048]{2,1,0:T(8,128)(2,1)S(1)}, u32[]{:S(2)}, u32[]{:S(2)}) collective-permute-start(bf16[1,64,2048]{2,1,0:T(8,128)(2,1)S(1)} %fusion.23), channel_id=1, source_target_pairs={{0,2},{1,3},{2,0},{3,1},{4,6},{5,7},{6,4},{7,5},{8,10},{9,11},{10,... | collective-permute-start | bytes 786440 | tf_op jit(solution)/shard_map/ppermute | solution.py:190
  76.4 2.4 %fusion.3 = f32[1,1,256,512]{3,2,1,0:T(8,128)} fusion(bf16[256,512]{1,0:T(8,128)(2,1)} %copy-done.15, f32[256]{0:T(256)S(1)} %get-tuple-element.91, pred[]{:T(512)S(6)} %ge.58, f32[256,512]{1,0:T(8,128)S(1)} %copy-done.2, bf16[257,512]{1,0:T(8,128)(2,1)} %copy-done.10, f32[256]{0:T(256)S(1)} %get-tuple-element.67, pred[]{:T(512)S(6)} %ge.60, ...), kind=kLoop, calls=%fused_computation.37 | loop fusion | flops 1572864 | bytes 1838083 | tf_op jit(solution)/shard_map/broadcast_in_dim | solution.py:265
  78.8 4.5 %collective-permute-done.7 = bf16[1,64,2048]{2,1,0:T(8,128)(2,1)S(1)} collective-permute-done((bf16[1,64,2048]{2,1,0:T(8,128)(2,1)S(1)}, bf16[1,64,2048]{2,1,0:T(8,128)(2,1)S(1)}, u32[]{:S(2)}, u32[]{:S(2)}) %collective-permute-start.7) | collective-permute-done | bytes 262176 | tf_op jit(solution)/shard_map/ppermute | solution.py:190
  83.3 2.0 %fusion.5 = bf16[64,2048]{1,0:T(8,128)(2,1)} fusion(bf16[1,64,2048]{2,1,0:T(8,128)(2,1)S(1)} %collective-permute-done.7, pred[]{:T(512)S(6)} %eq.50, bf16[2,64,2048]{2,1,0:T(8,128)(2,1)} %collective-permute-done.6, bf16[64,2048]{1,0:T(8,128)(2,1)S(1)} %convolution_convert_fusion.3, bf16[64,2048]{1,0:T(8,128)(2,1)S(1)} %convolution_convert_fusion.2, ...), kind=kLoop, calls=%fused_computation.43 | loop fusion | flops 1572864 | bytes 2097154 | tf_op jit(solution)/shard_map/convert_element_type | solution.py:196
  (85 shorter events, 5.4 us)
Async XLA Ops:
  0.6 67.1 %copy-start = (bf16[512,2048]{1,0:T(8,128)(2,1)S(1)}, bf16[512,2048]{1,0:T(8,128)(2,1)}, u32[]{:S(2)}) copy-start(bf16[512,2048]{1,0:T(8,128)(2,1)} %param.31) | copy-start | bytes 6291460
  0.6 11.3 %copy-start.3 = (bf16[64,2048]{1,0:T(8,128)(2,1)S(1)}, bf16[64,2048]{1,0:T(8,128)(2,1)}, u32[]{:S(2)}) copy-start(bf16[64,2048]{1,0:T(8,128)(2,1)} %param.18) | copy-start | bytes 786436
  0.7 8.3 %collective-permute-start = (bf16[64,2048]{1,0:T(8,128)(2,1)}, bf16[64,2048]{1,0:T(8,128)(2,1)S(1)}, u32[]{:S(2)}, u32[]{:S(2)}) collective-permute-start(bf16[64,2048]{1,0:T(8,128)(2,1)} %param.18), channel_id=1, source_target_pairs={{0,2},{1,3},{2,0},{3,1},{4,6},{5,7},{6,4},{7,5},{8,10},{9,11},{10,... | collective-permute-start | bytes 786440 | tf_op jit(solution)/shard_map/ppermute | solution.py:150
  10.0 2.0 %collective-permute-start.1 = (bf16[128,2048]{1,0:T(8,128)(2,1)S(1)}, bf16[128,2048]{1,0:T(8,128)(2,1)S(1)}, u32[]{:S(2)}, u32[]{:S(2)}) collective-permute-start(bf16[128,2048]{1,0:T(8,128)(2,1)S(1)} %pad_maximum_fusion.4), channel_id=1, source_target_pairs={{0,1},{1,0},{2,3},{3,2},{4,5},{5,4},{6,7},{7,6},{8,9},{9,8},{10,11... | collective-permute-start | bytes 1572872 | tf_op jit(solution)/shard_map/ppermute | solution.py:150
  12.0 1.8 %copy-start.19 = (bf16[2048,16]{0,1:T(8,128)(2,1)S(1)}, bf16[2048,16]{0,1:T(8,128)(2,1)}, u32[]{:S(2)}) copy-start(bf16[2048,16]{0,1:T(8,128)(2,1)} %param.26) | copy-start | bytes 196612
  12.0 1.8 %copy-start.20 = (bf16[16,256]{1,0:T(8,128)(2,1)S(1)}, bf16[16,256]{1,0:T(8,128)(2,1)}, u32[]{:S(2)}) copy-start(bf16[16,256]{1,0:T(8,128)(2,1)} %param.27) | copy-start | bytes 24580
  12.0 1.8 %copy-start.22 = (f32[256]{0:T(256)S(1)}, f32[256]{0:T(256)}, u32[]{:S(2)}) copy-start(f32[256]{0:T(256)} %param.28) | copy-start | bytes 3076
  12.1 0.7 copy-start.4
  16.5 2.7 %copy-start.11 = (f32[4,64,256]{2,1,0:T(8,128)}, f32[4,64,256]{2,1,0:T(8,128)S(1)}, u32[]{:S(2)}) copy-start(f32[4,64,256]{2,1,0:T(8,128)S(1)} %reduce_window_sum.23) | copy-start | bytes 786436
  16.5 2.0 %copy-start.17 = (bf16[2048,512]{1,0:T(8,128)(2,1)S(1)}, bf16[2048,512]{1,0:T(8,128)(2,1)}, u32[]{:S(2)}) copy-start(bf16[2048,512]{1,0:T(8,128)(2,1)} %param.22) | copy-start | bytes 6291460
  18.6 1.2 %copy-start.13 = (bf16[2048,256]{1,0:T(8,128)(2,1)S(1)}, bf16[2048,256]{1,0:T(8,128)(2,1)}, u32[]{:S(2)}) copy-start(bf16[2048,256]{1,0:T(8,128)(2,1)} %param.21) | copy-start | bytes 3145732
  20.2 7.8 %copy-start.12 = (f32[4,64,256]{2,1,0:T(8,128)S(1)}, f32[4,64,256]{2,1,0:T(8,128)}, u32[]{:S(2)}) copy-start(f32[4,64,256]{2,1,0:T(8,128)} %copy-done.11) | copy-start | bytes 786436
  20.9 6.4 %collective-permute-start.2 = (bf16[3,1024]{1,0:T(4,128)(2,1)S(1)}, bf16[3,1024]{1,0:T(4,128)(2,1)S(1)}, u32[]{:S(2)}, u32[]{:S(2)}) collective-permute-start(bf16[3,1024]{1,0:T(4,128)(2,1)S(1)} %get-tuple-element.59), channel_id=1, source_target_pairs={{0,4},{4,8},{8,12},{12,16},{16,20},{20,24},{24,28},{1,5},{5,9},{9,... | collective-permute-start | bytes 18440 | tf_op jit(solution)/shard_map/ppermute | solution.py:17
  28.0 1.1 %copy-start.16 = (f32[256,256]{1,0:T(8,128)}, f32[256,256]{1,0:T(8,128)S(1)}, u32[]{:S(2)}) copy-start(f32[256,256]{1,0:T(8,128)S(1)} %get-tuple-element.57) | copy-start | bytes 786436
  28.5 0.9 %copy-start.14 = (f32[256,512]{1,0:T(8,128)}, f32[256,512]{1,0:T(8,128)S(1)}, u32[]{:S(2)}) copy-start(f32[256,512]{1,0:T(8,128)S(1)} %multiply_reduce_fusion) | copy-start | bytes 1572868
  29.4 10.8 %copy-start.1 = (f32[256,512]{1,0:T(8,128)}, f32[256,512]{1,0:T(8,128)S(1)}, u32[]{:S(2)}) copy-start(f32[256,512]{1,0:T(8,128)S(1)} %get-tuple-element.64) | copy-start | bytes 1572868
  29.8 10.2 %collective-permute-start.3 = (bf16[257,512]{1,0:T(8,128)(2,1)S(1)}, bf16[257,512]{1,0:T(8,128)(2,1)S(1)}, u32[]{:S(2)}, u32[]{:S(2)}) collective-permute-start(bf16[257,512]{1,0:T(8,128)(2,1)S(1)} %pad_maximum_fusion.6), channel_id=1, source_target_pairs={{0,4},{4,8},{8,12},{12,16},{16,20},{20,24},{24,28},{1,5},{5,9},{9,... | collective-permute-start | bytes 789512 | tf_op jit(solution)/shard_map/ppermute | solution.py:17
  40.0 0.9 %copy-start.10 = (bf16[257,512]{1,0:T(8,128)(2,1)}, bf16[257,512]{1,0:T(8,128)(2,1)S(1)}, u32[]{:S(2)}) copy-start(bf16[257,512]{1,0:T(8,128)(2,1)S(1)} %collective-permute-done.3) | copy-start | bytes 789508
  40.9 8.7 %collective-permute-start.4 = (bf16[257,512]{1,0:T(8,128)(2,1)}, bf16[257,512]{1,0:T(8,128)(2,1)}, u32[]{:S(2)}, u32[]{:S(2)}) collective-permute-start(bf16[257,512]{1,0:T(8,128)(2,1)} %pad_maximum_fusion.7), channel_id=1, source_target_pairs={{0,8},{4,12},{8,16},{12,20},{16,24},{20,28},{1,9},{5,13},{9,17},{1... | collective-permute-start | bytes 789512 | tf_op jit(solution)/shard_map/ppermute | solution.py:17
  44.9 22.0 %copy-start.18 = (bf16[2048,512]{1,0:T(8,128)(2,1)S(1)}, bf16[2048,512]{1,0:T(8,128)(2,1)}, u32[]{:S(2)}) copy-start(bf16[2048,512]{1,0:T(8,128)(2,1)} %param.29) | copy-start | bytes 6291460
  44.9 22.0 %copy-start.21 = (f32[512]{0:T(512)S(1)}, f32[512]{0:T(512)}, u32[]{:S(2)}) copy-start(f32[512]{0:T(512)} %param.30) | copy-start | bytes 6148
  51.0 13.8 %collective-permute-start.5 = (bf16[256,512]{1,0:T(8,128)(2,1)S(1)}, bf16[256,512]{1,0:T(8,128)(2,1)S(1)}, u32[]{:S(2)}, u32[]{:S(2)}) collective-permute-start(bf16[256,512]{1,0:T(8,128)(2,1)S(1)} %fusion.71), channel_id=1, source_target_pairs={{0,16},{4,20},{8,24},{12,28},{1,17},{5,21},{9,25},{13,29},{2,18},{... | collective-permute-start | bytes 786440 | tf_op jit(solution)/shard_map/ppermute | solution.py:17
  64.8 2.1 %copy-start.15 = (bf16[256,512]{1,0:T(8,128)(2,1)}, bf16[256,512]{1,0:T(8,128)(2,1)S(1)}, u32[]{:S(2)}) copy-start(bf16[256,512]{1,0:T(8,128)(2,1)S(1)} %collective-permute-done.5) | copy-start | bytes 786436
  69.7 0.7 copy-start.8
  69.7 6.7 %copy-start.2 = (f32[256,512]{1,0:T(8,128)S(1)}, f32[256,512]{1,0:T(8,128)}, u32[]{:S(2)}) copy-start(f32[256,512]{1,0:T(8,128)} %copy-done.1) | copy-start | bytes 1572868
  71.3 2.3 %collective-permute-start.6 = (bf16[2,64,2048]{2,1,0:T(8,128)(2,1)}, bf16[2,64,2048]{2,1,0:T(8,128)(2,1)}, u32[]{:S(2)}, u32[]{:S(2)}) collective-permute-start(bf16[2,64,2048]{2,1,0:T(8,128)(2,1)} %pad_maximum_fusion.5), channel_id=1, source_target_pairs={{0,1},{1,0},{2,3},{3,2},{4,5},{5,4},{6,7},{7,6},{8,9},{9,8},{10,11... | collective-permute-start | bytes 1572872 | tf_op jit(solution)/shard_map/ppermute | solution.py:190
  71.3 12.0 %copy-start.9 = (bf16[64,2048]{1,0:T(8,128)(2,1)S(1)}, bf16[64,2048]{1,0:T(8,128)(2,1)}, u32[]{:S(2)}) copy-start(bf16[64,2048]{1,0:T(8,128)(2,1)} %copy-done.8) | copy-start | bytes 786436
  74.8 8.5 %collective-permute-start.7 = (bf16[1,64,2048]{2,1,0:T(8,128)(2,1)S(1)}, bf16[1,64,2048]{2,1,0:T(8,128)(2,1)S(1)}, u32[]{:S(2)}, u32[]{:S(2)}) collective-permute-start(bf16[1,64,2048]{2,1,0:T(8,128)(2,1)S(1)} %fusion.23), channel_id=1, source_target_pairs={{0,2},{1,3},{2,0},{3,1},{4,6},{5,7},{6,4},{7,5},{8,10},{9,11},{10,... | collective-permute-start | bytes 786440 | tf_op jit(solution)/shard_map/ppermute | solution.py:190

commit v9 on v8

--- a/solution.py
+++ b/solution.py
@@ -180,8 +180,17 @@
             outgoing = lax.dynamic_index_in_dim(chunks, (place + step) % count, 0, False)
             total = total + lax.ppermute(outgoing, axis, pairs).astype(jnp.float32)
         return total.astype(jnp.bfloat16)
-    held = [term(index) for index in range(count)]
-    mask = 1
+    held = [lax.slice_in_dim(gated, index * chunk, (index + 1) * chunk, axis=0) for index in range(count)]
+    odd = place % 2 == 1
+    pairs = list(zip(held[0::2], held[1::2]))
+    outgoing = jnp.concatenate([jnp.where(odd, low, high) for low, high in pairs])
+    outgoing = jnp.dot(outgoing, weight, preferred_element_type=jnp.float32).astype(jnp.bfloat16)
+    incoming = lax.ppermute(outgoing, axis, [(source, source ^ 1) for source in range(count)])
+    kept = jnp.concatenate([jnp.where(odd, high, low) for low, high in pairs])
+    kept = jnp.dot(kept, weight, preferred_element_type=jnp.float32).astype(jnp.bfloat16)
+    summed = kept.astype(jnp.float32) + incoming.astype(jnp.float32)
+    held = list(jnp.split(summed, len(pairs)))
+    mask = 2
     while mask < count:
         odd = (place // mask) % 2 == 1
         pairs = list(zip(held[0::2], held[1::2]))
@@ -234,15 +243,16 @@
     rim_rows = query_conv.shape[0] - 1
     joined = jnp.concatenate([raw_query, raw_key, raw_value], axis=1)
     before_rows = shifted(joined[row_count - rim_rows :], "tok", 1)
-    conv_query = short_conv(
-        raw_query, before_rows[:, :key_width], query_conv, positions, prompt_first
-    )
-    conv_key = short_conv(
-        raw_key, before_rows[:, key_width : 2 * key_width], key_conv, positions, prompt_first
-    )
-    conv_value = short_conv(
-        raw_value, before_rows[:, 2 * key_width :], value_conv, positions, prompt_first
-    )
+    conv_all = short_conv(
+        joined,
+        before_rows,
+        jnp.concatenate([query_conv, key_conv, value_conv], axis=1),
+        positions,
+        prompt_first,
+    )
+    conv_query = conv_all[:, :key_width]
+    conv_key = conv_all[:, key_width : 2 * key_width]
+    conv_value = conv_all[:, 2 * key_width :]
     decays = (
         jax.nn.log_sigmoid(
             jnp.dot(low_rank, decay_up, preferred_element_type=jnp.float32) + decay_bias

time: 86 us -> 91.1 us (1.059)
  matrix products: 15.1 us -> 17.7 us
  other arithmetic: 20.4 us -> 22.7 us
  local copies, waits for them, and re-layouts: 3.81 us -> 5.85 us
  waiting for transfers between devices: 33.2 us -> 31.2 us
    dot_general x4, matrix products: 3.77 us -> 7.28 us  [project(): jnp.dot(gathered, weight, preferred_element_type=jnp.float32)]
    concatenate x0 -> x2, other arithmetic: none -> 2.17 us  [the longest x1 1.11 us: short_conv(): extended = jnp.concatenate([before_rows, raw_rows], axis=0)]
    another operation x4 -> x1, other arithmetic: 2.15 us -> 0.05 us  [scatter_sum(): jnp.stack([jnp.where(odd, low, high).astype(jnp.bfloat16) for low, high i...]
    ppermute x2 -> x1, waiting for transfers between devices: 6.72 us -> 4.63 us  [scatter_sum(): lax.ppermute(outgoing, axis, [(source, source ^ mask) for source in range...]
    ppermute x2, waiting for transfers between devices: 2.33 us -> 0.44 us  [gather_rows(): lax.ppermute(jnp.concatenate(received), axis, [(source, source ^ mask) fo...]
    ppermute x0 -> x1, waiting for transfers between devices: none -> 1.87 us  [scatter_sum(): lax.ppermute(outgoing, axis, [(source, source ^ 1) for source in range(co...]
    convert_element_type x3 -> x1, other arithmetic: 2.06 us -> 0.72 us  [short_conv(): weight.astype(jnp.float32)[:, None, :] * windows.astype(jnp.float32)]
    convert_element_type x1, other arithmetic: 2.02 us -> 0.8 us  [scatter_sum(): return held[0].astype(jnp.bfloat16)]
  transfers between devices with their start and end apart: 8 -> 8, of which waited for: 8 -> 7; matrix products, arithmetic and copies ran while one was open for 18% -> 20% of each run, Pallas kernels for 0% -> 0%
where the time goes in v9:
time: 91.1 us; the launch traced here: 90.4 us
  waiting for transfers between devices  31.2 us (34%)
  other arithmetic  22.7 us (25%)
  matrix products  17.7 us (19%)
  starting transfers between devices  11.7 us (13%)
  local copies, waits for them, and re-layouts  5.85 us (6%)
  between operations  1.16 us (1%)
    ppermute x4, waiting for transfers between devices, shifted(): lax.ppermute(value, axis, [(source, source + steps) for source in range(i...  24.3 us
    ppermute x4, starting transfers between devices, shifted(): lax.ppermute(value, axis, [(source, source + steps) for source in range(i...  8.47 us
    dot_general x4, matrix products, project(): jnp.dot(gathered, weight, preferred_element_type=jnp.float32)  7.28 us
    ppermute x1, waiting for transfers between devices, scatter_sum(): lax.ppermute(outgoing, axis, [(source, source ^ mask) for source in range...  4.63 us
    dot_general x3, matrix products, segment_parts(): jnp.dot(lifted_intact[block], memory, precision=HIGH_PRECISION)  3.11 us
    dot_general x1, matrix products, segment_parts(): jnp.einsum('bac,bcv->bav', scores, head_values, preferred_element_type=jn...  2.31 us
    broadcast_in_dim x1, other arithmetic, shards(): segment_states = closing[None, None]  2.23 us
    dot_general x1, matrix products, shards(): jnp.dot(carry_lift.reshape((row_count, key_width)), entering, precision=H...  1.97 us
  transfers between devices with their start and end apart: 8, of which 7 were waited for; matrix products, arithmetic and copies ran while one was open for 20% of the time, Pallas kernels for 0%

profile of v9, /device:TPU:24, one launch (start us, length us, event | category | flops | bytes accessed | tf_op | source)
XLA Modules:
  0.0 90.4 jit_solution(7287313786611265217)
XLA Ops:
  0.7 1.6 %collective-permute-start = (bf16[64,2048]{1,0:T(8,128)(2,1)}, bf16[64,2048]{1,0:T(8,128)(2,1)S(1)}, u32[]{:S(2)}, u32[]{:S(2)}) collective-permute-start(bf16[64,2048]{1,0:T(8,128)(2,1)} %param.18), channel_id=1, source_target_pairs={{0,2},{1,3},{2,0},{3,1},{4,6},{5,7},{6,4},{7,5},{8,10},{9,11},{10,... | collective-permute-start | bytes 786440 | tf_op jit(solution)/shard_map/ppermute | solution.py:150
  2.2 0.8 select_reduce_fusion.1
  3.6 0.7 compare_convert_fusion.1
  4.3 0.7 slice_reduce_fusion.1
  5.5 0.7 reshape.253
  7.8 0.7 maximum_convert_fusion
  9.0 1.0 %pad_maximum_fusion.4 = bf16[128,2048]{1,0:T(8,128)(2,1)S(1)} fusion(bf16[64,2048]{1,0:T(8,128)(2,1)S(1)} %collective-permute-done, bf16[64,2048]{1,0:T(8,128)(2,1)} %param.18), kind=kLoop, calls=%fused_computation.43 | loop fusion | flops 1048576 | bytes 1048576 | tf_op jit(solution)/shard_map/concatenate | solution.py:151
  10.1 1.3 %slice_compare_fusion = pred[3]{0:T(512)(128)(4,1)} fusion(s32[256]{0:T(256)S(1)} %iota_add_fusion, s32[]{:T(128)} %bitcast.34), kind=kLoop, calls=%fused_computation.144 | loop fusion | flops 3 | bytes 19 | tf_op jit(solution)/shard_map/ge | solution.py:276
  11.4 0.7 fusion.58
  12.1 1.8 %conditional.1 = (bf16[256,2048]{1,0:T(8,128)(2,1)S(1)}) conditional(s32[]{:T(128)} %clamp.3, (bf16[64,2048]{1,0:T(8,128)(2,1)S(1)}, bf16[64,2048]{1,0:T(8,128)(2,1)S(1)}, bf16[64,2048]{1,0:T(8,128)(2,1)S(1)}, bf16[64,2048]{1,0:T(8,128)(2,1)S(1)}) %tuple.53, (bf16[64,2048]{1,0:T(8,128)(2,1)S(1)}, ...), branch_computations={%region_3.0_spmd, %region_4.5_spmd, %region_5.6_spmd, %region_6.7_... | conditional | flops 4194304 | bytes 3145764 | solution.py:164
  12.1 0.7 copy-done.4
  12.8 1.0 %pad_maximum_fusion = bf16[256,2048]{1,0:T(8,128)(2,1)S(1)} fusion(bf16[64,2048]{1,0:T(8,128)(2,1)S(1)} %get-tuple-element.40, bf16[64,2048]{1,0:T(8,128)(2,1)} %copy-done.4, bf16[64,2048]{1,0:T(8,128)(2,1)S(1)} %get-tuple-element.33, bf16[64,2048]{1,0:T(8,128)(2,1)S(1)} %get-tuple-element.32), kind=kLoop, calls=%fused_computation | loop fusion | flops 4194304 | bytes 2097152 | tf_op jit(solution)/shard_map/cond/branch_0_fun/concatenate | solution.py:162
  13.9 1.7 %convolution_convert_fusion.4 = bf16[256,256]{0,1:T(8,128)(2,1)S(1)} fusion(bf16[256,2048]{1,0:T(8,128)(2,1)S(1)} %get-tuple-element.94, bf16[2048,256]{1,0:T(8,128)(2,1)} %param.21), kind=kOutput, calls=%fused_computation.15 | convolution fusion | flops 268500992 | bytes 2228224 | tf_op jit(solution)/shard_map/dot_general | solution.py:227
  15.7 1.7 %convolution_convert_fusion.5 = bf16[256,256]{0,1:T(8,128)(2,1)S(1)} fusion(bf16[256,2048]{1,0:T(8,128)(2,1)S(1)} %get-tuple-element.94, bf16[2048,256]{1,0:T(8,128)(2,1)} %param.20), kind=kOutput, calls=%fused_computation.16 | convolution fusion | flops 268500992 | bytes 2228224 | tf_op jit(solution)/shard_map/dot_general | solution.py:227
  17.5 0.8 copy.21
  18.3 3.0 %convolution_convert_fusion.3 = bf16[256,512]{1,0:T(8,128)(2,1)} fusion(bf16[256,2048]{1,0:T(8,128)(2,1)S(1)} %get-tuple-element.94, bf16[2048,512]{1,0:T(8,128)(2,1)} %param.22), kind=kOutput, calls=%fused_computation.11 | convolution fusion | flops 537001984 | bytes 3407872 | tf_op jit(solution)/shard_map/dot_general | solution.py:227
  21.3 1.5 %fusion.22 = f32[256,256]{1,0:T(8,128)} fusion(bf16[16,256]{1,0:T(8,128)(2,1)S(1)} %copy-done.26, bf16[256,2048]{1,0:T(8,128)(2,1)S(1)} %get-tuple-element.94, bf16[2048,16]{0,1:T(8,128)(2,1)S(1)} %copy-done.25, f32[256]{0:T(256)S(1)} %copy-done.28), kind=kOutput, calls=%fused_computation.74 | convolution fusion | flops 19533824 | bytes 1385472 | tf_op jit(solution)/shard_map/dot_general | solution.py:258
  22.8 1.2 %reduce_window_sum.23 = f32[4,64,256]{2,1,0:T(8,128)S(1)} reduce-window(f32[4,64,256]{2,1,0:T(8,128)} %bitcast.118, f32[]{:T(128)} %constant.71.clone.1), window={size=1x64x1 pad=0_0x63_0x0_0}, to_apply=%region_8.9 | reduce-window | flops 4128768 | bytes 524292 | tf_op jit(solution)/shard_map/jit(cumsum)/reduce_window_sum | solution.py:49
  24.0 0.6 exponential_multiply_fusion
  24.6 1.1 %pad_maximum_fusion.5 = (bf16[256,1024]{1,0:T(8,128)(2,1)S(1)}, bf16[1,256,1024]{2,1,0:T(8,128)(2,1)S(1)}) fusion(bf16[256,512]{1,0:T(8,128)(2,1)} %convolution_convert_fusion.3, bf16[256,256]{1,0:T(8,128)(2,1)S(1)} %copy.22, bf16[256,256]{1,0:T(8,128)(2,1)} %copy.21), kind=kLoop, calls=%fused_computation.44 | loop fusion | flops 1572864 | bytes 1572864 | tf_op jit(solution)/shard_map/concatenate | solution.py:244
  25.7 1.3 %select_bitcast_fusion = (bf16[1,3,1,1024]{3,1,2,0:T(4,128)(2,1)}, bf16[3,1024]{1,0:T(4,128)(2,1)S(1)}) fusion(pred[3]{0:T(512)(128)(4,1)} %slice_compare_fusion, bf16[256,1024]{1,0:T(8,128)(2,1)S(1)} %get-tuple-element.73), kind=kLoop, calls=%fused_computation.115 | loop fusion | flops 3072 | bytes 18435 | tf_op jit(solution)/shard_map/reshape | solution.py:279
  27.0 3.4 %collective-permute-start.2 = (bf16[3,1024]{1,0:T(4,128)(2,1)S(1)}, bf16[3,1024]{1,0:T(4,128)(2,1)S(1)}, u32[]{:S(2)}, u32[]{:S(2)}) collective-permute-start(bf16[3,1024]{1,0:T(4,128)(2,1)S(1)} %get-tuple-element.70), channel_id=1, source_target_pairs={{0,4},{4,8},{8,12},{12,16},{16,20},{20,24},{24,28},{1,5},{5,9},{9,... | collective-permute-start | bytes 18440 | tf_op jit(solution)/shard_map/ppermute | solution.py:17
  30.4 0.7 pad_maximum_fusion.8
  31.2 2.3 %collective-permute-done.2 = bf16[3,1024]{1,0:T(4,128)(2,1)S(1)} collective-permute-done((bf16[3,1024]{1,0:T(4,128)(2,1)S(1)}, bf16[3,1024]{1,0:T(4,128)(2,1)S(1)}, u32[]{:S(2)}, u32[]{:S(2)}) %collective-permute-start.2) | collective-permute-done | bytes 6176 | tf_op jit(solution)/shard_map/ppermute | solution.py:17
  33.5 1.1 %maximum_maximum_fusion = bf16[259,1024]{1,0:T(8,128)(2,1)S(1)} fusion(bf16[256,512]{1,0:T(8,128)(2,1)} %convolution_convert_fusion.3, bf16[256,256]{1,0:T(8,128)(2,1)S(1)} %copy.22, bf16[256,256]{1,0:T(8,128)(2,1)} %copy.21, bf16[3,1024]{1,0:T(4,128)(2,1)S(1)} %collective-permute-done.2), kind=kLoop, calls=%fused_computation.36 | loop fusion | flops 2121728 | bytes 1060864 | tf_op jit(solution)/shard_map/concatenate | solution.py:29
  34.9 0.7 multiply_reduce_fusion
  37.6 1.0 %convolution_bitcast_fusion.1 = f32[1,64,512]{2,1,0:T(8,128)} fusion(f32[4,64,256]{2,1,0:T(8,128)S(1)} %get-tuple-element.82, f32[4,256,512]{2,1,0:T(8,128)S(1)} %fusion.32, f32[256]{0:T(256)S(1)} %bitcast.121, f32[256]{0:T(256)S(1)} %get-tuple-element.91), kind=kOutput, calls=%fused_computation.18 | convolution fusion | flops 50724864 | bytes 1247232 | tf_op jit(solution)/shard_map/dot_general | solution.py:80
  38.7 2.5 %collective-permute-start.3 = (bf16[257,512]{1,0:T(8,128)(2,1)S(1)}, bf16[257,512]{1,0:T(8,128)(2,1)S(1)}, u32[]{:S(2)}, u32[]{:S(2)}) collective-permute-start(bf16[257,512]{1,0:T(8,128)(2,1)S(1)} %pad_maximum_fusion.6), channel_id=1, source_target_pairs={{0,4},{4,8},{8,12},{12,16},{16,20},{20,24},{24,28},{1,5},{5,9},{9,... | collective-permute-start | bytes 789512 | tf_op jit(solution)/shard_map/ppermute | solution.py:17
  41.2 0.8 bitcast_multiply_fusion
  42.1 1.0 %convolution_bitcast_fusion.2 = f32[1,64,512]{2,1,0:T(8,128)} fusion(f32[4,256,512]{2,1,0:T(8,128)S(1)} %fusion.32, f32[256]{0:T(256)S(1)} %get-tuple-element.91, f32[4,64,256]{2,1,0:T(8,128)S(1)} %get-tuple-element.82), kind=kOutput, calls=%fused_computation.19 | convolution fusion | flops 50462720 | bytes 721920 | tf_op jit(solution)/shard_map/dot_general | solution.py:80
  43.1 1.1 %convolution_bitcast_fusion = f32[1,64,512]{2,1,0:T(8,128)} fusion(f32[4,256,512]{2,1,0:T(8,128)S(1)} %fusion.32, f32[256]{0:T(256)S(1)} %bitcast.126, f32[4,64,256]{2,1,0:T(8,128)S(1)} %get-tuple-element.82, f32[256]{0:T(256)S(1)} %bitcast.122, f32[256]{0:T(256)S(1)} %get-tuple-element.91), kind=kOutput, calls=%fused_computation.17 | convolution fusion | flops 50987008 | bytes 1772544 | tf_op jit(solution)/shard_map/dot_general | solution.py:80
  44.1 5.1 %collective-permute-done.3 = bf16[257,512]{1,0:T(8,128)(2,1)S(1)} collective-permute-done((bf16[257,512]{1,0:T(8,128)(2,1)S(1)}, bf16[257,512]{1,0:T(8,128)(2,1)S(1)}, u32[]{:S(2)}, u32[]{:S(2)}) %collective-permute-start.3) | collective-permute-done | bytes 263200 | tf_op jit(solution)/shard_map/ppermute | solution.py:17
  50.0 0.7 pad_maximum_fusion.7
  50.8 1.3 %collective-permute-start.4 = (bf16[257,512]{1,0:T(8,128)(2,1)}, bf16[257,512]{1,0:T(8,128)(2,1)}, u32[]{:S(2)}, u32[]{:S(2)}) collective-permute-start(bf16[257,512]{1,0:T(8,128)(2,1)} %pad_maximum_fusion.7), channel_id=1, source_target_pairs={{0,8},{4,12},{8,16},{12,20},{16,24},{20,28},{1,9},{5,13},{9,17},{1... | collective-permute-start | bytes 789512 | tf_op jit(solution)/shard_map/ppermute | solution.py:17
  52.1 2.3 %convolution_add_fusion = f32[4,64,512]{2,1,0:T(8,128)} fusion(bf16[4,64,512]{2,1,0:T(8,128)(2,1)} %bitcast.112, f32[1,64,512]{2,1,0:T(8,128)} %convolution_bitcast_fusion, f32[1,64,512]{2,1,0:T(8,128)} %convolution_bitcast_fusion.1, f32[1,64,512]{2,1,0:T(8,128)} %convolution_bitcast_fusion.2, f32[4]{0:T(128)} %pad.32.clone, ...), kind=kOutput, calls=%fused_computation.8 | convolution fusion | flops 26148864 | bytes 1840144 | tf_op jit(solution)/shard_map/bac,bcv->bav/dot_general | solution.py:71
  54.4 5.4 %collective-permute-done.4 = bf16[257,512]{1,0:T(8,128)(2,1)} collective-permute-done((bf16[257,512]{1,0:T(8,128)(2,1)}, bf16[257,512]{1,0:T(8,128)(2,1)}, u32[]{:S(2)}, u32[]{:S(2)}) %collective-permute-start.4) | collective-permute-done | bytes 263200 | tf_op jit(solution)/shard_map/ppermute | solution.py:17
  59.8 1.4 %fusion.63 = bf16[256,512]{1,0:T(8,128)(2,1)S(1)} fusion(f32[256,512]{1,0:T(8,128)} %copy-done.1, bf16[257,512]{1,0:T(8,128)(2,1)} %copy-done.10, f32[256]{0:T(256)S(1)} %copy-done.18, pred[]{:T(512)S(6)} %ge.52, bf16[257,512]{1,0:T(8,128)(2,1)} %collective-permute-done.4, f32[256]{0:T(256)} %get-tuple-element.58, pred[]{:T(512)S(6)} %ge.51), kind=kLoop, calls=%fused_computation.152 | loop fusion | flops 1179648 | bytes 1312770 | tf_op jit(solution)/shard_map/convert_element_type | solution.py:119
  61.3 1.3 %collective-permute-start.5 = (bf16[256,512]{1,0:T(8,128)(2,1)S(1)}, bf16[256,512]{1,0:T(8,128)(2,1)S(1)}, u32[]{:S(2)}, u32[]{:S(2)}) collective-permute-start(bf16[256,512]{1,0:T(8,128)(2,1)S(1)} %fusion.63), channel_id=1, source_target_pairs={{0,16},{4,20},{8,24},{12,28},{1,17},{5,21},{9,25},{13,29},{2,18},{... | collective-permute-start | bytes 786440 | tf_op jit(solution)/shard_map/ppermute | solution.py:17
  62.6 0.7 slice_convert_fusion.1
  63.3 0.7 multiply_select_fusion
  63.9 11.5 %collective-permute-done.5 = bf16[256,512]{1,0:T(8,128)(2,1)S(1)} collective-permute-done((bf16[256,512]{1,0:T(8,128)(2,1)S(1)}, bf16[256,512]{1,0:T(8,128)(2,1)S(1)}, u32[]{:S(2)}, u32[]{:S(2)}) %collective-permute-start.5) | collective-permute-done | bytes 262176 | tf_op jit(solution)/shard_map/ppermute | solution.py:17
  75.4 2.0 %multiply_reduce_fusion.1 = (f32[256]{0:T(256)S(1)}, f32[256,512]{1,0:T(8,128)S(1)}) fusion(f32[256,512]{1,0:T(8,128)} %bitcast.117, f32[256,256]{1,0:T(8,128)} %bitcast_multiply_fusion, bf16[256,512]{1,0:T(8,128)(2,1)S(1)} %collective-permute-done.5, f32[256]{0:T(256)} %bitcast.132, f32[256]{0:T(256)S(1)} %get-tuple-element.90, pred[]{:T(512)S(6)} %ge.51, ...), kind=kOutput, calls=%fused_computation.58 | convolution fusion | flops 202899200 | bytes 2100226 | tf_op jit(solution)/shard_map/dot_general | solution.py:266
  77.4 0.8 multiply_convert_fusion.1
  78.8 1.9 %collective-permute-done.6 = bf16[128,2048]{1,0:T(8,128)(2,1)S(1)} collective-permute-done((bf16[128,2048]{1,0:T(8,128)(2,1)S(1)}, bf16[128,2048]{1,0:T(8,128)(2,1)S(1)}, u32[]{:S(2)}, u32[]{:S(2)}) %collective-permute-start.6) | collective-permute-done | bytes 524320 | tf_op jit(solution)/shard_map/ppermute | solution.py:188
  81.2 1.5 %collective-permute-start.7 = (bf16[1,64,2048]{2,1,0:T(8,128)(2,1)S(1)}, bf16[1,64,2048]{2,1,0:T(8,128)(2,1)S(1)}, u32[]{:S(2)}, u32[]{:S(2)}) collective-permute-start(bf16[1,64,2048]{2,1,0:T(8,128)(2,1)S(1)} %fusion.20), channel_id=1, source_target_pairs={{0,2},{1,3},{2,0},{3,1},{4,6},{5,7},{6,4},{7,5},{8,10},{9,11},{10,... | collective-permute-start | bytes 786440 | tf_op jit(solution)/shard_map/ppermute | solution.py:199
  82.7 2.2 %fusion.4 = f32[1,1,256,512]{3,2,1,0:T(8,128)} fusion(bf16[256,512]{1,0:T(8,128)(2,1)S(1)} %collective-permute-done.5, f32[256]{0:T(256)S(1)} %get-tuple-element.89, pred[]{:T(512)S(6)} %ge.50, f32[256,512]{1,0:T(8,128)S(1)} %copy-done.2, bf16[257,512]{1,0:T(8,128)(2,1)S(1)} %copy-done.11, f32[256]{0:T(256)S(1)} %copy-done.18, pred[]{:T(512)S(6)} %ge.52, ...), kind=kLoop, calls=%fused_computation.37 | loop fusion | flops 1572864 | bytes 1838083 | tf_op jit(solution)/shard_map/broadcast_in_dim | solution.py:275
  85.0 4.6 %collective-permute-done.7 = bf16[1,64,2048]{2,1,0:T(8,128)(2,1)S(1)} collective-permute-done((bf16[1,64,2048]{2,1,0:T(8,128)(2,1)S(1)}, bf16[1,64,2048]{2,1,0:T(8,128)(2,1)S(1)}, u32[]{:S(2)}, u32[]{:S(2)}) %collective-permute-start.7) | collective-permute-done | bytes 262176 | tf_op jit(solution)/shard_map/ppermute | solution.py:199
  89.6 0.8 fusion.6
  (94 shorter events, 7.6 us)
Async XLA Ops:
  0.6 77.6 %copy-start = (bf16[512,2048]{1,0:T(8,128)(2,1)S(1)}, bf16[512,2048]{1,0:T(8,128)(2,1)}, u32[]{:S(2)}) copy-start(bf16[512,2048]{1,0:T(8,128)(2,1)} %param.31) | copy-start | bytes 6291460
  0.6 11.4 %copy-start.3 = (bf16[64,2048]{1,0:T(8,128)(2,1)S(1)}, bf16[64,2048]{1,0:T(8,128)(2,1)}, u32[]{:S(2)}) copy-start(bf16[64,2048]{1,0:T(8,128)(2,1)} %param.18) | copy-start | bytes 786436
  0.7 8.3 %collective-permute-start = (bf16[64,2048]{1,0:T(8,128)(2,1)}, bf16[64,2048]{1,0:T(8,128)(2,1)S(1)}, u32[]{:S(2)}, u32[]{:S(2)}) collective-permute-start(bf16[64,2048]{1,0:T(8,128)(2,1)} %param.18), channel_id=1, source_target_pairs={{0,2},{1,3},{2,0},{3,1},{4,6},{5,7},{6,4},{7,5},{8,10},{9,11},{10,... | collective-permute-start | bytes 786440 | tf_op jit(solution)/shard_map/ppermute | solution.py:150
  3.4 5.5 %copy-start.12 = (f32[4,64]{1,0:T(4,128)}, f32[4,64]{1,0:T(4,128)S(1)}, u32[]{:S(2)}) copy-start(f32[4,64]{1,0:T(4,128)S(1)} %reduce_window_sum.22) | copy-start | bytes 3076
  4.3 4.7 %copy-start.15 = (f32[4,64]{1,0:T(4,128)}, f32[4,64]{1,0:T(4,128)S(1)}, u32[]{:S(2)}) copy-start(f32[4,64]{1,0:T(4,128)S(1)} %get-tuple-element.87) | copy-start | bytes 3076
  10.0 2.1 %collective-permute-start.1 = (bf16[128,2048]{1,0:T(8,128)(2,1)S(1)}, bf16[128,2048]{1,0:T(8,128)(2,1)S(1)}, u32[]{:S(2)}, u32[]{:S(2)}) collective-permute-start(bf16[128,2048]{1,0:T(8,128)(2,1)S(1)} %pad_maximum_fusion.4), channel_id=1, source_target_pairs={{0,1},{1,0},{2,3},{3,2},{4,5},{5,4},{6,7},{7,6},{8,9},{9,8},{10,11... | collective-permute-start | bytes 1572872 | tf_op jit(solution)/shard_map/ppermute | solution.py:150
  12.1 0.7 copy-start.4
  17.5 3.8 %copy-start.25 = (bf16[2048,16]{0,1:T(8,128)(2,1)S(1)}, bf16[2048,16]{0,1:T(8,128)(2,1)}, u32[]{:S(2)}) copy-start(bf16[2048,16]{0,1:T(8,128)(2,1)} %param.26) | copy-start | bytes 196612
  17.5 3.8 %copy-start.26 = (bf16[16,256]{1,0:T(8,128)(2,1)S(1)}, bf16[16,256]{1,0:T(8,128)(2,1)}, u32[]{:S(2)}) copy-start(bf16[16,256]{1,0:T(8,128)(2,1)} %param.27) | copy-start | bytes 24580
  17.5 3.8 %copy-start.28 = (f32[256]{0:T(256)S(1)}, f32[256]{0:T(256)}, u32[]{:S(2)}) copy-start(f32[256]{0:T(256)} %param.28) | copy-start | bytes 3076
  27.0 6.4 %collective-permute-start.2 = (bf16[3,1024]{1,0:T(4,128)(2,1)S(1)}, bf16[3,1024]{1,0:T(4,128)(2,1)S(1)}, u32[]{:S(2)}, u32[]{:S(2)}) collective-permute-start(bf16[3,1024]{1,0:T(4,128)(2,1)S(1)} %get-tuple-element.70), channel_id=1, source_target_pairs={{0,4},{4,8},{8,12},{12,16},{16,20},{20,24},{24,28},{1,5},{5,9},{9,... | collective-permute-start | bytes 18440 | tf_op jit(solution)/shard_map/ppermute | solution.py:17
  31.1 18.7 %copy-start.17 = (f32[256]{0:T(256)}, f32[256]{0:T(256)S(1)}, u32[]{:S(2)}) copy-start(f32[256]{0:T(256)S(1)} %get-tuple-element.63) | copy-start | bytes 3076
  31.2 3.7 %copy-start.19 = (f32[4,256]{1,0:T(4,128)S(1)}, f32[4,256]{1,0:T(4,128)}, u32[]{:S(2)}) copy-start(f32[4,256]{1,0:T(4,128)} %fusion.58) | copy-start | bytes 12292
  35.6 0.7 copy-start.16
  35.6 1.1 %copy-start.22 = (f32[4,64]{1,0:T(4,128)S(1)}, f32[4,64]{1,0:T(4,128)}, u32[]{:S(2)}) copy-start(f32[4,64]{1,0:T(4,128)} %get-tuple-element.88) | copy-start | bytes 3076
  36.0 1.4 %copy-start.8 = (bf16[256,512]{1,0:T(8,128)(2,1)}, bf16[256,512]{1,0:T(8,128)(2,1)S(1)}, u32[]{:S(2)}) copy-start(bf16[256,512]{1,0:T(8,128)(2,1)S(1)} %slice.164) | copy-start | bytes 786436
  36.0 0.7 copy-start.9
  37.4 3.8 %copy-start.23 = (f32[256]{0:T(256)S(1)}, f32[256]{0:T(256)}, u32[]{:S(2)}) copy-start(f32[256]{0:T(256)} %reshape.253) | copy-start | bytes 3076
  37.6 12.4 %copy-start.1 = (f32[256,512]{1,0:T(8,128)}, f32[256,512]{1,0:T(8,128)S(1)}, u32[]{:S(2)}) copy-start(f32[256,512]{1,0:T(8,128)S(1)} %get-tuple-element.60) | copy-start | bytes 1572868
  38.7 13.4 %copy-start.13 = (f32[4,64]{1,0:T(4,128)S(1)}, f32[4,64]{1,0:T(4,128)}, u32[]{:S(2)}) copy-start(f32[4,64]{1,0:T(4,128)} %copy-done.12) | copy-start | bytes 3076
  38.7 13.4 %copy-start.14 = (pred[64,64]{1,0:T(8,128)(4,1)S(1)}, pred[64,64]{1,0:T(8,128)(4,1)}, u32[]{:S(2)}) copy-start(pred[64,64]{1,0:T(8,128)(4,1)} %iota_compare_fusion) | copy-start | bytes 12292
  38.7 10.5 %collective-permute-start.3 = (bf16[257,512]{1,0:T(8,128)(2,1)S(1)}, bf16[257,512]{1,0:T(8,128)(2,1)S(1)}, u32[]{:S(2)}, u32[]{:S(2)}) collective-permute-start(bf16[257,512]{1,0:T(8,128)(2,1)S(1)} %pad_maximum_fusion.6), channel_id=1, source_target_pairs={{0,4},{4,8},{8,12},{12,16},{16,20},{20,24},{24,28},{1,5},{5,9},{9,... | collective-permute-start | bytes 789512 | tf_op jit(solution)/shard_map/ppermute | solution.py:17
  49.2 1.5 %copy-start.10 = (bf16[257,512]{1,0:T(8,128)(2,1)}, bf16[257,512]{1,0:T(8,128)(2,1)S(1)}, u32[]{:S(2)}) copy-start(bf16[257,512]{1,0:T(8,128)(2,1)S(1)} %collective-permute-done.3) | copy-start | bytes 789508
  49.2 0.6 copy-start.21
  50.0 9.8 %copy-start.18 = (f32[256]{0:T(256)S(1)}, f32[256]{0:T(256)}, u32[]{:S(2)}) copy-start(f32[256]{0:T(256)} %copy-done.17) | copy-start | bytes 3076
  50.8 9.1 %collective-permute-start.4 = (bf16[257,512]{1,0:T(8,128)(2,1)}, bf16[257,512]{1,0:T(8,128)(2,1)}, u32[]{:S(2)}, u32[]{:S(2)}) collective-permute-start(bf16[257,512]{1,0:T(8,128)(2,1)} %pad_maximum_fusion.7), channel_id=1, source_target_pairs={{0,8},{4,12},{8,16},{12,20},{16,24},{20,28},{1,9},{5,13},{9,17},{1... | collective-permute-start | bytes 789512 | tf_op jit(solution)/shard_map/ppermute | solution.py:17
  54.4 23.0 %copy-start.24 = (bf16[2048,512]{1,0:T(8,128)(2,1)S(1)}, bf16[2048,512]{1,0:T(8,128)(2,1)}, u32[]{:S(2)}) copy-start(bf16[2048,512]{1,0:T(8,128)(2,1)} %param.29) | copy-start | bytes 6291460
  54.4 23.0 %copy-start.27 = (f32[512]{0:T(512)S(1)}, f32[512]{0:T(512)}, u32[]{:S(2)}) copy-start(f32[512]{0:T(512)} %param.30) | copy-start | bytes 6148
  61.3 14.1 %collective-permute-start.5 = (bf16[256,512]{1,0:T(8,128)(2,1)S(1)}, bf16[256,512]{1,0:T(8,128)(2,1)S(1)}, u32[]{:S(2)}, u32[]{:S(2)}) collective-permute-start(bf16[256,512]{1,0:T(8,128)(2,1)S(1)} %fusion.63), channel_id=1, source_target_pairs={{0,16},{4,20},{8,24},{12,28},{1,17},{5,21},{9,25},{13,29},{2,18},{... | collective-permute-start | bytes 786440 | tf_op jit(solution)/shard_map/ppermute | solution.py:17
  78.7 2.0 %collective-permute-start.6 = (bf16[128,2048]{1,0:T(8,128)(2,1)S(1)}, bf16[128,2048]{1,0:T(8,128)(2,1)S(1)}, u32[]{:S(2)}, u32[]{:S(2)}) collective-permute-start(bf16[128,2048]{1,0:T(8,128)(2,1)S(1)} %convolution_convert_fusion), channel_id=1, source_target_pairs={{0,1},{1,0},{2,3},{3,2},{4,5},{5,4},{6,7},{7,6},{8,9},{9,8},{10,11... | collective-permute-start | bytes 1572872 | tf_op jit(solution)/shard_map/ppermute | solution.py:188
  80.7 2.1 %copy-start.2 = (f32[256,512]{1,0:T(8,128)S(1)}, f32[256,512]{1,0:T(8,128)}, u32[]{:S(2)}) copy-start(f32[256,512]{1,0:T(8,128)} %copy-done.1) | copy-start | bytes 1572868
  80.7 2.1 %copy-start.11 = (bf16[257,512]{1,0:T(8,128)(2,1)S(1)}, bf16[257,512]{1,0:T(8,128)(2,1)}, u32[]{:S(2)}) copy-start(bf16[257,512]{1,0:T(8,128)(2,1)} %copy-done.10) | copy-start | bytes 789508
  80.7 2.1 %copy-start.20 = (f32[256]{0:T(256)S(1)}, f32[256]{0:T(256)}, u32[]{:S(2)}) copy-start(f32[256]{0:T(256)} %get-tuple-element.58) | copy-start | bytes 3076
  81.2 8.4 %collective-permute-start.7 = (bf16[1,64,2048]{2,1,0:T(8,128)(2,1)S(1)}, bf16[1,64,2048]{2,1,0:T(8,128)(2,1)S(1)}, u32[]{:S(2)}, u32[]{:S(2)}) collective-permute-start(bf16[1,64,2048]{2,1,0:T(8,128)(2,1)S(1)} %fusion.20), channel_id=1, source_target_pairs={{0,2},{1,3},{2,0},{3,1},{4,6},{5,7},{6,4},{7,5},{8,10},{9,11},{10,... | collective-permute-start | bytes 786440 | tf_op jit(solution)/shard_map/ppermute | solution.py:199

commit v10 on v8

--- a/solution.py
+++ b/solution.py
@@ -180,8 +180,17 @@
             outgoing = lax.dynamic_index_in_dim(chunks, (place + step) % count, 0, False)
             total = total + lax.ppermute(outgoing, axis, pairs).astype(jnp.float32)
         return total.astype(jnp.bfloat16)
-    held = [term(index) for index in range(count)]
-    mask = 1
+    held = [lax.slice_in_dim(gated, index * chunk, (index + 1) * chunk, axis=0) for index in range(count)]
+    odd = place % 2 == 1
+    pairs = list(zip(held[0::2], held[1::2]))
+    outgoing = jnp.concatenate([jnp.where(odd, low, high) for low, high in pairs])
+    outgoing = jnp.dot(outgoing, weight, preferred_element_type=jnp.float32).astype(jnp.bfloat16)
+    incoming = lax.ppermute(outgoing, axis, [(source, source ^ 1) for source in range(count)])
+    kept = jnp.concatenate([jnp.where(odd, high, low) for low, high in pairs])
+    kept = jnp.dot(kept, weight, preferred_element_type=jnp.float32).astype(jnp.bfloat16)
+    summed = kept.astype(jnp.float32) + incoming.astype(jnp.float32)
+    held = list(jnp.split(summed, len(pairs)))
+    mask = 2
     while mask < count:
         odd = (place // mask) % 2 == 1
         pairs = list(zip(held[0::2], held[1::2]))

time: 86 us -> 82.3 us (0.957)
  other arithmetic: 20.4 us -> 16.9 us
    ppermute x2 -> x1, waiting for transfers between devices: 6.72 us -> 4.55 us  [scatter_sum(): lax.ppermute(outgoing, axis, [(source, source ^ mask) for source in range...]
    another operation x4 -> x1, other arithmetic: 2.15 us -> 0.05 us  [scatter_sum(): jnp.stack([jnp.where(odd, low, high).astype(jnp.bfloat16) for low, high i...]
    ppermute x0 -> x1, waiting for transfers between devices: none -> 1.87 us  [scatter_sum(): lax.ppermute(outgoing, axis, [(source, source ^ 1) for source in range(co...]
    convert_element_type x1, other arithmetic: 2.02 us -> 0.8 us  [scatter_sum(): return held[0].astype(jnp.bfloat16)]
    dot_general x4 -> x2, matrix products: 1.92 us -> 2.01 us  [the longest x1 1.56 us: scatter_sum(): jnp.dot(kept, weight, preferred_element_type=jnp.float32)]
where the time goes in v10:
time: 82.3 us; the launch traced here: 81.7 us
  waiting for transfers between devices  32.8 us (40%)
  other arithmetic  16.9 us (21%)
  matrix products  15 us (18%)
  starting transfers between devices  11.8 us (14%)
  local copies, waits for them, and re-layouts  3.95 us (5%)
  between operations  1.12 us (1%)
    ppermute x4, waiting for transfers between devices, shifted(): lax.ppermute(value, axis, [(source, source + steps) for source in range(i...  24.1 us
    ppermute x4, starting transfers between devices, shifted(): lax.ppermute(value, axis, [(source, source + steps) for source in range(i...  8.46 us
    ppermute x1, waiting for transfers between devices, scatter_sum(): lax.ppermute(outgoing, axis, [(source, source ^ mask) for source in range...  4.55 us
    dot_general x4, matrix products, project(): jnp.dot(gathered, weight, preferred_element_type=jnp.float32)  3.74 us
    dot_general x1, matrix products, segment_parts(): jnp.einsum('bac,bcv->bav', scores, head_values, preferred_element_type=jn...  2.69 us
    dot_general x3, matrix products, segment_parts(): jnp.dot(lifted_intact[block], memory, precision=HIGH_PRECISION)  2.48 us
    ppermute x2, waiting for transfers between devices, gather_rows(): lax.ppermute(jnp.concatenate(received), axis, [(source, source ^ mask) fo...  2.33 us
    broadcast_in_dim x1, other arithmetic, shards(): segment_states = closing[None, None]  2.23 us
  transfers between devices with their start and end apart: 8, of which 8 were waited for; matrix products, arithmetic and copies ran while one was open for 18% of the time, Pallas kernels for 0%

profile of v10, /device:TPU:24, one launch (start us, length us, event | category | flops | bytes accessed | tf_op | source)
XLA Modules:
  0.0 81.7 jit_solution(7894832437369748976)
XLA Ops:
  0.7 1.6 %collective-permute-start = (bf16[64,2048]{1,0:T(8,128)(2,1)}, bf16[64,2048]{1,0:T(8,128)(2,1)S(1)}, u32[]{:S(2)}, u32[]{:S(2)}) collective-permute-start(bf16[64,2048]{1,0:T(8,128)(2,1)} %param.18), channel_id=1, source_target_pairs={{0,2},{1,3},{2,0},{3,1},{4,6},{5,7},{6,4},{7,5},{8,10},{9,11},{10,... | collective-permute-start | bytes 786440 | tf_op jit(solution)/shard_map/ppermute | solution.py:150
  2.2 0.8 select_reduce_fusion.1
  3.7 0.6 slice.181
  4.3 0.7 convert_element_type.178
  5.0 0.7 convert_element_type.188
  5.7 0.7 convert_element_type.194
  6.4 0.5 pad.32.clone
  7.1 0.6 iota_compare_fusion
  7.7 1.2 %collective-permute-done = bf16[64,2048]{1,0:T(8,128)(2,1)S(1)} collective-permute-done((bf16[64,2048]{1,0:T(8,128)(2,1)}, bf16[64,2048]{1,0:T(8,128)(2,1)S(1)}, u32[]{:S(2)}, u32[]{:S(2)}) %collective-permute-start) | collective-permute-done | bytes 262176 | tf_op jit(solution)/shard_map/ppermute | solution.py:150
  9.0 1.0 %pad_maximum_fusion.4 = bf16[128,2048]{1,0:T(8,128)(2,1)S(1)} fusion(bf16[64,2048]{1,0:T(8,128)(2,1)S(1)} %collective-permute-done, bf16[64,2048]{1,0:T(8,128)(2,1)} %param.18), kind=kLoop, calls=%fused_computation.40 | loop fusion | flops 1048576 | bytes 1048576 | tf_op jit(solution)/shard_map/concatenate | solution.py:151
  10.1 0.7 slice_compare_fusion
  10.9 1.1 %collective-permute-done.1 = bf16[128,2048]{1,0:T(8,128)(2,1)S(1)} collective-permute-done((bf16[128,2048]{1,0:T(8,128)(2,1)S(1)}, bf16[128,2048]{1,0:T(8,128)(2,1)S(1)}, u32[]{:S(2)}, u32[]{:S(2)}) %collective-permute-start.1) | collective-permute-done | bytes 524320 | tf_op jit(solution)/shard_map/ppermute | solution.py:150
  12.0 1.8 %conditional.1 = (bf16[256,2048]{1,0:T(8,128)(2,1)S(1)}) conditional(s32[]{:T(128)} %clamp.3, (bf16[64,2048]{1,0:T(8,128)(2,1)S(1)}, bf16[64,2048]{1,0:T(8,128)(2,1)S(1)}, bf16[64,2048]{1,0:T(8,128)(2,1)S(1)}, bf16[64,2048]{1,0:T(8,128)(2,1)S(1)}) %tuple.60, (bf16[64,2048]{1,0:T(8,128)(2,1)S(1)}, ...), branch_computations={%region_3.0_spmd, %region_4.5_spmd, %region_5.6_spmd, %region_6.7_... | conditional | flops 4194304 | bytes 3145764 | solution.py:164
  12.1 0.7 copy-done.4
  12.8 1.0 %pad_maximum_fusion = bf16[256,2048]{1,0:T(8,128)(2,1)S(1)} fusion(bf16[64,2048]{1,0:T(8,128)(2,1)S(1)} %get-tuple-element.40, bf16[64,2048]{1,0:T(8,128)(2,1)} %copy-done.4, bf16[64,2048]{1,0:T(8,128)(2,1)S(1)} %get-tuple-element.33, bf16[64,2048]{1,0:T(8,128)(2,1)S(1)} %get-tuple-element.32), kind=kLoop, calls=%fused_computation | loop fusion | flops 4194304 | bytes 2097152 | tf_op jit(solution)/shard_map/cond/branch_0_fun/concatenate | solution.py:162
  13.8 1.5 %fusion.26 = f32[256,256]{1,0:T(8,128)} fusion(bf16[16,256]{1,0:T(8,128)(2,1)S(1)} %copy-done.19, bf16[256,2048]{1,0:T(8,128)(2,1)S(1)} %get-tuple-element.103, bf16[2048,16]{0,1:T(8,128)(2,1)S(1)} %copy-done.18, f32[256]{0:T(256)S(1)} %copy-done.21), kind=kOutput, calls=%fused_computation.77 | convolution fusion | flops 19533824 | bytes 1385472 | tf_op jit(solution)/shard_map/dot_general | solution.py:257
  15.3 1.2 %reduce_window_sum.23 = f32[4,64,256]{2,1,0:T(8,128)S(1)} reduce-window(f32[4,64,256]{2,1,0:T(8,128)} %bitcast.128, f32[]{:T(128)} %constant.74.clone.1), window={size=1x64x1 pad=0_0x63_0x0_0}, to_apply=%region_8.9 | reduce-window | flops 4128768 | bytes 524292 | tf_op jit(solution)/shard_map/jit(cumsum)/reduce_window_sum | solution.py:49
  16.6 1.8 %convolution_convert_fusion.5 = bf16[256,256]{1,0:T(8,128)(2,1)S(1)} fusion(bf16[256,2048]{1,0:T(8,128)(2,1)S(1)} %get-tuple-element.103, bf16[2048,256]{1,0:T(8,128)(2,1)} %param.20), kind=kOutput, calls=%fused_computation.16 | convolution fusion | flops 268500992 | bytes 2228224 | tf_op jit(solution)/shard_map/dot_general | solution.py:227
  18.6 0.7 convolution_convert_fusion.3
  19.3 0.5 copy-done.12
  19.8 0.4 convolution_convert_fusion.4
  20.2 0.7 select_bitcast_fusion
  20.9 3.4 %collective-permute-start.2 = (bf16[3,1024]{1,0:T(4,128)(2,1)S(1)}, bf16[3,1024]{1,0:T(4,128)(2,1)S(1)}, u32[]{:S(2)}, u32[]{:S(2)}) collective-permute-start(bf16[3,1024]{1,0:T(4,128)(2,1)S(1)} %get-tuple-element.59), channel_id=1, source_target_pairs={{0,4},{4,8},{8,12},{12,16},{16,20},{20,24},{24,28},{1,5},{5,9},{9,... | collective-permute-start | bytes 18440 | tf_op jit(solution)/shard_map/ppermute | solution.py:17
  24.5 2.8 %collective-permute-done.2 = bf16[3,1024]{1,0:T(4,128)(2,1)S(1)} collective-permute-done((bf16[3,1024]{1,0:T(4,128)(2,1)S(1)}, bf16[3,1024]{1,0:T(4,128)(2,1)S(1)}, u32[]{:S(2)}, u32[]{:S(2)}) %collective-permute-start.2) | collective-permute-done | bytes 6176 | tf_op jit(solution)/shard_map/ppermute | solution.py:17
  28.5 0.6 fusion.49
  29.8 2.5 %collective-permute-start.3 = (bf16[257,512]{1,0:T(8,128)(2,1)S(1)}, bf16[257,512]{1,0:T(8,128)(2,1)S(1)}, u32[]{:S(2)}, u32[]{:S(2)}) collective-permute-start(bf16[257,512]{1,0:T(8,128)(2,1)S(1)} %pad_maximum_fusion.5), channel_id=1, source_target_pairs={{0,4},{4,8},{8,12},{12,16},{16,20},{20,24},{24,28},{1,5},{5,9},{9,... | collective-permute-start | bytes 789512 | tf_op jit(solution)/shard_map/ppermute | solution.py:17
  32.3 0.8 bitcast_multiply_fusion
  33.1 1.0 %convolution_bitcast_fusion.2 = f32[1,64,512]{2,1,0:T(8,128)} fusion(f32[4,256,512]{2,1,0:T(8,128)S(1)} %fusion.49, f32[256]{0:T(256)S(1)} %get-tuple-element.97, f32[4,64,256]{2,1,0:T(8,128)S(1)} %get-tuple-element.80), kind=kOutput, calls=%fused_computation.19 | convolution fusion | flops 50462720 | bytes 721920 | tf_op jit(solution)/shard_map/dot_general | solution.py:80
  34.1 1.1 %convolution_bitcast_fusion = f32[1,64,512]{2,1,0:T(8,128)} fusion(f32[4,256,512]{2,1,0:T(8,128)S(1)} %fusion.49, f32[256]{0:T(256)S(1)} %bitcast.137, f32[4,64,256]{2,1,0:T(8,128)S(1)} %get-tuple-element.80, f32[256]{0:T(256)S(1)} %bitcast.134, f32[256]{0:T(256)S(1)} %get-tuple-element.97), kind=kOutput, calls=%fused_computation.17 | convolution fusion | flops 50987008 | bytes 1772544 | tf_op jit(solution)/shard_map/dot_general | solution.py:80
  35.2 4.8 %collective-permute-done.3 = bf16[257,512]{1,0:T(8,128)(2,1)S(1)} collective-permute-done((bf16[257,512]{1,0:T(8,128)(2,1)S(1)}, bf16[257,512]{1,0:T(8,128)(2,1)S(1)}, u32[]{:S(2)}, u32[]{:S(2)}) %collective-permute-start.3) | collective-permute-done | bytes 263200 | tf_op jit(solution)/shard_map/ppermute | solution.py:17
  40.2 0.7 pad_maximum_fusion.6
  40.9 1.3 %collective-permute-start.4 = (bf16[257,512]{1,0:T(8,128)(2,1)}, bf16[257,512]{1,0:T(8,128)(2,1)}, u32[]{:S(2)}, u32[]{:S(2)}) collective-permute-start(bf16[257,512]{1,0:T(8,128)(2,1)} %pad_maximum_fusion.6), channel_id=1, source_target_pairs={{0,8},{4,12},{8,16},{12,20},{16,24},{20,28},{1,9},{5,13},{9,17},{1... | collective-permute-start | bytes 789512 | tf_op jit(solution)/shard_map/ppermute | solution.py:17
  42.2 2.7 %convolution_add_fusion = f32[4,64,512]{2,1,0:T(8,128)} fusion(f32[1,64,512]{2,1,0:T(8,128)} %convolution_bitcast_fusion, f32[1,64,512]{2,1,0:T(8,128)S(1)} %convolution_bitcast_fusion.1, f32[1,64,512]{2,1,0:T(8,128)} %convolution_bitcast_fusion.2, f32[4]{0:T(128)} %pad.32.clone, f32[4,64,256]{2,1,0:T(8,128)} %copy-done.10, ...), kind=kOutput, calls=%fused_computation.8 | convolution fusion | flops 27525120 | bytes 2233360 | tf_op jit(solution)/shard_map/bac,bcv->bav/dot_general | solution.py:71
  44.9 4.7 %collective-permute-done.4 = bf16[257,512]{1,0:T(8,128)(2,1)} collective-permute-done((bf16[257,512]{1,0:T(8,128)(2,1)}, bf16[257,512]{1,0:T(8,128)(2,1)}, u32[]{:S(2)}, u32[]{:S(2)}) %collective-permute-start.4) | collective-permute-done | bytes 263200 | tf_op jit(solution)/shard_map/ppermute | solution.py:17
  49.6 1.4 %fusion.78 = bf16[256,512]{1,0:T(8,128)(2,1)S(1)} fusion(f32[256,512]{1,0:T(8,128)} %copy-done.1, bf16[257,512]{1,0:T(8,128)(2,1)} %copy-done.8, f32[256]{0:T(256)S(1)} %get-tuple-element.67, pred[]{:T(512)S(6)} %ge.60, bf16[257,512]{1,0:T(8,128)(2,1)} %collective-permute-done.4, f32[256]{0:T(256)S(1)} %get-tuple-element.62, pred[]{:T(512)S(6)} %ge.59), kind=kLoop, calls=%fused_computation.176 | loop fusion | flops 1179648 | bytes 1312770 | tf_op jit(solution)/shard_map/convert_element_type | solution.py:119
  51.0 1.3 %collective-permute-start.5 = (bf16[256,512]{1,0:T(8,128)(2,1)S(1)}, bf16[256,512]{1,0:T(8,128)(2,1)S(1)}, u32[]{:S(2)}, u32[]{:S(2)}) collective-permute-start(bf16[256,512]{1,0:T(8,128)(2,1)S(1)} %fusion.78), channel_id=1, source_target_pairs={{0,16},{4,20},{8,24},{12,28},{1,17},{5,21},{9,25},{13,29},{2,18},{... | collective-permute-start | bytes 786440 | tf_op jit(solution)/shard_map/ppermute | solution.py:17
  52.3 0.7 slice_convert_fusion
  53.1 11.8 %collective-permute-done.5 = bf16[256,512]{1,0:T(8,128)(2,1)S(1)} collective-permute-done((bf16[256,512]{1,0:T(8,128)(2,1)S(1)}, bf16[256,512]{1,0:T(8,128)(2,1)S(1)}, u32[]{:S(2)}, u32[]{:S(2)}) %collective-permute-start.5) | collective-permute-done | bytes 262176 | tf_op jit(solution)/shard_map/ppermute | solution.py:17
  64.8 2.0 %multiply_reduce_fusion.3 = (f32[256]{0:T(256)S(1)}, f32[256,512]{1,0:T(8,128)S(1)}) fusion(f32[256,512]{1,0:T(8,128)} %bitcast.146, f32[256,256]{1,0:T(8,128)} %bitcast_multiply_fusion, bf16[256,512]{1,0:T(8,128)(2,1)S(1)} %collective-permute-done.5, f32[256]{0:T(256)S(1)} %bitcast.143, f32[256]{0:T(256)S(1)} %get-tuple-element.96, pred[]{:T(512)S(6)} %ge.59, ...), kind=kOutput, calls=%fused_computation.54 | convolution fusion | flops 202899200 | bytes 2100226 | tf_op jit(solution)/shard_map/dot_general | solution.py:265
  66.8 0.8 multiply_convert_fusion
  67.7 0.4 convolution_convert_fusion
  68.2 1.9 %collective-permute-done.6 = bf16[128,2048]{1,0:T(8,128)(2,1)S(1)} collective-permute-done((bf16[128,2048]{1,0:T(8,128)(2,1)S(1)}, bf16[128,2048]{1,0:T(8,128)(2,1)S(1)}, u32[]{:S(2)}, u32[]{:S(2)}) %collective-permute-start.6) | collective-permute-done | bytes 524320 | tf_op jit(solution)/shard_map/ppermute | solution.py:188
  70.1 0.8 copy-done.14
  70.9 1.6 %convert_add_fusion = f32[128,2048]{1,0:T(8,128)S(1)} fusion(bf16[128,2048]{1,0:T(8,128)(2,1)} %copy-done.14, bf16[512,2048]{1,0:T(8,128)(2,1)S(1)} %copy-done, bf16[64,512]{1,0:T(8,128)(2,1)S(1)} %get-tuple-element.76, bf16[64,512]{1,0:T(8,128)(2,1)S(1)} %get-tuple-element.75), kind=kOutput, calls=%fused_computation.23 | convolution fusion | flops 269746176 | bytes 3801088 | tf_op jit(solution)/shard_map/dot_general | solution.py:190
  72.5 1.6 %collective-permute-start.7 = (bf16[1,64,2048]{2,1,0:T(8,128)(2,1)S(1)}, bf16[1,64,2048]{2,1,0:T(8,128)(2,1)S(1)}, u32[]{:S(2)}, u32[]{:S(2)}) collective-permute-start(bf16[1,64,2048]{2,1,0:T(8,128)(2,1)S(1)} %fusion.24), channel_id=1, source_target_pairs={{0,2},{1,3},{2,0},{3,1},{4,6},{5,7},{6,4},{7,5},{8,10},{9,11},{10,... | collective-permute-start | bytes 786440 | tf_op jit(solution)/shard_map/ppermute | solution.py:199
  74.1 2.2 %fusion.4 = f32[1,1,256,512]{3,2,1,0:T(8,128)} fusion(bf16[256,512]{1,0:T(8,128)(2,1)S(1)} %collective-permute-done.5, f32[256]{0:T(256)S(1)} %get-tuple-element.95, pred[]{:T(512)S(6)} %ge.58, f32[256,512]{1,0:T(8,128)S(1)} %copy-done.2, bf16[257,512]{1,0:T(8,128)(2,1)S(1)} %copy-done.9, f32[256]{0:T(256)S(1)} %get-tuple-element.67, pred[]{:T(512)S(6)} %ge.60, ...), kind=kLoop, calls=%fused_computation.37 | loop fusion | flops 1572864 | bytes 1838083 | tf_op jit(solution)/shard_map/broadcast_in_dim | solution.py:274
  76.4 4.6 %collective-permute-done.7 = bf16[1,64,2048]{2,1,0:T(8,128)(2,1)S(1)} collective-permute-done((bf16[1,64,2048]{2,1,0:T(8,128)(2,1)S(1)}, bf16[1,64,2048]{2,1,0:T(8,128)(2,1)S(1)}, u32[]{:S(2)}, u32[]{:S(2)}) %collective-permute-start.7) | collective-permute-done | bytes 262176 | tf_op jit(solution)/shard_map/ppermute | solution.py:199
  80.9 0.8 fusion.6
  (79 shorter events, 3.6 us)
Async XLA Ops:
  0.6 67.0 %copy-start = (bf16[512,2048]{1,0:T(8,128)(2,1)S(1)}, bf16[512,2048]{1,0:T(8,128)(2,1)}, u32[]{:S(2)}) copy-start(bf16[512,2048]{1,0:T(8,128)(2,1)} %param.31) | copy-start | bytes 6291460
  0.6 11.3 %copy-start.3 = (bf16[64,2048]{1,0:T(8,128)(2,1)S(1)}, bf16[64,2048]{1,0:T(8,128)(2,1)}, u32[]{:S(2)}) copy-start(bf16[64,2048]{1,0:T(8,128)(2,1)} %param.18) | copy-start | bytes 786436
  0.7 8.3 %collective-permute-start = (bf16[64,2048]{1,0:T(8,128)(2,1)}, bf16[64,2048]{1,0:T(8,128)(2,1)S(1)}, u32[]{:S(2)}, u32[]{:S(2)}) collective-permute-start(bf16[64,2048]{1,0:T(8,128)(2,1)} %param.18), channel_id=1, source_target_pairs={{0,2},{1,3},{2,0},{3,1},{4,6},{5,7},{6,4},{7,5},{8,10},{9,11},{10,... | collective-permute-start | bytes 786440 | tf_op jit(solution)/shard_map/ppermute | solution.py:150
  10.0 2.0 %collective-permute-start.1 = (bf16[128,2048]{1,0:T(8,128)(2,1)S(1)}, bf16[128,2048]{1,0:T(8,128)(2,1)S(1)}, u32[]{:S(2)}, u32[]{:S(2)}) collective-permute-start(bf16[128,2048]{1,0:T(8,128)(2,1)S(1)} %pad_maximum_fusion.4), channel_id=1, source_target_pairs={{0,1},{1,0},{2,3},{3,2},{4,5},{5,4},{6,7},{7,6},{8,9},{9,8},{10,11... | collective-permute-start | bytes 1572872 | tf_op jit(solution)/shard_map/ppermute | solution.py:150
  12.0 1.8 %copy-start.18 = (bf16[2048,16]{0,1:T(8,128)(2,1)S(1)}, bf16[2048,16]{0,1:T(8,128)(2,1)}, u32[]{:S(2)}) copy-start(bf16[2048,16]{0,1:T(8,128)(2,1)} %param.26) | copy-start | bytes 196612
  12.0 1.8 %copy-start.19 = (bf16[16,256]{1,0:T(8,128)(2,1)S(1)}, bf16[16,256]{1,0:T(8,128)(2,1)}, u32[]{:S(2)}) copy-start(bf16[16,256]{1,0:T(8,128)(2,1)} %param.27) | copy-start | bytes 24580
  12.0 1.8 %copy-start.21 = (f32[256]{0:T(256)S(1)}, f32[256]{0:T(256)}, u32[]{:S(2)}) copy-start(f32[256]{0:T(256)} %param.28) | copy-start | bytes 3076
  12.1 0.7 copy-start.4
  16.5 2.7 %copy-start.10 = (f32[4,64,256]{2,1,0:T(8,128)}, f32[4,64,256]{2,1,0:T(8,128)S(1)}, u32[]{:S(2)}) copy-start(f32[4,64,256]{2,1,0:T(8,128)S(1)} %reduce_window_sum.23) | copy-start | bytes 786436
  16.5 2.0 %copy-start.16 = (bf16[2048,512]{1,0:T(8,128)(2,1)S(1)}, bf16[2048,512]{1,0:T(8,128)(2,1)}, u32[]{:S(2)}) copy-start(bf16[2048,512]{1,0:T(8,128)(2,1)} %param.22) | copy-start | bytes 6291460
  18.6 1.2 %copy-start.12 = (bf16[2048,256]{1,0:T(8,128)(2,1)S(1)}, bf16[2048,256]{1,0:T(8,128)(2,1)}, u32[]{:S(2)}) copy-start(bf16[2048,256]{1,0:T(8,128)(2,1)} %param.21) | copy-start | bytes 3145732
  20.2 7.8 %copy-start.11 = (f32[4,64,256]{2,1,0:T(8,128)S(1)}, f32[4,64,256]{2,1,0:T(8,128)}, u32[]{:S(2)}) copy-start(f32[4,64,256]{2,1,0:T(8,128)} %copy-done.10) | copy-start | bytes 786436
  20.9 6.4 %collective-permute-start.2 = (bf16[3,1024]{1,0:T(4,128)(2,1)S(1)}, bf16[3,1024]{1,0:T(4,128)(2,1)S(1)}, u32[]{:S(2)}, u32[]{:S(2)}) collective-permute-start(bf16[3,1024]{1,0:T(4,128)(2,1)S(1)} %get-tuple-element.59), channel_id=1, source_target_pairs={{0,4},{4,8},{8,12},{12,16},{16,20},{20,24},{24,28},{1,5},{5,9},{9,... | collective-permute-start | bytes 18440 | tf_op jit(solution)/shard_map/ppermute | solution.py:17
  28.0 1.1 %copy-start.15 = (f32[256,256]{1,0:T(8,128)}, f32[256,256]{1,0:T(8,128)S(1)}, u32[]{:S(2)}) copy-start(f32[256,256]{1,0:T(8,128)S(1)} %get-tuple-element.57) | copy-start | bytes 786436
  28.5 0.9 %copy-start.13 = (f32[256,512]{1,0:T(8,128)}, f32[256,512]{1,0:T(8,128)S(1)}, u32[]{:S(2)}) copy-start(f32[256,512]{1,0:T(8,128)S(1)} %multiply_reduce_fusion) | copy-start | bytes 1572868
  29.4 10.8 %copy-start.1 = (f32[256,512]{1,0:T(8,128)}, f32[256,512]{1,0:T(8,128)S(1)}, u32[]{:S(2)}) copy-start(f32[256,512]{1,0:T(8,128)S(1)} %get-tuple-element.64) | copy-start | bytes 1572868
  29.8 10.2 %collective-permute-start.3 = (bf16[257,512]{1,0:T(8,128)(2,1)S(1)}, bf16[257,512]{1,0:T(8,128)(2,1)S(1)}, u32[]{:S(2)}, u32[]{:S(2)}) collective-permute-start(bf16[257,512]{1,0:T(8,128)(2,1)S(1)} %pad_maximum_fusion.5), channel_id=1, source_target_pairs={{0,4},{4,8},{8,12},{12,16},{16,20},{20,24},{24,28},{1,5},{5,9},{9,... | collective-permute-start | bytes 789512 | tf_op jit(solution)/shard_map/ppermute | solution.py:17
  40.0 0.9 %copy-start.8 = (bf16[257,512]{1,0:T(8,128)(2,1)}, bf16[257,512]{1,0:T(8,128)(2,1)S(1)}, u32[]{:S(2)}) copy-start(bf16[257,512]{1,0:T(8,128)(2,1)S(1)} %collective-permute-done.3) | copy-start | bytes 789508
  40.9 8.7 %collective-permute-start.4 = (bf16[257,512]{1,0:T(8,128)(2,1)}, bf16[257,512]{1,0:T(8,128)(2,1)}, u32[]{:S(2)}, u32[]{:S(2)}) collective-permute-start(bf16[257,512]{1,0:T(8,128)(2,1)} %pad_maximum_fusion.6), channel_id=1, source_target_pairs={{0,8},{4,12},{8,16},{12,20},{16,24},{20,28},{1,9},{5,13},{9,17},{1... | collective-permute-start | bytes 789512 | tf_op jit(solution)/shard_map/ppermute | solution.py:17
  44.9 21.9 %copy-start.17 = (bf16[2048,512]{1,0:T(8,128)(2,1)S(1)}, bf16[2048,512]{1,0:T(8,128)(2,1)}, u32[]{:S(2)}) copy-start(bf16[2048,512]{1,0:T(8,128)(2,1)} %param.29) | copy-start | bytes 6291460
  44.9 21.9 %copy-start.20 = (f32[512]{0:T(512)S(1)}, f32[512]{0:T(512)}, u32[]{:S(2)}) copy-start(f32[512]{0:T(512)} %param.30) | copy-start | bytes 6148
  51.0 13.8 %collective-permute-start.5 = (bf16[256,512]{1,0:T(8,128)(2,1)S(1)}, bf16[256,512]{1,0:T(8,128)(2,1)S(1)}, u32[]{:S(2)}, u32[]{:S(2)}) collective-permute-start(bf16[256,512]{1,0:T(8,128)(2,1)S(1)} %fusion.78), channel_id=1, source_target_pairs={{0,16},{4,20},{8,24},{12,28},{1,17},{5,21},{9,25},{13,29},{2,18},{... | collective-permute-start | bytes 786440 | tf_op jit(solution)/shard_map/ppermute | solution.py:17
  68.1 2.0 %collective-permute-start.6 = (bf16[128,2048]{1,0:T(8,128)(2,1)S(1)}, bf16[128,2048]{1,0:T(8,128)(2,1)S(1)}, u32[]{:S(2)}, u32[]{:S(2)}) collective-permute-start(bf16[128,2048]{1,0:T(8,128)(2,1)S(1)} %convolution_convert_fusion), channel_id=1, source_target_pairs={{0,1},{1,0},{2,3},{3,2},{4,5},{5,4},{6,7},{7,6},{8,9},{9,8},{10,11... | collective-permute-start | bytes 1572872 | tf_op jit(solution)/shard_map/ppermute | solution.py:188
  70.1 0.8 copy-start.14
  70.9 3.3 %copy-start.2 = (f32[256,512]{1,0:T(8,128)S(1)}, f32[256,512]{1,0:T(8,128)}, u32[]{:S(2)}) copy-start(f32[256,512]{1,0:T(8,128)} %copy-done.1) | copy-start | bytes 1572868
  70.9 3.3 %copy-start.9 = (bf16[257,512]{1,0:T(8,128)(2,1)S(1)}, bf16[257,512]{1,0:T(8,128)(2,1)}, u32[]{:S(2)}) copy-start(bf16[257,512]{1,0:T(8,128)(2,1)} %copy-done.8) | copy-start | bytes 789508
  72.5 8.4 %collective-permute-start.7 = (bf16[1,64,2048]{2,1,0:T(8,128)(2,1)S(1)}, bf16[1,64,2048]{2,1,0:T(8,128)(2,1)S(1)}, u32[]{:S(2)}, u32[]{:S(2)}) collective-permute-start(bf16[1,64,2048]{2,1,0:T(8,128)(2,1)S(1)} %fusion.24), channel_id=1, source_target_pairs={{0,2},{1,3},{2,0},{3,1},{4,6},{5,7},{6,4},{7,5},{8,10},{9,11},{10,... | collective-permute-start | bytes 786440 | tf_op jit(solution)/shard_map/ppermute | solution.py:199

commit v11 on v10

--- a/solution.py
+++ b/solution.py
@@ -147,10 +147,8 @@
         order = [0]
         mask = count // 2
         while mask >= 1:
-            incoming = lax.ppermute(
-                jnp.concatenate(received), axis, [(source, source ^ mask) for source in range(count)]
-            )
-            received = received + list(jnp.split(incoming, len(received)))
+            pairs = [(source, source ^ mask) for source in range(count)]
+            received = received + [lax.ppermute(block, axis, pairs) for block in received]
             order = order + [flip ^ mask for flip in order]
             mask //= 2
 

time: 82.3 us -> 82 us (level)
  waiting for transfers between devices: 32.8 us -> 35.4 us
  matrix products: 15 us -> 13.9 us
  local copies, waits for them, and re-layouts: 3.95 us -> 3.11 us
    ppermute x2 -> x3, waiting for transfers between devices: 2.33 us -> 3.78 us  [gather_rows(): lax.ppermute(block, axis, pairs)]
    dot_general x1, matrix products: 1.56 us -> 0.44 us  [scatter_sum(): jnp.dot(kept, weight, preferred_element_type=jnp.float32)]
    ppermute x4, waiting for transfers between devices: 24.1 us -> 25.2 us  [shifted(): lax.ppermute(value, axis, [(source, source + steps) for source in range(i...]
    concatenate x1 -> x0, other arithmetic: 0.99 us -> none  [gather_rows(): jnp.concatenate(received)]
    ppermute x2 -> x3, starting transfers between devices: 1.66 us -> 1.66 us  [gather_rows(): lax.ppermute(block, axis, pairs)]
  transfers between devices with their start and end apart: 8 -> 9, of which waited for: 8 -> 7; matrix products, arithmetic and copies ran while one was open for 18% -> 18% of each run, Pallas kernels for 0% -> 0%
where the time goes in v11:
time: 82 us; the launch traced here: 81.4 us
  waiting for transfers between devices  35.4 us (43%)
  other arithmetic  16.1 us (20%)
  matrix products  13.9 us (17%)
  starting transfers between devices  11.8 us (14%)
  local copies, waits for them, and re-layouts  3.11 us (4%)
  between operations  1.08 us (1%)
    ppermute x4, waiting for transfers between devices, shifted(): lax.ppermute(value, axis, [(source, source + steps) for source in range(i...  25.2 us
    ppermute x4, starting transfers between devices, shifted(): lax.ppermute(value, axis, [(source, source + steps) for source in range(i...  8.46 us
    ppermute x1, waiting for transfers between devices, scatter_sum(): lax.ppermute(outgoing, axis, [(source, source ^ mask) for source in range...  4.57 us
    ppermute x3, waiting for transfers between devices, gather_rows(): lax.ppermute(block, axis, pairs)  3.78 us
    dot_general x4, matrix products, project(): jnp.dot(gathered, weight, preferred_element_type=jnp.float32)  3.74 us
    dot_general x1, matrix products, segment_parts(): jnp.einsum('bac,bcv->bav', scores, head_values, preferred_element_type=jn...  2.7 us
    dot_general x3, matrix products, segment_parts(): jnp.dot(lifted_intact[block], memory, precision=HIGH_PRECISION)  2.47 us
    broadcast_in_dim x1, other arithmetic, shards(): segment_states = closing[None, None]  2.23 us
  transfers between devices with their start and end apart: 9, of which 7 were waited for; matrix products, arithmetic and copies ran while one was open for 18% of the time, Pallas kernels for 0%

profile of v11, /device:TPU:24, one launch (start us, length us, event | category | flops | bytes accessed | tf_op | source)
XLA Modules:
  0.0 81.4 jit_solution(10743970622897045072)
XLA Ops:
  0.7 1.6 %collective-permute-start.1 = (bf16[64,2048]{1,0:T(8,128)(2,1)}, bf16[64,2048]{1,0:T(8,128)(2,1)S(1)}, u32[]{:S(2)}, u32[]{:S(2)}) collective-permute-start(bf16[64,2048]{1,0:T(8,128)(2,1)} %param.18), channel_id=1, source_target_pairs={{0,2},{1,3},{2,0},{3,1},{4,6},{5,7},{6,4},{7,5},{8,10},{9,11},{10,... | collective-permute-start | bytes 786440 | tf_op jit(solution)/shard_map/ppermute | solution.py:151
  2.3 0.6 iota_compare_fusion
  2.9 0.8 select_reduce_fusion.1
  4.6 0.6 slice.181
  5.2 0.7 slice_compare_fusion
  5.9 3.8 %collective-permute-done.1 = bf16[64,2048]{1,0:T(8,128)(2,1)S(1)} collective-permute-done((bf16[64,2048]{1,0:T(8,128)(2,1)}, bf16[64,2048]{1,0:T(8,128)(2,1)S(1)}, u32[]{:S(2)}, u32[]{:S(2)}) %collective-permute-start.1) | collective-permute-done | bytes 262176 | tf_op jit(solution)/shard_map/ppermute | solution.py:151
  9.7 0.7 convert_element_type.178
  10.4 0.7 convert_element_type.188
  11.1 0.7 convert_element_type.194
  11.8 0.5 pad.32.clone
  12.4 1.9 %conditional.1 = (bf16[256,2048]{1,0:T(8,128)(2,1)S(1)}) conditional(s32[]{:T(128)} %clamp.3, (bf16[64,2048]{1,0:T(8,128)(2,1)}, bf16[64,2048]{1,0:T(8,128)(2,1)S(1)}, bf16[64,2048]{1,0:T(8,128)(2,1)S(1)}, bf16[64,2048]{1,0:T(8,128)(2,1)}) %tuple.20, (bf16[64,2048]{1,0:T(8,128)(2,1)S(1)}, bf16[64,2048]{1,0:T(8,128)(2,1)}, ...), branch_computations={%region_3.0_spmd, %region_4.5_spmd, %region_5.6_spmd, %region_6.7_... | conditional | flops 4194304 | bytes 3145764 | solution.py:162
  12.5 0.7 copy-done.3
  13.2 1.2 %pad_maximum_fusion = bf16[256,2048]{1,0:T(8,128)(2,1)S(1)} fusion(bf16[64,2048]{1,0:T(8,128)(2,1)} %get-tuple-element.40, bf16[64,2048]{1,0:T(8,128)(2,1)} %copy-done.3, bf16[64,2048]{1,0:T(8,128)(2,1)S(1)} %get-tuple-element.33, bf16[64,2048]{1,0:T(8,128)(2,1)} %get-tuple-element.32), kind=kLoop, calls=%fused_computation | loop fusion | flops 4194304 | bytes 2097152 | tf_op jit(solution)/shard_map/cond/branch_0_fun/concatenate | solution.py:160
  14.4 1.5 %fusion.26 = f32[256,256]{1,0:T(8,128)} fusion(bf16[16,256]{1,0:T(8,128)(2,1)S(1)} %copy-done.17, bf16[256,2048]{1,0:T(8,128)(2,1)S(1)} %get-tuple-element.101, bf16[2048,16]{0,1:T(8,128)(2,1)S(1)} %copy-done.16, f32[256]{0:T(256)S(1)} %copy-done.19), kind=kOutput, calls=%fused_computation.76 | convolution fusion | flops 19533824 | bytes 1385472 | tf_op jit(solution)/shard_map/dot_general | solution.py:255
  15.9 1.2 %reduce_window_sum.23 = f32[4,64,256]{2,1,0:T(8,128)S(1)} reduce-window(f32[4,64,256]{2,1,0:T(8,128)} %bitcast.128, f32[]{:T(128)} %constant.74.clone.1), window={size=1x64x1 pad=0_0x63_0x0_0}, to_apply=%region_8.9 | reduce-window | flops 4128768 | bytes 524292 | tf_op jit(solution)/shard_map/jit(cumsum)/reduce_window_sum | solution.py:49
  17.1 1.8 %convolution_convert_fusion.5 = bf16[256,256]{1,0:T(8,128)(2,1)S(1)} fusion(bf16[256,2048]{1,0:T(8,128)(2,1)S(1)} %get-tuple-element.101, bf16[2048,256]{1,0:T(8,128)(2,1)} %param.20), kind=kOutput, calls=%fused_computation.16 | convolution fusion | flops 268500992 | bytes 2228224 | tf_op jit(solution)/shard_map/dot_general | solution.py:225
  19.1 0.7 convolution_convert_fusion.3
  19.8 0.5 copy-done.11
  20.3 0.4 convolution_convert_fusion.4
  20.8 0.7 select_bitcast_fusion
  21.5 3.4 %collective-permute-start.3 = (bf16[3,1024]{1,0:T(4,128)(2,1)S(1)}, bf16[3,1024]{1,0:T(4,128)(2,1)S(1)}, u32[]{:S(2)}, u32[]{:S(2)}) collective-permute-start(bf16[3,1024]{1,0:T(4,128)(2,1)S(1)} %get-tuple-element.59), channel_id=1, source_target_pairs={{0,4},{4,8},{8,12},{12,16},{16,20},{20,24},{24,28},{1,5},{5,9},{9,... | collective-permute-start | bytes 18440 | tf_op jit(solution)/shard_map/ppermute | solution.py:17
  25.0 2.8 %collective-permute-done.3 = bf16[3,1024]{1,0:T(4,128)(2,1)S(1)} collective-permute-done((bf16[3,1024]{1,0:T(4,128)(2,1)S(1)}, bf16[3,1024]{1,0:T(4,128)(2,1)S(1)}, u32[]{:S(2)}, u32[]{:S(2)}) %collective-permute-start.3) | collective-permute-done | bytes 6176 | tf_op jit(solution)/shard_map/ppermute | solution.py:17
  28.2 0.3 multiply_reduce_fusion.2
  28.7 0.3 multiply_reduce_fusion
  29.1 0.6 fusion.49
  29.9 0.4 convolution_bitcast_fusion.1
  30.4 2.5 %collective-permute-start.4 = (bf16[257,512]{1,0:T(8,128)(2,1)S(1)}, bf16[257,512]{1,0:T(8,128)(2,1)S(1)}, u32[]{:S(2)}, u32[]{:S(2)}) collective-permute-start(bf16[257,512]{1,0:T(8,128)(2,1)S(1)} %pad_maximum_fusion.4), channel_id=1, source_target_pairs={{0,4},{4,8},{8,12},{12,16},{16,20},{20,24},{24,28},{1,5},{5,9},{9,... | collective-permute-start | bytes 789512 | tf_op jit(solution)/shard_map/ppermute | solution.py:17
  32.9 0.8 bitcast_multiply_fusion
  33.7 1.0 %convolution_bitcast_fusion.2 = f32[1,64,512]{2,1,0:T(8,128)} fusion(f32[4,256,512]{2,1,0:T(8,128)S(1)} %fusion.49, f32[256]{0:T(256)S(1)} %get-tuple-element.95, f32[4,64,256]{2,1,0:T(8,128)S(1)} %get-tuple-element.78), kind=kOutput, calls=%fused_computation.19 | convolution fusion | flops 50462720 | bytes 721920 | tf_op jit(solution)/shard_map/dot_general | solution.py:80
  34.7 1.1 %convolution_bitcast_fusion = f32[1,64,512]{2,1,0:T(8,128)} fusion(f32[4,256,512]{2,1,0:T(8,128)S(1)} %fusion.49, f32[256]{0:T(256)S(1)} %bitcast.137, f32[4,64,256]{2,1,0:T(8,128)S(1)} %get-tuple-element.78, f32[256]{0:T(256)S(1)} %bitcast.134, f32[256]{0:T(256)S(1)} %get-tuple-element.95), kind=kOutput, calls=%fused_computation.17 | convolution fusion | flops 50987008 | bytes 1772544 | tf_op jit(solution)/shard_map/dot_general | solution.py:80
  35.8 5.1 %collective-permute-done.4 = bf16[257,512]{1,0:T(8,128)(2,1)S(1)} collective-permute-done((bf16[257,512]{1,0:T(8,128)(2,1)S(1)}, bf16[257,512]{1,0:T(8,128)(2,1)S(1)}, u32[]{:S(2)}, u32[]{:S(2)}) %collective-permute-start.4) | collective-permute-done | bytes 263200 | tf_op jit(solution)/shard_map/ppermute | solution.py:17
  41.1 0.7 pad_maximum_fusion.5
  41.8 1.3 %collective-permute-start.5 = (bf16[257,512]{1,0:T(8,128)(2,1)}, bf16[257,512]{1,0:T(8,128)(2,1)}, u32[]{:S(2)}, u32[]{:S(2)}) collective-permute-start(bf16[257,512]{1,0:T(8,128)(2,1)} %pad_maximum_fusion.5), channel_id=1, source_target_pairs={{0,8},{4,12},{8,16},{12,20},{16,24},{20,28},{1,9},{5,13},{9,17},{1... | collective-permute-start | bytes 789512 | tf_op jit(solution)/shard_map/ppermute | solution.py:17
  43.1 2.7 %convolution_add_fusion = f32[4,64,512]{2,1,0:T(8,128)} fusion(f32[1,64,512]{2,1,0:T(8,128)} %convolution_bitcast_fusion, f32[1,64,512]{2,1,0:T(8,128)S(1)} %convolution_bitcast_fusion.1, f32[1,64,512]{2,1,0:T(8,128)} %convolution_bitcast_fusion.2, f32[4]{0:T(128)} %pad.32.clone, f32[4,64,256]{2,1,0:T(8,128)} %copy-done.9, ...), kind=kOutput, calls=%fused_computation.8 | convolution fusion | flops 27525120 | bytes 2233360 | tf_op jit(solution)/shard_map/bac,bcv->bav/dot_general | solution.py:71
  45.8 5.1 %collective-permute-done.5 = bf16[257,512]{1,0:T(8,128)(2,1)} collective-permute-done((bf16[257,512]{1,0:T(8,128)(2,1)}, bf16[257,512]{1,0:T(8,128)(2,1)}, u32[]{:S(2)}, u32[]{:S(2)}) %collective-permute-start.5) | collective-permute-done | bytes 263200 | tf_op jit(solution)/shard_map/ppermute | solution.py:17
  50.9 1.4 %fusion.78 = bf16[256,512]{1,0:T(8,128)(2,1)S(1)} fusion(f32[256,512]{1,0:T(8,128)} %copy-done.1, bf16[257,512]{1,0:T(8,128)(2,1)} %copy-done.7, f32[256]{0:T(256)S(1)} %get-tuple-element.67, pred[]{:T(512)S(6)} %ge.60, bf16[257,512]{1,0:T(8,128)(2,1)} %collective-permute-done.5, f32[256]{0:T(256)S(1)} %get-tuple-element.62, pred[]{:T(512)S(6)} %ge.59), kind=kLoop, calls=%fused_computation.175 | loop fusion | flops 1179648 | bytes 1312770 | tf_op jit(solution)/shard_map/convert_element_type | solution.py:119
  52.3 1.3 %collective-permute-start.6 = (bf16[256,512]{1,0:T(8,128)(2,1)S(1)}, bf16[256,512]{1,0:T(8,128)(2,1)S(1)}, u32[]{:S(2)}, u32[]{:S(2)}) collective-permute-start(bf16[256,512]{1,0:T(8,128)(2,1)S(1)} %fusion.78), channel_id=1, source_target_pairs={{0,16},{4,20},{8,24},{12,28},{1,17},{5,21},{9,25},{13,29},{2,18},{... | collective-permute-start | bytes 786440 | tf_op jit(solution)/shard_map/ppermute | solution.py:17
  53.6 0.7 slice_convert_fusion
  54.3 12.1 %collective-permute-done.6 = bf16[256,512]{1,0:T(8,128)(2,1)S(1)} collective-permute-done((bf16[256,512]{1,0:T(8,128)(2,1)S(1)}, bf16[256,512]{1,0:T(8,128)(2,1)S(1)}, u32[]{:S(2)}, u32[]{:S(2)}) %collective-permute-start.6) | collective-permute-done | bytes 262176 | tf_op jit(solution)/shard_map/ppermute | solution.py:17
  66.5 2.0 %multiply_reduce_fusion.3 = (f32[256]{0:T(256)S(1)}, f32[256,512]{1,0:T(8,128)S(1)}) fusion(f32[256,512]{1,0:T(8,128)} %bitcast.146, f32[256,256]{1,0:T(8,128)} %bitcast_multiply_fusion, bf16[256,512]{1,0:T(8,128)(2,1)S(1)} %collective-permute-done.6, f32[256]{0:T(256)S(1)} %bitcast.143, f32[256]{0:T(256)S(1)} %get-tuple-element.94, pred[]{:T(512)S(6)} %ge.59, ...), kind=kOutput, calls=%fused_computation.53 | convolution fusion | flops 202899200 | bytes 2100226 | tf_op jit(solution)/shard_map/dot_general | solution.py:263
  68.5 0.8 multiply_convert_fusion
  69.3 0.4 convolution_convert_fusion
  69.9 1.9 %collective-permute-done.7 = bf16[128,2048]{1,0:T(8,128)(2,1)S(1)} collective-permute-done((bf16[128,2048]{1,0:T(8,128)(2,1)S(1)}, bf16[128,2048]{1,0:T(8,128)(2,1)S(1)}, u32[]{:S(2)}, u32[]{:S(2)}) %collective-permute-start.7) | collective-permute-done | bytes 524320 | tf_op jit(solution)/shard_map/ppermute | solution.py:186
  71.7 0.4 convert_add_fusion
  72.2 1.6 %collective-permute-start.8 = (bf16[1,64,2048]{2,1,0:T(8,128)(2,1)S(1)}, bf16[1,64,2048]{2,1,0:T(8,128)(2,1)S(1)}, u32[]{:S(2)}, u32[]{:S(2)}) collective-permute-start(bf16[1,64,2048]{2,1,0:T(8,128)(2,1)S(1)} %fusion.24), channel_id=1, source_target_pairs={{0,2},{1,3},{2,0},{3,1},{4,6},{5,7},{6,4},{7,5},{8,10},{9,11},{10,... | collective-permute-start | bytes 786440 | tf_op jit(solution)/shard_map/ppermute | solution.py:197
  73.8 2.2 %fusion.4 = f32[1,1,256,512]{3,2,1,0:T(8,128)} fusion(bf16[256,512]{1,0:T(8,128)(2,1)S(1)} %collective-permute-done.6, f32[256]{0:T(256)S(1)} %get-tuple-element.93, pred[]{:T(512)S(6)} %ge.58, f32[256,512]{1,0:T(8,128)S(1)} %copy-done.2, bf16[257,512]{1,0:T(8,128)(2,1)S(1)} %copy-done.8, f32[256]{0:T(256)S(1)} %get-tuple-element.67, pred[]{:T(512)S(6)} %ge.60, ...), kind=kLoop, calls=%fused_computation.37 | loop fusion | flops 1572864 | bytes 1838083 | tf_op jit(solution)/shard_map/broadcast_in_dim | solution.py:272
  76.1 4.6 %collective-permute-done.8 = bf16[1,64,2048]{2,1,0:T(8,128)(2,1)S(1)} collective-permute-done((bf16[1,64,2048]{2,1,0:T(8,128)(2,1)S(1)}, bf16[1,64,2048]{2,1,0:T(8,128)(2,1)S(1)}, u32[]{:S(2)}, u32[]{:S(2)}) %collective-permute-start.8) | collective-permute-done | bytes 262176 | tf_op jit(solution)/shard_map/ppermute | solution.py:197
  80.6 0.8 fusion.6
  (75 shorter events, 2.6 us)
Async XLA Ops:
  0.6 68.7 %copy-start = (bf16[512,2048]{1,0:T(8,128)(2,1)S(1)}, bf16[512,2048]{1,0:T(8,128)(2,1)}, u32[]{:S(2)}) copy-start(bf16[512,2048]{1,0:T(8,128)(2,1)} %param.31) | copy-start | bytes 6291460
  0.6 11.7 %collective-permute-start = (bf16[64,2048]{1,0:T(8,128)(2,1)}, bf16[64,2048]{1,0:T(8,128)(2,1)S(1)}, u32[]{:S(2)}, u32[]{:S(2)}) collective-permute-start(bf16[64,2048]{1,0:T(8,128)(2,1)} %param.18), channel_id=1, source_target_pairs={{0,1},{1,0},{2,3},{3,2},{4,5},{5,4},{6,7},{7,6},{8,9},{9,8},{10,11... | collective-permute-start | bytes 786440 | tf_op jit(solution)/shard_map/ppermute | solution.py:151
  0.7 8.9 %collective-permute-start.1 = (bf16[64,2048]{1,0:T(8,128)(2,1)}, bf16[64,2048]{1,0:T(8,128)(2,1)S(1)}, u32[]{:S(2)}, u32[]{:S(2)}) collective-permute-start(bf16[64,2048]{1,0:T(8,128)(2,1)} %param.18), channel_id=1, source_target_pairs={{0,2},{1,3},{2,0},{3,1},{4,6},{5,7},{6,4},{7,5},{8,10},{9,11},{10,... | collective-permute-start | bytes 786440 | tf_op jit(solution)/shard_map/ppermute | solution.py:151
  9.6 2.8 %collective-permute-start.2 = (bf16[64,2048]{1,0:T(8,128)(2,1)S(1)}, bf16[64,2048]{1,0:T(8,128)(2,1)}, u32[]{:S(2)}, u32[]{:S(2)}) collective-permute-start(bf16[64,2048]{1,0:T(8,128)(2,1)S(1)} %collective-permute-done.1), channel_id=1, source_target_pairs={{0,1},{1,0},{2,3},{3,2},{4,5},{5,4},{6,7},{7,6},{8,9},{9,8},{10,11... | collective-permute-start | bytes 786440 | tf_op jit(solution)/shard_map/ppermute | solution.py:151
  12.4 2.0 %copy-start.16 = (bf16[2048,16]{0,1:T(8,128)(2,1)S(1)}, bf16[2048,16]{0,1:T(8,128)(2,1)}, u32[]{:S(2)}) copy-start(bf16[2048,16]{0,1:T(8,128)(2,1)} %param.26) | copy-start | bytes 196612
  12.4 2.0 %copy-start.17 = (bf16[16,256]{1,0:T(8,128)(2,1)S(1)}, bf16[16,256]{1,0:T(8,128)(2,1)}, u32[]{:S(2)}) copy-start(bf16[16,256]{1,0:T(8,128)(2,1)} %param.27) | copy-start | bytes 24580
  12.4 2.0 %copy-start.19 = (f32[256]{0:T(256)S(1)}, f32[256]{0:T(256)}, u32[]{:S(2)}) copy-start(f32[256]{0:T(256)} %param.28) | copy-start | bytes 3076
  12.4 0.7 copy-start.3
  17.1 2.7 %copy-start.9 = (f32[4,64,256]{2,1,0:T(8,128)}, f32[4,64,256]{2,1,0:T(8,128)S(1)}, u32[]{:S(2)}) copy-start(f32[4,64,256]{2,1,0:T(8,128)S(1)} %reduce_window_sum.23) | copy-start | bytes 786436
  17.1 2.0 %copy-start.14 = (bf16[2048,512]{1,0:T(8,128)(2,1)S(1)}, bf16[2048,512]{1,0:T(8,128)(2,1)}, u32[]{:S(2)}) copy-start(bf16[2048,512]{1,0:T(8,128)(2,1)} %param.22) | copy-start | bytes 6291460
  19.1 1.2 %copy-start.11 = (bf16[2048,256]{1,0:T(8,128)(2,1)S(1)}, bf16[2048,256]{1,0:T(8,128)(2,1)}, u32[]{:S(2)}) copy-start(bf16[2048,256]{1,0:T(8,128)(2,1)} %param.21) | copy-start | bytes 3145732
  20.8 7.8 %copy-start.10 = (f32[4,64,256]{2,1,0:T(8,128)S(1)}, f32[4,64,256]{2,1,0:T(8,128)}, u32[]{:S(2)}) copy-start(f32[4,64,256]{2,1,0:T(8,128)} %copy-done.9) | copy-start | bytes 786436
  21.5 6.4 %collective-permute-start.3 = (bf16[3,1024]{1,0:T(4,128)(2,1)S(1)}, bf16[3,1024]{1,0:T(4,128)(2,1)S(1)}, u32[]{:S(2)}, u32[]{:S(2)}) collective-permute-start(bf16[3,1024]{1,0:T(4,128)(2,1)S(1)} %get-tuple-element.59), channel_id=1, source_target_pairs={{0,4},{4,8},{8,12},{12,16},{16,20},{20,24},{24,28},{1,5},{5,9},{9,... | collective-permute-start | bytes 18440 | tf_op jit(solution)/shard_map/ppermute | solution.py:17
  28.6 1.1 %copy-start.13 = (f32[256,256]{1,0:T(8,128)}, f32[256,256]{1,0:T(8,128)S(1)}, u32[]{:S(2)}) copy-start(f32[256,256]{1,0:T(8,128)S(1)} %get-tuple-element.57) | copy-start | bytes 786436
  29.0 0.9 %copy-start.12 = (f32[256,512]{1,0:T(8,128)}, f32[256,512]{1,0:T(8,128)S(1)}, u32[]{:S(2)}) copy-start(f32[256,512]{1,0:T(8,128)S(1)} %multiply_reduce_fusion) | copy-start | bytes 1572868
  29.9 11.2 %copy-start.1 = (f32[256,512]{1,0:T(8,128)}, f32[256,512]{1,0:T(8,128)S(1)}, u32[]{:S(2)}) copy-start(f32[256,512]{1,0:T(8,128)S(1)} %get-tuple-element.64) | copy-start | bytes 1572868
  30.4 10.5 %collective-permute-start.4 = (bf16[257,512]{1,0:T(8,128)(2,1)S(1)}, bf16[257,512]{1,0:T(8,128)(2,1)S(1)}, u32[]{:S(2)}, u32[]{:S(2)}) collective-permute-start(bf16[257,512]{1,0:T(8,128)(2,1)S(1)} %pad_maximum_fusion.4), channel_id=1, source_target_pairs={{0,4},{4,8},{8,12},{12,16},{16,20},{20,24},{24,28},{1,5},{5,9},{9,... | collective-permute-start | bytes 789512 | tf_op jit(solution)/shard_map/ppermute | solution.py:17
  40.9 0.9 %copy-start.7 = (bf16[257,512]{1,0:T(8,128)(2,1)}, bf16[257,512]{1,0:T(8,128)(2,1)S(1)}, u32[]{:S(2)}) copy-start(bf16[257,512]{1,0:T(8,128)(2,1)S(1)} %collective-permute-done.4) | copy-start | bytes 789508
  41.8 9.1 %collective-permute-start.5 = (bf16[257,512]{1,0:T(8,128)(2,1)}, bf16[257,512]{1,0:T(8,128)(2,1)}, u32[]{:S(2)}, u32[]{:S(2)}) collective-permute-start(bf16[257,512]{1,0:T(8,128)(2,1)} %pad_maximum_fusion.5), channel_id=1, source_target_pairs={{0,8},{4,12},{8,16},{12,20},{16,24},{20,28},{1,9},{5,13},{9,17},{1... | collective-permute-start | bytes 789512 | tf_op jit(solution)/shard_map/ppermute | solution.py:17
  45.8 22.6 %copy-start.15 = (bf16[2048,512]{1,0:T(8,128)(2,1)S(1)}, bf16[2048,512]{1,0:T(8,128)(2,1)}, u32[]{:S(2)}) copy-start(bf16[2048,512]{1,0:T(8,128)(2,1)} %param.29) | copy-start | bytes 6291460
  45.8 22.6 %copy-start.18 = (f32[512]{0:T(512)S(1)}, f32[512]{0:T(512)}, u32[]{:S(2)}) copy-start(f32[512]{0:T(512)} %param.30) | copy-start | bytes 6148
  52.3 14.1 %collective-permute-start.6 = (bf16[256,512]{1,0:T(8,128)(2,1)S(1)}, bf16[256,512]{1,0:T(8,128)(2,1)S(1)}, u32[]{:S(2)}, u32[]{:S(2)}) collective-permute-start(bf16[256,512]{1,0:T(8,128)(2,1)S(1)} %fusion.78), channel_id=1, source_target_pairs={{0,16},{4,20},{8,24},{12,28},{1,17},{5,21},{9,25},{13,29},{2,18},{... | collective-permute-start | bytes 786440 | tf_op jit(solution)/shard_map/ppermute | solution.py:17
  69.7 2.0 %collective-permute-start.7 = (bf16[128,2048]{1,0:T(8,128)(2,1)S(1)}, bf16[128,2048]{1,0:T(8,128)(2,1)S(1)}, u32[]{:S(2)}, u32[]{:S(2)}) collective-permute-start(bf16[128,2048]{1,0:T(8,128)(2,1)S(1)} %convolution_convert_fusion), channel_id=1, source_target_pairs={{0,1},{1,0},{2,3},{3,2},{4,5},{5,4},{6,7},{7,6},{8,9},{9,8},{10,11... | collective-permute-start | bytes 1572872 | tf_op jit(solution)/shard_map/ppermute | solution.py:186
  71.7 2.1 %copy-start.2 = (f32[256,512]{1,0:T(8,128)S(1)}, f32[256,512]{1,0:T(8,128)}, u32[]{:S(2)}) copy-start(f32[256,512]{1,0:T(8,128)} %copy-done.1) | copy-start | bytes 1572868
  71.7 2.1 %copy-start.8 = (bf16[257,512]{1,0:T(8,128)(2,1)S(1)}, bf16[257,512]{1,0:T(8,128)(2,1)}, u32[]{:S(2)}) copy-start(bf16[257,512]{1,0:T(8,128)(2,1)} %copy-done.7) | copy-start | bytes 789508
  72.2 8.4 %collective-permute-start.8 = (bf16[1,64,2048]{2,1,0:T(8,128)(2,1)S(1)}, bf16[1,64,2048]{2,1,0:T(8,128)(2,1)S(1)}, u32[]{:S(2)}, u32[]{:S(2)}) collective-permute-start(bf16[1,64,2048]{2,1,0:T(8,128)(2,1)S(1)} %fusion.24), channel_id=1, source_target_pairs={{0,2},{1,3},{2,0},{3,1},{4,6},{5,7},{6,4},{7,5},{8,10},{9,11},{10,... | collective-permute-start | bytes 786440 | tf_op jit(solution)/shard_map/ppermute | solution.py:197

commit v12 on v11

--- a/solution.py
+++ b/solution.py
@@ -152,14 +152,17 @@
             order = order + [flip ^ mask for flip in order]
             mask //= 2
 
-    def ordered(shift):
-        if count & (count - 1):
-            picks = [order.index((index - shift) % count) for index in range(count)]
-        else:
-            picks = [order.index(shift ^ index) for index in range(count)]
-        return jnp.concatenate([received[pick] for pick in picks])
-
-    return lax.switch(place, [functools.partial(ordered, shift) for shift in range(count)])
+    block = rows.shape[0]
+    lookup = jnp.asarray([order.index(index) for index in range(count)], jnp.int32)
+    target = jnp.arange(count * block, dtype=jnp.int32)
+    if count & (count - 1):
+        source_block = lookup[(target // block - place) % count]
+    else:
+        source_block = lookup[jnp.bitwise_xor(target // block, place)]
+    source = source_block * block + target % block
+    choose = (source[:, None] == target[None, :]).astype(rows.dtype)
+    unordered = jnp.concatenate(received)
+    return jnp.dot(choose, unordered, preferred_element_type=jnp.float32).astype(rows.dtype)
 
 
 def scatter_sum(gated, weight, axis):

time: 82 us -> 84.4 us (1.029)
  matrix products: 13.9 us -> 17.1 us
    dot_general x0 -> x1, matrix products: none -> 1.59 us  [gather_rows(): jnp.dot(choose, unordered, preferred_element_type=jnp.float32)]
    concatenate x1 -> x0, other arithmetic: 1.18 us -> none  [ordered(): return jnp.concatenate([received[pick] for pick in picks])]
    dot_general x1, matrix products: 0.44 us -> 1.49 us  [scatter_sum(): jnp.dot(kept, weight, preferred_element_type=jnp.float32)]
  transfers between devices with their start and end apart: 9 -> 9, of which waited for: 7 -> 7; matrix products, arithmetic and copies ran while one was open for 18% -> 19% of each run, Pallas kernels for 0% -> 0%
where the time goes in v12:
time: 84.4 us; the launch traced here: 83.9 us
  waiting for transfers between devices  34.7 us (41%)
  matrix products  17.1 us (20%)
  other arithmetic  15.9 us (19%)
  starting transfers between devices  11.6 us (14%)
  local copies, waits for them, and re-layouts  3.55 us (4%)
  between operations  1 us (1%)
    ppermute x4, waiting for transfers between devices, shifted(): lax.ppermute(value, axis, [(source, source + steps) for source in range(i...  24.7 us
    ppermute x4, starting transfers between devices, shifted(): lax.ppermute(value, axis, [(source, source + steps) for source in range(i...  8.47 us
    ppermute x1, waiting for transfers between devices, scatter_sum(): lax.ppermute(outgoing, axis, [(source, source ^ mask) for source in range...  4.59 us
    dot_general x4, matrix products, project(): jnp.dot(gathered, weight, preferred_element_type=jnp.float32)  3.73 us
    ppermute x3, waiting for transfers between devices, gather_rows(): lax.ppermute(block, axis, pairs)  3.16 us
    dot_general x1, matrix products, segment_parts(): jnp.einsum('bac,bcv->bav', scores, head_values, preferred_element_type=jn...  2.57 us
    dot_general x3, matrix products, segment_parts(): jnp.dot(lifted_intact[block], memory, precision=HIGH_PRECISION)  2.46 us
    ppermute x1, waiting for transfers between devices, scatter_sum(): lax.ppermute(outgoing, axis, [(source, source ^ 1) for source in range(co...  2.25 us
  transfers between devices with their start and end apart: 9, of which 7 were waited for; matrix products, arithmetic and copies ran while one was open for 19% of the time, Pallas kernels for 0%

profile of v12, /device:TPU:24, one launch (start us, length us, event | category | flops | bytes accessed | tf_op | source)
XLA Modules:
  0.0 83.9 jit_solution(16196168503412170419)
XLA Ops:
  0.6 1.6 %collective-permute-start = (bf16[64,2048]{1,0:T(8,128)(2,1)}, bf16[64,2048]{1,0:T(8,128)(2,1)S(1)}, u32[]{:S(2)}, u32[]{:S(2)}) collective-permute-start(bf16[64,2048]{1,0:T(8,128)(2,1)} %param.15), channel_id=1, source_target_pairs={{0,2},{1,3},{2,0},{3,1},{4,6},{5,7},{6,4},{7,5},{8,10},{9,11},{10,... | collective-permute-start | bytes 786440 | tf_op jit(solution)/shard_map/ppermute | solution.py:151
  2.2 0.8 select_reduce_fusion.1
  3.2 0.6 slice.181
  3.8 0.6 iota_compare_fusion.2
  4.9 0.7 slice_compare_fusion
  5.8 3.2 %collective-permute-done = bf16[64,2048]{1,0:T(8,128)(2,1)S(1)} collective-permute-done((bf16[64,2048]{1,0:T(8,128)(2,1)}, bf16[64,2048]{1,0:T(8,128)(2,1)S(1)}, u32[]{:S(2)}, u32[]{:S(2)}) %collective-permute-start) | collective-permute-done | bytes 262176 | tf_op jit(solution)/shard_map/ppermute | solution.py:151
  9.0 0.6 reshape.287
  9.6 0.7 convert_element_type.182
  10.3 0.7 convert_element_type.193
  11.0 0.7 convert_element_type.199
  11.7 0.5 pad.16.clone
  12.3 0.7 copy-done.11
  13.0 1.6 %convolution_convert_fusion = bf16[256,2048]{1,0:T(8,128)(2,1)S(1)} fusion(bf16[64,2048]{1,0:T(8,128)(2,1)} %collective-permute-done.2, bf16[64,2048]{1,0:T(8,128)(2,1)} %copy-done.11, bf16[64,2048]{1,0:T(8,128)(2,1)S(1)} %collective-permute-done, bf16[64,2048]{1,0:T(8,128)(2,1)} %param.15, s32[256]{0:T(256)S(1)} %fusion.81), kind=kOutput, calls=%fused_computation | convolution fusion | flops 273219584 | bytes 2098176 | tf_op jit(solution)/shard_map/dot_general | solution.py:165
  14.6 1.5 %fusion.33 = f32[256,256]{1,0:T(8,128)} fusion(bf16[16,256]{1,0:T(8,128)(2,1)S(1)} %copy-done.13, bf16[256,2048]{1,0:T(8,128)(2,1)S(1)} %convolution_convert_fusion, bf16[2048,16]{0,1:T(8,128)(2,1)S(1)} %copy-done.12, f32[256]{0:T(256)S(1)} %copy-done.15), kind=kOutput, calls=%fused_computation.80 | convolution fusion | flops 19533824 | bytes 1385472 | tf_op jit(solution)/shard_map/dot_general | solution.py:258
  16.1 1.2 %reduce_window_sum.23 = f32[4,64,256]{2,1,0:T(8,128)S(1)} reduce-window(f32[4,64,256]{2,1,0:T(8,128)} %bitcast.129, f32[]{:T(128)} %constant.103.clone.1), window={size=1x64x1 pad=0_0x63_0x0_0}, to_apply=%region_4.5 | reduce-window | flops 4128768 | bytes 524292 | tf_op jit(solution)/shard_map/jit(cumsum)/reduce_window_sum | solution.py:49
  17.3 1.8 %convolution_convert_fusion.6 = bf16[256,256]{1,0:T(8,128)(2,1)S(1)} fusion(bf16[256,2048]{1,0:T(8,128)(2,1)S(1)} %convolution_convert_fusion, bf16[2048,256]{1,0:T(8,128)(2,1)} %param.17), kind=kOutput, calls=%fused_computation.13 | convolution fusion | flops 268500992 | bytes 2228224 | tf_op jit(solution)/shard_map/dot_general | solution.py:228
  19.2 0.7 convolution_convert_fusion.4
  19.9 0.5 copy-done.3
  20.4 0.4 convolution_convert_fusion.5
  20.9 0.7 select_bitcast_fusion
  21.6 3.4 %collective-permute-start.3 = (bf16[3,1024]{1,0:T(4,128)(2,1)S(1)}, bf16[3,1024]{1,0:T(4,128)(2,1)S(1)}, u32[]{:S(2)}, u32[]{:S(2)}) collective-permute-start(bf16[3,1024]{1,0:T(4,128)(2,1)S(1)} %get-tuple-element.6), channel_id=1, source_target_pairs={{0,4},{4,8},{8,12},{12,16},{16,20},{20,24},{24,28},{1,5},{5,9},{9,... | collective-permute-start | bytes 18440 | tf_op jit(solution)/shard_map/ppermute | solution.py:17
  25.1 2.8 %collective-permute-done.3 = bf16[3,1024]{1,0:T(4,128)(2,1)S(1)} collective-permute-done((bf16[3,1024]{1,0:T(4,128)(2,1)S(1)}, bf16[3,1024]{1,0:T(4,128)(2,1)S(1)}, u32[]{:S(2)}, u32[]{:S(2)}) %collective-permute-start.3) | collective-permute-done | bytes 6176 | tf_op jit(solution)/shard_map/ppermute | solution.py:17
  29.1 0.6 fusion.56
  30.0 0.4 convolution_bitcast_fusion.1
  30.4 2.5 %collective-permute-start.4 = (bf16[257,512]{1,0:T(8,128)(2,1)S(1)}, bf16[257,512]{1,0:T(8,128)(2,1)S(1)}, u32[]{:S(2)}, u32[]{:S(2)}) collective-permute-start(bf16[257,512]{1,0:T(8,128)(2,1)S(1)} %pad_maximum_fusion), channel_id=1, source_target_pairs={{0,4},{4,8},{8,12},{12,16},{16,20},{20,24},{24,28},{1,5},{5,9},{9,... | collective-permute-start | bytes 789512 | tf_op jit(solution)/shard_map/ppermute | solution.py:17
  33.0 0.8 bitcast_multiply_fusion
  33.8 1.0 %convolution_bitcast_fusion.2 = f32[1,64,512]{2,1,0:T(8,128)} fusion(f32[4,256,512]{2,1,0:T(8,128)S(1)} %fusion.56, f32[256]{0:T(256)S(1)} %get-tuple-element.42, f32[4,64,256]{2,1,0:T(8,128)S(1)} %get-tuple-element.25), kind=kOutput, calls=%fused_computation.16 | convolution fusion | flops 50462720 | bytes 721920 | tf_op jit(solution)/shard_map/dot_general | solution.py:80
  34.8 1.1 %convolution_bitcast_fusion = f32[1,64,512]{2,1,0:T(8,128)} fusion(f32[4,256,512]{2,1,0:T(8,128)S(1)} %fusion.56, f32[256]{0:T(256)S(1)} %bitcast.138, f32[4,64,256]{2,1,0:T(8,128)S(1)} %get-tuple-element.25, f32[256]{0:T(256)S(1)} %bitcast.135, f32[256]{0:T(256)S(1)} %get-tuple-element.42), kind=kOutput, calls=%fused_computation.14 | convolution fusion | flops 50987008 | bytes 1772544 | tf_op jit(solution)/shard_map/dot_general | solution.py:80
  35.8 5.1 %collective-permute-done.4 = bf16[257,512]{1,0:T(8,128)(2,1)S(1)} collective-permute-done((bf16[257,512]{1,0:T(8,128)(2,1)S(1)}, bf16[257,512]{1,0:T(8,128)(2,1)S(1)}, u32[]{:S(2)}, u32[]{:S(2)}) %collective-permute-start.4) | collective-permute-done | bytes 263200 | tf_op jit(solution)/shard_map/ppermute | solution.py:17
  41.0 0.5 subtract_convert_fusion
  41.7 0.7 pad_maximum_fusion.1
  42.5 1.3 %collective-permute-start.5 = (bf16[257,512]{1,0:T(8,128)(2,1)}, bf16[257,512]{1,0:T(8,128)(2,1)}, u32[]{:S(2)}, u32[]{:S(2)}) collective-permute-start(bf16[257,512]{1,0:T(8,128)(2,1)} %pad_maximum_fusion.1), channel_id=1, source_target_pairs={{0,8},{4,12},{8,16},{12,20},{16,24},{20,28},{1,9},{5,13},{9,17},{1... | collective-permute-start | bytes 789512 | tf_op jit(solution)/shard_map/ppermute | solution.py:17
  43.8 2.6 %convolution_add_fusion = f32[4,64,512]{2,1,0:T(8,128)} fusion(f32[1,64,512]{2,1,0:T(8,128)} %convolution_bitcast_fusion, f32[1,64,512]{2,1,0:T(8,128)S(1)} %convolution_bitcast_fusion.1, f32[1,64,512]{2,1,0:T(8,128)} %convolution_bitcast_fusion.2, f32[4]{0:T(128)} %pad.16.clone, f32[4,64,256]{2,1,0:T(8,128)S(1)} %reduce_window_sum.23, ...), kind=kOutput, calls=%fused_computation.5 | convolution fusion | flops 27525120 | bytes 2233360 | tf_op jit(solution)/shard_map/bac,bcv->bav/dot_general | solution.py:71
  46.3 5.2 %collective-permute-done.5 = bf16[257,512]{1,0:T(8,128)(2,1)} collective-permute-done((bf16[257,512]{1,0:T(8,128)(2,1)}, bf16[257,512]{1,0:T(8,128)(2,1)}, u32[]{:S(2)}, u32[]{:S(2)}) %collective-permute-start.5) | collective-permute-done | bytes 263200 | tf_op jit(solution)/shard_map/ppermute | solution.py:17
  51.5 1.2 %fusion.90 = bf16[256,512]{1,0:T(8,128)(2,1)S(1)} fusion(f32[256,512]{1,0:T(8,128)S(1)} %get-tuple-element.11, bf16[257,512]{1,0:T(8,128)(2,1)S(1)} %collective-permute-done.4, f32[256]{0:T(256)S(1)} %get-tuple-element.14, pred[]{:T(512)S(6)} %ge.60, bf16[257,512]{1,0:T(8,128)(2,1)} %collective-permute-done.5, f32[256]{0:T(256)} %get-tuple-element.9, ...), kind=kLoop, calls=%fused_computation.194 | loop fusion | flops 1179648 | bytes 1312770 | tf_op jit(solution)/shard_map/convert_element_type | solution.py:119
  52.7 1.3 %collective-permute-start.6 = (bf16[256,512]{1,0:T(8,128)(2,1)S(1)}, bf16[256,512]{1,0:T(8,128)(2,1)S(1)}, u32[]{:S(2)}, u32[]{:S(2)}) collective-permute-start(bf16[256,512]{1,0:T(8,128)(2,1)S(1)} %fusion.90), channel_id=1, source_target_pairs={{0,16},{4,20},{8,24},{12,28},{1,17},{5,21},{9,25},{13,29},{2,18},{... | collective-permute-start | bytes 786440 | tf_op jit(solution)/shard_map/ppermute | solution.py:17
  54.0 0.7 slice_convert_fusion
  54.7 0.6 multiply_select_fusion
  55.4 11.5 %collective-permute-done.6 = bf16[256,512]{1,0:T(8,128)(2,1)S(1)} collective-permute-done((bf16[256,512]{1,0:T(8,128)(2,1)S(1)}, bf16[256,512]{1,0:T(8,128)(2,1)S(1)}, u32[]{:S(2)}, u32[]{:S(2)}) %collective-permute-start.6) | collective-permute-done | bytes 262176 | tf_op jit(solution)/shard_map/ppermute | solution.py:17
  66.9 1.9 %multiply_reduce_fusion.3 = (f32[256]{0:T(256)S(1)}, f32[256,512]{1,0:T(8,128)S(1)}) fusion(f32[256,512]{1,0:T(8,128)} %bitcast.148, f32[256,256]{1,0:T(8,128)} %bitcast_multiply_fusion, bf16[256,512]{1,0:T(8,128)(2,1)S(1)} %collective-permute-done.6, f32[256]{0:T(256)} %bitcast.144, f32[256]{0:T(256)S(1)} %get-tuple-element.41, pred[]{:T(512)S(6)} %ge.59, ...), kind=kOutput, calls=%fused_computation.57 | convolution fusion | flops 202899200 | bytes 2100226 | tf_op jit(solution)/shard_map/dot_general | solution.py:266
  68.8 0.8 multiply_convert_fusion
  69.6 1.2 %convolution_convert_fusion.1 = bf16[128,2048]{1,0:T(8,128)(2,1)} fusion(bf16[512,2048]{1,0:T(8,128)(2,1)S(1)} %copy-done, bf16[64,512]{1,0:T(8,128)(2,1)S(1)} %get-tuple-element.23, bf16[64,512]{1,0:T(8,128)(2,1)S(1)} %get-tuple-element.22), kind=kOutput, calls=%fused_computation.1 | convolution fusion | flops 268959744 | bytes 2752512 | tf_op jit(solution)/shard_map/dot_general | solution.py:188
  70.9 2.2 %collective-permute-done.7 = bf16[128,2048]{1,0:T(8,128)(2,1)} collective-permute-done((bf16[128,2048]{1,0:T(8,128)(2,1)}, bf16[128,2048]{1,0:T(8,128)(2,1)}, u32[]{:S(2)}, u32[]{:S(2)}) %collective-permute-start.7) | collective-permute-done | bytes 524320 | tf_op jit(solution)/shard_map/ppermute | solution.py:189
  73.1 1.5 %convert_add_fusion = f32[128,2048]{1,0:T(8,128)S(1)} fusion(bf16[128,2048]{1,0:T(8,128)(2,1)} %collective-permute-done.7, bf16[512,2048]{1,0:T(8,128)(2,1)S(1)} %copy-done, bf16[64,512]{1,0:T(8,128)(2,1)S(1)} %get-tuple-element.21, bf16[64,512]{1,0:T(8,128)(2,1)S(1)} %get-tuple-element.20), kind=kOutput, calls=%fused_computation.27 | convolution fusion | flops 269746176 | bytes 3801088 | tf_op jit(solution)/shard_map/dot_general | solution.py:191
  74.7 1.6 %collective-permute-start.8 = (bf16[1,64,2048]{2,1,0:T(8,128)(2,1)S(1)}, bf16[1,64,2048]{2,1,0:T(8,128)(2,1)S(1)}, u32[]{:S(2)}, u32[]{:S(2)}) collective-permute-start(bf16[1,64,2048]{2,1,0:T(8,128)(2,1)S(1)} %fusion.31), channel_id=1, source_target_pairs={{0,2},{1,3},{2,0},{3,1},{4,6},{5,7},{6,4},{7,5},{8,10},{9,11},{10,... | collective-permute-start | bytes 786440 | tf_op jit(solution)/shard_map/ppermute | solution.py:200
  76.3 2.2 %fusion.11 = f32[1,1,256,512]{3,2,1,0:T(8,128)} fusion(bf16[256,512]{1,0:T(8,128)(2,1)S(1)} %collective-permute-done.6, f32[256]{0:T(256)S(1)} %get-tuple-element.40, pred[]{:T(512)S(6)} %ge.58, f32[256,512]{1,0:T(8,128)S(1)} %get-tuple-element.11, bf16[257,512]{1,0:T(8,128)(2,1)S(1)} %collective-permute-done.4, f32[256]{0:T(256)S(1)} %get-tuple-element.14, ...), kind=kLoop, calls=%fused_computation.41 | loop fusion | flops 1572864 | bytes 1838083 | tf_op jit(solution)/shard_map/broadcast_in_dim | solution.py:275
  78.5 4.6 %collective-permute-done.8 = bf16[1,64,2048]{2,1,0:T(8,128)(2,1)S(1)} collective-permute-done((bf16[1,64,2048]{2,1,0:T(8,128)(2,1)S(1)}, bf16[1,64,2048]{2,1,0:T(8,128)(2,1)S(1)}, u32[]{:S(2)}, u32[]{:S(2)}) %collective-permute-start.8) | collective-permute-done | bytes 262176 | tf_op jit(solution)/shard_map/ppermute | solution.py:200
  83.1 0.8 fusion.13
  (74 shorter events, 2.9 us)
Async XLA Ops:
  0.6 69.0 %copy-start = (bf16[512,2048]{1,0:T(8,128)(2,1)S(1)}, bf16[512,2048]{1,0:T(8,128)(2,1)}, u32[]{:S(2)}) copy-start(bf16[512,2048]{1,0:T(8,128)(2,1)} %param.28) | copy-start | bytes 6291460
  0.6 8.3 %collective-permute-start = (bf16[64,2048]{1,0:T(8,128)(2,1)}, bf16[64,2048]{1,0:T(8,128)(2,1)S(1)}, u32[]{:S(2)}, u32[]{:S(2)}) collective-permute-start(bf16[64,2048]{1,0:T(8,128)(2,1)} %param.15), channel_id=1, source_target_pairs={{0,2},{1,3},{2,0},{3,1},{4,6},{5,7},{6,4},{7,5},{8,10},{9,11},{10,... | collective-permute-start | bytes 786440 | tf_op jit(solution)/shard_map/ppermute | solution.py:151
  2.2 10.0 %collective-permute-start.1 = (bf16[64,2048]{1,0:T(8,128)(2,1)}, bf16[64,2048]{1,0:T(8,128)(2,1)S(1)}, u32[]{:S(2)}, u32[]{:S(2)}) collective-permute-start(bf16[64,2048]{1,0:T(8,128)(2,1)} %param.15), channel_id=1, source_target_pairs={{0,1},{1,0},{2,3},{3,2},{4,5},{5,4},{6,7},{7,6},{8,9},{9,8},{10,11... | collective-permute-start | bytes 786440 | tf_op jit(solution)/shard_map/ppermute | solution.py:151
  9.0 4.0 %collective-permute-start.2 = (bf16[64,2048]{1,0:T(8,128)(2,1)S(1)}, bf16[64,2048]{1,0:T(8,128)(2,1)}, u32[]{:S(2)}, u32[]{:S(2)}) collective-permute-start(bf16[64,2048]{1,0:T(8,128)(2,1)S(1)} %collective-permute-done), channel_id=1, source_target_pairs={{0,1},{1,0},{2,3},{3,2},{4,5},{5,4},{6,7},{7,6},{8,9},{9,8},{10,11... | collective-permute-start | bytes 786440 | tf_op jit(solution)/shard_map/ppermute | solution.py:151
  12.2 2.3 %copy-start.12 = (bf16[2048,16]{0,1:T(8,128)(2,1)S(1)}, bf16[2048,16]{0,1:T(8,128)(2,1)}, u32[]{:S(2)}) copy-start(bf16[2048,16]{0,1:T(8,128)(2,1)} %param.23) | copy-start | bytes 196612
  12.3 2.3 %copy-start.13 = (bf16[16,256]{1,0:T(8,128)(2,1)S(1)}, bf16[16,256]{1,0:T(8,128)(2,1)}, u32[]{:S(2)}) copy-start(bf16[16,256]{1,0:T(8,128)(2,1)} %param.24) | copy-start | bytes 24580
  12.3 2.3 %copy-start.15 = (f32[256]{0:T(256)S(1)}, f32[256]{0:T(256)}, u32[]{:S(2)}) copy-start(f32[256]{0:T(256)} %param.25) | copy-start | bytes 3076
  12.3 0.7 copy-start.11
  14.6 5.3 %copy-start.1 = (bf16[256,2048]{1,0:T(8,128)(2,1)}, bf16[256,2048]{1,0:T(8,128)(2,1)S(1)}, u32[]{:S(2)}) copy-start(bf16[256,2048]{1,0:T(8,128)(2,1)S(1)} %convolution_convert_fusion) | copy-start | bytes 3145732
  17.3 1.9 %copy-start.9 = (bf16[2048,512]{1,0:T(8,128)(2,1)S(1)}, bf16[2048,512]{1,0:T(8,128)(2,1)}, u32[]{:S(2)}) copy-start(bf16[2048,512]{1,0:T(8,128)(2,1)} %param.19) | copy-start | bytes 6291460
  19.2 1.2 %copy-start.3 = (bf16[2048,256]{1,0:T(8,128)(2,1)S(1)}, bf16[2048,256]{1,0:T(8,128)(2,1)}, u32[]{:S(2)}) copy-start(bf16[2048,256]{1,0:T(8,128)(2,1)} %param.18) | copy-start | bytes 3145732
  21.6 6.4 %collective-permute-start.3 = (bf16[3,1024]{1,0:T(4,128)(2,1)S(1)}, bf16[3,1024]{1,0:T(4,128)(2,1)S(1)}, u32[]{:S(2)}, u32[]{:S(2)}) collective-permute-start(bf16[3,1024]{1,0:T(4,128)(2,1)S(1)} %get-tuple-element.6), channel_id=1, source_target_pairs={{0,4},{4,8},{8,12},{12,16},{16,20},{20,24},{24,28},{1,5},{5,9},{9,... | collective-permute-start | bytes 18440 | tf_op jit(solution)/shard_map/ppermute | solution.py:17
  28.7 1.1 %copy-start.5 = (f32[256,256]{1,0:T(8,128)}, f32[256,256]{1,0:T(8,128)S(1)}, u32[]{:S(2)}) copy-start(f32[256,256]{1,0:T(8,128)S(1)} %get-tuple-element.4) | copy-start | bytes 786436
  29.1 13.3 %copy-start.4 = (f32[256,512]{1,0:T(8,128)}, f32[256,512]{1,0:T(8,128)S(1)}, u32[]{:S(2)}) copy-start(f32[256,512]{1,0:T(8,128)S(1)} %multiply_reduce_fusion) | copy-start | bytes 1572868
  29.8 3.2 %copy-start.8 = (f32[256]{0:T(256)S(1)}, f32[256]{0:T(256)}, u32[]{:S(2)}) copy-start(f32[256]{0:T(256)} %reshape.287) | copy-start | bytes 3076
  30.4 10.5 %collective-permute-start.4 = (bf16[257,512]{1,0:T(8,128)(2,1)S(1)}, bf16[257,512]{1,0:T(8,128)(2,1)S(1)}, u32[]{:S(2)}, u32[]{:S(2)}) collective-permute-start(bf16[257,512]{1,0:T(8,128)(2,1)S(1)} %pad_maximum_fusion), channel_id=1, source_target_pairs={{0,4},{4,8},{8,12},{12,16},{16,20},{20,24},{24,28},{1,5},{5,9},{9,... | collective-permute-start | bytes 789512 | tf_op jit(solution)/shard_map/ppermute | solution.py:17
  41.0 0.6 copy-start.7
  42.5 9.1 %collective-permute-start.5 = (bf16[257,512]{1,0:T(8,128)(2,1)}, bf16[257,512]{1,0:T(8,128)(2,1)}, u32[]{:S(2)}, u32[]{:S(2)}) collective-permute-start(bf16[257,512]{1,0:T(8,128)(2,1)} %pad_maximum_fusion.1), channel_id=1, source_target_pairs={{0,8},{4,12},{8,16},{12,20},{16,24},{20,28},{1,9},{5,13},{9,17},{1... | collective-permute-start | bytes 789512 | tf_op jit(solution)/shard_map/ppermute | solution.py:17
  46.3 22.5 %copy-start.2 = (bf16[256,2048]{1,0:T(8,128)(2,1)S(1)}, bf16[256,2048]{1,0:T(8,128)(2,1)}, u32[]{:S(2)}) copy-start(bf16[256,2048]{1,0:T(8,128)(2,1)} %copy-done.1) | copy-start | bytes 3145732
  46.3 22.5 %copy-start.10 = (bf16[2048,512]{1,0:T(8,128)(2,1)S(1)}, bf16[2048,512]{1,0:T(8,128)(2,1)}, u32[]{:S(2)}) copy-start(bf16[2048,512]{1,0:T(8,128)(2,1)} %param.26) | copy-start | bytes 6291460
  46.3 22.5 %copy-start.14 = (f32[512]{0:T(512)S(1)}, f32[512]{0:T(512)}, u32[]{:S(2)}) copy-start(f32[512]{0:T(512)} %param.27) | copy-start | bytes 6148
  52.7 14.1 %collective-permute-start.6 = (bf16[256,512]{1,0:T(8,128)(2,1)S(1)}, bf16[256,512]{1,0:T(8,128)(2,1)S(1)}, u32[]{:S(2)}, u32[]{:S(2)}) collective-permute-start(bf16[256,512]{1,0:T(8,128)(2,1)S(1)} %fusion.90), channel_id=1, source_target_pairs={{0,16},{4,20},{8,24},{12,28},{1,17},{5,21},{9,25},{13,29},{2,18},{... | collective-permute-start | bytes 786440 | tf_op jit(solution)/shard_map/ppermute | solution.py:17
  70.9 2.3 %collective-permute-start.7 = (bf16[128,2048]{1,0:T(8,128)(2,1)}, bf16[128,2048]{1,0:T(8,128)(2,1)}, u32[]{:S(2)}, u32[]{:S(2)}) collective-permute-start(bf16[128,2048]{1,0:T(8,128)(2,1)} %convolution_convert_fusion.1), channel_id=1, source_target_pairs={{0,1},{1,0},{2,3},{3,2},{4,5},{5,4},{6,7},{7,6},{8,9},{9,8},{10,11... | collective-permute-start | bytes 1572872 | tf_op jit(solution)/shard_map/ppermute | solution.py:189
  73.1 3.1 %copy-start.6 = (f32[256]{0:T(256)S(1)}, f32[256]{0:T(256)}, u32[]{:S(2)}) copy-start(f32[256]{0:T(256)} %get-tuple-element.9) | copy-start | bytes 3076
  74.7 8.4 %collective-permute-start.8 = (bf16[1,64,2048]{2,1,0:T(8,128)(2,1)S(1)}, bf16[1,64,2048]{2,1,0:T(8,128)(2,1)S(1)}, u32[]{:S(2)}, u32[]{:S(2)}) collective-permute-start(bf16[1,64,2048]{2,1,0:T(8,128)(2,1)S(1)} %fusion.31), channel_id=1, source_target_pairs={{0,2},{1,3},{2,0},{3,1},{4,6},{5,7},{6,4},{7,5},{8,10},{9,11},{10,... | collective-permute-start | bytes 786440 | tf_op jit(solution)/shard_map/ppermute | solution.py:200

commit v13 on v10

--- a/solution.py
+++ b/solution.py
@@ -187,7 +187,9 @@
     outgoing = jnp.dot(outgoing, weight, preferred_element_type=jnp.float32).astype(jnp.bfloat16)
     incoming = lax.ppermute(outgoing, axis, [(source, source ^ 1) for source in range(count)])
     kept = jnp.concatenate([jnp.where(odd, high, low) for low, high in pairs])
-    kept = jnp.dot(kept, weight, preferred_element_type=jnp.float32).astype(jnp.bfloat16)
+    kept = lax.optimization_barrier(
+        jnp.dot(kept, weight, preferred_element_type=jnp.float32).astype(jnp.bfloat16)
+    )
     summed = kept.astype(jnp.float32) + incoming.astype(jnp.float32)
     held = list(jnp.split(summed, len(pairs)))
     mask = 2
@@ -229,7 +231,7 @@
     raw_query = project(query_weight)
     raw_key = project(key_weight)
     raw_value = project(value_weight)
-    gate_values = project(gate_weight)
+    gate_values = lax.optimization_barrier(project(gate_weight))
     low_rank = project(decay_down)
     row_count = raw_query.shape[0]
     key_width = raw_query.shape[1]

time: 82.3 us -> 84.9 us (1.032)
  other arithmetic: 16.9 us -> 19.3 us
  matrix products: 15 us -> 16.8 us
  waiting for transfers between devices: 32.8 us -> 31.6 us
    dot_general x4, matrix products: 3.74 us -> 5.98 us  [project(): jnp.dot(gathered, weight, preferred_element_type=jnp.float32)]
    add x0 -> x1, other arithmetic: none -> 1.17 us  [scatter_sum(): summed = kept.astype(jnp.float32) + incoming.astype(jnp.float32)]
    dot_general x1, matrix products: 1.56 us -> 0.44 us  [scatter_sum(): jnp.dot(kept, weight, preferred_element_type=jnp.float32)]
  transfers between devices with their start and end apart: 8 -> 8, of which waited for: 8 -> 8; matrix products, arithmetic and copies ran while one was open for 18% -> 20% of each run, Pallas kernels for 0% -> 0%
where the time goes in v13:
time: 84.9 us; the launch traced here: 84.2 us
  waiting for transfers between devices  31.6 us (37%)
  other arithmetic  19.3 us (23%)
  matrix products  16.8 us (20%)
  starting transfers between devices  11.7 us (14%)
  local copies, waits for them, and re-layouts  3.8 us (4%)
  between operations  1.04 us (1%)
    ppermute x4, waiting for transfers between devices, shifted(): lax.ppermute(value, axis, [(source, source + steps) for source in range(i...  23.5 us
    ppermute x4, starting transfers between devices, shifted(): lax.ppermute(value, axis, [(source, source + steps) for source in range(i...  8.46 us
    dot_general x4, matrix products, project(): jnp.dot(gathered, weight, preferred_element_type=jnp.float32)  5.98 us
    ppermute x1, waiting for transfers between devices, scatter_sum(): lax.ppermute(outgoing, axis, [(source, source ^ mask) for source in range...  4.63 us
    dot_general x1, matrix products, segment_parts(): jnp.einsum('bac,bcv->bav', scores, head_values, preferred_element_type=jn...  2.56 us
    dot_general x3, matrix products, segment_parts(): jnp.dot(lifted_intact[block], memory, precision=HIGH_PRECISION)  2.51 us
    broadcast_in_dim x1, other arithmetic, shards(): segment_states = closing[None, None]  2.24 us
    convert_element_type x3, other arithmetic, short_conv(): weight.astype(jnp.float32)[:, None, :] * windows.astype(jnp.float32)  2.06 us
  transfers between devices with their start and end apart: 8, of which 8 were waited for; matrix products, arithmetic and copies ran while one was open for 20% of the time, Pallas kernels for 0%

profile of v13, /device:TPU:24, one launch (start us, length us, event | category | flops | bytes accessed | tf_op | source)
XLA Modules:
  0.0 84.2 jit_solution(6608834127697073468)
XLA Ops:
  0.7 1.6 %collective-permute-start = (bf16[64,2048]{1,0:T(8,128)(2,1)}, bf16[64,2048]{1,0:T(8,128)(2,1)S(1)}, u32[]{:S(2)}, u32[]{:S(2)}) collective-permute-start(bf16[64,2048]{1,0:T(8,128)(2,1)} %param.18), channel_id=1, source_target_pairs={{0,2},{1,3},{2,0},{3,1},{4,6},{5,7},{6,4},{7,5},{8,10},{9,11},{10,... | collective-permute-start | bytes 786440 | tf_op jit(solution)/shard_map/ppermute | solution.py:150
  2.2 0.8 select_reduce_fusion.1
  3.7 0.6 slice.181
  4.3 0.7 convert_element_type.178
  5.0 0.7 convert_element_type.188
  5.7 0.7 convert_element_type.194
  6.4 0.6 pad.32.clone
  6.9 0.7 reshape.228
  7.8 0.6 iota_compare_fusion
  8.4 0.6 collective-permute-done
  9.0 1.0 %pad_maximum_fusion.4 = bf16[128,2048]{1,0:T(8,128)(2,1)S(1)} fusion(bf16[64,2048]{1,0:T(8,128)(2,1)S(1)} %collective-permute-done, bf16[64,2048]{1,0:T(8,128)(2,1)} %param.18), kind=kLoop, calls=%fused_computation.45 | loop fusion | flops 1048576 | bytes 1048576 | tf_op jit(solution)/shard_map/concatenate | solution.py:151
  10.1 0.7 slice_compare_fusion
  10.8 1.1 %collective-permute-done.1 = bf16[128,2048]{1,0:T(8,128)(2,1)S(1)} collective-permute-done((bf16[128,2048]{1,0:T(8,128)(2,1)S(1)}, bf16[128,2048]{1,0:T(8,128)(2,1)S(1)}, u32[]{:S(2)}, u32[]{:S(2)}) %collective-permute-start.1) | collective-permute-done | bytes 524320 | tf_op jit(solution)/shard_map/ppermute | solution.py:150
  12.0 1.8 %conditional.1 = (bf16[256,2048]{1,0:T(8,128)(2,1)S(1)}) conditional(s32[]{:T(128)} %clamp.3, (bf16[64,2048]{1,0:T(8,128)(2,1)S(1)}, bf16[64,2048]{1,0:T(8,128)(2,1)S(1)}, bf16[64,2048]{1,0:T(8,128)(2,1)S(1)}, bf16[64,2048]{1,0:T(8,128)(2,1)S(1)}) %tuple.60, (bf16[64,2048]{1,0:T(8,128)(2,1)S(1)}, ...), branch_computations={%region_3.0_spmd, %region_4.5_spmd, %region_5.6_spmd, %region_6.7_... | conditional | flops 4194304 | bytes 3145764 | solution.py:164
  12.0 0.7 copy-done.2
  12.7 1.0 %pad_maximum_fusion = bf16[256,2048]{1,0:T(8,128)(2,1)S(1)} fusion(bf16[64,2048]{1,0:T(8,128)(2,1)S(1)} %get-tuple-element.40, bf16[64,2048]{1,0:T(8,128)(2,1)} %copy-done.2, bf16[64,2048]{1,0:T(8,128)(2,1)S(1)} %get-tuple-element.33, bf16[64,2048]{1,0:T(8,128)(2,1)S(1)} %get-tuple-element.32), kind=kLoop, calls=%fused_computation | loop fusion | flops 4194304 | bytes 2097152 | tf_op jit(solution)/shard_map/cond/branch_0_fun/concatenate | solution.py:162
  13.8 3.0 %convolution_convert_fusion.2 = bf16[256,512]{1,0:T(8,128)(2,1)} fusion(bf16[256,2048]{1,0:T(8,128)(2,1)S(1)} %get-tuple-element.103, bf16[2048,512]{1,0:T(8,128)(2,1)} %param.29), kind=kOutput, calls=%fused_computation.9 | convolution fusion | flops 537001984 | bytes 3407872 | tf_op jit(solution)/shard_map/dot_general | solution.py:229
  16.9 1.5 %fusion.29 = f32[256,256]{1,0:T(8,128)} fusion(bf16[16,256]{1,0:T(8,128)(2,1)S(1)} %copy-done.18, bf16[256,2048]{1,0:T(8,128)(2,1)S(1)} %get-tuple-element.103, bf16[2048,16]{0,1:T(8,128)(2,1)S(1)} %copy-done.17, f32[256]{0:T(256)S(1)} %copy-done.19), kind=kOutput, calls=%fused_computation.81 | convolution fusion | flops 19533824 | bytes 1385472 | tf_op jit(solution)/shard_map/dot_general | solution.py:259
  18.4 1.2 %reduce_window_sum.23 = f32[4,64,256]{2,1,0:T(8,128)S(1)} reduce-window(f32[4,64,256]{2,1,0:T(8,128)} %bitcast.128, f32[]{:T(128)} %constant.74.clone.1), window={size=1x64x1 pad=0_0x63_0x0_0}, to_apply=%region_8.9 | reduce-window | flops 4128768 | bytes 524292 | tf_op jit(solution)/shard_map/jit(cumsum)/reduce_window_sum | solution.py:49
  19.6 1.8 %convolution_convert_fusion.5 = bf16[256,256]{1,0:T(8,128)(2,1)S(1)} fusion(bf16[256,2048]{1,0:T(8,128)(2,1)S(1)} %get-tuple-element.103, bf16[2048,256]{1,0:T(8,128)(2,1)} %param.20), kind=kOutput, calls=%fused_computation.14 | convolution fusion | flops 268500992 | bytes 2228224 | tf_op jit(solution)/shard_map/dot_general | solution.py:229
  21.6 0.7 convolution_convert_fusion.3
  23.2 0.7 select_bitcast_fusion
  23.9 3.4 %collective-permute-start.2 = (bf16[3,1024]{1,0:T(4,128)(2,1)S(1)}, bf16[3,1024]{1,0:T(4,128)(2,1)S(1)}, u32[]{:S(2)}, u32[]{:S(2)}) collective-permute-start(bf16[3,1024]{1,0:T(4,128)(2,1)S(1)} %get-tuple-element.59), channel_id=1, source_target_pairs={{0,4},{4,8},{8,12},{12,16},{16,20},{20,24},{24,28},{1,5},{5,9},{9,... | collective-permute-start | bytes 18440 | tf_op jit(solution)/shard_map/ppermute | solution.py:17
  27.5 2.8 %collective-permute-done.2 = bf16[3,1024]{1,0:T(4,128)(2,1)S(1)} collective-permute-done((bf16[3,1024]{1,0:T(4,128)(2,1)S(1)}, bf16[3,1024]{1,0:T(4,128)(2,1)S(1)}, u32[]{:S(2)}, u32[]{:S(2)}) %collective-permute-start.2) | collective-permute-done | bytes 6176 | tf_op jit(solution)/shard_map/ppermute | solution.py:17
  31.5 0.6 fusion.52
  32.8 2.5 %collective-permute-start.3 = (bf16[257,512]{1,0:T(8,128)(2,1)S(1)}, bf16[257,512]{1,0:T(8,128)(2,1)S(1)}, u32[]{:S(2)}, u32[]{:S(2)}) collective-permute-start(bf16[257,512]{1,0:T(8,128)(2,1)S(1)} %pad_maximum_fusion.5), channel_id=1, source_target_pairs={{0,4},{4,8},{8,12},{12,16},{16,20},{20,24},{24,28},{1,5},{5,9},{9,... | collective-permute-start | bytes 789512 | tf_op jit(solution)/shard_map/ppermute | solution.py:17
  35.3 0.8 bitcast_multiply_fusion
  36.1 1.0 %convolution_bitcast_fusion.2 = f32[1,64,512]{2,1,0:T(8,128)} fusion(f32[4,256,512]{2,1,0:T(8,128)S(1)} %fusion.52, f32[256]{0:T(256)S(1)} %get-tuple-element.97, f32[4,64,256]{2,1,0:T(8,128)S(1)} %get-tuple-element.80), kind=kOutput, calls=%fused_computation.17 | convolution fusion | flops 50462720 | bytes 721920 | tf_op jit(solution)/shard_map/dot_general | solution.py:80
  37.2 1.1 %convolution_bitcast_fusion = f32[1,64,512]{2,1,0:T(8,128)} fusion(f32[4,256,512]{2,1,0:T(8,128)S(1)} %fusion.52, f32[256]{0:T(256)S(1)} %bitcast.137, f32[4,64,256]{2,1,0:T(8,128)S(1)} %get-tuple-element.80, f32[256]{0:T(256)S(1)} %bitcast.134, f32[256]{0:T(256)S(1)} %get-tuple-element.97), kind=kOutput, calls=%fused_computation.15 | convolution fusion | flops 50987008 | bytes 1772544 | tf_op jit(solution)/shard_map/dot_general | solution.py:80
  38.3 4.7 %collective-permute-done.3 = bf16[257,512]{1,0:T(8,128)(2,1)S(1)} collective-permute-done((bf16[257,512]{1,0:T(8,128)(2,1)S(1)}, bf16[257,512]{1,0:T(8,128)(2,1)S(1)}, u32[]{:S(2)}, u32[]{:S(2)}) %collective-permute-start.3) | collective-permute-done | bytes 263200 | tf_op jit(solution)/shard_map/ppermute | solution.py:17
  43.0 0.6 subtract_convert_fusion
  43.7 0.7 pad_maximum_fusion.6
  44.5 1.3 %collective-permute-start.4 = (bf16[257,512]{1,0:T(8,128)(2,1)}, bf16[257,512]{1,0:T(8,128)(2,1)}, u32[]{:S(2)}, u32[]{:S(2)}) collective-permute-start(bf16[257,512]{1,0:T(8,128)(2,1)} %pad_maximum_fusion.6), channel_id=1, source_target_pairs={{0,8},{4,12},{8,16},{12,20},{16,24},{20,28},{1,9},{5,13},{9,17},{1... | collective-permute-start | bytes 789512 | tf_op jit(solution)/shard_map/ppermute | solution.py:17
  45.8 2.6 %convolution_add_fusion = f32[4,64,512]{2,1,0:T(8,128)} fusion(f32[1,64,512]{2,1,0:T(8,128)} %convolution_bitcast_fusion, f32[1,64,512]{2,1,0:T(8,128)S(1)} %convolution_bitcast_fusion.1, f32[1,64,512]{2,1,0:T(8,128)} %convolution_bitcast_fusion.2, f32[4]{0:T(128)} %pad.32.clone, f32[4,64,256]{2,1,0:T(8,128)S(1)} %copy-done.7, ...), kind=kOutput, calls=%fused_computation.7 | convolution fusion | flops 27525120 | bytes 2233360 | tf_op jit(solution)/shard_map/bac,bcv->bav/dot_general | solution.py:71
  48.3 4.9 %collective-permute-done.4 = bf16[257,512]{1,0:T(8,128)(2,1)} collective-permute-done((bf16[257,512]{1,0:T(8,128)(2,1)}, bf16[257,512]{1,0:T(8,128)(2,1)}, u32[]{:S(2)}, u32[]{:S(2)}) %collective-permute-start.4) | collective-permute-done | bytes 263200 | tf_op jit(solution)/shard_map/ppermute | solution.py:17
  53.2 1.2 %fusion.79 = bf16[256,512]{1,0:T(8,128)(2,1)S(1)} fusion(f32[256,512]{1,0:T(8,128)S(1)} %get-tuple-element.64, bf16[257,512]{1,0:T(8,128)(2,1)S(1)} %collective-permute-done.3, f32[256]{0:T(256)S(1)} %get-tuple-element.67, pred[]{:T(512)S(6)} %ge.60, bf16[257,512]{1,0:T(8,128)(2,1)} %collective-permute-done.4, f32[256]{0:T(256)} %get-tuple-element.62, ...), kind=kLoop, calls=%fused_computation.180 | loop fusion | flops 1179648 | bytes 1312770 | tf_op jit(solution)/shard_map/convert_element_type | solution.py:119
  54.4 1.3 %collective-permute-start.5 = (bf16[256,512]{1,0:T(8,128)(2,1)S(1)}, bf16[256,512]{1,0:T(8,128)(2,1)S(1)}, u32[]{:S(2)}, u32[]{:S(2)}) collective-permute-start(bf16[256,512]{1,0:T(8,128)(2,1)S(1)} %fusion.79), channel_id=1, source_target_pairs={{0,16},{4,20},{8,24},{12,28},{1,17},{5,21},{9,25},{13,29},{2,18},{... | collective-permute-start | bytes 786440 | tf_op jit(solution)/shard_map/ppermute | solution.py:17
  55.7 0.7 slice_convert_fusion
  56.4 0.7 multiply_select_fusion
  57.0 11.1 %collective-permute-done.5 = bf16[256,512]{1,0:T(8,128)(2,1)S(1)} collective-permute-done((bf16[256,512]{1,0:T(8,128)(2,1)S(1)}, bf16[256,512]{1,0:T(8,128)(2,1)S(1)}, u32[]{:S(2)}, u32[]{:S(2)}) %collective-permute-start.5) | collective-permute-done | bytes 262176 | tf_op jit(solution)/shard_map/ppermute | solution.py:17
  68.1 1.9 %multiply_reduce_fusion.3 = (f32[256]{0:T(256)S(1)}, f32[256,512]{1,0:T(8,128)S(1)}) fusion(f32[256,512]{1,0:T(8,128)} %bitcast.146, f32[256,256]{1,0:T(8,128)} %bitcast_multiply_fusion, bf16[256,512]{1,0:T(8,128)(2,1)S(1)} %collective-permute-done.5, f32[256]{0:T(256)} %bitcast.143, f32[256]{0:T(256)S(1)} %get-tuple-element.96, pred[]{:T(512)S(6)} %ge.59, ...), kind=kOutput, calls=%fused_computation.58 | convolution fusion | flops 202899200 | bytes 2100226 | tf_op jit(solution)/shard_map/dot_general | solution.py:267
  70.3 1.2 %convolution_convert_fusion = bf16[128,2048]{1,0:T(8,128)(2,1)} fusion(bf16[512,2048]{1,0:T(8,128)(2,1)S(1)} %copy-done, bf16[64,512]{1,0:T(8,128)(2,1)S(1)} %get-tuple-element.78, bf16[64,512]{1,0:T(8,128)(2,1)S(1)} %get-tuple-element.77), kind=kOutput, calls=%fused_computation.4 | convolution fusion | flops 268959744 | bytes 2752512 | tf_op jit(solution)/shard_map/dot_general | solution.py:187
  72.0 1.8 %collective-permute-done.6 = bf16[128,2048]{1,0:T(8,128)(2,1)} collective-permute-done((bf16[128,2048]{1,0:T(8,128)(2,1)}, bf16[128,2048]{1,0:T(8,128)(2,1)}, u32[]{:S(2)}, u32[]{:S(2)}) %collective-permute-start.6) | collective-permute-done | bytes 524320 | tf_op jit(solution)/shard_map/ppermute | solution.py:188
  73.8 1.2 %convert_add_fusion = f32[128,2048]{1,0:T(8,128)S(1)} fusion(bf16[128,2048]{1,0:T(8,128)(2,1)} %collective-permute-done.6, bf16[128,2048]{1,0:T(8,128)(2,1)S(1)} %convolution_convert_fusion.1), kind=kLoop, calls=%fused_computation.21 | loop fusion | flops 786432 | bytes 2097152 | tf_op jit(solution)/shard_map/add | solution.py:193
  75.1 1.5 %collective-permute-start.7 = (bf16[1,64,2048]{2,1,0:T(8,128)(2,1)S(1)}, bf16[1,64,2048]{2,1,0:T(8,128)(2,1)S(1)}, u32[]{:S(2)}, u32[]{:S(2)}) collective-permute-start(bf16[1,64,2048]{2,1,0:T(8,128)(2,1)S(1)} %fusion.27), channel_id=1, source_target_pairs={{0,2},{1,3},{2,0},{3,1},{4,6},{5,7},{6,4},{7,5},{8,10},{9,11},{10,... | collective-permute-start | bytes 786440 | tf_op jit(solution)/shard_map/ppermute | solution.py:201
  76.6 2.2 %fusion.7 = f32[1,1,256,512]{3,2,1,0:T(8,128)} fusion(bf16[256,512]{1,0:T(8,128)(2,1)S(1)} %collective-permute-done.5, f32[256]{0:T(256)S(1)} %get-tuple-element.95, pred[]{:T(512)S(6)} %ge.58, f32[256,512]{1,0:T(8,128)S(1)} %get-tuple-element.64, bf16[257,512]{1,0:T(8,128)(2,1)S(1)} %collective-permute-done.3, f32[256]{0:T(256)S(1)} %get-tuple-element.67, ...), kind=kLoop, calls=%fused_computation.42 | loop fusion | flops 1572864 | bytes 1838083 | tf_op jit(solution)/shard_map/broadcast_in_dim | solution.py:276
  78.8 4.6 %collective-permute-done.7 = bf16[1,64,2048]{2,1,0:T(8,128)(2,1)S(1)} collective-permute-done((bf16[1,64,2048]{2,1,0:T(8,128)(2,1)S(1)}, bf16[1,64,2048]{2,1,0:T(8,128)(2,1)S(1)}, u32[]{:S(2)}, u32[]{:S(2)}) %collective-permute-start.7) | collective-permute-done | bytes 262176 | tf_op jit(solution)/shard_map/ppermute | solution.py:201
  83.5 0.8 fusion.9
  (77 shorter events, 5.1 us)
Async XLA Ops:
  0.6 69.7 %copy-start = (bf16[512,2048]{1,0:T(8,128)(2,1)S(1)}, bf16[512,2048]{1,0:T(8,128)(2,1)}, u32[]{:S(2)}) copy-start(bf16[512,2048]{1,0:T(8,128)(2,1)} %param.31) | copy-start | bytes 6291460
  0.6 11.3 %copy-start.1 = (bf16[64,2048]{1,0:T(8,128)(2,1)S(1)}, bf16[64,2048]{1,0:T(8,128)(2,1)}, u32[]{:S(2)}) copy-start(bf16[64,2048]{1,0:T(8,128)(2,1)} %param.18) | copy-start | bytes 786436
  0.7 8.3 %collective-permute-start = (bf16[64,2048]{1,0:T(8,128)(2,1)}, bf16[64,2048]{1,0:T(8,128)(2,1)S(1)}, u32[]{:S(2)}, u32[]{:S(2)}) collective-permute-start(bf16[64,2048]{1,0:T(8,128)(2,1)} %param.18), channel_id=1, source_target_pairs={{0,2},{1,3},{2,0},{3,1},{4,6},{5,7},{6,4},{7,5},{8,10},{9,11},{10,... | collective-permute-start | bytes 786440 | tf_op jit(solution)/shard_map/ppermute | solution.py:150
  10.0 2.0 %collective-permute-start.1 = (bf16[128,2048]{1,0:T(8,128)(2,1)S(1)}, bf16[128,2048]{1,0:T(8,128)(2,1)S(1)}, u32[]{:S(2)}, u32[]{:S(2)}) collective-permute-start(bf16[128,2048]{1,0:T(8,128)(2,1)S(1)} %pad_maximum_fusion.4), channel_id=1, source_target_pairs={{0,1},{1,0},{2,3},{3,2},{4,5},{5,4},{6,7},{7,6},{8,9},{9,8},{10,11... | collective-permute-start | bytes 1572872 | tf_op jit(solution)/shard_map/ppermute | solution.py:150
  12.0 0.7 copy-start.2
  13.8 3.1 %copy-start.17 = (bf16[2048,16]{0,1:T(8,128)(2,1)S(1)}, bf16[2048,16]{0,1:T(8,128)(2,1)}, u32[]{:S(2)}) copy-start(bf16[2048,16]{0,1:T(8,128)(2,1)} %param.26) | copy-start | bytes 196612
  13.8 3.1 %copy-start.18 = (bf16[16,256]{1,0:T(8,128)(2,1)S(1)}, bf16[16,256]{1,0:T(8,128)(2,1)}, u32[]{:S(2)}) copy-start(bf16[16,256]{1,0:T(8,128)(2,1)} %param.27) | copy-start | bytes 24580
  13.8 3.0 %copy-start.19 = (f32[256]{0:T(256)S(1)}, f32[256]{0:T(256)}, u32[]{:S(2)}) copy-start(f32[256]{0:T(256)} %param.28) | copy-start | bytes 3076
  19.6 11.9 %copy-start.6 = (f32[4,64,256]{2,1,0:T(8,128)}, f32[4,64,256]{2,1,0:T(8,128)S(1)}, u32[]{:S(2)}) copy-start(f32[4,64,256]{2,1,0:T(8,128)S(1)} %reduce_window_sum.23) | copy-start | bytes 786436
  19.6 2.0 %copy-start.16 = (bf16[2048,512]{1,0:T(8,128)(2,1)S(1)}, bf16[2048,512]{1,0:T(8,128)(2,1)}, u32[]{:S(2)}) copy-start(bf16[2048,512]{1,0:T(8,128)(2,1)} %param.22) | copy-start | bytes 6291460
  21.6 1.2 %copy-start.8 = (bf16[2048,256]{1,0:T(8,128)(2,1)S(1)}, bf16[2048,256]{1,0:T(8,128)(2,1)}, u32[]{:S(2)}) copy-start(bf16[2048,256]{1,0:T(8,128)(2,1)} %param.21) | copy-start | bytes 3145732
  23.9 6.4 %collective-permute-start.2 = (bf16[3,1024]{1,0:T(4,128)(2,1)S(1)}, bf16[3,1024]{1,0:T(4,128)(2,1)S(1)}, u32[]{:S(2)}, u32[]{:S(2)}) collective-permute-start(bf16[3,1024]{1,0:T(4,128)(2,1)S(1)} %get-tuple-element.59), channel_id=1, source_target_pairs={{0,4},{4,8},{8,12},{12,16},{16,20},{20,24},{24,28},{1,5},{5,9},{9,... | collective-permute-start | bytes 18440 | tf_op jit(solution)/shard_map/ppermute | solution.py:17
  31.0 1.1 %copy-start.11 = (f32[256,256]{1,0:T(8,128)}, f32[256,256]{1,0:T(8,128)S(1)}, u32[]{:S(2)}) copy-start(f32[256,256]{1,0:T(8,128)S(1)} %get-tuple-element.57) | copy-start | bytes 786436
  31.5 13.0 %copy-start.9 = (f32[256,512]{1,0:T(8,128)}, f32[256,512]{1,0:T(8,128)S(1)}, u32[]{:S(2)}) copy-start(f32[256,512]{1,0:T(8,128)S(1)} %multiply_reduce_fusion) | copy-start | bytes 1572868
  32.1 3.2 %copy-start.14 = (f32[256]{0:T(256)S(1)}, f32[256]{0:T(256)}, u32[]{:S(2)}) copy-start(f32[256]{0:T(256)} %reshape.228) | copy-start | bytes 3076
  32.8 10.2 %collective-permute-start.3 = (bf16[257,512]{1,0:T(8,128)(2,1)S(1)}, bf16[257,512]{1,0:T(8,128)(2,1)S(1)}, u32[]{:S(2)}, u32[]{:S(2)}) collective-permute-start(bf16[257,512]{1,0:T(8,128)(2,1)S(1)} %pad_maximum_fusion.5), channel_id=1, source_target_pairs={{0,4},{4,8},{8,12},{12,16},{16,20},{20,24},{24,28},{1,5},{5,9},{9,... | collective-permute-start | bytes 789512 | tf_op jit(solution)/shard_map/ppermute | solution.py:17
  35.3 10.4 %copy-start.7 = (f32[4,64,256]{2,1,0:T(8,128)S(1)}, f32[4,64,256]{2,1,0:T(8,128)}, u32[]{:S(2)}) copy-start(f32[4,64,256]{2,1,0:T(8,128)} %copy-done.6) | copy-start | bytes 786436
  43.0 0.6 copy-start.13
  44.5 8.7 %collective-permute-start.4 = (bf16[257,512]{1,0:T(8,128)(2,1)}, bf16[257,512]{1,0:T(8,128)(2,1)}, u32[]{:S(2)}, u32[]{:S(2)}) collective-permute-start(bf16[257,512]{1,0:T(8,128)(2,1)} %pad_maximum_fusion.6), channel_id=1, source_target_pairs={{0,8},{4,12},{8,16},{12,20},{16,24},{20,28},{1,9},{5,13},{9,17},{1... | collective-permute-start | bytes 789512 | tf_op jit(solution)/shard_map/ppermute | solution.py:17
  48.3 21.7 %copy-start.10 = (bf16[256,512]{1,0:T(8,128)(2,1)S(1)}, bf16[256,512]{1,0:T(8,128)(2,1)}, u32[]{:S(2)}) copy-start(bf16[256,512]{1,0:T(8,128)(2,1)} %convolution_convert_fusion.2) | copy-start | bytes 786436
  48.3 21.7 %copy-start.15 = (f32[512]{0:T(512)S(1)}, f32[512]{0:T(512)}, u32[]{:S(2)}) copy-start(f32[512]{0:T(512)} %param.30) | copy-start | bytes 6148
  54.4 13.8 %collective-permute-start.5 = (bf16[256,512]{1,0:T(8,128)(2,1)S(1)}, bf16[256,512]{1,0:T(8,128)(2,1)S(1)}, u32[]{:S(2)}, u32[]{:S(2)}) collective-permute-start(bf16[256,512]{1,0:T(8,128)(2,1)S(1)} %fusion.79), channel_id=1, source_target_pairs={{0,16},{4,20},{8,24},{12,28},{1,17},{5,21},{9,25},{13,29},{2,18},{... | collective-permute-start | bytes 786440 | tf_op jit(solution)/shard_map/ppermute | solution.py:17
  71.6 2.3 %collective-permute-start.6 = (bf16[128,2048]{1,0:T(8,128)(2,1)}, bf16[128,2048]{1,0:T(8,128)(2,1)}, u32[]{:S(2)}, u32[]{:S(2)}) collective-permute-start(bf16[128,2048]{1,0:T(8,128)(2,1)} %convolution_convert_fusion), channel_id=1, source_target_pairs={{0,1},{1,0},{2,3},{3,2},{4,5},{5,4},{6,7},{7,6},{8,9},{9,8},{10,11... | collective-permute-start | bytes 1572872 | tf_op jit(solution)/shard_map/ppermute | solution.py:188
  72.0 4.6 %copy-start.12 = (f32[256]{0:T(256)S(1)}, f32[256]{0:T(256)}, u32[]{:S(2)}) copy-start(f32[256]{0:T(256)} %get-tuple-element.62) | copy-start | bytes 3076
  75.1 8.4 %collective-permute-start.7 = (bf16[1,64,2048]{2,1,0:T(8,128)(2,1)S(1)}, bf16[1,64,2048]{2,1,0:T(8,128)(2,1)S(1)}, u32[]{:S(2)}, u32[]{:S(2)}) collective-permute-start(bf16[1,64,2048]{2,1,0:T(8,128)(2,1)S(1)} %fusion.27), channel_id=1, source_target_pairs={{0,2},{1,3},{2,0},{3,1},{4,6},{5,7},{6,4},{7,5},{8,10},{9,11},{10,... | collective-permute-start | bytes 786440 | tf_op jit(solution)/shard_map/ppermute | solution.py:201

commit v14 on v10

--- a/solution.py
+++ b/solution.py
@@ -263,7 +263,7 @@
     )
     closing, entering = prefix_states(local_decay, local_memory, "tok")
     heads_out = local_out.reshape((row_count, value_width)) + jnp.dot(
-        carry_lift.reshape((row_count, key_width)), entering, precision=HIGH_PRECISION
+        carry_lift.reshape((row_count, key_width)), entering
     )
     gate_float = gate_values.astype(jnp.float32)
     rescale = lax.rsqrt(jnp.mean(heads_out * heads_out, axis=1, keepdims=True) + 1e-05)

time: 82.3 us -> 82.7 us (level)
  transfers between devices with their start and end apart: 8 -> 8, of which waited for: 8 -> 8; matrix products, arithmetic and copies ran while one was open for 18% -> 17% of each run, Pallas kernels for 0% -> 0%
where the time goes in v14:
time: 82.7 us; the launch traced here: 82.1 us
  waiting for transfers between devices  33.5 us (41%)
  other arithmetic  16.3 us (20%)
  matrix products  15.5 us (19%)
  starting transfers between devices  11.8 us (14%)
  local copies, waits for them, and re-layouts  3.93 us (5%)
  between operations  1.12 us (1%)
    ppermute x4, waiting for transfers between devices, shifted(): lax.ppermute(value, axis, [(source, source + steps) for source in range(i...  24.7 us
    ppermute x4, starting transfers between devices, shifted(): lax.ppermute(value, axis, [(source, source + steps) for source in range(i...  8.46 us
    ppermute x1, waiting for transfers between devices, scatter_sum(): lax.ppermute(outgoing, axis, [(source, source ^ mask) for source in range...  4.55 us
    dot_general x4, matrix products, project(): jnp.dot(gathered, weight, preferred_element_type=jnp.float32)  3.74 us
    dot_general x3, matrix products, segment_parts(): jnp.dot(lifted_intact[block], memory, precision=HIGH_PRECISION)  3.13 us
    dot_general x1, matrix products, segment_parts(): jnp.einsum('bac,bcv->bav', scores, head_values, preferred_element_type=jn...  2.76 us
    ppermute x2, waiting for transfers between devices, gather_rows(): lax.ppermute(jnp.concatenate(received), axis, [(source, source ^ mask) fo...  2.34 us
    broadcast_in_dim x1, other arithmetic, shards(): segment_states = closing[None, None]  2.23 us
  transfers between devices with their start and end apart: 8, of which 8 were waited for; matrix products, arithmetic and copies ran while one was open for 17% of the time, Pallas kernels for 0%

profile of v14, /device:TPU:24, one launch (start us, length us, event | category | flops | bytes accessed | tf_op | source)
XLA Modules:
  0.0 82.1 jit_solution(16495492602502311703)
XLA Ops:
  0.7 1.6 %collective-permute-start = (bf16[64,2048]{1,0:T(8,128)(2,1)}, bf16[64,2048]{1,0:T(8,128)(2,1)S(1)}, u32[]{:S(2)}, u32[]{:S(2)}) collective-permute-start(bf16[64,2048]{1,0:T(8,128)(2,1)} %param.18), channel_id=1, source_target_pairs={{0,2},{1,3},{2,0},{3,1},{4,6},{5,7},{6,4},{7,5},{8,10},{9,11},{10,... | collective-permute-start | bytes 786440 | tf_op jit(solution)/shard_map/ppermute | solution.py:150
  2.2 0.8 select_reduce_fusion.1
  3.7 0.6 slice.181
  4.3 0.7 convert_element_type.178
  5.0 0.7 convert_element_type.188
  5.7 0.7 convert_element_type.194
  6.4 0.5 pad.32.clone
  7.1 0.6 iota_compare_fusion
  7.7 1.2 %collective-permute-done = bf16[64,2048]{1,0:T(8,128)(2,1)S(1)} collective-permute-done((bf16[64,2048]{1,0:T(8,128)(2,1)}, bf16[64,2048]{1,0:T(8,128)(2,1)S(1)}, u32[]{:S(2)}, u32[]{:S(2)}) %collective-permute-start) | collective-permute-done | bytes 262176 | tf_op jit(solution)/shard_map/ppermute | solution.py:150
  9.0 1.0 %pad_maximum_fusion.4 = bf16[128,2048]{1,0:T(8,128)(2,1)S(1)} fusion(bf16[64,2048]{1,0:T(8,128)(2,1)S(1)} %collective-permute-done, bf16[64,2048]{1,0:T(8,128)(2,1)} %param.18), kind=kLoop, calls=%fused_computation.40 | loop fusion | flops 1048576 | bytes 1048576 | tf_op jit(solution)/shard_map/concatenate | solution.py:151
  10.1 0.7 slice_compare_fusion
  10.9 1.1 %collective-permute-done.1 = bf16[128,2048]{1,0:T(8,128)(2,1)S(1)} collective-permute-done((bf16[128,2048]{1,0:T(8,128)(2,1)S(1)}, bf16[128,2048]{1,0:T(8,128)(2,1)S(1)}, u32[]{:S(2)}, u32[]{:S(2)}) %collective-permute-start.1) | collective-permute-done | bytes 524320 | tf_op jit(solution)/shard_map/ppermute | solution.py:150
  12.0 1.8 %conditional.1 = (bf16[256,2048]{1,0:T(8,128)(2,1)S(1)}) conditional(s32[]{:T(128)} %clamp.3, (bf16[64,2048]{1,0:T(8,128)(2,1)S(1)}, bf16[64,2048]{1,0:T(8,128)(2,1)S(1)}, bf16[64,2048]{1,0:T(8,128)(2,1)S(1)}, bf16[64,2048]{1,0:T(8,128)(2,1)S(1)}) %tuple.60, (bf16[64,2048]{1,0:T(8,128)(2,1)S(1)}, ...), branch_computations={%region_3.0_spmd, %region_4.5_spmd, %region_5.6_spmd, %region_6.7_... | conditional | flops 4194304 | bytes 3145764 | solution.py:164
  12.1 0.7 copy-done.4
  12.8 1.0 %pad_maximum_fusion = bf16[256,2048]{1,0:T(8,128)(2,1)S(1)} fusion(bf16[64,2048]{1,0:T(8,128)(2,1)S(1)} %get-tuple-element.40, bf16[64,2048]{1,0:T(8,128)(2,1)} %copy-done.4, bf16[64,2048]{1,0:T(8,128)(2,1)S(1)} %get-tuple-element.33, bf16[64,2048]{1,0:T(8,128)(2,1)S(1)} %get-tuple-element.32), kind=kLoop, calls=%fused_computation | loop fusion | flops 4194304 | bytes 2097152 | tf_op jit(solution)/shard_map/cond/branch_0_fun/concatenate | solution.py:162
  13.8 1.5 %fusion.26 = f32[256,256]{1,0:T(8,128)} fusion(bf16[16,256]{1,0:T(8,128)(2,1)S(1)} %copy-done.19, bf16[256,2048]{1,0:T(8,128)(2,1)S(1)} %get-tuple-element.103, bf16[2048,16]{0,1:T(8,128)(2,1)S(1)} %copy-done.18, f32[256]{0:T(256)S(1)} %copy-done.21), kind=kOutput, calls=%fused_computation.77 | convolution fusion | flops 19533824 | bytes 1385472 | tf_op jit(solution)/shard_map/dot_general | solution.py:257
  15.3 1.2 %reduce_window_sum.23 = f32[4,64,256]{2,1,0:T(8,128)S(1)} reduce-window(f32[4,64,256]{2,1,0:T(8,128)} %bitcast.128, f32[]{:T(128)} %constant.74.clone.1), window={size=1x64x1 pad=0_0x63_0x0_0}, to_apply=%region_8.9 | reduce-window | flops 4128768 | bytes 524292 | tf_op jit(solution)/shard_map/jit(cumsum)/reduce_window_sum | solution.py:49
  16.6 1.8 %convolution_convert_fusion.5 = bf16[256,256]{1,0:T(8,128)(2,1)S(1)} fusion(bf16[256,2048]{1,0:T(8,128)(2,1)S(1)} %get-tuple-element.103, bf16[2048,256]{1,0:T(8,128)(2,1)} %param.20), kind=kOutput, calls=%fused_computation.16 | convolution fusion | flops 268500992 | bytes 2228224 | tf_op jit(solution)/shard_map/dot_general | solution.py:227
  18.6 0.7 convolution_convert_fusion.3
  19.3 0.5 copy-done.12
  19.8 0.4 convolution_convert_fusion.4
  20.2 0.7 select_bitcast_fusion
  20.9 3.4 %collective-permute-start.2 = (bf16[3,1024]{1,0:T(4,128)(2,1)S(1)}, bf16[3,1024]{1,0:T(4,128)(2,1)S(1)}, u32[]{:S(2)}, u32[]{:S(2)}) collective-permute-start(bf16[3,1024]{1,0:T(4,128)(2,1)S(1)} %get-tuple-element.59), channel_id=1, source_target_pairs={{0,4},{4,8},{8,12},{12,16},{16,20},{20,24},{24,28},{1,5},{5,9},{9,... | collective-permute-start | bytes 18440 | tf_op jit(solution)/shard_map/ppermute | solution.py:17
  24.5 2.8 %collective-permute-done.2 = bf16[3,1024]{1,0:T(4,128)(2,1)S(1)} collective-permute-done((bf16[3,1024]{1,0:T(4,128)(2,1)S(1)}, bf16[3,1024]{1,0:T(4,128)(2,1)S(1)}, u32[]{:S(2)}, u32[]{:S(2)}) %collective-permute-start.2) | collective-permute-done | bytes 6176 | tf_op jit(solution)/shard_map/ppermute | solution.py:17
  28.5 0.6 fusion.49
  29.4 1.0 %convolution_bitcast_fusion.1 = f32[1,64,512]{2,1,0:T(8,128)} fusion(f32[4,64,256]{2,1,0:T(8,128)S(1)} %get-tuple-element.80, f32[4,256,512]{2,1,0:T(8,128)S(1)} %fusion.49, f32[256]{0:T(256)S(1)} %bitcast.133, f32[256]{0:T(256)S(1)} %get-tuple-element.97), kind=kOutput, calls=%fused_computation.18 | convolution fusion | flops 50724864 | bytes 1247232 | tf_op jit(solution)/shard_map/dot_general | solution.py:80
  30.4 2.5 %collective-permute-start.3 = (bf16[257,512]{1,0:T(8,128)(2,1)S(1)}, bf16[257,512]{1,0:T(8,128)(2,1)S(1)}, u32[]{:S(2)}, u32[]{:S(2)}) collective-permute-start(bf16[257,512]{1,0:T(8,128)(2,1)S(1)} %pad_maximum_fusion.5), channel_id=1, source_target_pairs={{0,4},{4,8},{8,12},{12,16},{16,20},{20,24},{24,28},{1,5},{5,9},{9,... | collective-permute-start | bytes 789512 | tf_op jit(solution)/shard_map/ppermute | solution.py:17
  33.1 1.0 %convolution_bitcast_fusion.2 = f32[1,64,512]{2,1,0:T(8,128)} fusion(f32[4,256,512]{2,1,0:T(8,128)S(1)} %fusion.49, f32[256]{0:T(256)S(1)} %get-tuple-element.97, f32[4,64,256]{2,1,0:T(8,128)S(1)} %get-tuple-element.80), kind=kOutput, calls=%fused_computation.19 | convolution fusion | flops 50462720 | bytes 721920 | tf_op jit(solution)/shard_map/dot_general | solution.py:80
  34.1 1.1 %convolution_bitcast_fusion = f32[1,64,512]{2,1,0:T(8,128)} fusion(f32[4,256,512]{2,1,0:T(8,128)S(1)} %fusion.49, f32[256]{0:T(256)S(1)} %bitcast.137, f32[4,64,256]{2,1,0:T(8,128)S(1)} %get-tuple-element.80, f32[256]{0:T(256)S(1)} %bitcast.134, f32[256]{0:T(256)S(1)} %get-tuple-element.97), kind=kOutput, calls=%fused_computation.17 | convolution fusion | flops 50987008 | bytes 1772544 | tf_op jit(solution)/shard_map/dot_general | solution.py:80
  35.2 5.4 %collective-permute-done.3 = bf16[257,512]{1,0:T(8,128)(2,1)S(1)} collective-permute-done((bf16[257,512]{1,0:T(8,128)(2,1)S(1)}, bf16[257,512]{1,0:T(8,128)(2,1)S(1)}, u32[]{:S(2)}, u32[]{:S(2)}) %collective-permute-start.3) | collective-permute-done | bytes 263200 | tf_op jit(solution)/shard_map/ppermute | solution.py:17
  40.8 0.7 pad_maximum_fusion.6
  41.5 1.3 %collective-permute-start.4 = (bf16[257,512]{1,0:T(8,128)(2,1)}, bf16[257,512]{1,0:T(8,128)(2,1)}, u32[]{:S(2)}, u32[]{:S(2)}) collective-permute-start(bf16[257,512]{1,0:T(8,128)(2,1)} %pad_maximum_fusion.6), channel_id=1, source_target_pairs={{0,8},{4,12},{8,16},{12,20},{16,24},{20,28},{1,9},{5,13},{9,17},{1... | collective-permute-start | bytes 789512 | tf_op jit(solution)/shard_map/ppermute | solution.py:17
  42.8 2.8 %convolution_add_fusion = f32[4,64,512]{2,1,0:T(8,128)} fusion(f32[1,64,512]{2,1,0:T(8,128)} %convolution_bitcast_fusion, f32[1,64,512]{2,1,0:T(8,128)} %convolution_bitcast_fusion.1, f32[1,64,512]{2,1,0:T(8,128)} %convolution_bitcast_fusion.2, f32[4]{0:T(128)} %pad.32.clone, f32[4,64,256]{2,1,0:T(8,128)} %copy-done.10, f32[4,64]{1,0:T(4,128)S(1)} %reduce_window_sum.22, ...), kind=kOutput, calls=%fused_computation.8 | convolution fusion | flops 27525120 | bytes 2233360 | tf_op jit(solution)/shard_map/bac,bcv->bav/dot_general | solution.py:71
  45.6 4.7 %collective-permute-done.4 = bf16[257,512]{1,0:T(8,128)(2,1)} collective-permute-done((bf16[257,512]{1,0:T(8,128)(2,1)}, bf16[257,512]{1,0:T(8,128)(2,1)}, u32[]{:S(2)}, u32[]{:S(2)}) %collective-permute-start.4) | collective-permute-done | bytes 263200 | tf_op jit(solution)/shard_map/ppermute | solution.py:17
  50.3 1.4 %fusion.78 = bf16[256,512]{1,0:T(8,128)(2,1)S(1)} fusion(f32[256,512]{1,0:T(8,128)} %copy-done.1, bf16[257,512]{1,0:T(8,128)(2,1)} %copy-done.8, f32[256]{0:T(256)S(1)} %get-tuple-element.67, pred[]{:T(512)S(6)} %ge.60, bf16[257,512]{1,0:T(8,128)(2,1)} %collective-permute-done.4, f32[256]{0:T(256)S(1)} %get-tuple-element.62, pred[]{:T(512)S(6)} %ge.59), kind=kLoop, calls=%fused_computation.176 | loop fusion | flops 1179648 | bytes 1312770 | tf_op jit(solution)/shard_map/convert_element_type | solution.py:119
  51.7 1.3 %collective-permute-start.5 = (bf16[256,512]{1,0:T(8,128)(2,1)S(1)}, bf16[256,512]{1,0:T(8,128)(2,1)S(1)}, u32[]{:S(2)}, u32[]{:S(2)}) collective-permute-start(bf16[256,512]{1,0:T(8,128)(2,1)S(1)} %fusion.78), channel_id=1, source_target_pairs={{0,16},{4,20},{8,24},{12,28},{1,17},{5,21},{9,25},{13,29},{2,18},{... | collective-permute-start | bytes 786440 | tf_op jit(solution)/shard_map/ppermute | solution.py:17
  53.0 0.7 slice_convert_fusion
  53.7 11.8 %collective-permute-done.5 = bf16[256,512]{1,0:T(8,128)(2,1)S(1)} collective-permute-done((bf16[256,512]{1,0:T(8,128)(2,1)S(1)}, bf16[256,512]{1,0:T(8,128)(2,1)S(1)}, u32[]{:S(2)}, u32[]{:S(2)}) %collective-permute-start.5) | collective-permute-done | bytes 262176 | tf_op jit(solution)/shard_map/ppermute | solution.py:17
  65.5 1.7 %multiply_reduce_fusion.3 = (f32[256]{0:T(256)S(1)}, f32[256,512]{1,0:T(8,128)S(1)}) fusion(f32[256,512]{1,0:T(8,128)} %bitcast.146, bf16[256,256]{1,0:T(8,128)(2,1)S(1)} %bitcast_multiply_fusion, bf16[256,512]{1,0:T(8,128)(2,1)S(1)} %collective-permute-done.5, f32[256]{0:T(256)S(1)} %bitcast.143, f32[256]{0:T(256)S(1)} %get-tuple-element.96, pred[]{:T(512)S(6)} %ge.59, ...), kind=kOutput, calls=%fused_computation.54 | convolution fusion | flops 68681472 | bytes 1969154 | tf_op jit(solution)/shard_map/dot_general | solution.py:265
  67.2 0.8 multiply_convert_fusion
  68.0 0.4 convolution_convert_fusion
  68.6 1.9 %collective-permute-done.6 = bf16[128,2048]{1,0:T(8,128)(2,1)S(1)} collective-permute-done((bf16[128,2048]{1,0:T(8,128)(2,1)S(1)}, bf16[128,2048]{1,0:T(8,128)(2,1)S(1)}, u32[]{:S(2)}, u32[]{:S(2)}) %collective-permute-start.6) | collective-permute-done | bytes 524320 | tf_op jit(solution)/shard_map/ppermute | solution.py:188
  70.5 0.8 copy-done.14
  71.3 1.6 %convert_add_fusion = f32[128,2048]{1,0:T(8,128)S(1)} fusion(bf16[128,2048]{1,0:T(8,128)(2,1)} %copy-done.14, bf16[512,2048]{1,0:T(8,128)(2,1)S(1)} %copy-done, bf16[64,512]{1,0:T(8,128)(2,1)S(1)} %get-tuple-element.76, bf16[64,512]{1,0:T(8,128)(2,1)S(1)} %get-tuple-element.75), kind=kOutput, calls=%fused_computation.23 | convolution fusion | flops 269746176 | bytes 3801088 | tf_op jit(solution)/shard_map/dot_general | solution.py:190
  72.9 1.6 %collective-permute-start.7 = (bf16[1,64,2048]{2,1,0:T(8,128)(2,1)S(1)}, bf16[1,64,2048]{2,1,0:T(8,128)(2,1)S(1)}, u32[]{:S(2)}, u32[]{:S(2)}) collective-permute-start(bf16[1,64,2048]{2,1,0:T(8,128)(2,1)S(1)} %fusion.24), channel_id=1, source_target_pairs={{0,2},{1,3},{2,0},{3,1},{4,6},{5,7},{6,4},{7,5},{8,10},{9,11},{10,... | collective-permute-start | bytes 786440 | tf_op jit(solution)/shard_map/ppermute | solution.py:199
  74.5 2.2 %fusion.4 = f32[1,1,256,512]{3,2,1,0:T(8,128)} fusion(bf16[256,512]{1,0:T(8,128)(2,1)S(1)} %collective-permute-done.5, f32[256]{0:T(256)S(1)} %get-tuple-element.95, pred[]{:T(512)S(6)} %ge.58, f32[256,512]{1,0:T(8,128)S(1)} %copy-done.2, bf16[257,512]{1,0:T(8,128)(2,1)S(1)} %copy-done.9, f32[256]{0:T(256)S(1)} %get-tuple-element.67, pred[]{:T(512)S(6)} %ge.60, ...), kind=kLoop, calls=%fused_computation.37 | loop fusion | flops 1572864 | bytes 1838083 | tf_op jit(solution)/shard_map/broadcast_in_dim | solution.py:274
  76.8 4.6 %collective-permute-done.7 = bf16[1,64,2048]{2,1,0:T(8,128)(2,1)S(1)} collective-permute-done((bf16[1,64,2048]{2,1,0:T(8,128)(2,1)S(1)}, bf16[1,64,2048]{2,1,0:T(8,128)(2,1)S(1)}, u32[]{:S(2)}, u32[]{:S(2)}) %collective-permute-start.7) | collective-permute-done | bytes 262176 | tf_op jit(solution)/shard_map/ppermute | solution.py:199
  81.3 0.8 fusion.6
  (79 shorter events, 3.3 us)
Async XLA Ops:
  0.6 67.4 %copy-start = (bf16[512,2048]{1,0:T(8,128)(2,1)S(1)}, bf16[512,2048]{1,0:T(8,128)(2,1)}, u32[]{:S(2)}) copy-start(bf16[512,2048]{1,0:T(8,128)(2,1)} %param.31) | copy-start | bytes 6291460
  0.6 11.3 %copy-start.3 = (bf16[64,2048]{1,0:T(8,128)(2,1)S(1)}, bf16[64,2048]{1,0:T(8,128)(2,1)}, u32[]{:S(2)}) copy-start(bf16[64,2048]{1,0:T(8,128)(2,1)} %param.18) | copy-start | bytes 786436
  0.7 8.3 %collective-permute-start = (bf16[64,2048]{1,0:T(8,128)(2,1)}, bf16[64,2048]{1,0:T(8,128)(2,1)S(1)}, u32[]{:S(2)}, u32[]{:S(2)}) collective-permute-start(bf16[64,2048]{1,0:T(8,128)(2,1)} %param.18), channel_id=1, source_target_pairs={{0,2},{1,3},{2,0},{3,1},{4,6},{5,7},{6,4},{7,5},{8,10},{9,11},{10,... | collective-permute-start | bytes 786440 | tf_op jit(solution)/shard_map/ppermute | solution.py:150
  10.0 2.0 %collective-permute-start.1 = (bf16[128,2048]{1,0:T(8,128)(2,1)S(1)}, bf16[128,2048]{1,0:T(8,128)(2,1)S(1)}, u32[]{:S(2)}, u32[]{:S(2)}) collective-permute-start(bf16[128,2048]{1,0:T(8,128)(2,1)S(1)} %pad_maximum_fusion.4), channel_id=1, source_target_pairs={{0,1},{1,0},{2,3},{3,2},{4,5},{5,4},{6,7},{7,6},{8,9},{9,8},{10,11... | collective-permute-start | bytes 1572872 | tf_op jit(solution)/shard_map/ppermute | solution.py:150
  12.0 1.8 %copy-start.18 = (bf16[2048,16]{0,1:T(8,128)(2,1)S(1)}, bf16[2048,16]{0,1:T(8,128)(2,1)}, u32[]{:S(2)}) copy-start(bf16[2048,16]{0,1:T(8,128)(2,1)} %param.26) | copy-start | bytes 196612
  12.0 1.8 %copy-start.19 = (bf16[16,256]{1,0:T(8,128)(2,1)S(1)}, bf16[16,256]{1,0:T(8,128)(2,1)}, u32[]{:S(2)}) copy-start(bf16[16,256]{1,0:T(8,128)(2,1)} %param.27) | copy-start | bytes 24580
  12.0 1.8 %copy-start.21 = (f32[256]{0:T(256)S(1)}, f32[256]{0:T(256)}, u32[]{:S(2)}) copy-start(f32[256]{0:T(256)} %param.28) | copy-start | bytes 3076
  12.1 0.7 copy-start.4
  16.5 2.7 %copy-start.10 = (f32[4,64,256]{2,1,0:T(8,128)}, f32[4,64,256]{2,1,0:T(8,128)S(1)}, u32[]{:S(2)}) copy-start(f32[4,64,256]{2,1,0:T(8,128)S(1)} %reduce_window_sum.23) | copy-start | bytes 786436
  16.5 2.0 %copy-start.16 = (bf16[2048,512]{1,0:T(8,128)(2,1)S(1)}, bf16[2048,512]{1,0:T(8,128)(2,1)}, u32[]{:S(2)}) copy-start(bf16[2048,512]{1,0:T(8,128)(2,1)} %param.22) | copy-start | bytes 6291460
  18.6 1.2 %copy-start.12 = (bf16[2048,256]{1,0:T(8,128)(2,1)S(1)}, bf16[2048,256]{1,0:T(8,128)(2,1)}, u32[]{:S(2)}) copy-start(bf16[2048,256]{1,0:T(8,128)(2,1)} %param.21) | copy-start | bytes 3145732
  20.2 7.8 %copy-start.11 = (f32[4,64,256]{2,1,0:T(8,128)S(1)}, f32[4,64,256]{2,1,0:T(8,128)}, u32[]{:S(2)}) copy-start(f32[4,64,256]{2,1,0:T(8,128)} %copy-done.10) | copy-start | bytes 786436
  20.9 6.4 %collective-permute-start.2 = (bf16[3,1024]{1,0:T(4,128)(2,1)S(1)}, bf16[3,1024]{1,0:T(4,128)(2,1)S(1)}, u32[]{:S(2)}, u32[]{:S(2)}) collective-permute-start(bf16[3,1024]{1,0:T(4,128)(2,1)S(1)} %get-tuple-element.59), channel_id=1, source_target_pairs={{0,4},{4,8},{8,12},{12,16},{16,20},{20,24},{24,28},{1,5},{5,9},{9,... | collective-permute-start | bytes 18440 | tf_op jit(solution)/shard_map/ppermute | solution.py:17
  28.0 1.1 %copy-start.15 = (f32[256,256]{1,0:T(8,128)}, f32[256,256]{1,0:T(8,128)S(1)}, u32[]{:S(2)}) copy-start(f32[256,256]{1,0:T(8,128)S(1)} %get-tuple-element.57) | copy-start | bytes 786436
  28.5 0.9 %copy-start.13 = (f32[256,512]{1,0:T(8,128)}, f32[256,512]{1,0:T(8,128)S(1)}, u32[]{:S(2)}) copy-start(f32[256,512]{1,0:T(8,128)S(1)} %multiply_reduce_fusion) | copy-start | bytes 1572868
  29.4 11.4 %copy-start.1 = (f32[256,512]{1,0:T(8,128)}, f32[256,512]{1,0:T(8,128)S(1)}, u32[]{:S(2)}) copy-start(f32[256,512]{1,0:T(8,128)S(1)} %get-tuple-element.64) | copy-start | bytes 1572868
  30.4 10.2 %collective-permute-start.3 = (bf16[257,512]{1,0:T(8,128)(2,1)S(1)}, bf16[257,512]{1,0:T(8,128)(2,1)S(1)}, u32[]{:S(2)}, u32[]{:S(2)}) collective-permute-start(bf16[257,512]{1,0:T(8,128)(2,1)S(1)} %pad_maximum_fusion.5), channel_id=1, source_target_pairs={{0,4},{4,8},{8,12},{12,16},{16,20},{20,24},{24,28},{1,5},{5,9},{9,... | collective-permute-start | bytes 789512 | tf_op jit(solution)/shard_map/ppermute | solution.py:17
  40.6 0.9 %copy-start.8 = (bf16[257,512]{1,0:T(8,128)(2,1)}, bf16[257,512]{1,0:T(8,128)(2,1)S(1)}, u32[]{:S(2)}) copy-start(bf16[257,512]{1,0:T(8,128)(2,1)S(1)} %collective-permute-done.3) | copy-start | bytes 789508
  41.5 8.7 %collective-permute-start.4 = (bf16[257,512]{1,0:T(8,128)(2,1)}, bf16[257,512]{1,0:T(8,128)(2,1)}, u32[]{:S(2)}, u32[]{:S(2)}) collective-permute-start(bf16[257,512]{1,0:T(8,128)(2,1)} %pad_maximum_fusion.6), channel_id=1, source_target_pairs={{0,8},{4,12},{8,16},{12,20},{16,24},{20,28},{1,9},{5,13},{9,17},{1... | collective-permute-start | bytes 789512 | tf_op jit(solution)/shard_map/ppermute | solution.py:17
  45.6 21.6 %copy-start.17 = (bf16[2048,512]{1,0:T(8,128)(2,1)S(1)}, bf16[2048,512]{1,0:T(8,128)(2,1)}, u32[]{:S(2)}) copy-start(bf16[2048,512]{1,0:T(8,128)(2,1)} %param.29) | copy-start | bytes 6291460
  45.6 21.6 %copy-start.20 = (f32[512]{0:T(512)S(1)}, f32[512]{0:T(512)}, u32[]{:S(2)}) copy-start(f32[512]{0:T(512)} %param.30) | copy-start | bytes 6148
  51.7 13.8 %collective-permute-start.5 = (bf16[256,512]{1,0:T(8,128)(2,1)S(1)}, bf16[256,512]{1,0:T(8,128)(2,1)S(1)}, u32[]{:S(2)}, u32[]{:S(2)}) collective-permute-start(bf16[256,512]{1,0:T(8,128)(2,1)S(1)} %fusion.78), channel_id=1, source_target_pairs={{0,16},{4,20},{8,24},{12,28},{1,17},{5,21},{9,25},{13,29},{2,18},{... | collective-permute-start | bytes 786440 | tf_op jit(solution)/shard_map/ppermute | solution.py:17
  68.5 2.0 %collective-permute-start.6 = (bf16[128,2048]{1,0:T(8,128)(2,1)S(1)}, bf16[128,2048]{1,0:T(8,128)(2,1)S(1)}, u32[]{:S(2)}, u32[]{:S(2)}) collective-permute-start(bf16[128,2048]{1,0:T(8,128)(2,1)S(1)} %convolution_convert_fusion), channel_id=1, source_target_pairs={{0,1},{1,0},{2,3},{3,2},{4,5},{5,4},{6,7},{7,6},{8,9},{9,8},{10,11... | collective-permute-start | bytes 1572872 | tf_op jit(solution)/shard_map/ppermute | solution.py:188
  70.5 0.8 copy-start.14
  71.3 3.3 %copy-start.2 = (f32[256,512]{1,0:T(8,128)S(1)}, f32[256,512]{1,0:T(8,128)}, u32[]{:S(2)}) copy-start(f32[256,512]{1,0:T(8,128)} %copy-done.1) | copy-start | bytes 1572868
  71.3 3.3 %copy-start.9 = (bf16[257,512]{1,0:T(8,128)(2,1)S(1)}, bf16[257,512]{1,0:T(8,128)(2,1)}, u32[]{:S(2)}) copy-start(bf16[257,512]{1,0:T(8,128)(2,1)} %copy-done.8) | copy-start | bytes 789508
  72.9 8.4 %collective-permute-start.7 = (bf16[1,64,2048]{2,1,0:T(8,128)(2,1)S(1)}, bf16[1,64,2048]{2,1,0:T(8,128)(2,1)S(1)}, u32[]{:S(2)}, u32[]{:S(2)}) collective-permute-start(bf16[1,64,2048]{2,1,0:T(8,128)(2,1)S(1)} %fusion.24), channel_id=1, source_target_pairs={{0,2},{1,3},{2,0},{3,1},{4,6},{5,7},{6,4},{7,5},{8,10},{9,11},{10,... | collective-permute-start | bytes 786440 | tf_op jit(solution)/shard_map/ppermute | solution.py:199

commit v15 on v10

--- a/solution.py
+++ b/solution.py
@@ -46,7 +46,9 @@
 
 
 def segment_parts(queries, head_keys, head_values, decays, starts):
-    cumulative = jnp.cumsum(decays, axis=1)
+    index_rows = jnp.arange(queries.shape[1])
+    lower = (index_rows[:, None] >= index_rows[None, :]).astype(jnp.float32)
+    cumulative = jnp.einsum("ac,bck->bak", lower, decays, precision=lax.Precision.HIGHEST)
     groups = jnp.cumsum(starts, axis=1)
     intact = (groups == 0.0).astype(jnp.float32)
     final_log = cumulative[:, -1]
@@ -58,7 +60,6 @@
     ).astype(jnp.bfloat16)
     update = jnp.einsum("bsk,bsv->bkv", weighted, head_values, preferred_element_type=jnp.float32)
     step_decay = jnp.exp(final_log) * intact[:, -1:]
-    index_rows = jnp.arange(queries.shape[1])
     allowed = (groups[:, :, None] == groups[:, None, :]) & (
         index_rows[None, :, None] >= index_rows[None, None, :]
     )

time: 82.3 us -> 81.9 us (level)
    another operation x1 -> x0, other arithmetic: 1.2 us -> none  [segment_parts(): cumulative = jnp.cumsum(decays, axis=1)]
where the time goes in v15:
time: 81.9 us; the launch traced here: 81.3 us
  waiting for transfers between devices  32.9 us (40%)
  other arithmetic  16.8 us (21%)
  matrix products  14.8 us (18%)
  starting transfers between devices  11.8 us (14%)
  local copies, waits for them, and re-layouts  3.79 us (5%)
  between operations  1.14 us (1%)
    ppermute x4, waiting for transfers between devices, shifted(): lax.ppermute(value, axis, [(source, source + steps) for source in range(i...  24.2 us
    ppermute x4, starting transfers between devices, shifted(): lax.ppermute(value, axis, [(source, source + steps) for source in range(i...  8.46 us
    ppermute x1, waiting for transfers between devices, scatter_sum(): lax.ppermute(outgoing, axis, [(source, source ^ mask) for source in range...  4.57 us
    dot_general x4, matrix products, project(): jnp.dot(gathered, weight, preferred_element_type=jnp.float32)  3.84 us
    dot_general x1, matrix products, segment_parts(): jnp.einsum('bac,bcv->bav', scores, head_values, preferred_element_type=jn...  2.76 us
    dot_general x3, matrix products, segment_parts(): jnp.dot(lifted_intact[block], memory, precision=HIGH_PRECISION)  2.49 us
    ppermute x2, waiting for transfers between devices, gather_rows(): lax.ppermute(jnp.concatenate(received), axis, [(source, source ^ mask) fo...  2.33 us
    broadcast_in_dim x1, other arithmetic, shards(): segment_states = closing[None, None]  2.23 us
  transfers between devices with their start and end apart: 8, of which 8 were waited for; matrix products, arithmetic and copies ran while one was open for 18% of the time, Pallas kernels for 0%

profile of v15, /device:TPU:24, one launch (start us, length us, event | category | flops | bytes accessed | tf_op | source)
XLA Modules:
  0.0 81.3 jit_solution(12981428367848669399)
XLA Ops:
  0.7 1.6 %collective-permute-start = (bf16[64,2048]{1,0:T(8,128)(2,1)}, bf16[64,2048]{1,0:T(8,128)(2,1)S(1)}, u32[]{:S(2)}, u32[]{:S(2)}) collective-permute-start(bf16[64,2048]{1,0:T(8,128)(2,1)} %param.18), channel_id=1, source_target_pairs={{0,2},{1,3},{2,0},{3,1},{4,6},{5,7},{6,4},{7,5},{8,10},{9,11},{10,... | collective-permute-start | bytes 786440 | tf_op jit(solution)/shard_map/ppermute | solution.py:151
  2.2 0.8 select_reduce_fusion.1
  3.7 0.6 slice.181
  4.3 0.7 convert_element_type.167
  5.0 0.7 convert_element_type.177
  5.7 0.7 convert_element_type.183
  6.4 0.6 pad.32.clone
  7.1 0.6 iota_compare_fusion
  7.7 1.2 %collective-permute-done = bf16[64,2048]{1,0:T(8,128)(2,1)S(1)} collective-permute-done((bf16[64,2048]{1,0:T(8,128)(2,1)}, bf16[64,2048]{1,0:T(8,128)(2,1)S(1)}, u32[]{:S(2)}, u32[]{:S(2)}) %collective-permute-start) | collective-permute-done | bytes 262176 | tf_op jit(solution)/shard_map/ppermute | solution.py:151
  9.0 1.0 %pad_maximum_fusion.4 = bf16[128,2048]{1,0:T(8,128)(2,1)S(1)} fusion(bf16[64,2048]{1,0:T(8,128)(2,1)S(1)} %collective-permute-done, bf16[64,2048]{1,0:T(8,128)(2,1)} %param.18), kind=kLoop, calls=%fused_computation.41 | loop fusion | flops 1048576 | bytes 1048576 | tf_op jit(solution)/shard_map/concatenate | solution.py:152
  10.1 0.7 slice_compare_fusion
  10.9 1.1 %collective-permute-done.1 = bf16[128,2048]{1,0:T(8,128)(2,1)S(1)} collective-permute-done((bf16[128,2048]{1,0:T(8,128)(2,1)S(1)}, bf16[128,2048]{1,0:T(8,128)(2,1)S(1)}, u32[]{:S(2)}, u32[]{:S(2)}) %collective-permute-start.1) | collective-permute-done | bytes 524320 | tf_op jit(solution)/shard_map/ppermute | solution.py:151
  12.0 1.8 %conditional.1 = (bf16[256,2048]{1,0:T(8,128)(2,1)S(1)}) conditional(s32[]{:T(128)} %clamp.3, (bf16[64,2048]{1,0:T(8,128)(2,1)S(1)}, bf16[64,2048]{1,0:T(8,128)(2,1)S(1)}, bf16[64,2048]{1,0:T(8,128)(2,1)S(1)}, bf16[64,2048]{1,0:T(8,128)(2,1)S(1)}) %tuple.60, (bf16[64,2048]{1,0:T(8,128)(2,1)S(1)}, ...), branch_computations={%region_3.0_spmd, %region_4.5_spmd, %region_5.6_spmd, %region_6.7_... | conditional | flops 4194304 | bytes 3145764 | solution.py:165
  12.1 0.7 copy-done.4
  12.8 1.0 %pad_maximum_fusion = bf16[256,2048]{1,0:T(8,128)(2,1)S(1)} fusion(bf16[64,2048]{1,0:T(8,128)(2,1)S(1)} %get-tuple-element.40, bf16[64,2048]{1,0:T(8,128)(2,1)} %copy-done.4, bf16[64,2048]{1,0:T(8,128)(2,1)S(1)} %get-tuple-element.33, bf16[64,2048]{1,0:T(8,128)(2,1)S(1)} %get-tuple-element.32), kind=kLoop, calls=%fused_computation | loop fusion | flops 4194304 | bytes 2097152 | tf_op jit(solution)/shard_map/cond/branch_0_fun/concatenate | solution.py:163
  13.8 0.8 fusion.26
  15.0 1.9 %convolution_convert_fusion.5 = bf16[256,256]{1,0:T(8,128)(2,1)S(1)} fusion(bf16[256,2048]{1,0:T(8,128)(2,1)S(1)} %get-tuple-element.103, bf16[2048,256]{1,0:T(8,128)(2,1)} %param.20), kind=kOutput, calls=%fused_computation.17 | convolution fusion | flops 268500992 | bytes 2228224 | tf_op jit(solution)/shard_map/dot_general | solution.py:228
  16.9 0.7 convolution_convert_fusion.3
  17.6 0.5 copy-done.9
  18.6 0.7 select_bitcast_fusion
  19.2 3.4 %collective-permute-start.2 = (bf16[3,1024]{1,0:T(4,128)(2,1)S(1)}, bf16[3,1024]{1,0:T(4,128)(2,1)S(1)}, u32[]{:S(2)}, u32[]{:S(2)}) collective-permute-start(bf16[3,1024]{1,0:T(4,128)(2,1)S(1)} %get-tuple-element.59), channel_id=1, source_target_pairs={{0,4},{4,8},{8,12},{12,16},{16,20},{20,24},{24,28},{1,5},{5,9},{9,... | collective-permute-start | bytes 18440 | tf_op jit(solution)/shard_map/ppermute | solution.py:17
  22.8 2.8 %collective-permute-done.2 = bf16[3,1024]{1,0:T(4,128)(2,1)S(1)} collective-permute-done((bf16[3,1024]{1,0:T(4,128)(2,1)S(1)}, bf16[3,1024]{1,0:T(4,128)(2,1)S(1)}, u32[]{:S(2)}, u32[]{:S(2)}) %collective-permute-start.2) | collective-permute-done | bytes 6176 | tf_op jit(solution)/shard_map/ppermute | solution.py:17
  26.4 0.9 %broadcast_multiply_fusion = (f32[4,64,256]{2,1,0:T(8,128)}, f32[4,64,256]{2,1,0:T(8,128)S(1)}) fusion(f32[4,256]{1,0:T(4,128)S(1)} %pad_maximum_fusion.12, f32[4,64]{1,0:T(4,128)S(1)} %get-tuple-element.93, f32[4,64,256]{2,1,0:T(8,128)S(1)} %convolution_bitcast_fusion, f32[4,64,256]{2,1,0:T(8,128)S(1)} %bitcast.123), kind=kLoop, calls=%fused_computation.117 | loop fusion | flops 589824 | bytes 1053696 | tf_op jit(solution)/shard_map/mul | solution.py:86
  27.6 0.6 fusion.48
  28.9 2.5 %collective-permute-start.3 = (bf16[257,512]{1,0:T(8,128)(2,1)S(1)}, bf16[257,512]{1,0:T(8,128)(2,1)S(1)}, u32[]{:S(2)}, u32[]{:S(2)}) collective-permute-start(bf16[257,512]{1,0:T(8,128)(2,1)S(1)} %pad_maximum_fusion.5), channel_id=1, source_target_pairs={{0,4},{4,8},{8,12},{12,16},{16,20},{20,24},{24,28},{1,5},{5,9},{9,... | collective-permute-start | bytes 789512 | tf_op jit(solution)/shard_map/ppermute | solution.py:17
  31.4 1.0 %convolution_bitcast_fusion.3 = f32[1,64,512]{2,1,0:T(8,128)} fusion(f32[4,256,512]{2,1,0:T(8,128)S(1)} %fusion.48, f32[256]{0:T(256)S(1)} %get-tuple-element.97, f32[4,64,256]{2,1,0:T(8,128)S(1)} %get-tuple-element.69), kind=kOutput, calls=%fused_computation.20 | convolution fusion | flops 50462720 | bytes 721920 | tf_op jit(solution)/shard_map/dot_general | solution.py:81
  32.4 1.1 %convolution_bitcast_fusion.1 = f32[1,64,512]{2,1,0:T(8,128)} fusion(f32[4,256,512]{2,1,0:T(8,128)S(1)} %fusion.48, f32[256]{0:T(256)S(1)} %bitcast.137, f32[4,64,256]{2,1,0:T(8,128)S(1)} %get-tuple-element.69, f32[256]{0:T(256)S(1)} %bitcast.134, f32[256]{0:T(256)S(1)} %get-tuple-element.97), kind=kOutput, calls=%fused_computation.18 | convolution fusion | flops 50987008 | bytes 1772544 | tf_op jit(solution)/shard_map/dot_general | solution.py:81
  33.5 5.6 %collective-permute-done.3 = bf16[257,512]{1,0:T(8,128)(2,1)S(1)} collective-permute-done((bf16[257,512]{1,0:T(8,128)(2,1)S(1)}, bf16[257,512]{1,0:T(8,128)(2,1)S(1)}, u32[]{:S(2)}, u32[]{:S(2)}) %collective-permute-start.3) | collective-permute-done | bytes 263200 | tf_op jit(solution)/shard_map/ppermute | solution.py:17
  39.0 0.6 subtract_convert_fusion
  39.8 0.7 pad_maximum_fusion.6
  40.5 1.3 %collective-permute-start.4 = (bf16[257,512]{1,0:T(8,128)(2,1)}, bf16[257,512]{1,0:T(8,128)(2,1)}, u32[]{:S(2)}, u32[]{:S(2)}) collective-permute-start(bf16[257,512]{1,0:T(8,128)(2,1)} %pad_maximum_fusion.6), channel_id=1, source_target_pairs={{0,8},{4,12},{8,16},{12,20},{16,24},{20,28},{1,9},{5,13},{9,17},{1... | collective-permute-start | bytes 789512 | tf_op jit(solution)/shard_map/ppermute | solution.py:17
  41.8 2.8 %convolution_add_fusion = f32[4,64,512]{2,1,0:T(8,128)} fusion(f32[1,64,512]{2,1,0:T(8,128)} %convolution_bitcast_fusion.1, f32[1,64,512]{2,1,0:T(8,128)S(1)} %convolution_bitcast_fusion.2, f32[1,64,512]{2,1,0:T(8,128)} %convolution_bitcast_fusion.3, f32[4]{0:T(128)} %pad.32.clone, f32[4,64,256]{2,1,0:T(8,128)} %copy-done.8, ...), kind=kOutput, calls=%fused_computation.8 | convolution fusion | flops 27525120 | bytes 2233360 | tf_op jit(solution)/shard_map/bac,bcv->bav/dot_general | solution.py:72
  44.6 4.7 %collective-permute-done.4 = bf16[257,512]{1,0:T(8,128)(2,1)} collective-permute-done((bf16[257,512]{1,0:T(8,128)(2,1)}, bf16[257,512]{1,0:T(8,128)(2,1)}, u32[]{:S(2)}, u32[]{:S(2)}) %collective-permute-start.4) | collective-permute-done | bytes 263200 | tf_op jit(solution)/shard_map/ppermute | solution.py:17
  49.3 1.3 %fusion.76 = bf16[256,512]{1,0:T(8,128)(2,1)S(1)} fusion(f32[256,512]{1,0:T(8,128)} %copy-done.1, bf16[257,512]{1,0:T(8,128)(2,1)S(1)} %collective-permute-done.3, f32[256]{0:T(256)S(1)} %get-tuple-element.67, pred[]{:T(512)S(6)} %ge.73, bf16[257,512]{1,0:T(8,128)(2,1)} %collective-permute-done.4, f32[256]{0:T(256)} %get-tuple-element.62, pred[]{:T(512)S(6)} %ge.72), kind=kLoop, calls=%fused_computation.174 | loop fusion | flops 1179648 | bytes 1312770 | tf_op jit(solution)/shard_map/convert_element_type | solution.py:120
  50.6 1.3 %collective-permute-start.5 = (bf16[256,512]{1,0:T(8,128)(2,1)S(1)}, bf16[256,512]{1,0:T(8,128)(2,1)S(1)}, u32[]{:S(2)}, u32[]{:S(2)}) collective-permute-start(bf16[256,512]{1,0:T(8,128)(2,1)S(1)} %fusion.76), channel_id=1, source_target_pairs={{0,16},{4,20},{8,24},{12,28},{1,17},{5,21},{9,25},{13,29},{2,18},{... | collective-permute-start | bytes 786440 | tf_op jit(solution)/shard_map/ppermute | solution.py:17
  51.9 0.7 slice_convert_fusion
  52.6 0.7 multiply_select_fusion
  53.3 11.1 %collective-permute-done.5 = bf16[256,512]{1,0:T(8,128)(2,1)S(1)} collective-permute-done((bf16[256,512]{1,0:T(8,128)(2,1)S(1)}, bf16[256,512]{1,0:T(8,128)(2,1)S(1)}, u32[]{:S(2)}, u32[]{:S(2)}) %collective-permute-start.5) | collective-permute-done | bytes 262176 | tf_op jit(solution)/shard_map/ppermute | solution.py:17
  64.4 2.0 %multiply_reduce_fusion.3 = (f32[256]{0:T(256)S(1)}, f32[256,512]{1,0:T(8,128)S(1)}) fusion(f32[256,512]{1,0:T(8,128)} %bitcast.146, f32[256,256]{1,0:T(8,128)} %bitcast.128, bf16[256,512]{1,0:T(8,128)(2,1)S(1)} %collective-permute-done.5, f32[256]{0:T(256)} %bitcast.143, f32[256]{0:T(256)S(1)} %get-tuple-element.96, pred[]{:T(512)S(6)} %ge.72, ...), kind=kOutput, calls=%fused_computation.55 | convolution fusion | flops 202899200 | bytes 2100226 | tf_op jit(solution)/shard_map/dot_general | solution.py:266
  66.4 0.8 multiply_convert_fusion
  67.2 0.4 convolution_convert_fusion
  67.8 1.9 %collective-permute-done.6 = bf16[128,2048]{1,0:T(8,128)(2,1)S(1)} collective-permute-done((bf16[128,2048]{1,0:T(8,128)(2,1)S(1)}, bf16[128,2048]{1,0:T(8,128)(2,1)S(1)}, u32[]{:S(2)}, u32[]{:S(2)}) %collective-permute-start.6) | collective-permute-done | bytes 524320 | tf_op jit(solution)/shard_map/ppermute | solution.py:189
  69.7 0.8 copy-done.12
  70.5 1.6 %convert_add_fusion = f32[128,2048]{1,0:T(8,128)S(1)} fusion(bf16[128,2048]{1,0:T(8,128)(2,1)} %copy-done.12, bf16[512,2048]{1,0:T(8,128)(2,1)S(1)} %copy-done, bf16[64,512]{1,0:T(8,128)(2,1)S(1)} %get-tuple-element.78, bf16[64,512]{1,0:T(8,128)(2,1)S(1)} %get-tuple-element.77), kind=kOutput, calls=%fused_computation.24 | convolution fusion | flops 269746176 | bytes 3801088 | tf_op jit(solution)/shard_map/dot_general | solution.py:191
  72.1 1.6 %collective-permute-start.7 = (bf16[1,64,2048]{2,1,0:T(8,128)(2,1)S(1)}, bf16[1,64,2048]{2,1,0:T(8,128)(2,1)S(1)}, u32[]{:S(2)}, u32[]{:S(2)}) collective-permute-start(bf16[1,64,2048]{2,1,0:T(8,128)(2,1)S(1)} %fusion.24), channel_id=1, source_target_pairs={{0,2},{1,3},{2,0},{3,1},{4,6},{5,7},{6,4},{7,5},{8,10},{9,11},{10,... | collective-permute-start | bytes 786440 | tf_op jit(solution)/shard_map/ppermute | solution.py:200
  73.7 2.2 %fusion.4 = f32[1,1,256,512]{3,2,1,0:T(8,128)} fusion(bf16[256,512]{1,0:T(8,128)(2,1)S(1)} %copy-done.14, f32[256]{0:T(256)S(1)} %get-tuple-element.95, pred[]{:T(512)S(6)} %ge.71, f32[256,512]{1,0:T(8,128)S(1)} %copy-done.2, bf16[257,512]{1,0:T(8,128)(2,1)S(1)} %collective-permute-done.3, f32[256]{0:T(256)S(1)} %get-tuple-element.67, pred[]{:T(512)S(6)} %ge.73, ...), kind=kLoop, calls=%fused_computation.38 | loop fusion | flops 1572864 | bytes 1838083 | tf_op jit(solution)/shard_map/broadcast_in_dim | solution.py:275
  75.9 4.6 %collective-permute-done.7 = bf16[1,64,2048]{2,1,0:T(8,128)(2,1)S(1)} collective-permute-done((bf16[1,64,2048]{2,1,0:T(8,128)(2,1)S(1)}, bf16[1,64,2048]{2,1,0:T(8,128)(2,1)S(1)}, u32[]{:S(2)}, u32[]{:S(2)}) %collective-permute-start.7) | collective-permute-done | bytes 262176 | tf_op jit(solution)/shard_map/ppermute | solution.py:200
  80.5 0.8 fusion.6
  (81 shorter events, 4.0 us)
Async XLA Ops:
  0.6 66.6 %copy-start = (bf16[512,2048]{1,0:T(8,128)(2,1)S(1)}, bf16[512,2048]{1,0:T(8,128)(2,1)}, u32[]{:S(2)}) copy-start(bf16[512,2048]{1,0:T(8,128)(2,1)} %param.31) | copy-start | bytes 6291460
  0.6 11.3 %copy-start.3 = (bf16[64,2048]{1,0:T(8,128)(2,1)S(1)}, bf16[64,2048]{1,0:T(8,128)(2,1)}, u32[]{:S(2)}) copy-start(bf16[64,2048]{1,0:T(8,128)(2,1)} %param.18) | copy-start | bytes 786436
  0.7 8.3 %collective-permute-start = (bf16[64,2048]{1,0:T(8,128)(2,1)}, bf16[64,2048]{1,0:T(8,128)(2,1)S(1)}, u32[]{:S(2)}, u32[]{:S(2)}) collective-permute-start(bf16[64,2048]{1,0:T(8,128)(2,1)} %param.18), channel_id=1, source_target_pairs={{0,2},{1,3},{2,0},{3,1},{4,6},{5,7},{6,4},{7,5},{8,10},{9,11},{10,... | collective-permute-start | bytes 786440 | tf_op jit(solution)/shard_map/ppermute | solution.py:151
  10.0 2.0 %collective-permute-start.1 = (bf16[128,2048]{1,0:T(8,128)(2,1)S(1)}, bf16[128,2048]{1,0:T(8,128)(2,1)S(1)}, u32[]{:S(2)}, u32[]{:S(2)}) collective-permute-start(bf16[128,2048]{1,0:T(8,128)(2,1)S(1)} %pad_maximum_fusion.4), channel_id=1, source_target_pairs={{0,1},{1,0},{2,3},{3,2},{4,5},{5,4},{6,7},{7,6},{8,9},{9,8},{10,11... | collective-permute-start | bytes 1572872 | tf_op jit(solution)/shard_map/ppermute | solution.py:151
  12.0 1.8 %copy-start.20 = (bf16[2048,16]{0,1:T(8,128)(2,1)S(1)}, bf16[2048,16]{0,1:T(8,128)(2,1)}, u32[]{:S(2)}) copy-start(bf16[2048,16]{0,1:T(8,128)(2,1)} %param.26) | copy-start | bytes 196612
  12.0 1.8 %copy-start.21 = (bf16[16,256]{1,0:T(8,128)(2,1)S(1)}, bf16[16,256]{1,0:T(8,128)(2,1)}, u32[]{:S(2)}) copy-start(bf16[16,256]{1,0:T(8,128)(2,1)} %param.27) | copy-start | bytes 24580
  12.0 1.8 %copy-start.23 = (f32[256]{0:T(256)S(1)}, f32[256]{0:T(256)}, u32[]{:S(2)}) copy-start(f32[256]{0:T(256)} %param.28) | copy-start | bytes 3076
  12.1 0.7 copy-start.4
  14.6 2.2 %copy-start.18 = (bf16[2048,512]{1,0:T(8,128)(2,1)S(1)}, bf16[2048,512]{1,0:T(8,128)(2,1)}, u32[]{:S(2)}) copy-start(bf16[2048,512]{1,0:T(8,128)(2,1)} %param.22) | copy-start | bytes 6291460
  14.9 12.6 %copy-start.8 = (f32[4,64,256]{2,1,0:T(8,128)}, f32[4,64,256]{2,1,0:T(8,128)S(1)}, u32[]{:S(2)}) copy-start(f32[4,64,256]{2,1,0:T(8,128)S(1)} %convolution_bitcast_fusion) | copy-start | bytes 786436
  16.9 1.2 %copy-start.9 = (bf16[2048,256]{1,0:T(8,128)(2,1)S(1)}, bf16[2048,256]{1,0:T(8,128)(2,1)}, u32[]{:S(2)}) copy-start(bf16[2048,256]{1,0:T(8,128)(2,1)} %param.21) | copy-start | bytes 3145732
  19.2 6.4 %collective-permute-start.2 = (bf16[3,1024]{1,0:T(4,128)(2,1)S(1)}, bf16[3,1024]{1,0:T(4,128)(2,1)S(1)}, u32[]{:S(2)}, u32[]{:S(2)}) collective-permute-start(bf16[3,1024]{1,0:T(4,128)(2,1)S(1)} %get-tuple-element.59), channel_id=1, source_target_pairs={{0,4},{4,8},{8,12},{12,16},{16,20},{20,24},{24,28},{1,5},{5,9},{9,... | collective-permute-start | bytes 18440 | tf_op jit(solution)/shard_map/ppermute | solution.py:17
  26.3 1.2 %copy-start.10 = (f32[256,256]{1,0:T(8,128)}, f32[256,256]{1,0:T(8,128)S(1)}, u32[]{:S(2)}) copy-start(f32[256,256]{1,0:T(8,128)S(1)} %get-tuple-element.56) | copy-start | bytes 786436
  26.3 1.8 %copy-start.15 = (f32[256,256]{1,0:T(8,128)}, f32[256,256]{1,0:T(8,128)S(1)}, u32[]{:S(2)}) copy-start(f32[256,256]{1,0:T(8,128)S(1)} %get-tuple-element.57) | copy-start | bytes 786436
  27.5 0.9 %copy-start.11 = (f32[256,512]{1,0:T(8,128)}, f32[256,512]{1,0:T(8,128)S(1)}, u32[]{:S(2)}) copy-start(f32[256,512]{1,0:T(8,128)S(1)} %multiply_reduce_fusion) | copy-start | bytes 1572868
  28.4 12.1 %copy-start.1 = (f32[256,512]{1,0:T(8,128)}, f32[256,512]{1,0:T(8,128)S(1)}, u32[]{:S(2)}) copy-start(f32[256,512]{1,0:T(8,128)S(1)} %get-tuple-element.64) | copy-start | bytes 1572868
  28.9 10.2 %collective-permute-start.3 = (bf16[257,512]{1,0:T(8,128)(2,1)S(1)}, bf16[257,512]{1,0:T(8,128)(2,1)S(1)}, u32[]{:S(2)}, u32[]{:S(2)}) collective-permute-start(bf16[257,512]{1,0:T(8,128)(2,1)S(1)} %pad_maximum_fusion.5), channel_id=1, source_target_pairs={{0,4},{4,8},{8,12},{12,16},{16,20},{20,24},{24,28},{1,5},{5,9},{9,... | collective-permute-start | bytes 789512 | tf_op jit(solution)/shard_map/ppermute | solution.py:17
  39.0 0.6 copy-start.17
  40.5 8.7 %collective-permute-start.4 = (bf16[257,512]{1,0:T(8,128)(2,1)}, bf16[257,512]{1,0:T(8,128)(2,1)}, u32[]{:S(2)}, u32[]{:S(2)}) collective-permute-start(bf16[257,512]{1,0:T(8,128)(2,1)} %pad_maximum_fusion.6), channel_id=1, source_target_pairs={{0,8},{4,12},{8,16},{12,20},{16,24},{20,28},{1,9},{5,13},{9,17},{1... | collective-permute-start | bytes 789512 | tf_op jit(solution)/shard_map/ppermute | solution.py:17
  44.6 21.8 %copy-start.19 = (bf16[2048,512]{1,0:T(8,128)(2,1)S(1)}, bf16[2048,512]{1,0:T(8,128)(2,1)}, u32[]{:S(2)}) copy-start(bf16[2048,512]{1,0:T(8,128)(2,1)} %param.29) | copy-start | bytes 6291460
  44.6 21.8 %copy-start.22 = (f32[512]{0:T(512)S(1)}, f32[512]{0:T(512)}, u32[]{:S(2)}) copy-start(f32[512]{0:T(512)} %param.30) | copy-start | bytes 6148
  50.6 13.8 %collective-permute-start.5 = (bf16[256,512]{1,0:T(8,128)(2,1)S(1)}, bf16[256,512]{1,0:T(8,128)(2,1)S(1)}, u32[]{:S(2)}, u32[]{:S(2)}) collective-permute-start(bf16[256,512]{1,0:T(8,128)(2,1)S(1)} %fusion.76), channel_id=1, source_target_pairs={{0,16},{4,20},{8,24},{12,28},{1,17},{5,21},{9,25},{13,29},{2,18},{... | collective-permute-start | bytes 786440 | tf_op jit(solution)/shard_map/ppermute | solution.py:17
  64.4 2.0 %copy-start.13 = (bf16[256,512]{1,0:T(8,128)(2,1)}, bf16[256,512]{1,0:T(8,128)(2,1)S(1)}, u32[]{:S(2)}) copy-start(bf16[256,512]{1,0:T(8,128)(2,1)S(1)} %collective-permute-done.5) | copy-start | bytes 786436
  67.7 2.0 %collective-permute-start.6 = (bf16[128,2048]{1,0:T(8,128)(2,1)S(1)}, bf16[128,2048]{1,0:T(8,128)(2,1)S(1)}, u32[]{:S(2)}, u32[]{:S(2)}) collective-permute-start(bf16[128,2048]{1,0:T(8,128)(2,1)S(1)} %convolution_convert_fusion), channel_id=1, source_target_pairs={{0,1},{1,0},{2,3},{3,2},{4,5},{5,4},{6,7},{7,6},{8,9},{9,8},{10,11... | collective-permute-start | bytes 1572872 | tf_op jit(solution)/shard_map/ppermute | solution.py:189
  69.7 0.8 copy-start.12
  70.5 3.2 %copy-start.2 = (f32[256,512]{1,0:T(8,128)S(1)}, f32[256,512]{1,0:T(8,128)}, u32[]{:S(2)}) copy-start(f32[256,512]{1,0:T(8,128)} %copy-done.1) | copy-start | bytes 1572868
  70.5 3.2 %copy-start.14 = (bf16[256,512]{1,0:T(8,128)(2,1)S(1)}, bf16[256,512]{1,0:T(8,128)(2,1)}, u32[]{:S(2)}) copy-start(bf16[256,512]{1,0:T(8,128)(2,1)} %copy-done.13) | copy-start | bytes 786436
  70.5 3.2 %copy-start.16 = (f32[256]{0:T(256)S(1)}, f32[256]{0:T(256)}, u32[]{:S(2)}) copy-start(f32[256]{0:T(256)} %get-tuple-element.62) | copy-start | bytes 3076
  72.1 8.4 %collective-permute-start.7 = (bf16[1,64,2048]{2,1,0:T(8,128)(2,1)S(1)}, bf16[1,64,2048]{2,1,0:T(8,128)(2,1)S(1)}, u32[]{:S(2)}, u32[]{:S(2)}) collective-permute-start(bf16[1,64,2048]{2,1,0:T(8,128)(2,1)S(1)} %fusion.24), channel_id=1, source_target_pairs={{0,2},{1,3},{2,0},{3,1},{4,6},{5,7},{6,4},{7,5},{8,10},{9,11},{10,... | collective-permute-start | bytes 786440 | tf_op jit(solution)/shard_map/ppermute | solution.py:200

commit v16 on v8

--- a/solution.py
+++ b/solution.py
@@ -46,7 +46,9 @@
 
 
 def segment_parts(queries, head_keys, head_values, decays, starts):
-    cumulative = jnp.cumsum(decays, axis=1)
+    index_rows = jnp.arange(queries.shape[1])
+    lower = (index_rows[:, None] >= index_rows[None, :]).astype(jnp.float32)
+    cumulative = jnp.einsum("ac,bck->bak", lower, decays, precision=lax.Precision.HIGHEST)
     groups = jnp.cumsum(starts, axis=1)
     intact = (groups == 0.0).astype(jnp.float32)
     final_log = cumulative[:, -1]
@@ -58,7 +60,6 @@
     ).astype(jnp.bfloat16)
     update = jnp.einsum("bsk,bsv->bkv", weighted, head_values, preferred_element_type=jnp.float32)
     step_decay = jnp.exp(final_log) * intact[:, -1:]
-    index_rows = jnp.arange(queries.shape[1])
     allowed = (groups[:, :, None] == groups[:, None, :]) & (
         index_rows[None, :, None] >= index_rows[None, None, :]
     )
@@ -180,20 +181,29 @@
             outgoing = lax.dynamic_index_in_dim(chunks, (place + step) % count, 0, False)
             total = total + lax.ppermute(outgoing, axis, pairs).astype(jnp.float32)
         return total.astype(jnp.bfloat16)
-    held = [term(index) for index in range(count)]
+    def term(rows):
+        return jnp.dot(rows, weight, preferred_element_type=jnp.float32).astype(jnp.bfloat16)
+
+    held = [lax.slice_in_dim(gated, index * chunk, (index + 1) * chunk, axis=0) for index in range(count)]
+    sums = None
     mask = 1
     while mask < count:
         odd = (place // mask) % 2 == 1
-        pairs = list(zip(held[0::2], held[1::2]))
-        keep = [jnp.where(odd, high, low) for low, high in pairs]
-        outgoing = jnp.stack([jnp.where(odd, low, high).astype(jnp.bfloat16) for low, high in pairs])
+        rows = list(zip(held[0::2], held[1::2]))
+        outgoing = term(jnp.concatenate([jnp.where(odd, low, high) for low, high in rows]))
+        if sums is not None:
+            parts = list(zip(sums[0::2], sums[1::2]))
+            carried = jnp.concatenate([jnp.where(odd, low, high) for low, high in parts])
+            outgoing = (outgoing.astype(jnp.float32) + carried).astype(jnp.bfloat16)
+            kept_sums = [jnp.where(odd, high, low) for low, high in parts]
+        else:
+            kept_sums = [0.0] * len(rows)
         incoming = lax.ppermute(outgoing, axis, [(source, source ^ mask) for source in range(count)])
-        held = [
-            kept.astype(jnp.float32) + incoming[index].astype(jnp.float32)
-            for index, kept in enumerate(keep)
-        ]
+        incoming = jnp.split(incoming.astype(jnp.float32), len(rows))
+        sums = [kept + arrived for kept, arrived in zip(kept_sums, incoming)]
+        held = [jnp.where(odd, high, low) for low, high in rows]
         mask *= 2
-    return held[0].astype(jnp.bfloat16)
+    return (term(held[0]).astype(jnp.float32) + sums[0]).astype(jnp.bfloat16)
 
 
 def shards(

time: 86 us -> 83.9 us (0.976)
  other arithmetic: 20.4 us -> 17.9 us
  matrix products: 15.1 us -> 16.8 us
  waiting for transfers between devices: 33.2 us -> 31.9 us
    another operation x5 -> x0, other arithmetic: 3.36 us -> none  [the longest x4 2.15 us: scatter_sum(): jnp.stack([jnp.where(odd, low, high).astype(jnp.bfloat16) for low, high i...]
    dot_general x4 -> x3, matrix products: 1.92 us -> 4.05 us  [term(): jnp.dot(rows, weight, preferred_element_type=jnp.float32)]
    ppermute x2, waiting for transfers between devices: 6.72 us -> 5.38 us  [scatter_sum(): lax.ppermute(outgoing, axis, [(source, source ^ mask) for source in range...]
    convert_element_type x1 -> x2, other arithmetic: 2.02 us -> 1.93 us  [the longest x1 1.13 us: scatter_sum(): incoming = jnp.split(incoming.astype(jnp.float32), len(rows))]
  transfers between devices with their start and end apart: 8 -> 8, of which waited for: 8 -> 8; matrix products, arithmetic and copies ran while one was open for 18% -> 20% of each run, Pallas kernels for 0% -> 0%
where the time goes in v16:
time: 83.9 us; the launch traced here: 83.2 us
  waiting for transfers between devices  31.9 us (38%)
  other arithmetic  17.9 us (21%)
  matrix products  16.8 us (20%)
  starting transfers between devices  11.7 us (14%)
  local copies, waits for them, and re-layouts  3.69 us (4%)
  between operations  1.12 us (1%)
    ppermute x4, waiting for transfers between devices, shifted(): lax.ppermute(value, axis, [(source, source + steps) for source in range(i...  24.2 us
    ppermute x4, starting transfers between devices, shifted(): lax.ppermute(value, axis, [(source, source + steps) for source in range(i...  8.46 us
    ppermute x2, waiting for transfers between devices, scatter_sum(): lax.ppermute(outgoing, axis, [(source, source ^ mask) for source in range...  5.38 us
    dot_general x3, matrix products, term(): jnp.dot(rows, weight, preferred_element_type=jnp.float32)  4.05 us
    dot_general x4, matrix products, project(): jnp.dot(gathered, weight, preferred_element_type=jnp.float32)  3.84 us
    dot_general x1, matrix products, segment_parts(): jnp.einsum('bac,bcv->bav', scores, head_values, preferred_element_type=jn...  2.76 us
    dot_general x3, matrix products, segment_parts(): jnp.dot(lifted_intact[block], memory, precision=HIGH_PRECISION)  2.49 us
    ppermute x2, waiting for transfers between devices, gather_rows(): lax.ppermute(jnp.concatenate(received), axis, [(source, source ^ mask) fo...  2.33 us
  transfers between devices with their start and end apart: 8, of which 8 were waited for; matrix products, arithmetic and copies ran while one was open for 20% of the time, Pallas kernels for 0%

profile of v16, /device:TPU:24, one launch (start us, length us, event | category | flops | bytes accessed | tf_op | source)
XLA Modules:
  0.0 83.2 jit_solution(11047866208976481304)
XLA Ops:
  0.7 1.6 %collective-permute-start = (bf16[64,2048]{1,0:T(8,128)(2,1)}, bf16[64,2048]{1,0:T(8,128)(2,1)S(1)}, u32[]{:S(2)}, u32[]{:S(2)}) collective-permute-start(bf16[64,2048]{1,0:T(8,128)(2,1)} %param.18), channel_id=1, source_target_pairs={{0,2},{1,3},{2,0},{3,1},{4,6},{5,7},{6,4},{7,5},{8,10},{9,11},{10,... | collective-permute-start | bytes 786440 | tf_op jit(solution)/shard_map/ppermute | solution.py:151
  2.2 0.8 select_reduce_fusion.1
  4.3 0.7 convert_element_type.170
  5.0 0.7 convert_element_type.180
  5.7 0.7 convert_element_type.186
  6.4 0.6 pad.30.clone
  7.1 0.6 iota_compare_fusion
  7.7 1.2 %collective-permute-done = bf16[64,2048]{1,0:T(8,128)(2,1)S(1)} collective-permute-done((bf16[64,2048]{1,0:T(8,128)(2,1)}, bf16[64,2048]{1,0:T(8,128)(2,1)S(1)}, u32[]{:S(2)}, u32[]{:S(2)}) %collective-permute-start) | collective-permute-done | bytes 262176 | tf_op jit(solution)/shard_map/ppermute | solution.py:151
  9.0 1.0 %pad_maximum_fusion.4 = bf16[128,2048]{1,0:T(8,128)(2,1)S(1)} fusion(bf16[64,2048]{1,0:T(8,128)(2,1)S(1)} %collective-permute-done, bf16[64,2048]{1,0:T(8,128)(2,1)} %param.18), kind=kLoop, calls=%fused_computation.42 | loop fusion | flops 1048576 | bytes 1048576 | tf_op jit(solution)/shard_map/concatenate | solution.py:152
  10.1 0.7 slice_compare_fusion
  10.9 1.1 %collective-permute-done.1 = bf16[128,2048]{1,0:T(8,128)(2,1)S(1)} collective-permute-done((bf16[128,2048]{1,0:T(8,128)(2,1)S(1)}, bf16[128,2048]{1,0:T(8,128)(2,1)S(1)}, u32[]{:S(2)}, u32[]{:S(2)}) %collective-permute-start.1) | collective-permute-done | bytes 524320 | tf_op jit(solution)/shard_map/ppermute | solution.py:151
  12.0 1.8 %conditional.1 = (bf16[256,2048]{1,0:T(8,128)(2,1)S(1)}) conditional(s32[]{:T(128)} %clamp.3, (bf16[64,2048]{1,0:T(8,128)(2,1)S(1)}, bf16[64,2048]{1,0:T(8,128)(2,1)S(1)}, bf16[64,2048]{1,0:T(8,128)(2,1)S(1)}, bf16[64,2048]{1,0:T(8,128)(2,1)S(1)}) %tuple.58, (bf16[64,2048]{1,0:T(8,128)(2,1)S(1)}, ...), branch_computations={%region_3.0_spmd, %region_4.5_spmd, %region_5.6_spmd, %region_6.7_... | conditional | flops 4194304 | bytes 3145764 | solution.py:165
  12.1 0.7 copy-done.4
  12.8 1.0 %pad_maximum_fusion = bf16[256,2048]{1,0:T(8,128)(2,1)S(1)} fusion(bf16[64,2048]{1,0:T(8,128)(2,1)S(1)} %get-tuple-element.40, bf16[64,2048]{1,0:T(8,128)(2,1)} %copy-done.4, bf16[64,2048]{1,0:T(8,128)(2,1)S(1)} %get-tuple-element.33, bf16[64,2048]{1,0:T(8,128)(2,1)S(1)} %get-tuple-element.32), kind=kLoop, calls=%fused_computation | loop fusion | flops 4194304 | bytes 2097152 | tf_op jit(solution)/shard_map/cond/branch_0_fun/concatenate | solution.py:163
  13.8 0.8 fusion.25
  15.0 1.9 %convolution_convert_fusion.6 = bf16[256,256]{1,0:T(8,128)(2,1)S(1)} fusion(bf16[256,2048]{1,0:T(8,128)(2,1)S(1)} %get-tuple-element.101, bf16[2048,256]{1,0:T(8,128)(2,1)} %param.20), kind=kOutput, calls=%fused_computation.19 | convolution fusion | flops 268500992 | bytes 2228224 | tf_op jit(solution)/shard_map/dot_general | solution.py:228
  16.9 0.7 convolution_convert_fusion.4
  18.6 0.7 select_bitcast_fusion
  19.2 3.4 %collective-permute-start.2 = (bf16[3,1024]{1,0:T(4,128)(2,1)S(1)}, bf16[3,1024]{1,0:T(4,128)(2,1)S(1)}, u32[]{:S(2)}, u32[]{:S(2)}) collective-permute-start(bf16[3,1024]{1,0:T(4,128)(2,1)S(1)} %get-tuple-element.59), channel_id=1, source_target_pairs={{0,4},{4,8},{8,12},{12,16},{16,20},{20,24},{24,28},{1,5},{5,9},{9,... | collective-permute-start | bytes 18440 | tf_op jit(solution)/shard_map/ppermute | solution.py:17
  22.8 2.8 %collective-permute-done.2 = bf16[3,1024]{1,0:T(4,128)(2,1)S(1)} collective-permute-done((bf16[3,1024]{1,0:T(4,128)(2,1)S(1)}, bf16[3,1024]{1,0:T(4,128)(2,1)S(1)}, u32[]{:S(2)}, u32[]{:S(2)}) %collective-permute-start.2) | collective-permute-done | bytes 6176 | tf_op jit(solution)/shard_map/ppermute | solution.py:17
  26.4 0.9 %broadcast_multiply_fusion = (f32[4,64,256]{2,1,0:T(8,128)}, f32[4,64,256]{2,1,0:T(8,128)S(1)}) fusion(f32[4,256]{1,0:T(4,128)S(1)} %pad_maximum_fusion.12, f32[4,64]{1,0:T(4,128)S(1)} %get-tuple-element.91, f32[4,64,256]{2,1,0:T(8,128)S(1)} %convolution_bitcast_fusion, f32[4,64,256]{2,1,0:T(8,128)S(1)} %bitcast.119), kind=kLoop, calls=%fused_computation.113 | loop fusion | flops 589824 | bytes 1053696 | tf_op jit(solution)/shard_map/mul | solution.py:86
  27.6 0.6 fusion.47
  28.9 2.5 %collective-permute-start.3 = (bf16[257,512]{1,0:T(8,128)(2,1)S(1)}, bf16[257,512]{1,0:T(8,128)(2,1)S(1)}, u32[]{:S(2)}, u32[]{:S(2)}) collective-permute-start(bf16[257,512]{1,0:T(8,128)(2,1)S(1)} %pad_maximum_fusion.5), channel_id=1, source_target_pairs={{0,4},{4,8},{8,12},{12,16},{16,20},{20,24},{24,28},{1,5},{5,9},{9,... | collective-permute-start | bytes 789512 | tf_op jit(solution)/shard_map/ppermute | solution.py:17
  31.4 1.0 %convolution_bitcast_fusion.3 = f32[1,64,512]{2,1,0:T(8,128)} fusion(f32[4,256,512]{2,1,0:T(8,128)S(1)} %fusion.47, f32[256]{0:T(256)S(1)} %get-tuple-element.95, f32[4,64,256]{2,1,0:T(8,128)S(1)} %get-tuple-element.69), kind=kOutput, calls=%fused_computation.22 | convolution fusion | flops 50462720 | bytes 721920 | tf_op jit(solution)/shard_map/dot_general | solution.py:81
  32.4 1.1 %convolution_bitcast_fusion.1 = f32[1,64,512]{2,1,0:T(8,128)} fusion(f32[4,256,512]{2,1,0:T(8,128)S(1)} %fusion.47, f32[256]{0:T(256)S(1)} %bitcast.133, f32[4,64,256]{2,1,0:T(8,128)S(1)} %get-tuple-element.69, f32[256]{0:T(256)S(1)} %bitcast.130, f32[256]{0:T(256)S(1)} %get-tuple-element.95), kind=kOutput, calls=%fused_computation.20 | convolution fusion | flops 50987008 | bytes 1772544 | tf_op jit(solution)/shard_map/dot_general | solution.py:81
  33.5 5.6 %collective-permute-done.3 = bf16[257,512]{1,0:T(8,128)(2,1)S(1)} collective-permute-done((bf16[257,512]{1,0:T(8,128)(2,1)S(1)}, bf16[257,512]{1,0:T(8,128)(2,1)S(1)}, u32[]{:S(2)}, u32[]{:S(2)}) %collective-permute-start.3) | collective-permute-done | bytes 263200 | tf_op jit(solution)/shard_map/ppermute | solution.py:17
  39.0 0.6 subtract_convert_fusion
  39.8 0.7 pad_maximum_fusion.6
  40.5 1.3 %collective-permute-start.4 = (bf16[257,512]{1,0:T(8,128)(2,1)}, bf16[257,512]{1,0:T(8,128)(2,1)}, u32[]{:S(2)}, u32[]{:S(2)}) collective-permute-start(bf16[257,512]{1,0:T(8,128)(2,1)} %pad_maximum_fusion.6), channel_id=1, source_target_pairs={{0,8},{4,12},{8,16},{12,20},{16,24},{20,28},{1,9},{5,13},{9,17},{1... | collective-permute-start | bytes 789512 | tf_op jit(solution)/shard_map/ppermute | solution.py:17
  41.8 2.8 %convolution_add_fusion = f32[4,64,512]{2,1,0:T(8,128)} fusion(f32[1,64,512]{2,1,0:T(8,128)} %convolution_bitcast_fusion.1, f32[1,64,512]{2,1,0:T(8,128)S(1)} %convolution_bitcast_fusion.2, f32[1,64,512]{2,1,0:T(8,128)} %convolution_bitcast_fusion.3, f32[4]{0:T(128)} %pad.30.clone, f32[4,64,256]{2,1,0:T(8,128)} %copy-done.8, ...), kind=kOutput, calls=%fused_computation.10 | convolution fusion | flops 27525120 | bytes 2233360 | tf_op jit(solution)/shard_map/bac,bcv->bav/dot_general | solution.py:72
  44.6 4.7 %collective-permute-done.4 = bf16[257,512]{1,0:T(8,128)(2,1)} collective-permute-done((bf16[257,512]{1,0:T(8,128)(2,1)}, bf16[257,512]{1,0:T(8,128)(2,1)}, u32[]{:S(2)}, u32[]{:S(2)}) %collective-permute-start.4) | collective-permute-done | bytes 263200 | tf_op jit(solution)/shard_map/ppermute | solution.py:17
  49.3 1.3 %fusion.75 = bf16[256,512]{1,0:T(8,128)(2,1)S(1)} fusion(f32[256,512]{1,0:T(8,128)} %copy-done.1, bf16[257,512]{1,0:T(8,128)(2,1)S(1)} %collective-permute-done.3, f32[256]{0:T(256)S(1)} %get-tuple-element.67, pred[]{:T(512)S(6)} %ge.73, bf16[257,512]{1,0:T(8,128)(2,1)} %collective-permute-done.4, f32[256]{0:T(256)} %get-tuple-element.62, pred[]{:T(512)S(6)} %ge.72), kind=kLoop, calls=%fused_computation.173 | loop fusion | flops 1179648 | bytes 1312770 | tf_op jit(solution)/shard_map/convert_element_type | solution.py:120
  50.6 1.3 %collective-permute-start.5 = (bf16[256,512]{1,0:T(8,128)(2,1)S(1)}, bf16[256,512]{1,0:T(8,128)(2,1)S(1)}, u32[]{:S(2)}, u32[]{:S(2)}) collective-permute-start(bf16[256,512]{1,0:T(8,128)(2,1)S(1)} %fusion.75), channel_id=1, source_target_pairs={{0,16},{4,20},{8,24},{12,28},{1,17},{5,21},{9,25},{13,29},{2,18},{... | collective-permute-start | bytes 786440 | tf_op jit(solution)/shard_map/ppermute | solution.py:17
  51.9 0.7 slice_convert_fusion
  52.6 0.7 multiply_select_fusion
  53.3 11.1 %collective-permute-done.5 = bf16[256,512]{1,0:T(8,128)(2,1)S(1)} collective-permute-done((bf16[256,512]{1,0:T(8,128)(2,1)S(1)}, bf16[256,512]{1,0:T(8,128)(2,1)S(1)}, u32[]{:S(2)}, u32[]{:S(2)}) %collective-permute-start.5) | collective-permute-done | bytes 262176 | tf_op jit(solution)/shard_map/ppermute | solution.py:17
  64.4 2.0 %multiply_reduce_fusion.3 = (f32[256]{0:T(256)S(1)}, f32[256,512]{1,0:T(8,128)S(1)}) fusion(f32[256,512]{1,0:T(8,128)} %bitcast.142, f32[256,256]{1,0:T(8,128)} %bitcast.124, bf16[256,512]{1,0:T(8,128)(2,1)S(1)} %collective-permute-done.5, f32[256]{0:T(256)} %bitcast.139, f32[256]{0:T(256)S(1)} %get-tuple-element.94, pred[]{:T(512)S(6)} %ge.72, ...), kind=kOutput, calls=%fused_computation.55 | convolution fusion | flops 202899200 | bytes 2100226 | tf_op jit(solution)/shard_map/dot_general | solution.py:266
  66.4 0.8 multiply_convert_fusion
  67.2 0.7 copy-done.11
  67.9 1.2 %convolution_convert_fusion = bf16[128,2048]{1,0:T(8,128)(2,1)} fusion(bf16[512,2048]{1,0:T(8,128)(2,1)S(1)} %copy-done, bf16[64,512]{1,0:T(8,128)(2,1)S(1)} %get-tuple-element.78, bf16[64,512]{1,0:T(8,128)(2,1)S(1)} %get-tuple-element.77), kind=kOutput, calls=%fused_computation.4 | convolution fusion | flops 268959744 | bytes 2752512 | tf_op jit(solution)/shard_map/dot_general | solution.py:185
  69.2 1.4 %fusion.1 = f32[64,2048]{1,0:T(8,128)S(1)} fusion(bf16[512,2048]{1,0:T(8,128)(2,1)S(1)} %copy-done, pred[]{:T(512)S(6)} %eq.48, pred[]{:T(512)S(6)} %eq.49, bf16[256,512]{1,0:T(8,128)(2,1)} %copy-done.11), kind=kOutput, calls=%fused_computation.8 | convolution fusion | flops 134578176 | bytes 2883586 | tf_op jit(solution)/shard_map/dot_general | solution.py:185
  70.6 0.8 collective-permute-done.6
  71.4 1.1 %convert_element_type.212 = f32[128,2048]{1,0:T(8,128)S(1)} convert(bf16[128,2048]{1,0:T(8,128)(2,1)} %collective-permute-done.6) | non-fusion elementwise | flops 262144 | bytes 1572864 | tf_op jit(solution)/shard_map/convert_element_type | solution.py:202
  72.6 1.4 %add_convert_fusion.1 = bf16[64,2048]{1,0:T(8,128)(2,1)S(1)} fusion(f32[128,2048]{1,0:T(8,128)S(1)} %convert_element_type.212, pred[]{:T(512)S(6)} %eq.48, bf16[512,2048]{1,0:T(8,128)(2,1)S(1)} %copy-done, pred[]{:T(512)S(6)} %eq.49, bf16[256,512]{1,0:T(8,128)(2,1)} %copy-done.11), kind=kOutput, calls=%fused_computation.53 | convolution fusion | flops 134971392 | bytes 3671552 | tf_op jit(solution)/shard_map/dot_general | solution.py:185
  74.0 1.6 %collective-permute-start.7 = (bf16[64,2048]{1,0:T(8,128)(2,1)S(1)}, bf16[64,2048]{1,0:T(8,128)(2,1)S(1)}, u32[]{:S(2)}, u32[]{:S(2)}) collective-permute-start(bf16[64,2048]{1,0:T(8,128)(2,1)S(1)} %add_convert_fusion.1), channel_id=1, source_target_pairs={{0,2},{1,3},{2,0},{3,1},{4,6},{5,7},{6,4},{7,5},{8,10},{9,11},{10,... | collective-permute-start | bytes 786440 | tf_op jit(solution)/shard_map/ppermute | solution.py:201
  75.6 2.2 %fusion.5 = f32[1,1,256,512]{3,2,1,0:T(8,128)} fusion(bf16[256,512]{1,0:T(8,128)(2,1)S(1)} %copy-done.14, f32[256]{0:T(256)S(1)} %get-tuple-element.93, pred[]{:T(512)S(6)} %ge.71, f32[256,512]{1,0:T(8,128)S(1)} %copy-done.2, bf16[257,512]{1,0:T(8,128)(2,1)S(1)} %collective-permute-done.3, f32[256]{0:T(256)S(1)} %get-tuple-element.67, pred[]{:T(512)S(6)} %ge.73, ...), kind=kLoop, calls=%fused_computation.39 | loop fusion | flops 1572864 | bytes 1838083 | tf_op jit(solution)/shard_map/broadcast_in_dim | solution.py:275
  77.8 4.6 %collective-permute-done.7 = bf16[64,2048]{1,0:T(8,128)(2,1)S(1)} collective-permute-done((bf16[64,2048]{1,0:T(8,128)(2,1)S(1)}, bf16[64,2048]{1,0:T(8,128)(2,1)S(1)}, u32[]{:S(2)}, u32[]{:S(2)}) %collective-permute-start.7) | collective-permute-done | bytes 262176 | tf_op jit(solution)/shard_map/ppermute | solution.py:201
  82.4 0.8 add_convert_fusion
  (82 shorter events, 4.9 us)
Async XLA Ops:
  0.6 67.3 %copy-start = (bf16[512,2048]{1,0:T(8,128)(2,1)S(1)}, bf16[512,2048]{1,0:T(8,128)(2,1)}, u32[]{:S(2)}) copy-start(bf16[512,2048]{1,0:T(8,128)(2,1)} %param.31) | copy-start | bytes 6291460
  0.6 11.3 %copy-start.3 = (bf16[64,2048]{1,0:T(8,128)(2,1)S(1)}, bf16[64,2048]{1,0:T(8,128)(2,1)}, u32[]{:S(2)}) copy-start(bf16[64,2048]{1,0:T(8,128)(2,1)} %param.18) | copy-start | bytes 786436
  0.7 8.3 %collective-permute-start = (bf16[64,2048]{1,0:T(8,128)(2,1)}, bf16[64,2048]{1,0:T(8,128)(2,1)S(1)}, u32[]{:S(2)}, u32[]{:S(2)}) collective-permute-start(bf16[64,2048]{1,0:T(8,128)(2,1)} %param.18), channel_id=1, source_target_pairs={{0,2},{1,3},{2,0},{3,1},{4,6},{5,7},{6,4},{7,5},{8,10},{9,11},{10,... | collective-permute-start | bytes 786440 | tf_op jit(solution)/shard_map/ppermute | solution.py:151
  10.0 2.0 %collective-permute-start.1 = (bf16[128,2048]{1,0:T(8,128)(2,1)S(1)}, bf16[128,2048]{1,0:T(8,128)(2,1)S(1)}, u32[]{:S(2)}, u32[]{:S(2)}) collective-permute-start(bf16[128,2048]{1,0:T(8,128)(2,1)S(1)} %pad_maximum_fusion.4), channel_id=1, source_target_pairs={{0,1},{1,0},{2,3},{3,2},{4,5},{5,4},{6,7},{7,6},{8,9},{9,8},{10,11... | collective-permute-start | bytes 1572872 | tf_op jit(solution)/shard_map/ppermute | solution.py:151
  12.0 1.8 %copy-start.20 = (bf16[2048,16]{0,1:T(8,128)(2,1)S(1)}, bf16[2048,16]{0,1:T(8,128)(2,1)}, u32[]{:S(2)}) copy-start(bf16[2048,16]{0,1:T(8,128)(2,1)} %param.26) | copy-start | bytes 196612
  12.0 1.8 %copy-start.21 = (bf16[16,256]{1,0:T(8,128)(2,1)S(1)}, bf16[16,256]{1,0:T(8,128)(2,1)}, u32[]{:S(2)}) copy-start(bf16[16,256]{1,0:T(8,128)(2,1)} %param.27) | copy-start | bytes 24580
  12.0 1.8 %copy-start.23 = (f32[256]{0:T(256)S(1)}, f32[256]{0:T(256)}, u32[]{:S(2)}) copy-start(f32[256]{0:T(256)} %param.28) | copy-start | bytes 3076
  12.1 0.7 copy-start.4
  14.6 2.2 %copy-start.18 = (bf16[2048,512]{1,0:T(8,128)(2,1)S(1)}, bf16[2048,512]{1,0:T(8,128)(2,1)}, u32[]{:S(2)}) copy-start(bf16[2048,512]{1,0:T(8,128)(2,1)} %param.22) | copy-start | bytes 6291460
  14.9 12.6 %copy-start.8 = (f32[4,64,256]{2,1,0:T(8,128)}, f32[4,64,256]{2,1,0:T(8,128)S(1)}, u32[]{:S(2)}) copy-start(f32[4,64,256]{2,1,0:T(8,128)S(1)} %convolution_bitcast_fusion) | copy-start | bytes 786436
  16.9 1.2 %copy-start.9 = (bf16[2048,256]{1,0:T(8,128)(2,1)S(1)}, bf16[2048,256]{1,0:T(8,128)(2,1)}, u32[]{:S(2)}) copy-start(bf16[2048,256]{1,0:T(8,128)(2,1)} %param.21) | copy-start | bytes 3145732
  19.2 6.4 %collective-permute-start.2 = (bf16[3,1024]{1,0:T(4,128)(2,1)S(1)}, bf16[3,1024]{1,0:T(4,128)(2,1)S(1)}, u32[]{:S(2)}, u32[]{:S(2)}) collective-permute-start(bf16[3,1024]{1,0:T(4,128)(2,1)S(1)} %get-tuple-element.59), channel_id=1, source_target_pairs={{0,4},{4,8},{8,12},{12,16},{16,20},{20,24},{24,28},{1,5},{5,9},{9,... | collective-permute-start | bytes 18440 | tf_op jit(solution)/shard_map/ppermute | solution.py:17
  26.3 1.2 %copy-start.10 = (f32[256,256]{1,0:T(8,128)}, f32[256,256]{1,0:T(8,128)S(1)}, u32[]{:S(2)}) copy-start(f32[256,256]{1,0:T(8,128)S(1)} %get-tuple-element.56) | copy-start | bytes 786436
  26.3 1.8 %copy-start.15 = (f32[256,256]{1,0:T(8,128)}, f32[256,256]{1,0:T(8,128)S(1)}, u32[]{:S(2)}) copy-start(f32[256,256]{1,0:T(8,128)S(1)} %get-tuple-element.57) | copy-start | bytes 786436
  27.5 0.9 %copy-start.12 = (f32[256,512]{1,0:T(8,128)}, f32[256,512]{1,0:T(8,128)S(1)}, u32[]{:S(2)}) copy-start(f32[256,512]{1,0:T(8,128)S(1)} %multiply_reduce_fusion) | copy-start | bytes 1572868
  28.4 12.1 %copy-start.1 = (f32[256,512]{1,0:T(8,128)}, f32[256,512]{1,0:T(8,128)S(1)}, u32[]{:S(2)}) copy-start(f32[256,512]{1,0:T(8,128)S(1)} %get-tuple-element.64) | copy-start | bytes 1572868
  28.9 10.2 %collective-permute-start.3 = (bf16[257,512]{1,0:T(8,128)(2,1)S(1)}, bf16[257,512]{1,0:T(8,128)(2,1)S(1)}, u32[]{:S(2)}, u32[]{:S(2)}) collective-permute-start(bf16[257,512]{1,0:T(8,128)(2,1)S(1)} %pad_maximum_fusion.5), channel_id=1, source_target_pairs={{0,4},{4,8},{8,12},{12,16},{16,20},{20,24},{24,28},{1,5},{5,9},{9,... | collective-permute-start | bytes 789512 | tf_op jit(solution)/shard_map/ppermute | solution.py:17
  39.0 0.6 copy-start.17
  40.5 8.7 %collective-permute-start.4 = (bf16[257,512]{1,0:T(8,128)(2,1)}, bf16[257,512]{1,0:T(8,128)(2,1)}, u32[]{:S(2)}, u32[]{:S(2)}) collective-permute-start(bf16[257,512]{1,0:T(8,128)(2,1)} %pad_maximum_fusion.6), channel_id=1, source_target_pairs={{0,8},{4,12},{8,16},{12,20},{16,24},{20,28},{1,9},{5,13},{9,17},{1... | collective-permute-start | bytes 789512 | tf_op jit(solution)/shard_map/ppermute | solution.py:17
  44.6 21.8 %copy-start.19 = (bf16[2048,512]{1,0:T(8,128)(2,1)S(1)}, bf16[2048,512]{1,0:T(8,128)(2,1)}, u32[]{:S(2)}) copy-start(bf16[2048,512]{1,0:T(8,128)(2,1)} %param.29) | copy-start | bytes 6291460
  44.6 21.8 %copy-start.22 = (f32[512]{0:T(512)S(1)}, f32[512]{0:T(512)}, u32[]{:S(2)}) copy-start(f32[512]{0:T(512)} %param.30) | copy-start | bytes 6148
  50.6 13.8 %collective-permute-start.5 = (bf16[256,512]{1,0:T(8,128)(2,1)S(1)}, bf16[256,512]{1,0:T(8,128)(2,1)S(1)}, u32[]{:S(2)}, u32[]{:S(2)}) collective-permute-start(bf16[256,512]{1,0:T(8,128)(2,1)S(1)} %fusion.75), channel_id=1, source_target_pairs={{0,16},{4,20},{8,24},{12,28},{1,17},{5,21},{9,25},{13,29},{2,18},{... | collective-permute-start | bytes 786440 | tf_op jit(solution)/shard_map/ppermute | solution.py:17
  64.4 2.0 %copy-start.13 = (bf16[256,512]{1,0:T(8,128)(2,1)}, bf16[256,512]{1,0:T(8,128)(2,1)S(1)}, u32[]{:S(2)}) copy-start(bf16[256,512]{1,0:T(8,128)(2,1)S(1)} %collective-permute-done.5) | copy-start | bytes 786436
  67.2 0.7 copy-start.11
  69.2 2.3 %collective-permute-start.6 = (bf16[128,2048]{1,0:T(8,128)(2,1)}, bf16[128,2048]{1,0:T(8,128)(2,1)}, u32[]{:S(2)}, u32[]{:S(2)}) collective-permute-start(bf16[128,2048]{1,0:T(8,128)(2,1)} %convolution_convert_fusion), channel_id=1, source_target_pairs={{0,1},{1,0},{2,3},{3,2},{4,5},{5,4},{6,7},{7,6},{8,9},{9,8},{10,11... | collective-permute-start | bytes 1572872 | tf_op jit(solution)/shard_map/ppermute | solution.py:201
  70.6 5.0 %copy-start.2 = (f32[256,512]{1,0:T(8,128)S(1)}, f32[256,512]{1,0:T(8,128)}, u32[]{:S(2)}) copy-start(f32[256,512]{1,0:T(8,128)} %copy-done.1) | copy-start | bytes 1572868
  70.6 5.0 %copy-start.14 = (bf16[256,512]{1,0:T(8,128)(2,1)S(1)}, bf16[256,512]{1,0:T(8,128)(2,1)}, u32[]{:S(2)}) copy-start(bf16[256,512]{1,0:T(8,128)(2,1)} %copy-done.13) | copy-start | bytes 786436
  70.6 5.0 %copy-start.16 = (f32[256]{0:T(256)S(1)}, f32[256]{0:T(256)}, u32[]{:S(2)}) copy-start(f32[256]{0:T(256)} %get-tuple-element.62) | copy-start | bytes 3076
  74.0 8.4 %collective-permute-start.7 = (bf16[64,2048]{1,0:T(8,128)(2,1)S(1)}, bf16[64,2048]{1,0:T(8,128)(2,1)S(1)}, u32[]{:S(2)}, u32[]{:S(2)}) collective-permute-start(bf16[64,2048]{1,0:T(8,128)(2,1)S(1)} %add_convert_fusion.1), channel_id=1, source_target_pairs={{0,2},{1,3},{2,0},{3,1},{4,6},{5,7},{6,4},{7,5},{8,10},{9,11},{10,... | collective-permute-start | bytes 786440 | tf_op jit(solution)/shard_map/ppermute | solution.py:201

commit v17 on v15

--- a/solution.py
+++ b/solution.py
@@ -222,7 +222,10 @@
     norm_gain,
     out_weight,
 ):
-    gathered = gather_rows(tokens, "hv")
+    width = tokens.shape[1]
+    own_low_rank = jnp.dot(tokens, decay_down, preferred_element_type=jnp.float32).astype(jnp.bfloat16)
+    gathered_all = gather_rows(jnp.concatenate([tokens, own_low_rank], axis=1), "hv")
+    gathered = gathered_all[:, :width]
 
     def project(weight):
         return jnp.dot(gathered, weight, preferred_element_type=jnp.float32).astype(jnp.bfloat16)
@@ -231,7 +234,7 @@
     raw_key = project(key_weight)
     raw_value = project(value_weight)
     gate_values = project(gate_weight)
-    low_rank = project(decay_down)
+    low_rank = gathered_all[:, width:]
     row_count = raw_query.shape[0]
     key_width = raw_query.shape[1]
     value_width = raw_value.shape[1]

time: 81.9 us -> 86.8 us (1.060)
  waiting for transfers between devices: 32.9 us -> 36.6 us
  matrix products: 14.8 us -> 17.7 us
  other arithmetic: 16.8 us -> 15 us
    ppermute x2, waiting for transfers between devices: 2.33 us -> 3.88 us  [gather_rows(): lax.ppermute(jnp.concatenate(received), axis, [(source, source ^ mask) fo...]
    dot_general x0 -> x1, matrix products: none -> 1.27 us  [shards(): jnp.dot(tokens, decay_down, preferred_element_type=jnp.float32)]
    another operation x0 -> x2, local copies, waits for them, and re-layouts: none -> 1.19 us
    concatenate x1, other arithmetic: 1.02 us -> 2.14 us  [ordered(): return jnp.concatenate([received[pick] for pick in picks])]
    convert_element_type x1, other arithmetic: 1.34 us -> 0.24 us  [prefix_states(): memory.astype(jnp.bfloat16)]
    concatenate x0 -> x1, local copies, waits for them, and re-layouts: none -> 1.01 us  [gather_rows(): jnp.concatenate(received)]
    concatenate x0 -> x1, other arithmetic: none -> 0.98 us  [shards(): jnp.concatenate([tokens, own_low_rank], axis=1)]
    ppermute x1, waiting for transfers between devices: 4.57 us -> 5.54 us  [scatter_sum(): lax.ppermute(outgoing, axis, [(source, source ^ mask) for source in range...]
  transfers between devices with their start and end apart: 8 -> 8, of which waited for: 8 -> 8; matrix products, arithmetic and copies ran while one was open for 18% -> 14% of each run, Pallas kernels for 0% -> 0%
where the time goes in v17:
time: 86.8 us; the launch traced here: 86.3 us
  waiting for transfers between devices  36.6 us (42%)
  matrix products  17.7 us (20%)
  other arithmetic  15 us (17%)
  starting transfers between devices  11.6 us (13%)
  local copies, waits for them, and re-layouts  4.17 us (5%)
  between operations  1.07 us (1%)
    ppermute x4, waiting for transfers between devices, shifted(): lax.ppermute(value, axis, [(source, source + steps) for source in range(i...  24.9 us
    ppermute x4, starting transfers between devices, shifted(): lax.ppermute(value, axis, [(source, source + steps) for source in range(i...  8.46 us
    ppermute x1, waiting for transfers between devices, scatter_sum(): lax.ppermute(outgoing, axis, [(source, source ^ mask) for source in range...  5.54 us
    dot_general x4, matrix products, project(): jnp.dot(gathered, weight, preferred_element_type=jnp.float32)  3.93 us
    ppermute x2, waiting for transfers between devices, gather_rows(): lax.ppermute(jnp.concatenate(received), axis, [(source, source ^ mask) fo...  3.88 us
    dot_general x3, matrix products, segment_parts(): jnp.dot(lifted_intact[block], memory, precision=HIGH_PRECISION)  3.14 us
    dot_general x1, matrix products, segment_parts(): jnp.einsum('bac,bcv->bav', scores, head_values, preferred_element_type=jn...  2.65 us
    ppermute x1, waiting for transfers between devices, scatter_sum(): lax.ppermute(outgoing, axis, [(source, source ^ 1) for source in range(co...  2.25 us
  transfers between devices with their start and end apart: 8, of which 8 were waited for; matrix products, arithmetic and copies ran while one was open for 14% of the time, Pallas kernels for 0%

profile of v17, /device:TPU:24, one launch (start us, length us, event | category | flops | bytes accessed | tf_op | source)
XLA Modules:
  0.0 86.3 jit_solution(5902051070087785978)
XLA Ops:
  0.6 1.3 %convolution_convert_fusion.6 = bf16[64,16]{0,1:T(8,128)(2,1)S(1)} fusion(bf16[64,2048]{1,0:T(8,128)(2,1)} %param.18, bf16[2048,16]{0,1:T(8,128)(2,1)} %param.26), kind=kOutput, calls=%fused_computation.23 | convolution fusion | flops 4195328 | bytes 329728 | tf_op jit(solution)/shard_map/dot_general | solution.py:226
  2.0 1.0 %pad_maximum_fusion.5 = bf16[64,2064]{1,0:T(8,128)(2,1)S(1)} fusion(bf16[64,16]{1,0:T(8,128)(2,1)S(1)} %copy.46, bf16[64,2048]{1,0:T(8,128)(2,1)} %param.18), kind=kLoop, calls=%fused_computation.71 | loop fusion | flops 528384 | bytes 528384 | tf_op jit(solution)/shard_map/concatenate | solution.py:227
  3.0 1.6 %collective-permute-start = (bf16[64,2064]{1,0:T(8,128)(2,1)S(1)}, bf16[64,2064]{1,0:T(8,128)(2,1)S(1)}, u32[]{:S(2)}, u32[]{:S(2)}) collective-permute-start(bf16[64,2064]{1,0:T(8,128)(2,1)S(1)} %pad_maximum_fusion.5), channel_id=1, source_target_pairs={{0,2},{1,3},{2,0},{3,1},{4,6},{5,7},{6,4},{7,5},{8,10},{9,11},{10,... | collective-permute-start | bytes 792584 | tf_op jit(solution)/shard_map/ppermute | solution.py:151
  4.6 0.8 select_reduce_fusion.1
  6.1 0.6 slice.225
  6.6 0.7 convert_element_type.167
  7.3 0.7 convert_element_type.177
  8.0 0.7 convert_element_type.183
  8.9 2.6 %collective-permute-done = bf16[64,2064]{1,0:T(8,128)(2,1)S(1)} collective-permute-done((bf16[64,2064]{1,0:T(8,128)(2,1)S(1)}, bf16[64,2064]{1,0:T(8,128)(2,1)S(1)}, u32[]{:S(2)}, u32[]{:S(2)}) %collective-permute-start) | collective-permute-done | bytes 264224 | tf_op jit(solution)/shard_map/ppermute | solution.py:151
  11.5 1.1 %pad_maximum_fusion.4 = bf16[128,2064]{1,0:T(8,128)(2,1)S(1)} fusion(bf16[64,2064]{1,0:T(8,128)(2,1)S(1)} %collective-permute-done, bf16[64,16]{1,0:T(8,128)(2,1)S(1)} %copy.46, bf16[64,2048]{1,0:T(8,128)(2,1)} %param.18), kind=kLoop, calls=%fused_computation.42 | loop fusion | flops 1585152 | bytes 1056768 | tf_op jit(solution)/shard_map/concatenate | solution.py:152
  12.6 1.0 %copy.47 = bf16[128,2064]{0,1:T(8,128)(2,1)} copy(bf16[128,2064]{1,0:T(8,128)(2,1)S(1)} %pad_maximum_fusion.4) | data formatting | bytes 1056768 | tf_op jit(solution)/shard_map/concatenate | solution.py:152
  13.6 0.7 slice_compare_fusion
  14.4 1.3 %collective-permute-done.1 = bf16[128,2064]{0,1:T(8,128)(2,1)S(1)} collective-permute-done((bf16[128,2064]{0,1:T(8,128)(2,1)}, bf16[128,2064]{0,1:T(8,128)(2,1)S(1)}, u32[]{:S(2)}, u32[]{:S(2)}) %collective-permute-start.1) | collective-permute-done | bytes 528416 | tf_op jit(solution)/shard_map/ppermute | solution.py:151
  16.0 3.4 %conditional.1 = (bf16[256,2064]{1,0:T(8,128)(2,1)}) conditional(s32[]{:T(128)} %clamp.3, (bf16[64,2064]{1,0:T(8,128)(2,1)S(1)}, bf16[64,2064]{0,1:T(8,128)(2,1)S(1)}, bf16[64,2064]{1,0:T(8,128)(2,1)}, bf16[64,2064]{0,1:T(8,128)(2,1)S(1)}) %tuple.122, (bf16[64,2064]{0,1:T(8,128)(2,1)S(1)}, ...), branch_computations={%region_3.0_spmd, %region_4.5_spmd, %region_5.6_spmd, %region_6.7_... | conditional | flops 4227072 | bytes 3170312 | solution.py:165
  16.0 0.9 %copy.49 = bf16[64,2064]{1,0:T(8,128)(2,1)} copy(bf16[64,2064]{0,1:T(8,128)(2,1)S(1)} %get-tuple-element.187) | data formatting | bytes 528384 | tf_op jit(solution)/shard_map
  17.2 2.1 %pad_maximum_fusion = bf16[256,2064]{1,0:T(8,128)(2,1)} fusion(bf16[64,2064]{1,0:T(8,128)(2,1)} %copy.49, bf16[64,2064]{1,0:T(8,128)(2,1)} %get-tuple-element.135, bf16[64,2064]{1,0:T(8,128)(2,1)S(1)} %copy.48, bf16[64,2064]{1,0:T(8,128)(2,1)S(1)} %get-tuple-element.133), kind=kLoop, calls=%fused_computation | loop fusion | flops 4227072 | bytes 2113536 | tf_op jit(solution)/shard_map/cond/branch_0_fun/concatenate | solution.py:163
  19.3 1.3 %fusion.32 = f32[256,256]{1,0:T(8,128)S(1)} fusion(bf16[16,256]{1,0:T(8,128)(2,1)S(1)} %copy-done.15, f32[256]{0:T(256)S(1)} %copy-done.17, bf16[256,2064]{1,0:T(8,128)(2,1)} %get-tuple-element.247), kind=kOutput, calls=%fused_computation.83 | convolution fusion | flops 2752512 | bytes 336896 | tf_op jit(solution)/shard_map/dot_general | solution.py:261
  20.9 2.0 %convolution_convert_fusion.5 = bf16[256,256]{1,0:T(8,128)(2,1)S(1)} fusion(bf16[2048,256]{1,0:T(8,128)(2,1)} %param.20, bf16[256,2064]{1,0:T(8,128)(2,1)} %get-tuple-element.247), kind=kOutput, calls=%fused_computation.17 | convolution fusion | flops 268500992 | bytes 2228224 | tf_op jit(solution)/shard_map/dot_general | solution.py:231
  22.9 0.7 convolution_convert_fusion.3
  23.6 0.5 copy-done.14
  24.1 0.4 convolution_convert_fusion.4
  24.6 0.7 select_bitcast_fusion
  25.3 3.4 %collective-permute-start.2 = (bf16[3,1024]{1,0:T(4,128)(2,1)S(1)}, bf16[3,1024]{1,0:T(4,128)(2,1)S(1)}, u32[]{:S(2)}, u32[]{:S(2)}) collective-permute-start(bf16[3,1024]{1,0:T(4,128)(2,1)S(1)} %get-tuple-element.203), channel_id=1, source_target_pairs={{0,4},{4,8},{8,12},{12,16},{16,20},{20,24},{24,28},{1,5},{5,9},{9,... | collective-permute-start | bytes 18440 | tf_op jit(solution)/shard_map/ppermute | solution.py:17
  28.9 2.8 %collective-permute-done.2 = bf16[3,1024]{1,0:T(4,128)(2,1)S(1)} collective-permute-done((bf16[3,1024]{1,0:T(4,128)(2,1)S(1)}, bf16[3,1024]{1,0:T(4,128)(2,1)S(1)}, u32[]{:S(2)}, u32[]{:S(2)}) %collective-permute-start.2) | collective-permute-done | bytes 6176 | tf_op jit(solution)/shard_map/ppermute | solution.py:17
  32.0 0.3 multiply_reduce_fusion.2
  32.4 0.9 broadcast_multiply_fusion
  33.6 0.6 fusion.54
  34.5 1.0 %convolution_bitcast_fusion.2 = f32[1,64,512]{2,1,0:T(8,128)} fusion(f32[4,64,256]{2,1,0:T(8,128)S(1)} %get-tuple-element.213, f32[4,256,512]{2,1,0:T(8,128)S(1)} %fusion.54, f32[256]{0:T(256)S(1)} %bitcast.129, f32[256]{0:T(256)S(1)} %get-tuple-element.241), kind=kOutput, calls=%fused_computation.19 | convolution fusion | flops 50724864 | bytes 1247232 | tf_op jit(solution)/shard_map/dot_general | solution.py:81
  35.5 2.5 %collective-permute-start.3 = (bf16[257,512]{1,0:T(8,128)(2,1)S(1)}, bf16[257,512]{1,0:T(8,128)(2,1)S(1)}, u32[]{:S(2)}, u32[]{:S(2)}) collective-permute-start(bf16[257,512]{1,0:T(8,128)(2,1)S(1)} %pad_maximum_fusion.6), channel_id=1, source_target_pairs={{0,4},{4,8},{8,12},{12,16},{16,20},{20,24},{24,28},{1,5},{5,9},{9,... | collective-permute-start | bytes 789512 | tf_op jit(solution)/shard_map/ppermute | solution.py:17
  38.0 1.0 %convolution_bitcast_fusion.3 = f32[1,64,512]{2,1,0:T(8,128)} fusion(f32[4,256,512]{2,1,0:T(8,128)S(1)} %fusion.54, f32[256]{0:T(256)S(1)} %get-tuple-element.241, f32[4,64,256]{2,1,0:T(8,128)S(1)} %get-tuple-element.213), kind=kOutput, calls=%fused_computation.20 | convolution fusion | flops 50462720 | bytes 721920 | tf_op jit(solution)/shard_map/dot_general | solution.py:81
  39.1 1.1 %convolution_bitcast_fusion.1 = f32[1,64,512]{2,1,0:T(8,128)} fusion(f32[4,256,512]{2,1,0:T(8,128)S(1)} %fusion.54, f32[256]{0:T(256)S(1)} %bitcast.133, f32[4,64,256]{2,1,0:T(8,128)S(1)} %get-tuple-element.213, f32[256]{0:T(256)S(1)} %bitcast.130, f32[256]{0:T(256)S(1)} %get-tuple-element.241), kind=kOutput, calls=%fused_computation.18 | convolution fusion | flops 50987008 | bytes 1772544 | tf_op jit(solution)/shard_map/dot_general | solution.py:81
  40.1 5.6 %collective-permute-done.3 = bf16[257,512]{1,0:T(8,128)(2,1)S(1)} collective-permute-done((bf16[257,512]{1,0:T(8,128)(2,1)S(1)}, bf16[257,512]{1,0:T(8,128)(2,1)S(1)}, u32[]{:S(2)}, u32[]{:S(2)}) %collective-permute-start.3) | collective-permute-done | bytes 263200 | tf_op jit(solution)/shard_map/ppermute | solution.py:17
  45.9 0.7 pad_maximum_fusion.7
  46.6 1.3 %collective-permute-start.4 = (bf16[257,512]{1,0:T(8,128)(2,1)}, bf16[257,512]{1,0:T(8,128)(2,1)S(1)}, u32[]{:S(2)}, u32[]{:S(2)}) collective-permute-start(bf16[257,512]{1,0:T(8,128)(2,1)} %pad_maximum_fusion.7), channel_id=1, source_target_pairs={{0,8},{4,12},{8,16},{12,20},{16,24},{20,28},{1,9},{5,13},{9,17},{1... | collective-permute-start | bytes 789512 | tf_op jit(solution)/shard_map/ppermute | solution.py:17
  47.9 2.6 %convolution_add_fusion = f32[4,64,512]{2,1,0:T(8,128)} fusion(f32[1,64,512]{2,1,0:T(8,128)} %convolution_bitcast_fusion.1, f32[1,64,512]{2,1,0:T(8,128)} %convolution_bitcast_fusion.2, f32[1,64,512]{2,1,0:T(8,128)} %convolution_bitcast_fusion.3, f32[4]{0:T(128)S(1)} %pad.32.clone, f32[4,64,256]{2,1,0:T(8,128)S(1)} %convolution_bitcast_fusion, ...), kind=kOutput, calls=%fused_computation.8 | convolution fusion | flops 27525120 | bytes 2233360 | tf_op jit(solution)/shard_map/bac,bcv->bav/dot_general | solution.py:72
  50.6 4.7 %collective-permute-done.4 = bf16[257,512]{1,0:T(8,128)(2,1)S(1)} collective-permute-done((bf16[257,512]{1,0:T(8,128)(2,1)}, bf16[257,512]{1,0:T(8,128)(2,1)S(1)}, u32[]{:S(2)}, u32[]{:S(2)}) %collective-permute-start.4) | collective-permute-done | bytes 263200 | tf_op jit(solution)/shard_map/ppermute | solution.py:17
  55.5 1.3 %collective-permute-start.5 = (bf16[256,512]{1,0:T(8,128)(2,1)S(1)}, bf16[256,512]{1,0:T(8,128)(2,1)S(1)}, u32[]{:S(2)}, u32[]{:S(2)}) collective-permute-start(bf16[256,512]{1,0:T(8,128)(2,1)S(1)} %fusion.83), channel_id=1, source_target_pairs={{0,16},{4,20},{8,24},{12,28},{1,17},{5,21},{9,25},{13,29},{2,18},{... | collective-permute-start | bytes 786440 | tf_op jit(solution)/shard_map/ppermute | solution.py:17
  56.8 0.6 multiply_select_fusion
  57.4 11.9 %collective-permute-done.5 = bf16[256,512]{1,0:T(8,128)(2,1)S(1)} collective-permute-done((bf16[256,512]{1,0:T(8,128)(2,1)S(1)}, bf16[256,512]{1,0:T(8,128)(2,1)S(1)}, u32[]{:S(2)}, u32[]{:S(2)}) %collective-permute-start.5) | collective-permute-done | bytes 262176 | tf_op jit(solution)/shard_map/ppermute | solution.py:17
  69.3 1.8 %multiply_reduce_fusion.3 = (f32[256]{0:T(256)S(1)}, f32[256,512]{1,0:T(8,128)S(1)}) fusion(f32[256,512]{1,0:T(8,128)} %bitcast.142, f32[256,256]{1,0:T(8,128)} %bitcast.124, bf16[256,512]{1,0:T(8,128)(2,1)S(1)} %collective-permute-done.5, f32[256]{0:T(256)S(1)} %bitcast.139, f32[256]{0:T(256)S(1)} %get-tuple-element.240, pred[]{:T(512)S(6)} %ge.72, ...), kind=kOutput, calls=%fused_computation.59 | convolution fusion | flops 202899200 | bytes 2100226 | tf_op jit(solution)/shard_map/dot_general | solution.py:269
  71.2 0.8 multiply_convert_fusion
  72.0 1.2 %convolution_convert_fusion = bf16[128,2048]{1,0:T(8,128)(2,1)} fusion(bf16[512,2048]{1,0:T(8,128)(2,1)S(1)} %copy-done, bf16[64,512]{1,0:T(8,128)(2,1)S(1)} %get-tuple-element.224, bf16[64,512]{1,0:T(8,128)(2,1)S(1)} %get-tuple-element.223), kind=kOutput, calls=%fused_computation.4 | convolution fusion | flops 268959744 | bytes 2752512 | tf_op jit(solution)/shard_map/dot_general | solution.py:188
  73.3 2.2 %collective-permute-done.6 = bf16[128,2048]{1,0:T(8,128)(2,1)} collective-permute-done((bf16[128,2048]{1,0:T(8,128)(2,1)}, bf16[128,2048]{1,0:T(8,128)(2,1)}, u32[]{:S(2)}, u32[]{:S(2)}) %collective-permute-start.6) | collective-permute-done | bytes 524320 | tf_op jit(solution)/shard_map/ppermute | solution.py:189
  75.5 1.5 %convert_add_fusion = f32[128,2048]{1,0:T(8,128)S(1)} fusion(bf16[128,2048]{1,0:T(8,128)(2,1)} %collective-permute-done.6, bf16[512,2048]{1,0:T(8,128)(2,1)S(1)} %copy-done, bf16[64,512]{1,0:T(8,128)(2,1)S(1)} %get-tuple-element.222, bf16[64,512]{1,0:T(8,128)(2,1)S(1)} %get-tuple-element.221), kind=kOutput, calls=%fused_computation.24 | convolution fusion | flops 269746176 | bytes 3801088 | tf_op jit(solution)/shard_map/dot_general | solution.py:191
  77.1 1.6 %collective-permute-start.7 = (bf16[1,64,2048]{2,1,0:T(8,128)(2,1)S(1)}, bf16[1,64,2048]{2,1,0:T(8,128)(2,1)S(1)}, u32[]{:S(2)}, u32[]{:S(2)}) collective-permute-start(bf16[1,64,2048]{2,1,0:T(8,128)(2,1)S(1)} %fusion.30), channel_id=1, source_target_pairs={{0,2},{1,3},{2,0},{3,1},{4,6},{5,7},{6,4},{7,5},{8,10},{9,11},{10,... | collective-permute-start | bytes 786440 | tf_op jit(solution)/shard_map/ppermute | solution.py:200
  78.7 1.3 %fusion.8 = f32[1,1,256,512]{3,2,1,0:T(8,128)} fusion(bf16[256,512]{1,0:T(8,128)(2,1)S(1)} %collective-permute-done.5, f32[256]{0:T(256)S(1)} %copy-done.11, pred[]{:T(512)S(6)} %ge.71, f32[256,512]{1,0:T(8,128)S(1)} %get-tuple-element.208, bf16[257,512]{1,0:T(8,128)(2,1)S(1)} %collective-permute-done.3, f32[256]{0:T(256)S(1)} %copy-done.8, pred[]{:T(512)S(6)} %ge.73, ...), kind=kLoop, calls=%fused_computation.43 | loop fusion | flops 1572864 | bytes 1838083 | tf_op jit(solution)/shard_map/broadcast_in_dim | solution.py:278
  79.9 5.5 %collective-permute-done.7 = bf16[1,64,2048]{2,1,0:T(8,128)(2,1)S(1)} collective-permute-done((bf16[1,64,2048]{2,1,0:T(8,128)(2,1)S(1)}, bf16[1,64,2048]{2,1,0:T(8,128)(2,1)S(1)}, u32[]{:S(2)}, u32[]{:S(2)}) %collective-permute-start.7) | collective-permute-done | bytes 262176 | tf_op jit(solution)/shard_map/ppermute | solution.py:200
  85.5 0.8 fusion.10
  (81 shorter events, 3.4 us)
Async XLA Ops:
  0.6 71.4 %copy-start = (bf16[512,2048]{1,0:T(8,128)(2,1)S(1)}, bf16[512,2048]{1,0:T(8,128)(2,1)}, u32[]{:S(2)}) copy-start(bf16[512,2048]{1,0:T(8,128)(2,1)} %param.31) | copy-start | bytes 6291460
  3.0 8.5 %collective-permute-start = (bf16[64,2064]{1,0:T(8,128)(2,1)S(1)}, bf16[64,2064]{1,0:T(8,128)(2,1)S(1)}, u32[]{:S(2)}, u32[]{:S(2)}) collective-permute-start(bf16[64,2064]{1,0:T(8,128)(2,1)S(1)} %pad_maximum_fusion.5), channel_id=1, source_target_pairs={{0,2},{1,3},{2,0},{3,1},{4,6},{5,7},{6,4},{7,5},{8,10},{9,11},{10,... | collective-permute-start | bytes 792584 | tf_op jit(solution)/shard_map/ppermute | solution.py:151
  11.5 2.9 %copy-start.1 = (bf16[64,2064]{1,0:T(8,128)(2,1)}, bf16[64,2064]{1,0:T(8,128)(2,1)S(1)}, u32[]{:S(2)}) copy-start(bf16[64,2064]{1,0:T(8,128)(2,1)S(1)} %collective-permute-done) | copy-start | bytes 792580
  13.6 2.1 %collective-permute-start.1 = (bf16[128,2064]{0,1:T(8,128)(2,1)}, bf16[128,2064]{0,1:T(8,128)(2,1)S(1)}, u32[]{:S(2)}, u32[]{:S(2)}) collective-permute-start(bf16[128,2064]{0,1:T(8,128)(2,1)} %copy.47), channel_id=1, source_target_pairs={{0,1},{1,0},{2,3},{3,2},{4,5},{5,4},{6,7},{7,6},{8,9},{9,8},{10,11... | collective-permute-start | bytes 1585160 | tf_op jit(solution)/shard_map/ppermute | solution.py:151
  15.9 3.4 %copy-start.15 = (bf16[16,256]{1,0:T(8,128)(2,1)S(1)}, bf16[16,256]{1,0:T(8,128)(2,1)}, u32[]{:S(2)}) copy-start(bf16[16,256]{1,0:T(8,128)(2,1)} %param.27) | copy-start | bytes 24580
  15.9 3.4 %copy-start.17 = (f32[256]{0:T(256)S(1)}, f32[256]{0:T(256)}, u32[]{:S(2)}) copy-start(f32[256]{0:T(256)} %param.28) | copy-start | bytes 3076
  19.3 3.6 %copy-start.2 = (bf16[256,2064]{1,0:T(8,128)(2,1)S(1)}, bf16[256,2064]{1,0:T(8,128)(2,1)}, u32[]{:S(2)}) copy-start(bf16[256,2064]{1,0:T(8,128)(2,1)} %get-tuple-element.247) | copy-start | bytes 3170308
  19.3 3.6 %copy-start.12 = (bf16[2048,512]{1,0:T(8,128)(2,1)S(1)}, bf16[2048,512]{1,0:T(8,128)(2,1)}, u32[]{:S(2)}) copy-start(bf16[2048,512]{1,0:T(8,128)(2,1)} %param.22) | copy-start | bytes 6291460
  22.9 1.2 %copy-start.14 = (bf16[2048,256]{1,0:T(8,128)(2,1)S(1)}, bf16[2048,256]{1,0:T(8,128)(2,1)}, u32[]{:S(2)}) copy-start(bf16[2048,256]{1,0:T(8,128)(2,1)} %param.21) | copy-start | bytes 3145732
  25.3 6.4 %collective-permute-start.2 = (bf16[3,1024]{1,0:T(4,128)(2,1)S(1)}, bf16[3,1024]{1,0:T(4,128)(2,1)S(1)}, u32[]{:S(2)}, u32[]{:S(2)}) collective-permute-start(bf16[3,1024]{1,0:T(4,128)(2,1)S(1)} %get-tuple-element.203), channel_id=1, source_target_pairs={{0,4},{4,8},{8,12},{12,16},{16,20},{20,24},{24,28},{1,5},{5,9},{9,... | collective-permute-start | bytes 18440 | tf_op jit(solution)/shard_map/ppermute | solution.py:17
  28.8 26.4 %copy-start.7 = (f32[256]{0:T(256)}, f32[256]{0:T(256)S(1)}, u32[]{:S(2)}) copy-start(f32[256]{0:T(256)S(1)} %get-tuple-element.211) | copy-start | bytes 3076
  32.4 1.2 %copy-start.4 = (f32[256,256]{1,0:T(8,128)}, f32[256,256]{1,0:T(8,128)S(1)}, u32[]{:S(2)}) copy-start(f32[256,256]{1,0:T(8,128)S(1)} %get-tuple-element.200) | copy-start | bytes 786436
  32.4 1.8 %copy-start.6 = (f32[256,256]{1,0:T(8,128)}, f32[256,256]{1,0:T(8,128)S(1)}, u32[]{:S(2)}) copy-start(f32[256,256]{1,0:T(8,128)S(1)} %get-tuple-element.201) | copy-start | bytes 786436
  33.6 0.9 %copy-start.5 = (f32[256,512]{1,0:T(8,128)}, f32[256,512]{1,0:T(8,128)S(1)}, u32[]{:S(2)}) copy-start(f32[256,512]{1,0:T(8,128)S(1)} %multiply_reduce_fusion) | copy-start | bytes 1572868
  35.5 10.2 %collective-permute-start.3 = (bf16[257,512]{1,0:T(8,128)(2,1)S(1)}, bf16[257,512]{1,0:T(8,128)(2,1)S(1)}, u32[]{:S(2)}, u32[]{:S(2)}) collective-permute-start(bf16[257,512]{1,0:T(8,128)(2,1)S(1)} %pad_maximum_fusion.6), channel_id=1, source_target_pairs={{0,4},{4,8},{8,12},{12,16},{16,20},{20,24},{24,28},{1,5},{5,9},{9,... | collective-permute-start | bytes 789512 | tf_op jit(solution)/shard_map/ppermute | solution.py:17
  45.7 11.1 %copy-start.9 = (f32[256]{0:T(256)}, f32[256]{0:T(256)S(1)}, u32[]{:S(2)}) copy-start(f32[256]{0:T(256)S(1)} %get-tuple-element.206) | copy-start | bytes 3076
  46.6 8.6 %collective-permute-start.4 = (bf16[257,512]{1,0:T(8,128)(2,1)}, bf16[257,512]{1,0:T(8,128)(2,1)S(1)}, u32[]{:S(2)}, u32[]{:S(2)}) collective-permute-start(bf16[257,512]{1,0:T(8,128)(2,1)} %pad_maximum_fusion.7), channel_id=1, source_target_pairs={{0,8},{4,12},{8,16},{12,20},{16,24},{20,28},{1,9},{5,13},{9,17},{1... | collective-permute-start | bytes 789512 | tf_op jit(solution)/shard_map/ppermute | solution.py:17
  50.6 20.6 %copy-start.3 = (bf16[256,2064]{1,0:T(8,128)(2,1)S(1)}, bf16[256,2064]{1,0:T(8,128)(2,1)}, u32[]{:S(2)}) copy-start(bf16[256,2064]{1,0:T(8,128)(2,1)} %get-tuple-element.247) | copy-start | bytes 3170308
  50.6 20.6 %copy-start.13 = (bf16[2048,512]{1,0:T(8,128)(2,1)S(1)}, bf16[2048,512]{1,0:T(8,128)(2,1)}, u32[]{:S(2)}) copy-start(bf16[2048,512]{1,0:T(8,128)(2,1)} %param.29) | copy-start | bytes 6291460
  50.6 20.6 %copy-start.16 = (f32[512]{0:T(512)S(1)}, f32[512]{0:T(512)}, u32[]{:S(2)}) copy-start(f32[512]{0:T(512)} %param.30) | copy-start | bytes 6148
  55.5 13.8 %collective-permute-start.5 = (bf16[256,512]{1,0:T(8,128)(2,1)S(1)}, bf16[256,512]{1,0:T(8,128)(2,1)S(1)}, u32[]{:S(2)}, u32[]{:S(2)}) collective-permute-start(bf16[256,512]{1,0:T(8,128)(2,1)S(1)} %fusion.83), channel_id=1, source_target_pairs={{0,16},{4,20},{8,24},{12,28},{1,17},{5,21},{9,25},{13,29},{2,18},{... | collective-permute-start | bytes 786440 | tf_op jit(solution)/shard_map/ppermute | solution.py:17
  73.3 2.3 %collective-permute-start.6 = (bf16[128,2048]{1,0:T(8,128)(2,1)}, bf16[128,2048]{1,0:T(8,128)(2,1)}, u32[]{:S(2)}, u32[]{:S(2)}) collective-permute-start(bf16[128,2048]{1,0:T(8,128)(2,1)} %convolution_convert_fusion), channel_id=1, source_target_pairs={{0,1},{1,0},{2,3},{3,2},{4,5},{5,4},{6,7},{7,6},{8,9},{9,8},{10,11... | collective-permute-start | bytes 1572872 | tf_op jit(solution)/shard_map/ppermute | solution.py:189
  75.5 3.1 %copy-start.8 = (f32[256]{0:T(256)S(1)}, f32[256]{0:T(256)}, u32[]{:S(2)}) copy-start(f32[256]{0:T(256)} %copy-done.7) | copy-start | bytes 3076
  75.5 3.1 %copy-start.10 = (f32[256]{0:T(256)S(1)}, f32[256]{0:T(256)}, u32[]{:S(2)}) copy-start(f32[256]{0:T(256)} %copy-done.9) | copy-start | bytes 3076
  75.5 3.1 %copy-start.11 = (f32[256]{0:T(256)S(1)}, f32[256]{0:T(256)}, u32[]{:S(2)}) copy-start(f32[256]{0:T(256)} %get-tuple-element.239) | copy-start | bytes 3076
  77.1 8.4 %collective-permute-start.7 = (bf16[1,64,2048]{2,1,0:T(8,128)(2,1)S(1)}, bf16[1,64,2048]{2,1,0:T(8,128)(2,1)S(1)}, u32[]{:S(2)}, u32[]{:S(2)}) collective-permute-start(bf16[1,64,2048]{2,1,0:T(8,128)(2,1)S(1)} %fusion.30), channel_id=1, source_target_pairs={{0,2},{1,3},{2,0},{3,1},{4,6},{5,7},{6,4},{7,5},{8,10},{9,11},{10,... | collective-permute-start | bytes 786440 | tf_op jit(solution)/shard_map/ppermute | solution.py:200

commit v18 on v15

--- a/solution.py
+++ b/solution.py
@@ -45,14 +45,13 @@
     return array_in.reshape((array_in.shape[0] // SPAN, SPAN) + array_in.shape[1:])
 
 
-def segment_parts(queries, head_keys, head_values, decays, starts):
+def segment_parts(queries, head_keys, head_values, decays, firsts, block_starts):
     index_rows = jnp.arange(queries.shape[1])
     lower = (index_rows[:, None] >= index_rows[None, :]).astype(jnp.float32)
     cumulative = jnp.einsum("ac,bck->bak", lower, decays, precision=lax.Precision.HIGHEST)
-    groups = jnp.cumsum(starts, axis=1)
-    intact = (groups == 0.0).astype(jnp.float32)
+    intact = (firsts < block_starts[:, None]).astype(jnp.float32)
     final_log = cumulative[:, -1]
-    in_tail = (groups == groups[:, -1:]).astype(jnp.float32)
+    in_tail = (firsts == firsts[:, -1:]).astype(jnp.float32)
     weighted = (
         head_keys.astype(jnp.float32)
         * jnp.exp(final_log[:, None, :] - cumulative)
@@ -60,7 +59,7 @@
     ).astype(jnp.bfloat16)
     update = jnp.einsum("bsk,bsv->bkv", weighted, head_values, preferred_element_type=jnp.float32)
     step_decay = jnp.exp(final_log) * intact[:, -1:]
-    allowed = (groups[:, :, None] == groups[:, None, :]) & (
+    allowed = (firsts[:, :, None] == firsts[:, None, :]) & (
         index_rows[None, :, None] >= index_rows[None, None, :]
     )
     lifted = queries.astype(jnp.float32) * jnp.exp(cumulative)
@@ -260,7 +259,12 @@
         / 16.0
     )
     local_out, carry_lift, local_memory, local_decay = segment_parts(
-        blocked(conv_query), blocked(conv_key), blocked(conv_value), blocked(decays), blocked(starts)
+        blocked(conv_query),
+        blocked(conv_key),
+        blocked(conv_value),
+        blocked(decays),
+        blocked(prompt_first),
+        blocked(positions)[:, 0],
     )
     closing, entering = prefix_states(local_decay, local_memory, "tok")
     heads_out = local_out.reshape((row_count, value_width)) + jnp.dot(

time: 81.9 us -> 80 us (0.977)
  matrix products: 14.8 us -> 13.7 us
  local copies, waits for them, and re-layouts: 3.79 us -> 2.93 us
    dot_general x1, matrix products: 1.56 us -> 0.44 us  [scatter_sum(): jnp.dot(kept, weight, preferred_element_type=jnp.float32)]
where the time goes in v18:
time: 80 us; the launch traced here: 79.4 us
  waiting for transfers between devices  33.3 us (42%)
  other arithmetic  16.6 us (21%)
  matrix products  13.7 us (17%)
  starting transfers between devices  11.7 us (15%)
  local copies, waits for them, and re-layouts  2.93 us (4%)
  between operations  1.13 us (1%)
    ppermute x4, waiting for transfers between devices, shifted(): lax.ppermute(value, axis, [(source, source + steps) for source in range(i...  24.2 us
    ppermute x4, starting transfers between devices, shifted(): lax.ppermute(value, axis, [(source, source + steps) for source in range(i...  8.45 us
    ppermute x1, waiting for transfers between devices, scatter_sum(): lax.ppermute(outgoing, axis, [(source, source ^ mask) for source in range...  4.63 us
    dot_general x4, matrix products, project(): jnp.dot(gathered, weight, preferred_element_type=jnp.float32)  3.84 us
    dot_general x1, matrix products, segment_parts(): jnp.einsum('bac,bcv->bav', scores, head_values, preferred_element_type=jn...  2.77 us
    ppermute x2, waiting for transfers between devices, gather_rows(): lax.ppermute(jnp.concatenate(received), axis, [(source, source ^ mask) fo...  2.65 us
    dot_general x3, matrix products, segment_parts(): jnp.dot(lifted_intact[block], memory, precision=HIGH_PRECISION)  2.48 us
    broadcast_in_dim x1, other arithmetic, shards(): segment_states = closing[None, None]  2.23 us
  transfers between devices with their start and end apart: 8, of which 8 were waited for; matrix products, arithmetic and copies ran while one was open for 18% of the time, Pallas kernels for 0%

profile of v18, /device:TPU:24, one launch (start us, length us, event | category | flops | bytes accessed | tf_op | source)
XLA Modules:
  0.0 79.4 jit_solution(9152359898531631775)
XLA Ops:
  0.7 1.6 %collective-permute-start = (bf16[64,2048]{1,0:T(8,128)(2,1)}, bf16[64,2048]{1,0:T(8,128)(2,1)S(1)}, u32[]{:S(2)}, u32[]{:S(2)}) collective-permute-start(bf16[64,2048]{1,0:T(8,128)(2,1)} %param.18), channel_id=1, source_target_pairs={{0,2},{1,3},{2,0},{3,1},{4,6},{5,7},{6,4},{7,5},{8,10},{9,11},{10,... | collective-permute-start | bytes 786440 | tf_op jit(solution)/shard_map/ppermute | solution.py:150
  2.3 0.8 select_reduce_fusion.1
  3.5 0.6 slice.188
  4.0 0.7 convert_element_type.162
  4.7 0.7 convert_element_type.172
  5.4 0.7 convert_element_type.178
  6.1 0.5 pad.32.clone
  6.8 0.6 iota_compare_fusion
  7.4 1.6 %collective-permute-done = bf16[64,2048]{1,0:T(8,128)(2,1)S(1)} collective-permute-done((bf16[64,2048]{1,0:T(8,128)(2,1)}, bf16[64,2048]{1,0:T(8,128)(2,1)S(1)}, u32[]{:S(2)}, u32[]{:S(2)}) %collective-permute-start) | collective-permute-done | bytes 262176 | tf_op jit(solution)/shard_map/ppermute | solution.py:150
  9.0 1.0 %pad_maximum_fusion.4 = bf16[128,2048]{1,0:T(8,128)(2,1)S(1)} fusion(bf16[64,2048]{1,0:T(8,128)(2,1)S(1)} %collective-permute-done, bf16[64,2048]{1,0:T(8,128)(2,1)} %param.18), kind=kLoop, calls=%fused_computation.41 | loop fusion | flops 1048576 | bytes 1048576 | tf_op jit(solution)/shard_map/concatenate | solution.py:151
  10.1 0.7 slice_compare_fusion
  10.8 1.1 %collective-permute-done.1 = bf16[128,2048]{1,0:T(8,128)(2,1)S(1)} collective-permute-done((bf16[128,2048]{1,0:T(8,128)(2,1)S(1)}, bf16[128,2048]{1,0:T(8,128)(2,1)S(1)}, u32[]{:S(2)}, u32[]{:S(2)}) %collective-permute-start.1) | collective-permute-done | bytes 524320 | tf_op jit(solution)/shard_map/ppermute | solution.py:150
  12.0 1.8 %conditional.1 = (bf16[256,2048]{1,0:T(8,128)(2,1)S(1)}) conditional(s32[]{:T(128)} %clamp.3, (bf16[64,2048]{1,0:T(8,128)(2,1)S(1)}, bf16[64,2048]{1,0:T(8,128)(2,1)S(1)}, bf16[64,2048]{1,0:T(8,128)(2,1)S(1)}, bf16[64,2048]{1,0:T(8,128)(2,1)S(1)}) %tuple.60, (bf16[64,2048]{1,0:T(8,128)(2,1)S(1)}, ...), branch_computations={%region_2.0_spmd, %region_3.0_spmd, %region_4.5_spmd, %region_5.6_... | conditional | flops 4194304 | bytes 3145764 | solution.py:164
  12.1 0.7 copy-done.4
  12.8 1.0 %pad_maximum_fusion = bf16[256,2048]{1,0:T(8,128)(2,1)S(1)} fusion(bf16[64,2048]{1,0:T(8,128)(2,1)S(1)} %get-tuple-element.40, bf16[64,2048]{1,0:T(8,128)(2,1)} %copy-done.4, bf16[64,2048]{1,0:T(8,128)(2,1)S(1)} %get-tuple-element.33, bf16[64,2048]{1,0:T(8,128)(2,1)S(1)} %get-tuple-element.32), kind=kLoop, calls=%fused_computation | loop fusion | flops 4194304 | bytes 2097152 | tf_op jit(solution)/shard_map/cond/branch_0_fun/concatenate | solution.py:162
  13.8 0.8 fusion.26
  15.0 1.9 %convolution_convert_fusion.5 = bf16[256,256]{1,0:T(8,128)(2,1)S(1)} fusion(bf16[256,2048]{1,0:T(8,128)(2,1)S(1)} %get-tuple-element.103, bf16[2048,256]{1,0:T(8,128)(2,1)} %param.20), kind=kOutput, calls=%fused_computation.17 | convolution fusion | flops 268500992 | bytes 2228224 | tf_op jit(solution)/shard_map/dot_general | solution.py:227
  16.9 0.7 convolution_convert_fusion.3
  17.6 0.5 copy-done.9
  18.1 0.4 convolution_convert_fusion.4
  18.6 0.7 select_bitcast_fusion
  19.2 3.4 %collective-permute-start.2 = (bf16[3,1024]{1,0:T(4,128)(2,1)S(1)}, bf16[3,1024]{1,0:T(4,128)(2,1)S(1)}, u32[]{:S(2)}, u32[]{:S(2)}) collective-permute-start(bf16[3,1024]{1,0:T(4,128)(2,1)S(1)} %get-tuple-element.59), channel_id=1, source_target_pairs={{0,4},{4,8},{8,12},{12,16},{16,20},{20,24},{24,28},{1,5},{5,9},{9,... | collective-permute-start | bytes 18440 | tf_op jit(solution)/shard_map/ppermute | solution.py:17
  22.8 2.8 %collective-permute-done.2 = bf16[3,1024]{1,0:T(4,128)(2,1)S(1)} collective-permute-done((bf16[3,1024]{1,0:T(4,128)(2,1)S(1)}, bf16[3,1024]{1,0:T(4,128)(2,1)S(1)}, u32[]{:S(2)}, u32[]{:S(2)}) %collective-permute-start.2) | collective-permute-done | bytes 6176 | tf_op jit(solution)/shard_map/ppermute | solution.py:17
  26.4 0.9 %broadcast_multiply_fusion = (f32[4,64,256]{2,1,0:T(8,128)}, f32[4,64,256]{2,1,0:T(8,128)S(1)}) fusion(f32[4,256]{1,0:T(4,128)S(1)} %pad_maximum_fusion.12, f32[4,64]{1,0:T(4,128)S(1)} %get-tuple-element.93, f32[4,64,256]{2,1,0:T(8,128)S(1)} %convolution_bitcast_fusion, f32[4,64,256]{2,1,0:T(8,128)S(1)} %bitcast.125), kind=kLoop, calls=%fused_computation.117 | loop fusion | flops 589824 | bytes 1053696 | tf_op jit(solution)/shard_map/mul | solution.py:85
  27.6 0.6 fusion.48
  28.9 2.5 %collective-permute-start.3 = (bf16[257,512]{1,0:T(8,128)(2,1)S(1)}, bf16[257,512]{1,0:T(8,128)(2,1)S(1)}, u32[]{:S(2)}, u32[]{:S(2)}) collective-permute-start(bf16[257,512]{1,0:T(8,128)(2,1)S(1)} %pad_maximum_fusion.5), channel_id=1, source_target_pairs={{0,4},{4,8},{8,12},{12,16},{16,20},{20,24},{24,28},{1,5},{5,9},{9,... | collective-permute-start | bytes 789512 | tf_op jit(solution)/shard_map/ppermute | solution.py:17
  31.4 1.0 %convolution_bitcast_fusion.3 = f32[1,64,512]{2,1,0:T(8,128)} fusion(f32[4,256,512]{2,1,0:T(8,128)S(1)} %fusion.48, f32[256]{0:T(256)S(1)} %get-tuple-element.97, f32[4,64,256]{2,1,0:T(8,128)S(1)} %get-tuple-element.69), kind=kOutput, calls=%fused_computation.20 | convolution fusion | flops 50462720 | bytes 721920 | tf_op jit(solution)/shard_map/dot_general | solution.py:80
  32.4 1.1 %convolution_bitcast_fusion.1 = f32[1,64,512]{2,1,0:T(8,128)} fusion(f32[4,256,512]{2,1,0:T(8,128)S(1)} %fusion.48, f32[256]{0:T(256)S(1)} %bitcast.139, f32[4,64,256]{2,1,0:T(8,128)S(1)} %get-tuple-element.69, f32[256]{0:T(256)S(1)} %bitcast.136, f32[256]{0:T(256)S(1)} %get-tuple-element.97), kind=kOutput, calls=%fused_computation.18 | convolution fusion | flops 50987008 | bytes 1772544 | tf_op jit(solution)/shard_map/dot_general | solution.py:80
  33.5 5.6 %collective-permute-done.3 = bf16[257,512]{1,0:T(8,128)(2,1)S(1)} collective-permute-done((bf16[257,512]{1,0:T(8,128)(2,1)S(1)}, bf16[257,512]{1,0:T(8,128)(2,1)S(1)}, u32[]{:S(2)}, u32[]{:S(2)}) %collective-permute-start.3) | collective-permute-done | bytes 263200 | tf_op jit(solution)/shard_map/ppermute | solution.py:17
  39.1 0.6 subtract_convert_fusion
  39.8 0.7 pad_maximum_fusion.6
  40.6 1.3 %collective-permute-start.4 = (bf16[257,512]{1,0:T(8,128)(2,1)}, bf16[257,512]{1,0:T(8,128)(2,1)}, u32[]{:S(2)}, u32[]{:S(2)}) collective-permute-start(bf16[257,512]{1,0:T(8,128)(2,1)} %pad_maximum_fusion.6), channel_id=1, source_target_pairs={{0,8},{4,12},{8,16},{12,20},{16,24},{20,28},{1,9},{5,13},{9,17},{1... | collective-permute-start | bytes 789512 | tf_op jit(solution)/shard_map/ppermute | solution.py:17
  41.8 2.8 %convolution_add_fusion = f32[4,64,512]{2,1,0:T(8,128)} fusion(f32[1,64,512]{2,1,0:T(8,128)} %convolution_bitcast_fusion.1, f32[1,64,512]{2,1,0:T(8,128)S(1)} %convolution_bitcast_fusion.2, f32[1,64,512]{2,1,0:T(8,128)} %convolution_bitcast_fusion.3, f32[4]{0:T(128)} %pad.32.clone, f32[4,64,256]{2,1,0:T(8,128)} %copy-done.8, s32[4,64]{1,0:T(4,128)S(1)} %eq.38, ...), kind=kOutput, calls=%fused_computation.8 | convolution fusion | flops 27525120 | bytes 2233360 | tf_op jit(solution)/shard_map/bac,bcv->bav/dot_general | solution.py:71
  44.6 4.7 %collective-permute-done.4 = bf16[257,512]{1,0:T(8,128)(2,1)} collective-permute-done((bf16[257,512]{1,0:T(8,128)(2,1)}, bf16[257,512]{1,0:T(8,128)(2,1)}, u32[]{:S(2)}, u32[]{:S(2)}) %collective-permute-start.4) | collective-permute-done | bytes 263200 | tf_op jit(solution)/shard_map/ppermute | solution.py:17
  49.3 1.3 %fusion.77 = bf16[256,512]{1,0:T(8,128)(2,1)S(1)} fusion(f32[256,512]{1,0:T(8,128)} %copy-done.1, bf16[257,512]{1,0:T(8,128)(2,1)S(1)} %collective-permute-done.3, f32[256]{0:T(256)S(1)} %get-tuple-element.67, pred[]{:T(512)S(6)} %ge.73, bf16[257,512]{1,0:T(8,128)(2,1)} %collective-permute-done.4, f32[256]{0:T(256)} %get-tuple-element.62, pred[]{:T(512)S(6)} %ge.72), kind=kLoop, calls=%fused_computation.176 | loop fusion | flops 1179648 | bytes 1312770 | tf_op jit(solution)/shard_map/convert_element_type | solution.py:119
  50.6 1.3 %collective-permute-start.5 = (bf16[256,512]{1,0:T(8,128)(2,1)S(1)}, bf16[256,512]{1,0:T(8,128)(2,1)S(1)}, u32[]{:S(2)}, u32[]{:S(2)}) collective-permute-start(bf16[256,512]{1,0:T(8,128)(2,1)S(1)} %fusion.77), channel_id=1, source_target_pairs={{0,16},{4,20},{8,24},{12,28},{1,17},{5,21},{9,25},{13,29},{2,18},{... | collective-permute-start | bytes 786440 | tf_op jit(solution)/shard_map/ppermute | solution.py:17
  51.9 0.7 slice_convert_fusion
  52.6 0.7 multiply_select_fusion
  53.3 11.1 %collective-permute-done.5 = bf16[256,512]{1,0:T(8,128)(2,1)S(1)} collective-permute-done((bf16[256,512]{1,0:T(8,128)(2,1)S(1)}, bf16[256,512]{1,0:T(8,128)(2,1)S(1)}, u32[]{:S(2)}, u32[]{:S(2)}) %collective-permute-start.5) | collective-permute-done | bytes 262176 | tf_op jit(solution)/shard_map/ppermute | solution.py:17
  64.4 2.0 %multiply_reduce_fusion.3 = (f32[256]{0:T(256)S(1)}, f32[256,512]{1,0:T(8,128)S(1)}) fusion(f32[256,512]{1,0:T(8,128)} %bitcast.148, f32[256,256]{1,0:T(8,128)} %bitcast.130, bf16[256,512]{1,0:T(8,128)(2,1)S(1)} %collective-permute-done.5, f32[256]{0:T(256)} %bitcast.145, f32[256]{0:T(256)S(1)} %get-tuple-element.96, pred[]{:T(512)S(6)} %ge.72, ...), kind=kOutput, calls=%fused_computation.55 | convolution fusion | flops 202899200 | bytes 2100226 | tf_op jit(solution)/shard_map/dot_general | solution.py:270
  66.4 0.8 multiply_convert_fusion
  67.3 0.4 convolution_convert_fusion
  67.8 1.9 %collective-permute-done.6 = bf16[128,2048]{1,0:T(8,128)(2,1)S(1)} collective-permute-done((bf16[128,2048]{1,0:T(8,128)(2,1)S(1)}, bf16[128,2048]{1,0:T(8,128)(2,1)S(1)}, u32[]{:S(2)}, u32[]{:S(2)}) %collective-permute-start.6) | collective-permute-done | bytes 524320 | tf_op jit(solution)/shard_map/ppermute | solution.py:188
  69.7 0.4 convert_add_fusion
  70.2 1.5 %collective-permute-start.7 = (bf16[1,64,2048]{2,1,0:T(8,128)(2,1)S(1)}, bf16[1,64,2048]{2,1,0:T(8,128)(2,1)S(1)}, u32[]{:S(2)}, u32[]{:S(2)}) collective-permute-start(bf16[1,64,2048]{2,1,0:T(8,128)(2,1)S(1)} %fusion.24), channel_id=1, source_target_pairs={{0,2},{1,3},{2,0},{3,1},{4,6},{5,7},{6,4},{7,5},{8,10},{9,11},{10,... | collective-permute-start | bytes 786440 | tf_op jit(solution)/shard_map/ppermute | solution.py:199
  71.8 2.2 %fusion.4 = f32[1,1,256,512]{3,2,1,0:T(8,128)} fusion(bf16[256,512]{1,0:T(8,128)(2,1)S(1)} %copy-done.13, f32[256]{0:T(256)S(1)} %get-tuple-element.95, pred[]{:T(512)S(6)} %ge.71, f32[256,512]{1,0:T(8,128)S(1)} %copy-done.2, bf16[257,512]{1,0:T(8,128)(2,1)S(1)} %collective-permute-done.3, f32[256]{0:T(256)S(1)} %get-tuple-element.67, pred[]{:T(512)S(6)} %ge.73, ...), kind=kLoop, calls=%fused_computation.38 | loop fusion | flops 1572864 | bytes 1838083 | tf_op jit(solution)/shard_map/broadcast_in_dim | solution.py:279
  74.0 4.6 %collective-permute-done.7 = bf16[1,64,2048]{2,1,0:T(8,128)(2,1)S(1)} collective-permute-done((bf16[1,64,2048]{2,1,0:T(8,128)(2,1)S(1)}, bf16[1,64,2048]{2,1,0:T(8,128)(2,1)S(1)}, u32[]{:S(2)}, u32[]{:S(2)}) %collective-permute-start.7) | collective-permute-done | bytes 262176 | tf_op jit(solution)/shard_map/ppermute | solution.py:199
  78.6 0.8 fusion.6
  (78 shorter events, 3.3 us)
Async XLA Ops:
  0.6 66.6 %copy-start = (bf16[512,2048]{1,0:T(8,128)(2,1)S(1)}, bf16[512,2048]{1,0:T(8,128)(2,1)}, u32[]{:S(2)}) copy-start(bf16[512,2048]{1,0:T(8,128)(2,1)} %param.31) | copy-start | bytes 6291460
  0.6 11.3 %copy-start.3 = (bf16[64,2048]{1,0:T(8,128)(2,1)S(1)}, bf16[64,2048]{1,0:T(8,128)(2,1)}, u32[]{:S(2)}) copy-start(bf16[64,2048]{1,0:T(8,128)(2,1)} %param.18) | copy-start | bytes 786436
  0.7 8.3 %collective-permute-start = (bf16[64,2048]{1,0:T(8,128)(2,1)}, bf16[64,2048]{1,0:T(8,128)(2,1)S(1)}, u32[]{:S(2)}, u32[]{:S(2)}) collective-permute-start(bf16[64,2048]{1,0:T(8,128)(2,1)} %param.18), channel_id=1, source_target_pairs={{0,2},{1,3},{2,0},{3,1},{4,6},{5,7},{6,4},{7,5},{8,10},{9,11},{10,... | collective-permute-start | bytes 786440 | tf_op jit(solution)/shard_map/ppermute | solution.py:150
  10.0 2.0 %collective-permute-start.1 = (bf16[128,2048]{1,0:T(8,128)(2,1)S(1)}, bf16[128,2048]{1,0:T(8,128)(2,1)S(1)}, u32[]{:S(2)}, u32[]{:S(2)}) collective-permute-start(bf16[128,2048]{1,0:T(8,128)(2,1)S(1)} %pad_maximum_fusion.4), channel_id=1, source_target_pairs={{0,1},{1,0},{2,3},{3,2},{4,5},{5,4},{6,7},{7,6},{8,9},{9,8},{10,11... | collective-permute-start | bytes 1572872 | tf_op jit(solution)/shard_map/ppermute | solution.py:150
  12.0 1.8 %copy-start.19 = (bf16[2048,16]{0,1:T(8,128)(2,1)S(1)}, bf16[2048,16]{0,1:T(8,128)(2,1)}, u32[]{:S(2)}) copy-start(bf16[2048,16]{0,1:T(8,128)(2,1)} %param.26) | copy-start | bytes 196612
  12.0 1.8 %copy-start.20 = (bf16[16,256]{1,0:T(8,128)(2,1)S(1)}, bf16[16,256]{1,0:T(8,128)(2,1)}, u32[]{:S(2)}) copy-start(bf16[16,256]{1,0:T(8,128)(2,1)} %param.27) | copy-start | bytes 24580
  12.0 1.8 %copy-start.22 = (f32[256]{0:T(256)S(1)}, f32[256]{0:T(256)}, u32[]{:S(2)}) copy-start(f32[256]{0:T(256)} %param.28) | copy-start | bytes 3076
  12.1 0.7 copy-start.4
  14.6 2.2 %copy-start.17 = (bf16[2048,512]{1,0:T(8,128)(2,1)S(1)}, bf16[2048,512]{1,0:T(8,128)(2,1)}, u32[]{:S(2)}) copy-start(bf16[2048,512]{1,0:T(8,128)(2,1)} %param.22) | copy-start | bytes 6291460
  14.9 12.6 %copy-start.8 = (f32[4,64,256]{2,1,0:T(8,128)}, f32[4,64,256]{2,1,0:T(8,128)S(1)}, u32[]{:S(2)}) copy-start(f32[4,64,256]{2,1,0:T(8,128)S(1)} %convolution_bitcast_fusion) | copy-start | bytes 786436
  16.9 1.2 %copy-start.9 = (bf16[2048,256]{1,0:T(8,128)(2,1)S(1)}, bf16[2048,256]{1,0:T(8,128)(2,1)}, u32[]{:S(2)}) copy-start(bf16[2048,256]{1,0:T(8,128)(2,1)} %param.21) | copy-start | bytes 3145732
  19.2 6.4 %collective-permute-start.2 = (bf16[3,1024]{1,0:T(4,128)(2,1)S(1)}, bf16[3,1024]{1,0:T(4,128)(2,1)S(1)}, u32[]{:S(2)}, u32[]{:S(2)}) collective-permute-start(bf16[3,1024]{1,0:T(4,128)(2,1)S(1)} %get-tuple-element.59), channel_id=1, source_target_pairs={{0,4},{4,8},{8,12},{12,16},{16,20},{20,24},{24,28},{1,5},{5,9},{9,... | collective-permute-start | bytes 18440 | tf_op jit(solution)/shard_map/ppermute | solution.py:17
  26.3 1.2 %copy-start.10 = (f32[256,256]{1,0:T(8,128)}, f32[256,256]{1,0:T(8,128)S(1)}, u32[]{:S(2)}) copy-start(f32[256,256]{1,0:T(8,128)S(1)} %get-tuple-element.56) | copy-start | bytes 786436
  26.4 1.9 %copy-start.14 = (f32[256,256]{1,0:T(8,128)}, f32[256,256]{1,0:T(8,128)S(1)}, u32[]{:S(2)}) copy-start(f32[256,256]{1,0:T(8,128)S(1)} %get-tuple-element.57) | copy-start | bytes 786436
  27.5 0.9 %copy-start.11 = (f32[256,512]{1,0:T(8,128)}, f32[256,512]{1,0:T(8,128)S(1)}, u32[]{:S(2)}) copy-start(f32[256,512]{1,0:T(8,128)S(1)} %multiply_reduce_fusion) | copy-start | bytes 1572868
  28.4 12.1 %copy-start.1 = (f32[256,512]{1,0:T(8,128)}, f32[256,512]{1,0:T(8,128)S(1)}, u32[]{:S(2)}) copy-start(f32[256,512]{1,0:T(8,128)S(1)} %get-tuple-element.64) | copy-start | bytes 1572868
  28.9 10.2 %collective-permute-start.3 = (bf16[257,512]{1,0:T(8,128)(2,1)S(1)}, bf16[257,512]{1,0:T(8,128)(2,1)S(1)}, u32[]{:S(2)}, u32[]{:S(2)}) collective-permute-start(bf16[257,512]{1,0:T(8,128)(2,1)S(1)} %pad_maximum_fusion.5), channel_id=1, source_target_pairs={{0,4},{4,8},{8,12},{12,16},{16,20},{20,24},{24,28},{1,5},{5,9},{9,... | collective-permute-start | bytes 789512 | tf_op jit(solution)/shard_map/ppermute | solution.py:17
  39.1 0.6 copy-start.16
  40.6 8.7 %collective-permute-start.4 = (bf16[257,512]{1,0:T(8,128)(2,1)}, bf16[257,512]{1,0:T(8,128)(2,1)}, u32[]{:S(2)}, u32[]{:S(2)}) collective-permute-start(bf16[257,512]{1,0:T(8,128)(2,1)} %pad_maximum_fusion.6), channel_id=1, source_target_pairs={{0,8},{4,12},{8,16},{12,20},{16,24},{20,28},{1,9},{5,13},{9,17},{1... | collective-permute-start | bytes 789512 | tf_op jit(solution)/shard_map/ppermute | solution.py:17
  44.6 21.8 %copy-start.18 = (bf16[2048,512]{1,0:T(8,128)(2,1)S(1)}, bf16[2048,512]{1,0:T(8,128)(2,1)}, u32[]{:S(2)}) copy-start(bf16[2048,512]{1,0:T(8,128)(2,1)} %param.29) | copy-start | bytes 6291460
  44.6 21.8 %copy-start.21 = (f32[512]{0:T(512)S(1)}, f32[512]{0:T(512)}, u32[]{:S(2)}) copy-start(f32[512]{0:T(512)} %param.30) | copy-start | bytes 6148
  50.6 13.8 %collective-permute-start.5 = (bf16[256,512]{1,0:T(8,128)(2,1)S(1)}, bf16[256,512]{1,0:T(8,128)(2,1)S(1)}, u32[]{:S(2)}, u32[]{:S(2)}) collective-permute-start(bf16[256,512]{1,0:T(8,128)(2,1)S(1)} %fusion.77), channel_id=1, source_target_pairs={{0,16},{4,20},{8,24},{12,28},{1,17},{5,21},{9,25},{13,29},{2,18},{... | collective-permute-start | bytes 786440 | tf_op jit(solution)/shard_map/ppermute | solution.py:17
  64.4 2.0 %copy-start.12 = (bf16[256,512]{1,0:T(8,128)(2,1)}, bf16[256,512]{1,0:T(8,128)(2,1)S(1)}, u32[]{:S(2)}) copy-start(bf16[256,512]{1,0:T(8,128)(2,1)S(1)} %collective-permute-done.5) | copy-start | bytes 786436
  67.7 2.0 %collective-permute-start.6 = (bf16[128,2048]{1,0:T(8,128)(2,1)S(1)}, bf16[128,2048]{1,0:T(8,128)(2,1)S(1)}, u32[]{:S(2)}, u32[]{:S(2)}) collective-permute-start(bf16[128,2048]{1,0:T(8,128)(2,1)S(1)} %convolution_convert_fusion), channel_id=1, source_target_pairs={{0,1},{1,0},{2,3},{3,2},{4,5},{5,4},{6,7},{7,6},{8,9},{9,8},{10,11... | collective-permute-start | bytes 1572872 | tf_op jit(solution)/shard_map/ppermute | solution.py:188
  69.7 2.1 %copy-start.2 = (f32[256,512]{1,0:T(8,128)S(1)}, f32[256,512]{1,0:T(8,128)}, u32[]{:S(2)}) copy-start(f32[256,512]{1,0:T(8,128)} %copy-done.1) | copy-start | bytes 1572868
  69.7 2.1 %copy-start.13 = (bf16[256,512]{1,0:T(8,128)(2,1)S(1)}, bf16[256,512]{1,0:T(8,128)(2,1)}, u32[]{:S(2)}) copy-start(bf16[256,512]{1,0:T(8,128)(2,1)} %copy-done.12) | copy-start | bytes 786436
  69.7 2.1 %copy-start.15 = (f32[256]{0:T(256)S(1)}, f32[256]{0:T(256)}, u32[]{:S(2)}) copy-start(f32[256]{0:T(256)} %get-tuple-element.62) | copy-start | bytes 3076
  70.2 8.4 %collective-permute-start.7 = (bf16[1,64,2048]{2,1,0:T(8,128)(2,1)S(1)}, bf16[1,64,2048]{2,1,0:T(8,128)(2,1)S(1)}, u32[]{:S(2)}, u32[]{:S(2)}) collective-permute-start(bf16[1,64,2048]{2,1,0:T(8,128)(2,1)S(1)} %fusion.24), channel_id=1, source_target_pairs={{0,2},{1,3},{2,0},{3,1},{4,6},{5,7},{6,4},{7,5},{8,10},{9,11},{10,... | collective-permute-start | bytes 786440 | tf_op jit(solution)/shard_map/ppermute | solution.py:199

commit v19 on v18

--- a/solution.py
+++ b/solution.py
@@ -154,14 +154,19 @@
             order = order + [flip ^ mask for flip in order]
             mask //= 2
 
-    def ordered(shift):
+    def pick(index):
         if count & (count - 1):
-            picks = [order.index((index - shift) % count) for index in range(count)]
+            wanted = (place - index) % count
+            table = [order.index((-step) % count) for step in range(count)]
         else:
-            picks = [order.index(shift ^ index) for index in range(count)]
-        return jnp.concatenate([received[pick] for pick in picks])
-
-    return lax.switch(place, [functools.partial(ordered, shift) for shift in range(count)])
+            wanted = jnp.bitwise_xor(place, index)
+            table = [order.index(flip) for flip in range(count)]
+        chosen = received[table[count - 1]]
+        for flip in range(count - 2, -1, -1):
+            chosen = jnp.where(wanted == flip, received[table[flip]], chosen)
+        return chosen
+
+    return jnp.concatenate([pick(index) for index in range(count)])
 
 
 def scatter_sum(gated, weight, axis):

time: 80 us -> 82.1 us (1.026)
  matrix products: 13.7 us -> 16.3 us
  waiting for transfers between devices: 33.3 us -> 35.4 us
  starting transfers between devices: 11.7 us -> 10.2 us
    ppermute x1, starting transfers between devices: 1.54 us -> 0.07 us  [scatter_sum(): lax.ppermute(outgoing, axis, [(source, source ^ mask) for source in range...]
    ppermute x1, waiting for transfers between devices: 4.63 us -> 6.1 us  [scatter_sum(): lax.ppermute(outgoing, axis, [(source, source ^ mask) for source in range...]
    dot_general x1, matrix products: 0.79 us -> 1.93 us  [shards(): jnp.dot(low_rank, decay_up, preferred_element_type=jnp.float32) + decay_bias]
    dot_general x1, matrix products: 0.44 us -> 1.49 us  [scatter_sum(): jnp.dot(kept, weight, preferred_element_type=jnp.float32)]
    concatenate x1 -> x0, other arithmetic: 1.04 us -> none  [ordered(): return jnp.concatenate([received[pick] for pick in picks])]
    select_n x0 -> x2, other arithmetic: none -> 0.85 us  [pick(): chosen = jnp.where(wanted == flip, received[table[flip]], chosen)]
where the time goes in v19:
time: 82.1 us; the launch traced here: 81.5 us
  waiting for transfers between devices  35.4 us (43%)
  matrix products  16.3 us (20%)
  other arithmetic  16.2 us (20%)
  starting transfers between devices  10.2 us (12%)
  local copies, waits for them, and re-layouts  2.29 us (3%)
  between operations  1.1 us (1%)
    ppermute x4, waiting for transfers between devices, shifted(): lax.ppermute(value, axis, [(source, source + steps) for source in range(i...  24.3 us
    ppermute x4, starting transfers between devices, shifted(): lax.ppermute(value, axis, [(source, source + steps) for source in range(i...  8.46 us
    ppermute x1, waiting for transfers between devices, scatter_sum(): lax.ppermute(outgoing, axis, [(source, source ^ mask) for source in range...  6.1 us
    dot_general x4, matrix products, project(): jnp.dot(gathered, weight, preferred_element_type=jnp.float32)  3.85 us
    ppermute x2, waiting for transfers between devices, gather_rows(): lax.ppermute(jnp.concatenate(received), axis, [(source, source ^ mask) fo...  2.66 us
    dot_general x1, matrix products, segment_parts(): jnp.einsum('bac,bcv->bav', scores, head_values, preferred_element_type=jn...  2.55 us
    dot_general x3, matrix products, segment_parts(): jnp.dot(lifted_intact[block], memory, precision=HIGH_PRECISION)  2.49 us
    ppermute x1, waiting for transfers between devices, scatter_sum(): lax.ppermute(outgoing, axis, [(source, source ^ 1) for source in range(co...  2.25 us
  transfers between devices with their start and end apart: 8, of which 8 were waited for; matrix products, arithmetic and copies ran while one was open for 18% of the time, Pallas kernels for 0%

profile of v19, /device:TPU:24, one launch (start us, length us, event | category | flops | bytes accessed | tf_op | source)
XLA Modules:
  0.0 81.5 jit_solution(9348247959608582954)
XLA Ops:
  0.7 1.6 %collective-permute-start = (bf16[64,2048]{1,0:T(8,128)(2,1)}, bf16[64,2048]{1,0:T(8,128)(2,1)S(1)}, u32[]{:S(2)}, u32[]{:S(2)}) collective-permute-start(bf16[64,2048]{1,0:T(8,128)(2,1)} %param.14), channel_id=1, source_target_pairs={{0,2},{1,3},{2,0},{3,1},{4,6},{5,7},{6,4},{7,5},{8,10},{9,11},{10,... | collective-permute-start | bytes 786440 | tf_op jit(solution)/shard_map/ppermute | solution.py:150
  2.3 0.8 select_reduce_fusion.1
  3.5 0.6 slice.188
  4.0 0.7 convert_element_type.162
  4.7 0.7 convert_element_type.172
  5.4 0.7 convert_element_type.178
  6.1 0.5 pad.16.clone
  6.8 0.6 iota_compare_fusion
  7.4 1.6 %collective-permute-done = bf16[64,2048]{1,0:T(8,128)(2,1)S(1)} collective-permute-done((bf16[64,2048]{1,0:T(8,128)(2,1)}, bf16[64,2048]{1,0:T(8,128)(2,1)S(1)}, u32[]{:S(2)}, u32[]{:S(2)}) %collective-permute-start) | collective-permute-done | bytes 262176 | tf_op jit(solution)/shard_map/ppermute | solution.py:150
  9.0 1.0 %pad_maximum_fusion.1 = bf16[128,2048]{1,0:T(8,128)(2,1)S(1)} fusion(bf16[64,2048]{1,0:T(8,128)(2,1)S(1)} %collective-permute-done, bf16[64,2048]{1,0:T(8,128)(2,1)} %param.14), kind=kLoop, calls=%fused_computation.38 | loop fusion | flops 1048576 | bytes 1048576 | tf_op jit(solution)/shard_map/concatenate | solution.py:151
  10.1 0.7 slice_compare_fusion
  10.8 1.1 %collective-permute-done.1 = bf16[128,2048]{1,0:T(8,128)(2,1)S(1)} collective-permute-done((bf16[128,2048]{1,0:T(8,128)(2,1)S(1)}, bf16[128,2048]{1,0:T(8,128)(2,1)S(1)}, u32[]{:S(2)}, u32[]{:S(2)}) %collective-permute-start.1) | collective-permute-done | bytes 524320 | tf_op jit(solution)/shard_map/ppermute | solution.py:150
  12.0 0.8 select_select_fusion.3
  12.8 1.9 %fusion.26 = f32[256,256]{1,0:T(8,128)S(1)} fusion(bf16[16,256]{1,0:T(8,128)(2,1)S(1)} %copy-done.18, bf16[2048,16]{0,1:T(8,128)(2,1)S(1)} %copy-done.17, f32[256]{0:T(256)S(1)} %copy-done.20, bf16[64,2048]{1,0:T(8,128)(2,1)} %get-tuple-element.21, bf16[64,2048]{1,0:T(8,128)(2,1)S(1)} %select_select_fusion.1, bf16[64,2048]{1,0:T(8,128)(2,1)S(1)} %get-tuple-element.20, ...), kind=kOutput, calls=%fused_computation.75 | convolution fusion | flops 23728128 | bytes 1385472 | tf_op jit(solution)/shard_map/dot_general | solution.py:262
  15.1 1.9 %convolution_convert_fusion.5 = bf16[256,256]{1,0:T(8,128)(2,1)S(1)} fusion(bf16[2048,256]{1,0:T(8,128)(2,1)} %param.16, bf16[64,2048]{1,0:T(8,128)(2,1)} %get-tuple-element.21, bf16[64,2048]{1,0:T(8,128)(2,1)S(1)} %select_select_fusion.1, bf16[64,2048]{1,0:T(8,128)(2,1)S(1)} %get-tuple-element.20, bf16[64,2048]{1,0:T(8,128)(2,1)S(1)} %get-tuple-element.19), kind=kOutput, calls=%fused_computation.13 | convolution fusion | flops 272695296 | bytes 2228224 | tf_op jit(solution)/shard_map/dot_general | solution.py:232
  17.2 0.7 convolution_convert_fusion.3
  17.9 0.5 copy-done.16
  18.4 0.4 convolution_convert_fusion.4
  18.8 0.7 select_bitcast_fusion
  19.5 3.4 %collective-permute-start.2 = (bf16[3,1024]{1,0:T(4,128)(2,1)S(1)}, bf16[3,1024]{1,0:T(4,128)(2,1)S(1)}, u32[]{:S(2)}, u32[]{:S(2)}) collective-permute-start(bf16[3,1024]{1,0:T(4,128)(2,1)S(1)} %get-tuple-element.6), channel_id=1, source_target_pairs={{0,4},{4,8},{8,12},{12,16},{16,20},{20,24},{24,28},{1,5},{5,9},{9,... | collective-permute-start | bytes 18440 | tf_op jit(solution)/shard_map/ppermute | solution.py:17
  23.1 2.8 %collective-permute-done.2 = bf16[3,1024]{1,0:T(4,128)(2,1)S(1)} collective-permute-done((bf16[3,1024]{1,0:T(4,128)(2,1)S(1)}, bf16[3,1024]{1,0:T(4,128)(2,1)S(1)}, u32[]{:S(2)}, u32[]{:S(2)}) %collective-permute-start.2) | collective-permute-done | bytes 6176 | tf_op jit(solution)/shard_map/ppermute | solution.py:17
  26.3 0.3 multiply_reduce_fusion.2
  26.6 0.8 %broadcast_multiply_fusion = (f32[4,64,256]{2,1,0:T(8,128)}, f32[4,64,256]{2,1,0:T(8,128)S(1)}) fusion(f32[4,256]{1,0:T(4,128)S(1)} %pad_maximum_fusion.9, f32[4,64]{1,0:T(4,128)S(1)} %get-tuple-element.41, f32[4,64,256]{2,1,0:T(8,128)S(1)} %convolution_bitcast_fusion, f32[4,64,256]{2,1,0:T(8,128)S(1)} %bitcast.120), kind=kLoop, calls=%fused_computation.118 | loop fusion | flops 589824 | bytes 1053696 | tf_op jit(solution)/shard_map/mul | solution.py:85
  27.5 0.3 multiply_reduce_fusion
  27.8 0.6 fusion.48
  28.7 0.4 convolution_bitcast_fusion.2
  29.1 2.5 %collective-permute-start.3 = (bf16[257,512]{1,0:T(8,128)(2,1)S(1)}, bf16[257,512]{1,0:T(8,128)(2,1)S(1)}, u32[]{:S(2)}, u32[]{:S(2)}) collective-permute-start(bf16[257,512]{1,0:T(8,128)(2,1)S(1)} %pad_maximum_fusion.2), channel_id=1, source_target_pairs={{0,4},{4,8},{8,12},{12,16},{16,20},{20,24},{24,28},{1,5},{5,9},{9,... | collective-permute-start | bytes 789512 | tf_op jit(solution)/shard_map/ppermute | solution.py:17
  31.6 1.0 %convolution_bitcast_fusion.3 = f32[1,64,512]{2,1,0:T(8,128)} fusion(f32[4,256,512]{2,1,0:T(8,128)S(1)} %fusion.48, f32[256]{0:T(256)S(1)} %get-tuple-element.45, f32[4,64,256]{2,1,0:T(8,128)S(1)} %get-tuple-element.16), kind=kOutput, calls=%fused_computation.16 | convolution fusion | flops 50462720 | bytes 721920 | tf_op jit(solution)/shard_map/dot_general | solution.py:80
  32.6 1.1 %convolution_bitcast_fusion.1 = f32[1,64,512]{2,1,0:T(8,128)} fusion(f32[4,256,512]{2,1,0:T(8,128)S(1)} %fusion.48, f32[256]{0:T(256)S(1)} %bitcast.134, f32[4,64,256]{2,1,0:T(8,128)S(1)} %get-tuple-element.16, f32[256]{0:T(256)S(1)} %bitcast.131, f32[256]{0:T(256)S(1)} %get-tuple-element.45), kind=kOutput, calls=%fused_computation.14 | convolution fusion | flops 50987008 | bytes 1772544 | tf_op jit(solution)/shard_map/dot_general | solution.py:80
  33.7 5.6 %collective-permute-done.3 = bf16[257,512]{1,0:T(8,128)(2,1)S(1)} collective-permute-done((bf16[257,512]{1,0:T(8,128)(2,1)S(1)}, bf16[257,512]{1,0:T(8,128)(2,1)S(1)}, u32[]{:S(2)}, u32[]{:S(2)}) %collective-permute-start.3) | collective-permute-done | bytes 263200 | tf_op jit(solution)/shard_map/ppermute | solution.py:17
  39.3 0.6 subtract_convert_fusion
  40.0 0.7 pad_maximum_fusion.3
  40.7 1.3 %collective-permute-start.4 = (bf16[257,512]{1,0:T(8,128)(2,1)}, bf16[257,512]{1,0:T(8,128)(2,1)}, u32[]{:S(2)}, u32[]{:S(2)}) collective-permute-start(bf16[257,512]{1,0:T(8,128)(2,1)} %pad_maximum_fusion.3), channel_id=1, source_target_pairs={{0,8},{4,12},{8,16},{12,20},{16,24},{20,28},{1,9},{5,13},{9,17},{1... | collective-permute-start | bytes 789512 | tf_op jit(solution)/shard_map/ppermute | solution.py:17
  42.0 2.5 %convolution_add_fusion = f32[4,64,512]{2,1,0:T(8,128)} fusion(f32[1,64,512]{2,1,0:T(8,128)} %convolution_bitcast_fusion.1, f32[1,64,512]{2,1,0:T(8,128)S(1)} %convolution_bitcast_fusion.2, f32[1,64,512]{2,1,0:T(8,128)} %convolution_bitcast_fusion.3, f32[4]{0:T(128)} %pad.16.clone, f32[4,64,256]{2,1,0:T(8,128)S(1)} %convolution_bitcast_fusion, ...), kind=kOutput, calls=%fused_computation.4 | convolution fusion | flops 27525120 | bytes 2233360 | tf_op jit(solution)/shard_map/bac,bcv->bav/dot_general | solution.py:71
  44.6 4.8 %collective-permute-done.4 = bf16[257,512]{1,0:T(8,128)(2,1)} collective-permute-done((bf16[257,512]{1,0:T(8,128)(2,1)}, bf16[257,512]{1,0:T(8,128)(2,1)}, u32[]{:S(2)}, u32[]{:S(2)}) %collective-permute-start.4) | collective-permute-done | bytes 263200 | tf_op jit(solution)/shard_map/ppermute | solution.py:17
  49.5 1.2 %fusion.77 = bf16[256,512]{1,0:T(8,128)(2,1)S(1)} fusion(f32[256,512]{1,0:T(8,128)S(1)} %get-tuple-element.11, bf16[257,512]{1,0:T(8,128)(2,1)S(1)} %collective-permute-done.3, f32[256]{0:T(256)S(1)} %get-tuple-element.14, pred[]{:T(512)S(6)} %ge.73, bf16[257,512]{1,0:T(8,128)(2,1)} %collective-permute-done.4, f32[256]{0:T(256)} %get-tuple-element.9, ...), kind=kLoop, calls=%fused_computation.177 | loop fusion | flops 1179648 | bytes 1312770 | tf_op jit(solution)/shard_map/convert_element_type | solution.py:119
  50.6 1.3 %collective-permute-start.5 = (bf16[256,512]{1,0:T(8,128)(2,1)S(1)}, bf16[256,512]{1,0:T(8,128)(2,1)S(1)}, u32[]{:S(2)}, u32[]{:S(2)}) collective-permute-start(bf16[256,512]{1,0:T(8,128)(2,1)S(1)} %fusion.77), channel_id=1, source_target_pairs={{0,16},{4,20},{8,24},{12,28},{1,17},{5,21},{9,25},{13,29},{2,18},{... | collective-permute-start | bytes 786440 | tf_op jit(solution)/shard_map/ppermute | solution.py:17
  51.9 0.7 slice_convert_fusion
  52.6 0.7 multiply_select_fusion
  53.3 11.1 %collective-permute-done.5 = bf16[256,512]{1,0:T(8,128)(2,1)S(1)} collective-permute-done((bf16[256,512]{1,0:T(8,128)(2,1)S(1)}, bf16[256,512]{1,0:T(8,128)(2,1)S(1)}, u32[]{:S(2)}, u32[]{:S(2)}) %collective-permute-start.5) | collective-permute-done | bytes 262176 | tf_op jit(solution)/shard_map/ppermute | solution.py:17
  64.4 1.9 %multiply_reduce_fusion.3 = (f32[256]{0:T(256)S(1)}, f32[256,512]{1,0:T(8,128)S(1)}) fusion(f32[256,512]{1,0:T(8,128)} %bitcast.143, f32[256,256]{1,0:T(8,128)} %bitcast.125, bf16[256,512]{1,0:T(8,128)(2,1)S(1)} %collective-permute-done.5, f32[256]{0:T(256)} %bitcast.140, f32[256]{0:T(256)S(1)} %get-tuple-element.44, pred[]{:T(512)S(6)} %ge.72, ...), kind=kOutput, calls=%fused_computation.52 | convolution fusion | flops 202899200 | bytes 2100226 | tf_op jit(solution)/shard_map/dot_general | solution.py:275
  66.4 0.8 multiply_convert_fusion
  67.2 1.2 %convolution_convert_fusion = bf16[128,2048]{1,0:T(8,128)(2,1)} fusion(bf16[512,2048]{1,0:T(8,128)(2,1)S(1)} %copy-done, bf16[64,512]{1,0:T(8,128)(2,1)S(1)} %get-tuple-element.28, bf16[64,512]{1,0:T(8,128)(2,1)S(1)} %get-tuple-element.27), kind=kOutput, calls=%fused_computation | convolution fusion | flops 268959744 | bytes 2752512 | tf_op jit(solution)/shard_map/dot_general | solution.py:192
  68.5 2.2 %collective-permute-done.6 = bf16[128,2048]{1,0:T(8,128)(2,1)} collective-permute-done((bf16[128,2048]{1,0:T(8,128)(2,1)}, bf16[128,2048]{1,0:T(8,128)(2,1)}, u32[]{:S(2)}, u32[]{:S(2)}) %collective-permute-start.6) | collective-permute-done | bytes 524320 | tf_op jit(solution)/shard_map/ppermute | solution.py:193
  70.7 1.5 %convert_add_fusion = f32[128,2048]{1,0:T(8,128)S(1)} fusion(bf16[128,2048]{1,0:T(8,128)(2,1)} %collective-permute-done.6, bf16[512,2048]{1,0:T(8,128)(2,1)S(1)} %copy-done, bf16[64,512]{1,0:T(8,128)(2,1)S(1)} %get-tuple-element.26, bf16[64,512]{1,0:T(8,128)(2,1)S(1)} %get-tuple-element.25), kind=kOutput, calls=%fused_computation.21 | convolution fusion | flops 269746176 | bytes 3801088 | tf_op jit(solution)/shard_map/dot_general | solution.py:195
  72.4 2.2 %fusion.4 = f32[1,1,256,512]{3,2,1,0:T(8,128)} fusion(bf16[256,512]{1,0:T(8,128)(2,1)S(1)} %collective-permute-done.5, f32[256]{0:T(256)S(1)} %get-tuple-element.43, pred[]{:T(512)S(6)} %ge.71, f32[256,512]{1,0:T(8,128)S(1)} %get-tuple-element.11, bf16[257,512]{1,0:T(8,128)(2,1)S(1)} %collective-permute-done.3, f32[256]{0:T(256)S(1)} %get-tuple-element.14, ...), kind=kLoop, calls=%fused_computation.35 | loop fusion | flops 1572864 | bytes 1838083 | tf_op jit(solution)/shard_map/broadcast_in_dim | solution.py:284
  74.6 6.1 %collective-permute-done.7 = bf16[1,64,2048]{2,1,0:T(8,128)(2,1)S(1)} collective-permute-done((bf16[1,64,2048]{2,1,0:T(8,128)(2,1)S(1)}, bf16[1,64,2048]{2,1,0:T(8,128)(2,1)S(1)}, u32[]{:S(2)}, u32[]{:S(2)}) %collective-permute-start.7) | collective-permute-done | bytes 262176 | tf_op jit(solution)/shard_map/ppermute | solution.py:204
  80.7 0.8 fusion.6
  (79 shorter events, 2.4 us)
Async XLA Ops:
  0.6 66.6 %copy-start = (bf16[512,2048]{1,0:T(8,128)(2,1)S(1)}, bf16[512,2048]{1,0:T(8,128)(2,1)}, u32[]{:S(2)}) copy-start(bf16[512,2048]{1,0:T(8,128)(2,1)} %param.27) | copy-start | bytes 6291460
  0.6 11.4 %copy-start.1 = (bf16[64,2048]{1,0:T(8,128)(2,1)S(1)}, bf16[64,2048]{1,0:T(8,128)(2,1)}, u32[]{:S(2)}) copy-start(bf16[64,2048]{1,0:T(8,128)(2,1)} %param.14) | copy-start | bytes 786436
  0.7 8.3 %collective-permute-start = (bf16[64,2048]{1,0:T(8,128)(2,1)}, bf16[64,2048]{1,0:T(8,128)(2,1)S(1)}, u32[]{:S(2)}, u32[]{:S(2)}) collective-permute-start(bf16[64,2048]{1,0:T(8,128)(2,1)} %param.14), channel_id=1, source_target_pairs={{0,2},{1,3},{2,0},{3,1},{4,6},{5,7},{6,4},{7,5},{8,10},{9,11},{10,... | collective-permute-start | bytes 786440 | tf_op jit(solution)/shard_map/ppermute | solution.py:150
  7.4 5.4 %copy-start.17 = (bf16[2048,16]{0,1:T(8,128)(2,1)S(1)}, bf16[2048,16]{0,1:T(8,128)(2,1)}, u32[]{:S(2)}) copy-start(bf16[2048,16]{0,1:T(8,128)(2,1)} %param.22) | copy-start | bytes 196612
  7.4 5.4 %copy-start.18 = (bf16[16,256]{1,0:T(8,128)(2,1)S(1)}, bf16[16,256]{1,0:T(8,128)(2,1)}, u32[]{:S(2)}) copy-start(bf16[16,256]{1,0:T(8,128)(2,1)} %param.23) | copy-start | bytes 24580
  7.4 5.4 %copy-start.20 = (f32[256]{0:T(256)S(1)}, f32[256]{0:T(256)}, u32[]{:S(2)}) copy-start(f32[256]{0:T(256)} %param.24) | copy-start | bytes 3076
  10.0 2.0 %collective-permute-start.1 = (bf16[128,2048]{1,0:T(8,128)(2,1)S(1)}, bf16[128,2048]{1,0:T(8,128)(2,1)S(1)}, u32[]{:S(2)}, u32[]{:S(2)}) collective-permute-start(bf16[128,2048]{1,0:T(8,128)(2,1)S(1)} %pad_maximum_fusion.1), channel_id=1, source_target_pairs={{0,1},{1,0},{2,3},{3,2},{4,5},{5,4},{6,7},{7,6},{8,9},{9,8},{10,11... | collective-permute-start | bytes 1572872 | tf_op jit(solution)/shard_map/ppermute | solution.py:150
  12.0 5.9 %copy-start.3 = (bf16[64,2048]{1,0:T(8,128)(2,1)}, bf16[64,2048]{1,0:T(8,128)(2,1)S(1)}, u32[]{:S(2)}) copy-start(bf16[64,2048]{1,0:T(8,128)(2,1)S(1)} %select_select_fusion.1) | copy-start | bytes 786436
  12.8 5.1 %copy-start.5 = (bf16[64,2048]{1,0:T(8,128)(2,1)}, bf16[64,2048]{1,0:T(8,128)(2,1)S(1)}, u32[]{:S(2)}) copy-start(bf16[64,2048]{1,0:T(8,128)(2,1)S(1)} %get-tuple-element.19) | copy-start | bytes 786436
  12.8 5.1 %copy-start.7 = (bf16[64,2048]{1,0:T(8,128)(2,1)}, bf16[64,2048]{1,0:T(8,128)(2,1)S(1)}, u32[]{:S(2)}) copy-start(bf16[64,2048]{1,0:T(8,128)(2,1)S(1)} %get-tuple-element.20) | copy-start | bytes 786436
  15.1 1.9 %copy-start.9 = (bf16[64,2048]{1,0:T(8,128)(2,1)S(1)}, bf16[64,2048]{1,0:T(8,128)(2,1)}, u32[]{:S(2)}) copy-start(bf16[64,2048]{1,0:T(8,128)(2,1)} %get-tuple-element.21) | copy-start | bytes 786436
  15.1 2.1 %copy-start.14 = (bf16[2048,512]{1,0:T(8,128)(2,1)S(1)}, bf16[2048,512]{1,0:T(8,128)(2,1)}, u32[]{:S(2)}) copy-start(bf16[2048,512]{1,0:T(8,128)(2,1)} %param.18) | copy-start | bytes 6291460
  17.1 1.2 %copy-start.16 = (bf16[2048,256]{1,0:T(8,128)(2,1)S(1)}, bf16[2048,256]{1,0:T(8,128)(2,1)}, u32[]{:S(2)}) copy-start(bf16[2048,256]{1,0:T(8,128)(2,1)} %param.17) | copy-start | bytes 3145732
  19.5 6.4 %collective-permute-start.2 = (bf16[3,1024]{1,0:T(4,128)(2,1)S(1)}, bf16[3,1024]{1,0:T(4,128)(2,1)S(1)}, u32[]{:S(2)}, u32[]{:S(2)}) collective-permute-start(bf16[3,1024]{1,0:T(4,128)(2,1)S(1)} %get-tuple-element.6), channel_id=1, source_target_pairs={{0,4},{4,8},{8,12},{12,16},{16,20},{20,24},{24,28},{1,5},{5,9},{9,... | collective-permute-start | bytes 18440 | tf_op jit(solution)/shard_map/ppermute | solution.py:17
  26.6 1.8 %copy-start.11 = (f32[256,256]{1,0:T(8,128)}, f32[256,256]{1,0:T(8,128)S(1)}, u32[]{:S(2)}) copy-start(f32[256,256]{1,0:T(8,128)S(1)} %get-tuple-element.4) | copy-start | bytes 786436
  27.8 0.9 %copy-start.2 = (f32[256,512]{1,0:T(8,128)}, f32[256,512]{1,0:T(8,128)S(1)}, u32[]{:S(2)}) copy-start(f32[256,512]{1,0:T(8,128)S(1)} %multiply_reduce_fusion) | copy-start | bytes 1572868
  29.1 10.2 %collective-permute-start.3 = (bf16[257,512]{1,0:T(8,128)(2,1)S(1)}, bf16[257,512]{1,0:T(8,128)(2,1)S(1)}, u32[]{:S(2)}, u32[]{:S(2)}) collective-permute-start(bf16[257,512]{1,0:T(8,128)(2,1)S(1)} %pad_maximum_fusion.2), channel_id=1, source_target_pairs={{0,4},{4,8},{8,12},{12,16},{16,20},{20,24},{24,28},{1,5},{5,9},{9,... | collective-permute-start | bytes 789512 | tf_op jit(solution)/shard_map/ppermute | solution.py:17
  39.3 0.6 copy-start.13
  40.7 8.7 %collective-permute-start.4 = (bf16[257,512]{1,0:T(8,128)(2,1)}, bf16[257,512]{1,0:T(8,128)(2,1)}, u32[]{:S(2)}, u32[]{:S(2)}) collective-permute-start(bf16[257,512]{1,0:T(8,128)(2,1)} %pad_maximum_fusion.3), channel_id=1, source_target_pairs={{0,8},{4,12},{8,16},{12,20},{16,24},{20,28},{1,9},{5,13},{9,17},{1... | collective-permute-start | bytes 789512 | tf_op jit(solution)/shard_map/ppermute | solution.py:17
  44.6 21.7 %copy-start.4 = (bf16[64,2048]{1,0:T(8,128)(2,1)S(1)}, bf16[64,2048]{1,0:T(8,128)(2,1)}, u32[]{:S(2)}) copy-start(bf16[64,2048]{1,0:T(8,128)(2,1)} %copy-done.3) | copy-start | bytes 786436
  44.6 21.8 %copy-start.6 = (bf16[64,2048]{1,0:T(8,128)(2,1)S(1)}, bf16[64,2048]{1,0:T(8,128)(2,1)}, u32[]{:S(2)}) copy-start(bf16[64,2048]{1,0:T(8,128)(2,1)} %copy-done.5) | copy-start | bytes 786436
  44.6 21.8 %copy-start.8 = (bf16[64,2048]{1,0:T(8,128)(2,1)S(1)}, bf16[64,2048]{1,0:T(8,128)(2,1)}, u32[]{:S(2)}) copy-start(bf16[64,2048]{1,0:T(8,128)(2,1)} %copy-done.7) | copy-start | bytes 786436
  44.6 21.8 %copy-start.10 = (bf16[64,2048]{1,0:T(8,128)(2,1)S(1)}, bf16[64,2048]{1,0:T(8,128)(2,1)}, u32[]{:S(2)}) copy-start(bf16[64,2048]{1,0:T(8,128)(2,1)} %get-tuple-element.21) | copy-start | bytes 786436
  44.6 21.8 %copy-start.15 = (bf16[2048,512]{1,0:T(8,128)(2,1)S(1)}, bf16[2048,512]{1,0:T(8,128)(2,1)}, u32[]{:S(2)}) copy-start(bf16[2048,512]{1,0:T(8,128)(2,1)} %param.25) | copy-start | bytes 6291460
  44.6 21.8 %copy-start.19 = (f32[512]{0:T(512)S(1)}, f32[512]{0:T(512)}, u32[]{:S(2)}) copy-start(f32[512]{0:T(512)} %param.26) | copy-start | bytes 6148
  50.6 13.8 %collective-permute-start.5 = (bf16[256,512]{1,0:T(8,128)(2,1)S(1)}, bf16[256,512]{1,0:T(8,128)(2,1)S(1)}, u32[]{:S(2)}, u32[]{:S(2)}) collective-permute-start(bf16[256,512]{1,0:T(8,128)(2,1)S(1)} %fusion.77), channel_id=1, source_target_pairs={{0,16},{4,20},{8,24},{12,28},{1,17},{5,21},{9,25},{13,29},{2,18},{... | collective-permute-start | bytes 786440 | tf_op jit(solution)/shard_map/ppermute | solution.py:17
  68.5 2.3 %collective-permute-start.6 = (bf16[128,2048]{1,0:T(8,128)(2,1)}, bf16[128,2048]{1,0:T(8,128)(2,1)}, u32[]{:S(2)}, u32[]{:S(2)}) collective-permute-start(bf16[128,2048]{1,0:T(8,128)(2,1)} %convolution_convert_fusion), channel_id=1, source_target_pairs={{0,1},{1,0},{2,3},{3,2},{4,5},{5,4},{6,7},{7,6},{8,9},{9,8},{10,11... | collective-permute-start | bytes 1572872 | tf_op jit(solution)/shard_map/ppermute | solution.py:193
  70.7 1.6 %copy-start.12 = (f32[256]{0:T(256)S(1)}, f32[256]{0:T(256)}, u32[]{:S(2)}) copy-start(f32[256]{0:T(256)} %get-tuple-element.9) | copy-start | bytes 3076
  72.3 8.4 %collective-permute-start.7 = (bf16[1,64,2048]{2,1,0:T(8,128)(2,1)S(1)}, bf16[1,64,2048]{2,1,0:T(8,128)(2,1)S(1)}, u32[]{:S(2)}, u32[]{:S(2)}) collective-permute-start(bf16[1,64,2048]{2,1,0:T(8,128)(2,1)S(1)} %fusion.24), channel_id=1, source_target_pairs={{0,2},{1,3},{2,0},{3,1},{4,6},{5,7},{6,4},{7,5},{8,10},{9,11},{10,... | collective-permute-start | bytes 786440 | tf_op jit(solution)/shard_map/ppermute | solution.py:204

commit v20 on v18

--- a/solution.py
+++ b/solution.py
@@ -117,12 +117,12 @@
         else:
             earlier_decay = None
             earlier_memory = shifted(memory.astype(jnp.bfloat16), axis, steps).astype(jnp.float32)
-        memory = jnp.where(valid, decay[:, None] * earlier_memory + memory, memory)
+        memory = decay[:, None] * earlier_memory + memory
         if steps == 1:
             entering = earlier_memory
             entering_decay = earlier_decay
         else:
-            entering = jnp.where(valid, entering_decay[:, None] * earlier_memory + entering, entering)
+            entering = entering_decay[:, None] * earlier_memory + entering
         if earlier_decay is not None:
             decay = jnp.where(valid, earlier_decay * decay, decay)
             if steps > 1:

time: 80 us -> 84.7 us (1.059)
  matrix products: 13.7 us -> 17.1 us
  local copies, waits for them, and re-layouts: 2.93 us -> 4.32 us
  other arithmetic: 16.6 us -> 15.7 us
    dot_general x1, matrix products: 0.79 us -> 2.34 us  [shards(): jnp.dot(low_rank, decay_up, preferred_element_type=jnp.float32) + decay_bias]
    unnamed x39, local copies, waits for them, and re-layouts: 0.6 us -> 2.04 us
    dot_general x1, matrix products: 0.44 us -> 1.56 us  [scatter_sum(): jnp.dot(kept, weight, preferred_element_type=jnp.float32)]
    dot_general x1, matrix products: 0.27 us -> 1.36 us  [segment_parts(): jnp.einsum('ac,bck->bak', lower, decays, precision=lax.Precision.HIGHEST)]
  transfers between devices with their start and end apart: 8 -> 8, of which waited for: 8 -> 8; matrix products, arithmetic and copies ran while one was open for 18% -> 17% of each run, Pallas kernels for 0% -> 0%
where the time goes in v20:
time: 84.7 us; the launch traced here: 84 us
  waiting for transfers between devices  33.8 us (40%)
  matrix products  17.1 us (20%)
  other arithmetic  15.7 us (19%)
  starting transfers between devices  11.9 us (14%)
  local copies, waits for them, and re-layouts  4.32 us (5%)
  between operations  1.12 us (1%)
    ppermute x4, waiting for transfers between devices, shifted(): lax.ppermute(value, axis, [(source, source + steps) for source in range(i...  24.4 us
    ppermute x4, starting transfers between devices, shifted(): lax.ppermute(value, axis, [(source, source + steps) for source in range(i...  8.6 us
    ppermute x1, waiting for transfers between devices, scatter_sum(): lax.ppermute(outgoing, axis, [(source, source ^ mask) for source in range...  4.85 us
    dot_general x4, matrix products, project(): jnp.dot(gathered, weight, preferred_element_type=jnp.float32)  3.71 us
    ppermute x2, waiting for transfers between devices, gather_rows(): lax.ppermute(jnp.concatenate(received), axis, [(source, source ^ mask) fo...  2.69 us
    dot_general x1, matrix products, segment_parts(): jnp.einsum('bac,bcv->bav', scores, head_values, preferred_element_type=jn...  2.62 us
    dot_general x3, matrix products, segment_parts(): jnp.dot(lifted_intact[block], memory, precision=HIGH_PRECISION)  2.48 us
    dot_general x1, matrix products, shards(): jnp.dot(low_rank, decay_up, preferred_element_type=jnp.float32) + decay_bias  2.34 us
  transfers between devices with their start and end apart: 8, of which 8 were waited for; matrix products, arithmetic and copies ran while one was open for 17% of the time, Pallas kernels for 0%

profile of v20, /device:TPU:24, one launch (start us, length us, event | category | flops | bytes accessed | tf_op | source)
XLA Modules:
  0.0 84.0 jit_solution(9008319681694128504)
XLA Ops:
  0.7 1.6 %collective-permute-start = (bf16[64,2048]{1,0:T(8,128)(2,1)}, bf16[64,2048]{1,0:T(8,128)(2,1)S(1)}, u32[]{:S(2)}, u32[]{:S(2)}) collective-permute-start(bf16[64,2048]{1,0:T(8,128)(2,1)} %param.18), channel_id=1, source_target_pairs={{0,2},{1,3},{2,0},{3,1},{4,6},{5,7},{6,4},{7,5},{8,10},{9,11},{10,... | collective-permute-start | bytes 786440 | tf_op jit(solution)/shard_map/ppermute | solution.py:150
  2.3 0.8 select_reduce_fusion.1
  3.5 0.6 slice.188
  4.0 0.7 convert_element_type.162
  4.7 0.7 convert_element_type.172
  5.4 0.7 convert_element_type.178
  6.1 0.5 pad.32.clone
  6.8 0.6 iota_compare_fusion
  7.4 1.6 %collective-permute-done = bf16[64,2048]{1,0:T(8,128)(2,1)S(1)} collective-permute-done((bf16[64,2048]{1,0:T(8,128)(2,1)}, bf16[64,2048]{1,0:T(8,128)(2,1)S(1)}, u32[]{:S(2)}, u32[]{:S(2)}) %collective-permute-start) | collective-permute-done | bytes 262176 | tf_op jit(solution)/shard_map/ppermute | solution.py:150
  9.0 1.0 %pad_maximum_fusion.4 = bf16[128,2048]{1,0:T(8,128)(2,1)S(1)} fusion(bf16[64,2048]{1,0:T(8,128)(2,1)S(1)} %collective-permute-done, bf16[64,2048]{1,0:T(8,128)(2,1)} %param.18), kind=kLoop, calls=%fused_computation.41 | loop fusion | flops 1048576 | bytes 1048576 | tf_op jit(solution)/shard_map/concatenate | solution.py:151
  10.1 0.7 slice_compare_fusion
  10.9 1.1 %collective-permute-done.1 = bf16[128,2048]{1,0:T(8,128)(2,1)S(1)} collective-permute-done((bf16[128,2048]{1,0:T(8,128)(2,1)S(1)}, bf16[128,2048]{1,0:T(8,128)(2,1)S(1)}, u32[]{:S(2)}, u32[]{:S(2)}) %collective-permute-start.1) | collective-permute-done | bytes 524320 | tf_op jit(solution)/shard_map/ppermute | solution.py:150
  12.0 1.8 %conditional.1 = (bf16[256,2048]{1,0:T(8,128)(2,1)S(1)}) conditional(s32[]{:T(128)} %clamp.3, (bf16[64,2048]{1,0:T(8,128)(2,1)S(1)}, bf16[64,2048]{1,0:T(8,128)(2,1)S(1)}, bf16[64,2048]{1,0:T(8,128)(2,1)S(1)}, bf16[64,2048]{1,0:T(8,128)(2,1)S(1)}) %tuple.60, (bf16[64,2048]{1,0:T(8,128)(2,1)S(1)}, ...), branch_computations={%region_2.0_spmd, %region_3.0_spmd, %region_4.5_spmd, %region_5.6_... | conditional | flops 4194304 | bytes 3145764 | solution.py:164
  12.1 0.7 copy-done.4
  12.7 1.0 %pad_maximum_fusion = bf16[256,2048]{1,0:T(8,128)(2,1)S(1)} fusion(bf16[64,2048]{1,0:T(8,128)(2,1)S(1)} %get-tuple-element.40, bf16[64,2048]{1,0:T(8,128)(2,1)} %copy-done.4, bf16[64,2048]{1,0:T(8,128)(2,1)S(1)} %get-tuple-element.33, bf16[64,2048]{1,0:T(8,128)(2,1)S(1)} %get-tuple-element.32), kind=kLoop, calls=%fused_computation | loop fusion | flops 4194304 | bytes 2097152 | tf_op jit(solution)/shard_map/cond/branch_0_fun/concatenate | solution.py:162
  13.8 2.3 %fusion.31 = f32[256,256]{1,0:T(8,128)} fusion(bf16[16,256]{1,0:T(8,128)(2,1)S(1)} %copy-done.20, bf16[256,2048]{1,0:T(8,128)(2,1)S(1)} %get-tuple-element.103, bf16[2048,16]{0,1:T(8,128)(2,1)} %param.26, f32[256]{0:T(256)S(1)} %copy-done.22), kind=kOutput, calls=%fused_computation.78 | convolution fusion | flops 19533824 | bytes 1385472 | tf_op jit(solution)/shard_map/dot_general | solution.py:257
  16.2 1.4 %convolution_bitcast_fusion = f32[4,64,256]{2,1,0:T(8,128)S(1)} fusion(f32[4,64,256]{2,1,0:T(8,128)} %bitcast.131), kind=kOutput, calls=%fused_computation.13 | convolution fusion | flops 50335744 | bytes 524288 | tf_op jit(solution)/shard_map/ac,bck->bak/dot_general | solution.py:51
  17.6 1.8 %convolution_convert_fusion.5 = bf16[256,256]{1,0:T(8,128)(2,1)S(1)} fusion(bf16[256,2048]{1,0:T(8,128)(2,1)S(1)} %get-tuple-element.103, bf16[2048,256]{1,0:T(8,128)(2,1)} %param.20), kind=kOutput, calls=%fused_computation.17 | convolution fusion | flops 268500992 | bytes 2228224 | tf_op jit(solution)/shard_map/dot_general | solution.py:227
  19.3 0.7 convolution_convert_fusion.3
  20.0 0.5 copy-done.12
  21.0 0.7 select_bitcast_fusion
  21.7 3.4 %collective-permute-start.2 = (bf16[3,1024]{1,0:T(4,128)(2,1)S(1)}, bf16[3,1024]{1,0:T(4,128)(2,1)S(1)}, u32[]{:S(2)}, u32[]{:S(2)}) collective-permute-start(bf16[3,1024]{1,0:T(4,128)(2,1)S(1)} %get-tuple-element.59), channel_id=1, source_target_pairs={{0,4},{4,8},{8,12},{12,16},{16,20},{20,24},{24,28},{1,5},{5,9},{9,... | collective-permute-start | bytes 18440 | tf_op jit(solution)/shard_map/ppermute | solution.py:17
  25.3 2.8 %collective-permute-done.2 = bf16[3,1024]{1,0:T(4,128)(2,1)S(1)} collective-permute-done((bf16[3,1024]{1,0:T(4,128)(2,1)S(1)}, bf16[3,1024]{1,0:T(4,128)(2,1)S(1)}, u32[]{:S(2)}, u32[]{:S(2)}) %collective-permute-start.2) | collective-permute-done | bytes 6176 | tf_op jit(solution)/shard_map/ppermute | solution.py:17
  28.8 0.9 %broadcast_multiply_fusion = (f32[4,64,256]{2,1,0:T(8,128)}, f32[4,64,256]{2,1,0:T(8,128)S(1)}) fusion(f32[4,256]{1,0:T(4,128)S(1)} %pad_maximum_fusion.12, f32[4,64]{1,0:T(4,128)S(1)} %get-tuple-element.93, f32[4,64,256]{2,1,0:T(8,128)S(1)} %convolution_bitcast_fusion, f32[4,64,256]{2,1,0:T(8,128)S(1)} %bitcast.126), kind=kLoop, calls=%fused_computation.115 | loop fusion | flops 589824 | bytes 1053696 | tf_op jit(solution)/shard_map/mul | solution.py:85
  30.0 0.6 fusion.51
  31.3 2.6 %collective-permute-start.3 = (bf16[257,512]{1,0:T(8,128)(2,1)S(1)}, bf16[257,512]{1,0:T(8,128)(2,1)S(1)}, u32[]{:S(2)}, u32[]{:S(2)}) collective-permute-start(bf16[257,512]{1,0:T(8,128)(2,1)S(1)} %pad_maximum_fusion.5), channel_id=1, source_target_pairs={{0,4},{4,8},{8,12},{12,16},{16,20},{20,24},{24,28},{1,5},{5,9},{9,... | collective-permute-start | bytes 789512 | tf_op jit(solution)/shard_map/ppermute | solution.py:17
  34.0 1.0 %convolution_bitcast_fusion.3 = f32[1,64,512]{2,1,0:T(8,128)} fusion(f32[4,256,512]{2,1,0:T(8,128)S(1)} %fusion.51, f32[256]{0:T(256)S(1)} %get-tuple-element.97, f32[4,64,256]{2,1,0:T(8,128)S(1)} %get-tuple-element.69), kind=kOutput, calls=%fused_computation.20 | convolution fusion | flops 50462720 | bytes 721920 | tf_op jit(solution)/shard_map/dot_general | solution.py:80
  35.0 1.1 %convolution_bitcast_fusion.1 = f32[1,64,512]{2,1,0:T(8,128)} fusion(f32[4,256,512]{2,1,0:T(8,128)S(1)} %fusion.51, f32[256]{0:T(256)S(1)} %bitcast.143, f32[4,64,256]{2,1,0:T(8,128)S(1)} %get-tuple-element.69, f32[256]{0:T(256)S(1)} %bitcast.137, f32[256]{0:T(256)S(1)} %get-tuple-element.97), kind=kOutput, calls=%fused_computation.18 | convolution fusion | flops 50987008 | bytes 1772544 | tf_op jit(solution)/shard_map/dot_general | solution.py:80
  36.0 5.6 %collective-permute-done.3 = bf16[257,512]{1,0:T(8,128)(2,1)S(1)} collective-permute-done((bf16[257,512]{1,0:T(8,128)(2,1)S(1)}, bf16[257,512]{1,0:T(8,128)(2,1)S(1)}, u32[]{:S(2)}, u32[]{:S(2)}) %collective-permute-start.3) | collective-permute-done | bytes 263200 | tf_op jit(solution)/shard_map/ppermute | solution.py:17
  41.7 0.7 copy-done.8
  42.5 0.7 pad_maximum_fusion.6
  43.2 1.3 %collective-permute-start.4 = (bf16[257,512]{1,0:T(8,128)(2,1)}, bf16[257,512]{1,0:T(8,128)(2,1)}, u32[]{:S(2)}, u32[]{:S(2)}) collective-permute-start(bf16[257,512]{1,0:T(8,128)(2,1)} %pad_maximum_fusion.6), channel_id=1, source_target_pairs={{0,8},{4,12},{8,16},{12,20},{16,24},{20,28},{1,9},{5,13},{9,17},{1... | collective-permute-start | bytes 789512 | tf_op jit(solution)/shard_map/ppermute | solution.py:17
  44.5 2.6 %convolution_add_fusion = f32[4,64,512]{2,1,0:T(8,128)} fusion(f32[1,64,512]{2,1,0:T(8,128)} %convolution_bitcast_fusion.1, f32[1,64,512]{2,1,0:T(8,128)S(1)} %convolution_bitcast_fusion.2, f32[1,64,512]{2,1,0:T(8,128)} %convolution_bitcast_fusion.3, f32[4]{0:T(128)} %pad.32.clone, f32[4,64,256]{2,1,0:T(8,128)S(1)} %copy-done.11, s32[4,64]{1,0:T(4,128)S(1)} %eq.38, ...), kind=kOutput, calls=%fused_computation.8 | convolution fusion | flops 27525120 | bytes 2233360 | tf_op jit(solution)/shard_map/bac,bcv->bav/dot_general | solution.py:71
  47.1 4.8 %collective-permute-done.4 = bf16[257,512]{1,0:T(8,128)(2,1)} collective-permute-done((bf16[257,512]{1,0:T(8,128)(2,1)}, bf16[257,512]{1,0:T(8,128)(2,1)}, u32[]{:S(2)}, u32[]{:S(2)}) %collective-permute-start.4) | collective-permute-done | bytes 263200 | tf_op jit(solution)/shard_map/ppermute | solution.py:17
  51.9 1.4 %fusion.21 = bf16[256,512]{1,0:T(8,128)(2,1)S(1)} fusion(f32[256]{0:T(256)S(1)} %get-tuple-element.62, bf16[257,512]{1,0:T(8,128)(2,1)} %collective-permute-done.4, f32[256,512]{1,0:T(8,128)} %copy-done.1, bf16[257,512]{1,0:T(8,128)(2,1)} %copy-done.8, f32[256]{0:T(256)S(1)} %get-tuple-element.67), kind=kLoop, calls=%fused_computation.64 | loop fusion | flops 917504 | bytes 1312768 | tf_op jit(solution)/shard_map/convert_element_type | solution.py:119
  53.3 1.3 %collective-permute-start.5 = (bf16[256,512]{1,0:T(8,128)(2,1)S(1)}, bf16[256,512]{1,0:T(8,128)(2,1)S(1)}, u32[]{:S(2)}, u32[]{:S(2)}) collective-permute-start(bf16[256,512]{1,0:T(8,128)(2,1)S(1)} %fusion.21), channel_id=1, source_target_pairs={{0,16},{4,20},{8,24},{12,28},{1,17},{5,21},{9,25},{13,29},{2,18},{... | collective-permute-start | bytes 786440 | tf_op jit(solution)/shard_map/ppermute | solution.py:17
  54.6 0.7 slice_convert_fusion
  55.3 0.6 multiply_select_fusion
  55.9 11.2 %collective-permute-done.5 = bf16[256,512]{1,0:T(8,128)(2,1)S(1)} collective-permute-done((bf16[256,512]{1,0:T(8,128)(2,1)S(1)}, bf16[256,512]{1,0:T(8,128)(2,1)S(1)}, u32[]{:S(2)}, u32[]{:S(2)}) %collective-permute-start.5) | collective-permute-done | bytes 262176 | tf_op jit(solution)/shard_map/ppermute | solution.py:17
  67.1 1.9 %multiply_reduce_fusion.3 = (f32[256]{0:T(256)S(1)}, f32[256,512]{1,0:T(8,128)S(1)}) fusion(f32[256,512]{1,0:T(8,128)} %bitcast.130, f32[256,256]{1,0:T(8,128)} %bitcast.125, bf16[256,512]{1,0:T(8,128)(2,1)S(1)} %collective-permute-done.5, f32[256]{0:T(256)S(1)} %bitcast.140, f32[256]{0:T(256)S(1)} %get-tuple-element.96, bf16[257,512]{1,0:T(8,128)(2,1)} %copy-done.8, ...), kind=kOutput, calls=%fused_computation.55 | convolution fusion | flops 202637056 | bytes 2100224 | tf_op jit(solution)/shard_map/dot_general | solution.py:270
  69.1 0.8 multiply_convert_fusion
  70.5 1.9 %collective-permute-done.6 = bf16[128,2048]{1,0:T(8,128)(2,1)S(1)} collective-permute-done((bf16[128,2048]{1,0:T(8,128)(2,1)S(1)}, bf16[128,2048]{1,0:T(8,128)(2,1)S(1)}, u32[]{:S(2)}, u32[]{:S(2)}) %collective-permute-start.6) | collective-permute-done | bytes 524320 | tf_op jit(solution)/shard_map/ppermute | solution.py:188
  72.4 0.8 copy-done.15
  73.2 1.6 %convert_add_fusion = f32[128,2048]{1,0:T(8,128)S(1)} fusion(bf16[128,2048]{1,0:T(8,128)(2,1)} %copy-done.15, bf16[512,2048]{1,0:T(8,128)(2,1)S(1)} %copy-done, bf16[64,512]{1,0:T(8,128)(2,1)S(1)} %get-tuple-element.78, bf16[64,512]{1,0:T(8,128)(2,1)S(1)} %get-tuple-element.77), kind=kOutput, calls=%fused_computation.24 | convolution fusion | flops 269746176 | bytes 3801088 | tf_op jit(solution)/shard_map/dot_general | solution.py:190
  74.8 1.6 %collective-permute-start.7 = (bf16[1,64,2048]{2,1,0:T(8,128)(2,1)S(1)}, bf16[1,64,2048]{2,1,0:T(8,128)(2,1)S(1)}, u32[]{:S(2)}, u32[]{:S(2)}) collective-permute-start(bf16[1,64,2048]{2,1,0:T(8,128)(2,1)S(1)} %fusion.29), channel_id=1, source_target_pairs={{0,2},{1,3},{2,0},{3,1},{4,6},{5,7},{6,4},{7,5},{8,10},{9,11},{10,... | collective-permute-start | bytes 786440 | tf_op jit(solution)/shard_map/ppermute | solution.py:199
  76.4 2.0 %fusion.9 = f32[1,1,256,512]{3,2,1,0:T(8,128)} fusion(bf16[256,512]{1,0:T(8,128)(2,1)S(1)} %collective-permute-done.5, f32[256]{0:T(256)S(1)} %copy-done.17, f32[256]{0:T(256)S(1)} %get-tuple-element.62, bf16[257,512]{1,0:T(8,128)(2,1)} %collective-permute-done.4, f32[256,512]{1,0:T(8,128)S(1)} %copy-done.2, bf16[257,512]{1,0:T(8,128)(2,1)S(1)} %copy-done.9, ...), kind=kLoop, calls=%fused_computation.38 | loop fusion | flops 1179648 | bytes 1838080 | tf_op jit(solution)/shard_map/broadcast_in_dim | solution.py:279
  78.4 4.9 %collective-permute-done.7 = bf16[1,64,2048]{2,1,0:T(8,128)(2,1)S(1)} collective-permute-done((bf16[1,64,2048]{2,1,0:T(8,128)(2,1)S(1)}, bf16[1,64,2048]{2,1,0:T(8,128)(2,1)S(1)}, u32[]{:S(2)}, u32[]{:S(2)}) %collective-permute-start.7) | collective-permute-done | bytes 262176 | tf_op jit(solution)/shard_map/ppermute | solution.py:199
  83.2 0.8 fusion.11
  (78 shorter events, 3.9 us)
Async XLA Ops:
  0.6 69.3 %copy-start = (bf16[512,2048]{1,0:T(8,128)(2,1)S(1)}, bf16[512,2048]{1,0:T(8,128)(2,1)}, u32[]{:S(2)}) copy-start(bf16[512,2048]{1,0:T(8,128)(2,1)} %param.31) | copy-start | bytes 6291460
  0.6 11.3 %copy-start.3 = (bf16[64,2048]{1,0:T(8,128)(2,1)S(1)}, bf16[64,2048]{1,0:T(8,128)(2,1)}, u32[]{:S(2)}) copy-start(bf16[64,2048]{1,0:T(8,128)(2,1)} %param.18) | copy-start | bytes 786436
  0.7 8.3 %collective-permute-start = (bf16[64,2048]{1,0:T(8,128)(2,1)}, bf16[64,2048]{1,0:T(8,128)(2,1)S(1)}, u32[]{:S(2)}, u32[]{:S(2)}) collective-permute-start(bf16[64,2048]{1,0:T(8,128)(2,1)} %param.18), channel_id=1, source_target_pairs={{0,2},{1,3},{2,0},{3,1},{4,6},{5,7},{6,4},{7,5},{8,10},{9,11},{10,... | collective-permute-start | bytes 786440 | tf_op jit(solution)/shard_map/ppermute | solution.py:150
  10.0 2.0 %collective-permute-start.1 = (bf16[128,2048]{1,0:T(8,128)(2,1)S(1)}, bf16[128,2048]{1,0:T(8,128)(2,1)S(1)}, u32[]{:S(2)}, u32[]{:S(2)}) collective-permute-start(bf16[128,2048]{1,0:T(8,128)(2,1)S(1)} %pad_maximum_fusion.4), channel_id=1, source_target_pairs={{0,1},{1,0},{2,3},{3,2},{4,5},{5,4},{6,7},{7,6},{8,9},{9,8},{10,11... | collective-permute-start | bytes 1572872 | tf_op jit(solution)/shard_map/ppermute | solution.py:150
  12.0 1.8 %copy-start.20 = (bf16[16,256]{1,0:T(8,128)(2,1)S(1)}, bf16[16,256]{1,0:T(8,128)(2,1)}, u32[]{:S(2)}) copy-start(bf16[16,256]{1,0:T(8,128)(2,1)} %param.27) | copy-start | bytes 24580
  12.0 1.8 %copy-start.22 = (f32[256]{0:T(256)S(1)}, f32[256]{0:T(256)}, u32[]{:S(2)}) copy-start(f32[256]{0:T(256)} %param.28) | copy-start | bytes 3076
  12.0 0.7 copy-start.4
  16.2 3.2 %copy-start.18 = (bf16[2048,512]{1,0:T(8,128)(2,1)S(1)}, bf16[2048,512]{1,0:T(8,128)(2,1)}, u32[]{:S(2)}) copy-start(bf16[2048,512]{1,0:T(8,128)(2,1)} %param.22) | copy-start | bytes 6291460
  17.5 12.5 %copy-start.10 = (f32[4,64,256]{2,1,0:T(8,128)}, f32[4,64,256]{2,1,0:T(8,128)S(1)}, u32[]{:S(2)}) copy-start(f32[4,64,256]{2,1,0:T(8,128)S(1)} %convolution_bitcast_fusion) | copy-start | bytes 786436
  19.3 1.2 %copy-start.12 = (bf16[2048,256]{1,0:T(8,128)(2,1)S(1)}, bf16[2048,256]{1,0:T(8,128)(2,1)}, u32[]{:S(2)}) copy-start(bf16[2048,256]{1,0:T(8,128)(2,1)} %param.21) | copy-start | bytes 3145732
  21.7 6.4 %collective-permute-start.2 = (bf16[3,1024]{1,0:T(4,128)(2,1)S(1)}, bf16[3,1024]{1,0:T(4,128)(2,1)S(1)}, u32[]{:S(2)}, u32[]{:S(2)}) collective-permute-start(bf16[3,1024]{1,0:T(4,128)(2,1)S(1)} %get-tuple-element.59), channel_id=1, source_target_pairs={{0,4},{4,8},{8,12},{12,16},{16,20},{20,24},{24,28},{1,5},{5,9},{9,... | collective-permute-start | bytes 18440 | tf_op jit(solution)/shard_map/ppermute | solution.py:17
  28.8 1.2 %copy-start.13 = (f32[256,256]{1,0:T(8,128)}, f32[256,256]{1,0:T(8,128)S(1)}, u32[]{:S(2)}) copy-start(f32[256,256]{1,0:T(8,128)S(1)} %get-tuple-element.56) | copy-start | bytes 786436
  28.8 1.8 %copy-start.16 = (f32[256,256]{1,0:T(8,128)}, f32[256,256]{1,0:T(8,128)S(1)}, u32[]{:S(2)}) copy-start(f32[256,256]{1,0:T(8,128)S(1)} %get-tuple-element.57) | copy-start | bytes 786436
  30.0 0.9 %copy-start.14 = (f32[256,512]{1,0:T(8,128)}, f32[256,512]{1,0:T(8,128)S(1)}, u32[]{:S(2)}) copy-start(f32[256,512]{1,0:T(8,128)S(1)} %multiply_reduce_fusion) | copy-start | bytes 1572868
  30.9 12.3 %copy-start.1 = (f32[256,512]{1,0:T(8,128)}, f32[256,512]{1,0:T(8,128)S(1)}, u32[]{:S(2)}) copy-start(f32[256,512]{1,0:T(8,128)S(1)} %get-tuple-element.64) | copy-start | bytes 1572868
  31.3 13.2 %copy-start.11 = (f32[4,64,256]{2,1,0:T(8,128)S(1)}, f32[4,64,256]{2,1,0:T(8,128)}, u32[]{:S(2)}) copy-start(f32[4,64,256]{2,1,0:T(8,128)} %copy-done.10) | copy-start | bytes 786436
  31.3 10.3 %collective-permute-start.3 = (bf16[257,512]{1,0:T(8,128)(2,1)S(1)}, bf16[257,512]{1,0:T(8,128)(2,1)S(1)}, u32[]{:S(2)}, u32[]{:S(2)}) collective-permute-start(bf16[257,512]{1,0:T(8,128)(2,1)S(1)} %pad_maximum_fusion.5), channel_id=1, source_target_pairs={{0,4},{4,8},{8,12},{12,16},{16,20},{20,24},{24,28},{1,5},{5,9},{9,... | collective-permute-start | bytes 789512 | tf_op jit(solution)/shard_map/ppermute | solution.py:17
  41.6 0.7 copy-start.8
  43.2 8.7 %collective-permute-start.4 = (bf16[257,512]{1,0:T(8,128)(2,1)}, bf16[257,512]{1,0:T(8,128)(2,1)}, u32[]{:S(2)}, u32[]{:S(2)}) collective-permute-start(bf16[257,512]{1,0:T(8,128)(2,1)} %pad_maximum_fusion.6), channel_id=1, source_target_pairs={{0,8},{4,12},{8,16},{12,20},{16,24},{20,28},{1,9},{5,13},{9,17},{1... | collective-permute-start | bytes 789512 | tf_op jit(solution)/shard_map/ppermute | solution.py:17
  47.1 21.9 %copy-start.19 = (bf16[2048,512]{1,0:T(8,128)(2,1)S(1)}, bf16[2048,512]{1,0:T(8,128)(2,1)}, u32[]{:S(2)}) copy-start(bf16[2048,512]{1,0:T(8,128)(2,1)} %param.29) | copy-start | bytes 6291460
  47.1 21.9 %copy-start.21 = (f32[512]{0:T(512)S(1)}, f32[512]{0:T(512)}, u32[]{:S(2)}) copy-start(f32[512]{0:T(512)} %param.30) | copy-start | bytes 6148
  53.3 13.8 %collective-permute-start.5 = (bf16[256,512]{1,0:T(8,128)(2,1)S(1)}, bf16[256,512]{1,0:T(8,128)(2,1)S(1)}, u32[]{:S(2)}, u32[]{:S(2)}) collective-permute-start(bf16[256,512]{1,0:T(8,128)(2,1)S(1)} %fusion.21), channel_id=1, source_target_pairs={{0,16},{4,20},{8,24},{12,28},{1,17},{5,21},{9,25},{13,29},{2,18},{... | collective-permute-start | bytes 786440 | tf_op jit(solution)/shard_map/ppermute | solution.py:17
  70.4 2.0 %collective-permute-start.6 = (bf16[128,2048]{1,0:T(8,128)(2,1)S(1)}, bf16[128,2048]{1,0:T(8,128)(2,1)S(1)}, u32[]{:S(2)}, u32[]{:S(2)}) collective-permute-start(bf16[128,2048]{1,0:T(8,128)(2,1)S(1)} %convolution_convert_fusion), channel_id=1, source_target_pairs={{0,1},{1,0},{2,3},{3,2},{4,5},{5,4},{6,7},{7,6},{8,9},{9,8},{10,11... | collective-permute-start | bytes 1572872 | tf_op jit(solution)/shard_map/ppermute | solution.py:188
  72.4 0.8 copy-start.15
  73.2 3.2 %copy-start.2 = (f32[256,512]{1,0:T(8,128)S(1)}, f32[256,512]{1,0:T(8,128)}, u32[]{:S(2)}) copy-start(f32[256,512]{1,0:T(8,128)} %copy-done.1) | copy-start | bytes 1572868
  73.2 3.2 %copy-start.9 = (bf16[257,512]{1,0:T(8,128)(2,1)S(1)}, bf16[257,512]{1,0:T(8,128)(2,1)}, u32[]{:S(2)}) copy-start(bf16[257,512]{1,0:T(8,128)(2,1)} %copy-done.8) | copy-start | bytes 789508
  73.2 3.2 %copy-start.17 = (f32[256]{0:T(256)S(1)}, f32[256]{0:T(256)}, u32[]{:S(2)}) copy-start(f32[256]{0:T(256)} %get-tuple-element.95) | copy-start | bytes 3076
  74.8 8.4 %collective-permute-start.7 = (bf16[1,64,2048]{2,1,0:T(8,128)(2,1)S(1)}, bf16[1,64,2048]{2,1,0:T(8,128)(2,1)S(1)}, u32[]{:S(2)}, u32[]{:S(2)}) collective-permute-start(bf16[1,64,2048]{2,1,0:T(8,128)(2,1)S(1)} %fusion.29), channel_id=1, source_target_pairs={{0,2},{1,3},{2,0},{3,1},{4,6},{5,7},{6,4},{7,5},{8,10},{9,11},{10,... | collective-permute-start | bytes 786440 | tf_op jit(solution)/shard_map/ppermute | solution.py:199

commit v21 on v18

--- a/solution.py
+++ b/solution.py
@@ -147,10 +147,8 @@
         order = [0]
         mask = count // 2
         while mask >= 1:
-            incoming = lax.ppermute(
-                jnp.concatenate(received), axis, [(source, source ^ mask) for source in range(count)]
-            )
-            received = received + list(jnp.split(incoming, len(received)))
+            pairs = [(source, source ^ mask) for source in range(count)]
+            received = received + [lax.ppermute(block, axis, pairs) for block in received]
             order = order + [flip ^ mask for flip in order]
             mask //= 2
 

time: 80 us -> 81.5 us (1.019)
  waiting for transfers between devices: 33.3 us -> 35.7 us
    ppermute x2 -> x3, waiting for transfers between devices: 2.65 us -> 4.03 us  [gather_rows(): lax.ppermute(block, axis, pairs)]
    ppermute x4, waiting for transfers between devices: 24.2 us -> 25.2 us  [shifted(): lax.ppermute(value, axis, [(source, source + steps) for source in range(i...]
    concatenate x1 -> x0, other arithmetic: 0.98 us -> none  [gather_rows(): jnp.concatenate(received)]
    ppermute x2 -> x3, starting transfers between devices: 1.66 us -> 1.66 us  [gather_rows(): lax.ppermute(block, axis, pairs)]
  transfers between devices with their start and end apart: 8 -> 9, of which waited for: 8 -> 7; matrix products, arithmetic and copies ran while one was open for 18% -> 18% of each run, Pallas kernels for 0% -> 0%
where the time goes in v21:
time: 81.5 us; the launch traced here: 80.9 us
  waiting for transfers between devices  35.7 us (44%)
  other arithmetic  15.8 us (19%)
  matrix products  13.6 us (17%)
  starting transfers between devices  11.8 us (14%)
  local copies, waits for them, and re-layouts  2.84 us (3%)
  between operations  1.1 us (1%)
    ppermute x4, waiting for transfers between devices, shifted(): lax.ppermute(value, axis, [(source, source + steps) for source in range(i...  25.2 us
    ppermute x4, starting transfers between devices, shifted(): lax.ppermute(value, axis, [(source, source + steps) for source in range(i...  8.46 us
    ppermute x1, waiting for transfers between devices, scatter_sum(): lax.ppermute(outgoing, axis, [(source, source ^ mask) for source in range...  4.56 us
    ppermute x3, waiting for transfers between devices, gather_rows(): lax.ppermute(block, axis, pairs)  4.03 us
    dot_general x4, matrix products, project(): jnp.dot(gathered, weight, preferred_element_type=jnp.float32)  3.84 us
    dot_general x1, matrix products, segment_parts(): jnp.einsum('bac,bcv->bav', scores, head_values, preferred_element_type=jn...  2.76 us
    dot_general x3, matrix products, segment_parts(): jnp.dot(lifted_intact[block], memory, precision=HIGH_PRECISION)  2.48 us
    broadcast_in_dim x1, other arithmetic, shards(): segment_states = closing[None, None]  2.23 us
  transfers between devices with their start and end apart: 9, of which 7 were waited for; matrix products, arithmetic and copies ran while one was open for 18% of the time, Pallas kernels for 0%

profile of v21, /device:TPU:24, one launch (start us, length us, event | category | flops | bytes accessed | tf_op | source)
XLA Modules:
  0.0 80.9 jit_solution(14651922570812751553)
XLA Ops:
  0.7 1.6 %collective-permute-start.1 = (bf16[64,2048]{1,0:T(8,128)(2,1)}, bf16[64,2048]{1,0:T(8,128)(2,1)S(1)}, u32[]{:S(2)}, u32[]{:S(2)}) collective-permute-start(bf16[64,2048]{1,0:T(8,128)(2,1)} %param.18), channel_id=1, source_target_pairs={{0,2},{1,3},{2,0},{3,1},{4,6},{5,7},{6,4},{7,5},{8,10},{9,11},{10,... | collective-permute-start | bytes 786440 | tf_op jit(solution)/shard_map/ppermute | solution.py:151
  2.3 0.6 iota_compare_fusion
  2.9 0.8 select_reduce_fusion.1
  4.3 0.6 slice.188
  4.9 0.7 slice_compare_fusion
  5.6 4.0 %collective-permute-done.1 = bf16[64,2048]{1,0:T(8,128)(2,1)S(1)} collective-permute-done((bf16[64,2048]{1,0:T(8,128)(2,1)}, bf16[64,2048]{1,0:T(8,128)(2,1)S(1)}, u32[]{:S(2)}, u32[]{:S(2)}) %collective-permute-start.1) | collective-permute-done | bytes 262176 | tf_op jit(solution)/shard_map/ppermute | solution.py:151
  9.6 0.7 convert_element_type.162
  10.3 0.7 convert_element_type.172
  11.0 0.7 convert_element_type.178
  11.7 0.5 pad.32.clone
  12.3 1.9 %conditional.1 = (bf16[256,2048]{1,0:T(8,128)(2,1)S(1)}) conditional(s32[]{:T(128)} %clamp.3, (bf16[64,2048]{1,0:T(8,128)(2,1)}, bf16[64,2048]{1,0:T(8,128)(2,1)S(1)}, bf16[64,2048]{1,0:T(8,128)(2,1)S(1)}, bf16[64,2048]{1,0:T(8,128)(2,1)}) %tuple.20, (bf16[64,2048]{1,0:T(8,128)(2,1)S(1)}, bf16[64,2048]{1,0:T(8,128)(2,1)}, ...), branch_computations={%region_2.0_spmd, %region_3.0_spmd, %region_4.5_spmd, %region_5.6_... | conditional | flops 4194304 | bytes 3145764 | solution.py:162
  12.3 0.7 copy-done.3
  13.0 1.2 %pad_maximum_fusion = bf16[256,2048]{1,0:T(8,128)(2,1)S(1)} fusion(bf16[64,2048]{1,0:T(8,128)(2,1)} %get-tuple-element.40, bf16[64,2048]{1,0:T(8,128)(2,1)} %copy-done.3, bf16[64,2048]{1,0:T(8,128)(2,1)S(1)} %get-tuple-element.33, bf16[64,2048]{1,0:T(8,128)(2,1)} %get-tuple-element.32), kind=kLoop, calls=%fused_computation | loop fusion | flops 4194304 | bytes 2097152 | tf_op jit(solution)/shard_map/cond/branch_0_fun/concatenate | solution.py:160
  14.3 0.8 fusion.26
  15.4 1.9 %convolution_convert_fusion.5 = bf16[256,256]{1,0:T(8,128)(2,1)S(1)} fusion(bf16[256,2048]{1,0:T(8,128)(2,1)S(1)} %get-tuple-element.101, bf16[2048,256]{1,0:T(8,128)(2,1)} %param.20), kind=kOutput, calls=%fused_computation.17 | convolution fusion | flops 268500992 | bytes 2228224 | tf_op jit(solution)/shard_map/dot_general | solution.py:225
  17.3 0.7 convolution_convert_fusion.3
  18.0 0.5 copy-done.8
  18.5 0.4 convolution_convert_fusion.4
  19.0 0.7 select_bitcast_fusion
  19.7 3.4 %collective-permute-start.3 = (bf16[3,1024]{1,0:T(4,128)(2,1)S(1)}, bf16[3,1024]{1,0:T(4,128)(2,1)S(1)}, u32[]{:S(2)}, u32[]{:S(2)}) collective-permute-start(bf16[3,1024]{1,0:T(4,128)(2,1)S(1)} %get-tuple-element.59), channel_id=1, source_target_pairs={{0,4},{4,8},{8,12},{12,16},{16,20},{20,24},{24,28},{1,5},{5,9},{9,... | collective-permute-start | bytes 18440 | tf_op jit(solution)/shard_map/ppermute | solution.py:17
  23.2 2.8 %collective-permute-done.3 = bf16[3,1024]{1,0:T(4,128)(2,1)S(1)} collective-permute-done((bf16[3,1024]{1,0:T(4,128)(2,1)S(1)}, bf16[3,1024]{1,0:T(4,128)(2,1)S(1)}, u32[]{:S(2)}, u32[]{:S(2)}) %collective-permute-start.3) | collective-permute-done | bytes 6176 | tf_op jit(solution)/shard_map/ppermute | solution.py:17
  26.4 0.3 multiply_reduce_fusion.2
  26.8 0.9 %broadcast_multiply_fusion = (f32[4,64,256]{2,1,0:T(8,128)}, f32[4,64,256]{2,1,0:T(8,128)S(1)}) fusion(f32[4,256]{1,0:T(4,128)S(1)} %pad_maximum_fusion.11, f32[4,64]{1,0:T(4,128)S(1)} %get-tuple-element.91, f32[4,64,256]{2,1,0:T(8,128)S(1)} %convolution_bitcast_fusion, f32[4,64,256]{2,1,0:T(8,128)S(1)} %bitcast.125), kind=kLoop, calls=%fused_computation.116 | loop fusion | flops 589824 | bytes 1053696 | tf_op jit(solution)/shard_map/mul | solution.py:85
  28.0 0.6 fusion.48
  28.9 0.4 convolution_bitcast_fusion.2
  29.3 2.5 %collective-permute-start.4 = (bf16[257,512]{1,0:T(8,128)(2,1)S(1)}, bf16[257,512]{1,0:T(8,128)(2,1)S(1)}, u32[]{:S(2)}, u32[]{:S(2)}) collective-permute-start(bf16[257,512]{1,0:T(8,128)(2,1)S(1)} %pad_maximum_fusion.4), channel_id=1, source_target_pairs={{0,4},{4,8},{8,12},{12,16},{16,20},{20,24},{24,28},{1,5},{5,9},{9,... | collective-permute-start | bytes 789512 | tf_op jit(solution)/shard_map/ppermute | solution.py:17
  31.8 1.0 %convolution_bitcast_fusion.3 = f32[1,64,512]{2,1,0:T(8,128)} fusion(f32[4,256,512]{2,1,0:T(8,128)S(1)} %fusion.48, f32[256]{0:T(256)S(1)} %get-tuple-element.95, f32[4,64,256]{2,1,0:T(8,128)S(1)} %get-tuple-element.69), kind=kOutput, calls=%fused_computation.20 | convolution fusion | flops 50462720 | bytes 721920 | tf_op jit(solution)/shard_map/dot_general | solution.py:80
  32.8 1.1 %convolution_bitcast_fusion.1 = f32[1,64,512]{2,1,0:T(8,128)} fusion(f32[4,256,512]{2,1,0:T(8,128)S(1)} %fusion.48, f32[256]{0:T(256)S(1)} %bitcast.139, f32[4,64,256]{2,1,0:T(8,128)S(1)} %get-tuple-element.69, f32[256]{0:T(256)S(1)} %bitcast.136, f32[256]{0:T(256)S(1)} %get-tuple-element.95), kind=kOutput, calls=%fused_computation.18 | convolution fusion | flops 50987008 | bytes 1772544 | tf_op jit(solution)/shard_map/dot_general | solution.py:80
  33.9 5.9 %collective-permute-done.4 = bf16[257,512]{1,0:T(8,128)(2,1)S(1)} collective-permute-done((bf16[257,512]{1,0:T(8,128)(2,1)S(1)}, bf16[257,512]{1,0:T(8,128)(2,1)S(1)}, u32[]{:S(2)}, u32[]{:S(2)}) %collective-permute-start.4) | collective-permute-done | bytes 263200 | tf_op jit(solution)/shard_map/ppermute | solution.py:17
  39.8 0.6 subtract_convert_fusion
  40.6 0.7 pad_maximum_fusion.5
  41.3 1.3 %collective-permute-start.5 = (bf16[257,512]{1,0:T(8,128)(2,1)}, bf16[257,512]{1,0:T(8,128)(2,1)}, u32[]{:S(2)}, u32[]{:S(2)}) collective-permute-start(bf16[257,512]{1,0:T(8,128)(2,1)} %pad_maximum_fusion.5), channel_id=1, source_target_pairs={{0,8},{4,12},{8,16},{12,20},{16,24},{20,28},{1,9},{5,13},{9,17},{1... | collective-permute-start | bytes 789512 | tf_op jit(solution)/shard_map/ppermute | solution.py:17
  42.6 2.8 %convolution_add_fusion = f32[4,64,512]{2,1,0:T(8,128)} fusion(f32[1,64,512]{2,1,0:T(8,128)} %convolution_bitcast_fusion.1, f32[1,64,512]{2,1,0:T(8,128)S(1)} %convolution_bitcast_fusion.2, f32[1,64,512]{2,1,0:T(8,128)} %convolution_bitcast_fusion.3, f32[4]{0:T(128)} %pad.32.clone, f32[4,64,256]{2,1,0:T(8,128)} %copy-done.7, s32[4,64]{1,0:T(4,128)S(1)} %eq.38, ...), kind=kOutput, calls=%fused_computation.8 | convolution fusion | flops 27525120 | bytes 2233360 | tf_op jit(solution)/shard_map/bac,bcv->bav/dot_general | solution.py:71
  45.4 5.0 %collective-permute-done.5 = bf16[257,512]{1,0:T(8,128)(2,1)} collective-permute-done((bf16[257,512]{1,0:T(8,128)(2,1)}, bf16[257,512]{1,0:T(8,128)(2,1)}, u32[]{:S(2)}, u32[]{:S(2)}) %collective-permute-start.5) | collective-permute-done | bytes 263200 | tf_op jit(solution)/shard_map/ppermute | solution.py:17
  50.4 1.3 %fusion.77 = bf16[256,512]{1,0:T(8,128)(2,1)S(1)} fusion(f32[256,512]{1,0:T(8,128)} %copy-done.1, bf16[257,512]{1,0:T(8,128)(2,1)S(1)} %collective-permute-done.4, f32[256]{0:T(256)S(1)} %get-tuple-element.67, pred[]{:T(512)S(6)} %ge.73, bf16[257,512]{1,0:T(8,128)(2,1)} %collective-permute-done.5, f32[256]{0:T(256)} %get-tuple-element.62, pred[]{:T(512)S(6)} %ge.72), kind=kLoop, calls=%fused_computation.175 | loop fusion | flops 1179648 | bytes 1312770 | tf_op jit(solution)/shard_map/convert_element_type | solution.py:119
  51.8 1.3 %collective-permute-start.6 = (bf16[256,512]{1,0:T(8,128)(2,1)S(1)}, bf16[256,512]{1,0:T(8,128)(2,1)S(1)}, u32[]{:S(2)}, u32[]{:S(2)}) collective-permute-start(bf16[256,512]{1,0:T(8,128)(2,1)S(1)} %fusion.77), channel_id=1, source_target_pairs={{0,16},{4,20},{8,24},{12,28},{1,17},{5,21},{9,25},{13,29},{2,18},{... | collective-permute-start | bytes 786440 | tf_op jit(solution)/shard_map/ppermute | solution.py:17
  53.1 0.7 slice_convert_fusion
  53.8 0.7 multiply_select_fusion
  54.5 11.5 %collective-permute-done.6 = bf16[256,512]{1,0:T(8,128)(2,1)S(1)} collective-permute-done((bf16[256,512]{1,0:T(8,128)(2,1)S(1)}, bf16[256,512]{1,0:T(8,128)(2,1)S(1)}, u32[]{:S(2)}, u32[]{:S(2)}) %collective-permute-start.6) | collective-permute-done | bytes 262176 | tf_op jit(solution)/shard_map/ppermute | solution.py:17
  65.9 2.0 %multiply_reduce_fusion.3 = (f32[256]{0:T(256)S(1)}, f32[256,512]{1,0:T(8,128)S(1)}) fusion(f32[256,512]{1,0:T(8,128)} %bitcast.148, f32[256,256]{1,0:T(8,128)} %bitcast.130, bf16[256,512]{1,0:T(8,128)(2,1)S(1)} %collective-permute-done.6, f32[256]{0:T(256)} %bitcast.145, f32[256]{0:T(256)S(1)} %get-tuple-element.94, pred[]{:T(512)S(6)} %ge.72, ...), kind=kOutput, calls=%fused_computation.54 | convolution fusion | flops 202899200 | bytes 2100226 | tf_op jit(solution)/shard_map/dot_general | solution.py:268
  67.9 0.8 multiply_convert_fusion
  68.8 0.4 convolution_convert_fusion
  69.3 1.9 %collective-permute-done.7 = bf16[128,2048]{1,0:T(8,128)(2,1)S(1)} collective-permute-done((bf16[128,2048]{1,0:T(8,128)(2,1)S(1)}, bf16[128,2048]{1,0:T(8,128)(2,1)S(1)}, u32[]{:S(2)}, u32[]{:S(2)}) %collective-permute-start.7) | collective-permute-done | bytes 524320 | tf_op jit(solution)/shard_map/ppermute | solution.py:186
  71.2 0.4 convert_add_fusion
  71.7 1.6 %collective-permute-start.8 = (bf16[1,64,2048]{2,1,0:T(8,128)(2,1)S(1)}, bf16[1,64,2048]{2,1,0:T(8,128)(2,1)S(1)}, u32[]{:S(2)}, u32[]{:S(2)}) collective-permute-start(bf16[1,64,2048]{2,1,0:T(8,128)(2,1)S(1)} %fusion.24), channel_id=1, source_target_pairs={{0,2},{1,3},{2,0},{3,1},{4,6},{5,7},{6,4},{7,5},{8,10},{9,11},{10,... | collective-permute-start | bytes 786440 | tf_op jit(solution)/shard_map/ppermute | solution.py:197
  73.3 2.2 %fusion.4 = f32[1,1,256,512]{3,2,1,0:T(8,128)} fusion(bf16[256,512]{1,0:T(8,128)(2,1)S(1)} %copy-done.12, f32[256]{0:T(256)S(1)} %get-tuple-element.93, pred[]{:T(512)S(6)} %ge.71, f32[256,512]{1,0:T(8,128)S(1)} %copy-done.2, bf16[257,512]{1,0:T(8,128)(2,1)S(1)} %collective-permute-done.4, f32[256]{0:T(256)S(1)} %get-tuple-element.67, pred[]{:T(512)S(6)} %ge.73, ...), kind=kLoop, calls=%fused_computation.38 | loop fusion | flops 1572864 | bytes 1838083 | tf_op jit(solution)/shard_map/broadcast_in_dim | solution.py:277
  75.6 4.6 %collective-permute-done.8 = bf16[1,64,2048]{2,1,0:T(8,128)(2,1)S(1)} collective-permute-done((bf16[1,64,2048]{2,1,0:T(8,128)(2,1)S(1)}, bf16[1,64,2048]{2,1,0:T(8,128)(2,1)S(1)}, u32[]{:S(2)}, u32[]{:S(2)}) %collective-permute-start.8) | collective-permute-done | bytes 262176 | tf_op jit(solution)/shard_map/ppermute | solution.py:197
  80.1 0.8 fusion.6
  (76 shorter events, 2.5 us)
Async XLA Ops:
  0.6 68.1 %copy-start = (bf16[512,2048]{1,0:T(8,128)(2,1)S(1)}, bf16[512,2048]{1,0:T(8,128)(2,1)}, u32[]{:S(2)}) copy-start(bf16[512,2048]{1,0:T(8,128)(2,1)} %param.31) | copy-start | bytes 6291460
  0.6 11.6 %collective-permute-start = (bf16[64,2048]{1,0:T(8,128)(2,1)}, bf16[64,2048]{1,0:T(8,128)(2,1)S(1)}, u32[]{:S(2)}, u32[]{:S(2)}) collective-permute-start(bf16[64,2048]{1,0:T(8,128)(2,1)} %param.18), channel_id=1, source_target_pairs={{0,1},{1,0},{2,3},{3,2},{4,5},{5,4},{6,7},{7,6},{8,9},{9,8},{10,11... | collective-permute-start | bytes 786440 | tf_op jit(solution)/shard_map/ppermute | solution.py:151
  0.7 8.9 %collective-permute-start.1 = (bf16[64,2048]{1,0:T(8,128)(2,1)}, bf16[64,2048]{1,0:T(8,128)(2,1)S(1)}, u32[]{:S(2)}, u32[]{:S(2)}) collective-permute-start(bf16[64,2048]{1,0:T(8,128)(2,1)} %param.18), channel_id=1, source_target_pairs={{0,2},{1,3},{2,0},{3,1},{4,6},{5,7},{6,4},{7,5},{8,10},{9,11},{10,... | collective-permute-start | bytes 786440 | tf_op jit(solution)/shard_map/ppermute | solution.py:151
  9.6 2.6 %collective-permute-start.2 = (bf16[64,2048]{1,0:T(8,128)(2,1)S(1)}, bf16[64,2048]{1,0:T(8,128)(2,1)}, u32[]{:S(2)}, u32[]{:S(2)}) collective-permute-start(bf16[64,2048]{1,0:T(8,128)(2,1)S(1)} %collective-permute-done.1), channel_id=1, source_target_pairs={{0,1},{1,0},{2,3},{3,2},{4,5},{5,4},{6,7},{7,6},{8,9},{9,8},{10,11... | collective-permute-start | bytes 786440 | tf_op jit(solution)/shard_map/ppermute | solution.py:151
  12.3 2.0 %copy-start.18 = (bf16[2048,16]{0,1:T(8,128)(2,1)S(1)}, bf16[2048,16]{0,1:T(8,128)(2,1)}, u32[]{:S(2)}) copy-start(bf16[2048,16]{0,1:T(8,128)(2,1)} %param.26) | copy-start | bytes 196612
  12.3 2.0 %copy-start.19 = (bf16[16,256]{1,0:T(8,128)(2,1)S(1)}, bf16[16,256]{1,0:T(8,128)(2,1)}, u32[]{:S(2)}) copy-start(bf16[16,256]{1,0:T(8,128)(2,1)} %param.27) | copy-start | bytes 24580
  12.3 2.0 %copy-start.21 = (f32[256]{0:T(256)S(1)}, f32[256]{0:T(256)}, u32[]{:S(2)}) copy-start(f32[256]{0:T(256)} %param.28) | copy-start | bytes 3076
  12.3 0.7 copy-start.3
  15.1 2.2 %copy-start.16 = (bf16[2048,512]{1,0:T(8,128)(2,1)S(1)}, bf16[2048,512]{1,0:T(8,128)(2,1)}, u32[]{:S(2)}) copy-start(bf16[2048,512]{1,0:T(8,128)(2,1)} %param.22) | copy-start | bytes 6291460
  15.4 12.6 %copy-start.7 = (f32[4,64,256]{2,1,0:T(8,128)}, f32[4,64,256]{2,1,0:T(8,128)S(1)}, u32[]{:S(2)}) copy-start(f32[4,64,256]{2,1,0:T(8,128)S(1)} %convolution_bitcast_fusion) | copy-start | bytes 786436
  17.3 1.2 %copy-start.8 = (bf16[2048,256]{1,0:T(8,128)(2,1)S(1)}, bf16[2048,256]{1,0:T(8,128)(2,1)}, u32[]{:S(2)}) copy-start(bf16[2048,256]{1,0:T(8,128)(2,1)} %param.21) | copy-start | bytes 3145732
  19.7 6.4 %collective-permute-start.3 = (bf16[3,1024]{1,0:T(4,128)(2,1)S(1)}, bf16[3,1024]{1,0:T(4,128)(2,1)S(1)}, u32[]{:S(2)}, u32[]{:S(2)}) collective-permute-start(bf16[3,1024]{1,0:T(4,128)(2,1)S(1)} %get-tuple-element.59), channel_id=1, source_target_pairs={{0,4},{4,8},{8,12},{12,16},{16,20},{20,24},{24,28},{1,5},{5,9},{9,... | collective-permute-start | bytes 18440 | tf_op jit(solution)/shard_map/ppermute | solution.py:17
  26.8 1.2 %copy-start.9 = (f32[256,256]{1,0:T(8,128)}, f32[256,256]{1,0:T(8,128)S(1)}, u32[]{:S(2)}) copy-start(f32[256,256]{1,0:T(8,128)S(1)} %get-tuple-element.56) | copy-start | bytes 786436
  26.8 1.8 %copy-start.13 = (f32[256,256]{1,0:T(8,128)}, f32[256,256]{1,0:T(8,128)S(1)}, u32[]{:S(2)}) copy-start(f32[256,256]{1,0:T(8,128)S(1)} %get-tuple-element.57) | copy-start | bytes 786436
  28.0 0.9 %copy-start.10 = (f32[256,512]{1,0:T(8,128)}, f32[256,512]{1,0:T(8,128)S(1)}, u32[]{:S(2)}) copy-start(f32[256,512]{1,0:T(8,128)S(1)} %multiply_reduce_fusion) | copy-start | bytes 1572868
  28.9 12.5 %copy-start.1 = (f32[256,512]{1,0:T(8,128)}, f32[256,512]{1,0:T(8,128)S(1)}, u32[]{:S(2)}) copy-start(f32[256,512]{1,0:T(8,128)S(1)} %get-tuple-element.64) | copy-start | bytes 1572868
  29.3 10.5 %collective-permute-start.4 = (bf16[257,512]{1,0:T(8,128)(2,1)S(1)}, bf16[257,512]{1,0:T(8,128)(2,1)S(1)}, u32[]{:S(2)}, u32[]{:S(2)}) collective-permute-start(bf16[257,512]{1,0:T(8,128)(2,1)S(1)} %pad_maximum_fusion.4), channel_id=1, source_target_pairs={{0,4},{4,8},{8,12},{12,16},{16,20},{20,24},{24,28},{1,5},{5,9},{9,... | collective-permute-start | bytes 789512 | tf_op jit(solution)/shard_map/ppermute | solution.py:17
  39.8 0.6 copy-start.15
  41.3 9.1 %collective-permute-start.5 = (bf16[257,512]{1,0:T(8,128)(2,1)}, bf16[257,512]{1,0:T(8,128)(2,1)}, u32[]{:S(2)}, u32[]{:S(2)}) collective-permute-start(bf16[257,512]{1,0:T(8,128)(2,1)} %pad_maximum_fusion.5), channel_id=1, source_target_pairs={{0,8},{4,12},{8,16},{12,20},{16,24},{20,28},{1,9},{5,13},{9,17},{1... | collective-permute-start | bytes 789512 | tf_op jit(solution)/shard_map/ppermute | solution.py:17
  45.4 22.5 %copy-start.17 = (bf16[2048,512]{1,0:T(8,128)(2,1)S(1)}, bf16[2048,512]{1,0:T(8,128)(2,1)}, u32[]{:S(2)}) copy-start(bf16[2048,512]{1,0:T(8,128)(2,1)} %param.29) | copy-start | bytes 6291460
  45.4 22.5 %copy-start.20 = (f32[512]{0:T(512)S(1)}, f32[512]{0:T(512)}, u32[]{:S(2)}) copy-start(f32[512]{0:T(512)} %param.30) | copy-start | bytes 6148
  51.8 14.1 %collective-permute-start.6 = (bf16[256,512]{1,0:T(8,128)(2,1)S(1)}, bf16[256,512]{1,0:T(8,128)(2,1)S(1)}, u32[]{:S(2)}, u32[]{:S(2)}) collective-permute-start(bf16[256,512]{1,0:T(8,128)(2,1)S(1)} %fusion.77), channel_id=1, source_target_pairs={{0,16},{4,20},{8,24},{12,28},{1,17},{5,21},{9,25},{13,29},{2,18},{... | collective-permute-start | bytes 786440 | tf_op jit(solution)/shard_map/ppermute | solution.py:17
  65.9 2.0 %copy-start.11 = (bf16[256,512]{1,0:T(8,128)(2,1)}, bf16[256,512]{1,0:T(8,128)(2,1)S(1)}, u32[]{:S(2)}) copy-start(bf16[256,512]{1,0:T(8,128)(2,1)S(1)} %collective-permute-done.6) | copy-start | bytes 786436
  69.2 2.0 %collective-permute-start.7 = (bf16[128,2048]{1,0:T(8,128)(2,1)S(1)}, bf16[128,2048]{1,0:T(8,128)(2,1)S(1)}, u32[]{:S(2)}, u32[]{:S(2)}) collective-permute-start(bf16[128,2048]{1,0:T(8,128)(2,1)S(1)} %convolution_convert_fusion), channel_id=1, source_target_pairs={{0,1},{1,0},{2,3},{3,2},{4,5},{5,4},{6,7},{7,6},{8,9},{9,8},{10,11... | collective-permute-start | bytes 1572872 | tf_op jit(solution)/shard_map/ppermute | solution.py:186
  71.2 2.1 %copy-start.2 = (f32[256,512]{1,0:T(8,128)S(1)}, f32[256,512]{1,0:T(8,128)}, u32[]{:S(2)}) copy-start(f32[256,512]{1,0:T(8,128)} %copy-done.1) | copy-start | bytes 1572868
  71.2 2.1 %copy-start.12 = (bf16[256,512]{1,0:T(8,128)(2,1)S(1)}, bf16[256,512]{1,0:T(8,128)(2,1)}, u32[]{:S(2)}) copy-start(bf16[256,512]{1,0:T(8,128)(2,1)} %copy-done.11) | copy-start | bytes 786436
  71.2 2.1 %copy-start.14 = (f32[256]{0:T(256)S(1)}, f32[256]{0:T(256)}, u32[]{:S(2)}) copy-start(f32[256]{0:T(256)} %get-tuple-element.62) | copy-start | bytes 3076
  71.7 8.4 %collective-permute-start.8 = (bf16[1,64,2048]{2,1,0:T(8,128)(2,1)S(1)}, bf16[1,64,2048]{2,1,0:T(8,128)(2,1)S(1)}, u32[]{:S(2)}, u32[]{:S(2)}) collective-permute-start(bf16[1,64,2048]{2,1,0:T(8,128)(2,1)S(1)} %fusion.24), channel_id=1, source_target_pairs={{0,2},{1,3},{2,0},{3,1},{4,6},{5,7},{6,4},{7,5},{8,10},{9,11},{10,... | collective-permute-start | bytes 786440 | tf_op jit(solution)/shard_map/ppermute | solution.py:197
